TPU v7x, 768 devices: a whole 4x8x12 slice. The times are simulated.
768 devices in a mesh: ctx: 96 (over y, z), head: 8 (over x, core).
Axes of the slice: x: 4, y: 8, z: 12, core: 2. Of those that a mesh axis runs over, the one named last changes fastest.
Arguments:
- queries: bfloat16 [256, 12288], P('head', 'ctx'), may hold values from -6 to 6
- keys: bfloat16 [256, 12288], P('head', 'ctx'), may hold values from -6 to 6
- values: bfloat16 [12288, 2048], P('ctx', 'head'), may hold values from -6 to 6
- seg_ids: int32 [12288], P('ctx'), may hold values from 0 to 11, never falling along the last dimension, each value on 1 to 2048 neighbouring positions
- conv_weight: bfloat16 [3, 256], P(None, 'head'), may hold values from -3.5 to 3.5
- out_weight: bfloat16 [2048, 4096], P('head'), may hold values from -0.125 to 0.125
- out_grad: bfloat16 [12288, 4096], P('ctx', 'head'), may hold values from -6 to 6
Outputs:
- grad_queries: float32 [256, 12288], P('head', 'ctx')
- grad_keys: float32 [256, 12288], P('head', 'ctx')
- grad_values: float32 [12288, 2048], P('ctx', 'head')
Inputs may be any that keep to these rules, and one draw needn't show every extreme that they name: `seg_ids`: document numbers never fall along the sequence; each document holds 1 to 2048 tokens, and one holds exactly 2048.
All inputs are finite; a program needn't handle non-finite values.
Results may differ from a plain program's by a relative error of at most 0.0005.
Values may be sent and summed in bfloat16 or wider, within the bound.
No kernel may reach another device: no remote copies, remote signals or barrier semaphores. Data moves between devices by JAX's collectives and lax.ppermute only.
A program may use at most 64 MiB of HBM per device.

v0:
```python
import jax
import jax.numpy as jnp
import numpy as np
from jax import lax
from jax.sharding import PartitionSpec as P

FD = 16


half_root = 0.7071067811865476
split_mode = lax.Precision.HIGH


def entering(shard, axis, combine, identity, reverse):
    size, here = (lax.axis_size(axis), lax.axis_index(axis))
    everything = jax.tree.map(lambda part: lax.all_gather(part, axis), shard)
    start = jax.tree.map(
        lambda part, zero: jnp.broadcast_to(jnp.asarray(zero, part.dtype), part.shape),
        shard,
        identity,
    )

    def step(k, before):
        at = size - 1 - k if reverse else k
        reached = at > here if reverse else at < here
        new = combine(before, jax.tree.map(lambda part: part[at], everything))
        return jax.tree.map(lambda a, b: jnp.where(reached, a, b), new, before)

    return lax.fori_loop(0, size, step, start)


def features(entries):
    scaled = entries * 0.5
    row_index, col_index = np.triu_indices(scaled.shape[-2], 1)
    cross = jnp.take(scaled, row_index, axis=-2) * jnp.take(scaled, col_index, axis=-2)
    return jnp.concatenate(
        [jnp.ones_like(scaled[..., :1, :]), scaled, scaled * scaled * half_root, cross], axis=-2
    )


def block_output(q_feat, k_feat, head_values, doc_ids, carry_mask, state_in, normer_in):
    length = doc_ids.shape[0]
    causal = jnp.arange(length)[:, None] >= jnp.arange(length)[None, :]
    allowed = (causal & (doc_ids[:, None] == doc_ids[None, :])).astype(jnp.float32)
    scores = jnp.einsum("hft,hfs->hts", q_feat, k_feat, precision=split_mode) * allowed[None, :, :]
    numerator = jnp.einsum("hts,shd->thd", scores, head_values, precision=split_mode)
    numerator = numerator + carry_mask[:, None, None] * jnp.einsum(
        "hft,hfd->thd", q_feat, state_in, precision=split_mode
    )
    denominator = jnp.sum(scores, axis=2).T + carry_mask[:, None] * jnp.einsum(
        "hft,hf->th", q_feat, normer_in, precision=split_mode
    )
    return numerator / denominator[:, :, None]


def join_forward(earlier, later):
    empty_later = later[0][1] == 0.0
    same_doc = earlier[0][1] == later[0][1]
    state_out = jnp.where(empty_later, earlier[2], later[2] + jnp.where(same_doc, earlier[2], 0.0))
    normer_out = jnp.where(empty_later, earlier[3], later[3] + jnp.where(same_doc, earlier[3], 0.0))
    return (
        jnp.where(empty_later, earlier[0], later[0]),
        jnp.where(empty_later, earlier[1], later[1]),
        state_out,
        normer_out,
    )


def join_backward(earlier, later):
    empty_later = later[0][0] == 0.0
    same_doc = earlier[0][0] == later[0][0]
    state_out = jnp.where(empty_later, earlier[2], later[2] + jnp.where(same_doc, earlier[2], 0.0))
    normer_out = jnp.where(empty_later, earlier[3], later[3] + jnp.where(same_doc, earlier[3], 0.0))
    return (
        jnp.where(empty_later, earlier[0], later[0]),
        jnp.where(empty_later, earlier[1], later[1]),
        state_out,
        normer_out,
    )


def body(queries, keys, values, seg_ids, conv_weight, out_weight, out_grad):
    local_heads = queries.shape[0] // FD
    length = queries.shape[1]
    head_width = values.shape[1] // local_heads
    grad_attn = lax.dot_general(
        lax.all_gather(out_grad, "head", axis=1, tiled=True),
        out_weight,
        (((1,), (1,)), ((), ())),
        preferred_element_type=jnp.float32,
    )
    doc_ids = (seg_ids + 1).astype(jnp.float32)
    query_rows = queries.astype(jnp.float32)
    key_heads = keys.astype(jnp.float32).reshape(local_heads, FD, length)
    head_values = values.astype(jnp.float32).reshape(length, local_heads, head_width)
    taps = conv_weight.astype(jnp.float32)
    k_feat, feature_pullback = jax.vjp(features, key_heads)
    tail_mask = (doc_ids == doc_ids[length - 1]).astype(jnp.float32)
    tail_feat = k_feat * tail_mask[None, None, :]
    tail_state = jnp.einsum("hfs,shd->hfd", tail_feat, head_values, precision=split_mode)
    tail_normer = jnp.sum(tail_feat, axis=2)
    forward_piece = (doc_ids[length - 2 :], query_rows[:, length - 2 :], tail_state, tail_normer)
    before = entering(
        forward_piece, "ctx", join_forward, jax.tree.map(jnp.zeros_like, forward_piece), False
    )
    query_ext = jnp.concatenate([before[1], query_rows], axis=1)
    ids_before = jnp.concatenate([before[0], doc_ids])
    q_conv = taps[0][:, None] * query_rows
    for offset in (1, 2):
        same_doc = (ids_before[2 - offset : 2 - offset + length] == doc_ids).astype(jnp.float32)
        q_conv = (
            q_conv
            + taps[offset][:, None]
            * query_ext[:, 2 - offset : 2 - offset + length]
            * same_doc[None, :]
        )
    carry_mask = (doc_ids == before[0][1]).astype(jnp.float32)

    def local_forward(q_conv_in, k_feat_in, values_in, state_in, normer_in):
        q_feat = features(q_conv_in.reshape(local_heads, FD, length))
        result = block_output(
            q_feat, k_feat_in, values_in, doc_ids, carry_mask, state_in, normer_in
        )
        return result.reshape(length, local_heads * head_width)

    _, local_pullback = jax.vjp(local_forward, q_conv, k_feat, head_values, before[2], before[3])
    grad_qconv, grad_kfeat, grad_heads, grad_state, grad_normer = local_pullback(grad_attn)
    backward_piece = (doc_ids[:2], grad_qconv[:, :2], grad_state, grad_normer)
    after = entering(
        backward_piece, "ctx", join_backward, jax.tree.map(jnp.zeros_like, backward_piece), True
    )
    head_mask = (doc_ids == after[0][0]).astype(jnp.float32)
    flowing = (
        jnp.einsum("hfd,shd->hfs", after[2], head_values, precision=split_mode)
        + after[3][:, :, None]
    )
    grad_kfeat = grad_kfeat + flowing * head_mask[None, None, :]
    grad_heads = grad_heads + jnp.einsum(
        "hfs,hfd->shd", k_feat * head_mask[None, None, :], after[2], precision=split_mode
    )
    (grad_key_heads,) = feature_pullback(grad_kfeat)
    grad_ext = jnp.concatenate([grad_qconv, after[1]], axis=1)
    ids_after = jnp.concatenate([doc_ids, after[0]])
    grad_queries = taps[0][:, None] * grad_qconv
    for offset in (1, 2):
        same_doc = (ids_after[offset : offset + length] == doc_ids).astype(jnp.float32)
        grad_queries = (
            grad_queries
            + taps[offset][:, None] * grad_ext[:, offset : offset + length] * same_doc[None, :]
        )
    grad_keys = grad_key_heads.reshape(local_heads * FD, length)
    grad_values = grad_heads.reshape(length, local_heads * head_width)
    return (grad_queries, grad_keys, grad_values)


def solution(mesh):
    in_specs = (
        P("head", "ctx"),
        P("head", "ctx"),
        P("ctx", "head"),
        P("ctx"),
        P(None, "head"),
        P("head", None),
        P("ctx", "head"),
    )
    out_specs = (P("head", "ctx"), P("head", "ctx"), P("ctx", "head"))
    return jax.shard_map(body, mesh=mesh, in_specs=in_specs, out_specs=out_specs, check_vma=False)
```

profile of v0, /device:TPU:6, one launch (start us, length us, event | category | flops | bytes accessed | tf_op | source)
XLA Modules:
  0.0 1527.4 jit_solution(17527857951042291656)
XLA Ops:
  12.7 1.3 compare_convert_fusion.6
  14.8 1.7 fusion.8
  21.1 224.2 %all-reduce.2 = (f32[192]{0:T(256)S(1)}, f32[192]{0:T(256)}) all-reduce(f32[192]{0:T(256)S(1)} %slice_dynamic-update-slice_fusion.1, f32[192]{0:T(256)S(1)} %slice_dynamic-update-slice_fusion), channel_id=2, replica_groups=mesh['ctx'=96,'head'=8] {'ctx'}, use_global_device_ids=true, to_apply=%add | all-reduce | flops 384 | bytes 3072
  245.4 65.1 %all-gather.8 = f32[96,32,2]{1,2,0:T(2,128)S(1)} all-gather(f32[1,32,2]{1,2,0:T(2,128)S(1)} %bitcast.228), channel_id=3, replica_groups=mesh['ctx'=96,'head'=8] {'ctx'}, dimensions={0}, use_global_device_ids=true | all-gather | bytes 24832 | tf_op jit(solution)/shard_map/all_gather | solution.py:16
  310.8 74.4 %all-gather.9 = f32[96,2,153]{2,1,0:T(2,128)S(1)} all-gather(f32[1,2,153]{2,1,0:T(2,128)S(1)} %bitcast.226), channel_id=5, replica_groups=mesh['ctx'=96,'head'=8] {'ctx'}, dimensions={0}, use_global_device_ids=true | all-gather | bytes 118728 | tf_op jit(solution)/shard_map/all_gather | solution.py:16
  385.9 1.9 fusion.60
  387.9 404.8 %while.42 = (s32[]{:T(128)}, f32[2]{0:T(128)S(1)}, f32[32,2]{0,1:T(2,128)S(1)}, f32[2,153,128]{2,1,0:T(8,128)S(1)}, f32[2,153]{1,0:T(2,128)S(1)}, /*index=5*/s32...) while((s32[]{:T(128)}, f32[2]{0:T(128)S(1)}, ...), condition=%wide.region_2.4_spmd.clone, body=%wide.region_1.3_spmd.clone.sunk | while | flops 197574 | bytes 474723 | solution.py:29
  793.5 1.4 compare_convert_fusion.4
  797.4 1.4 fusion.59
  799.5 1.6 fusion.13
  801.1 1.4 reshape.170
  810.1 5.2 scatter_fusion
  815.4 5.4 scatter_fusion.1
  820.9 70.6 %all-gather.10 = f32[96,32,2]{1,2,0:T(2,128)} all-gather(f32[1,32,2]{1,2,0:T(2,128)S(1)} %bitcast.229), channel_id=7, replica_groups=mesh['ctx'=96,'head'=8] {'ctx'}, dimensions={0}, use_global_device_ids=true | all-gather | bytes 24832 | tf_op jit(solution)/shard_map/all_gather | solution.py:16
  891.4 75.1 %all-gather.11 = f32[96,2,153]{2,1,0:T(2,128)S(1)} all-gather(f32[1,2,153]{2,1,0:T(2,128)} %bitcast.227), channel_id=9, replica_groups=mesh['ctx'=96,'head'=8] {'ctx'}, dimensions={0}, use_global_device_ids=true | all-gather | bytes 118728 | tf_op jit(solution)/shard_map/all_gather | solution.py:16
  968.7 533.1 %while.43 = (s32[]{:T(128)}, f32[2]{0:T(128)}, f32[32,2]{0,1:T(2,128)}, f32[2,153,128]{2,1,0:T(8,128)S(1)}, f32[2,153]{1,0:T(2,128)}, /*index=5*/s32[]{:T(128)},...) while((s32[]{:T(128)}, f32[2]{0:T(128)}, ...), condition=%wide.region_8.10_spmd.clone, body=%wide.region_7.9_spmd.clone.sunk | while | flops 197578 | bytes 474769 | solution.py:29
  1002.1 1.3 select_select_fusion.15
  1007.7 1.3 select_select_fusion.15
  1024.3 1.3 select_select_fusion.15
  1035.4 1.3 select_select_fusion.15
  1041.0 1.3 select_select_fusion.15
  1057.7 1.3 select_select_fusion.15
  1068.8 1.3 select_select_fusion.15
  1096.5 1.3 select_select_fusion.15
  1140.9 1.3 select_select_fusion.15
  1146.5 1.3 select_select_fusion.15
  1190.9 1.3 select_select_fusion.15
  1202.0 1.3 select_select_fusion.15
  1218.8 1.3 select_select_fusion.15
  1229.9 1.3 select_select_fusion.15
  1241.0 1.3 select_select_fusion.15
  1257.7 1.3 select_select_fusion.15
  1263.3 1.3 select_select_fusion.15
  1291.1 1.3 select_select_fusion.15
  1324.5 1.3 select_select_fusion.15
  1380.0 1.3 select_select_fusion.15
  1385.6 1.3 select_select_fusion.15
  1402.3 1.3 select_select_fusion.15
  1413.4 1.3 select_select_fusion.15
  1419.0 1.3 select_select_fusion.15
  1435.7 1.3 select_select_fusion.15
  1469.1 1.3 select_select_fusion.15
  1474.7 1.3 select_select_fusion.15
  1497.0 1.3 select_select_fusion.15
  1502.5 1.4 compare_convert_fusion.2
  1508.3 5.2 scatter_fusion.2
  1513.5 5.4 scatter_fusion.3
  1519.5 1.4 fusion.40
  (1229 shorter events, 729.5 us)
Async XLA Ops:
  7.2 378.8 %copy-start = (bf16[256,4096]{1,0:T(8,128)(2,1)S(1)}, bf16[256,4096]{1,0:T(8,128)(2,1)}, u32[]{:S(2)}) copy-start(bf16[256,4096]{1,0:T(8,128)(2,1)} %param.22) | copy-start | bytes 6291460
  7.2 1496.6 %copy-start.1 = (bf16[128,256]{1,0:T(8,128)(2,1)S(1)}, bf16[128,256]{1,0:T(8,128)(2,1)}, u32[]{:S(2)}) copy-start(bf16[128,256]{1,0:T(8,128)(2,1)} %param.19) | copy-start | bytes 196612
  7.2 378.7 %all-gather.16.cloned.1.call-start = ((), (), s32[]{:S(2)}) async-start(), calls=%async_computation | async-start | bytes 1179648 | tf_op jit(solution)/shard_map/all_gather | solution.py:87
  7.9 379.9 %all-gather.18.cloned.1.call-start = ((), (), s32[]{:S(2)}) async-start(), calls=%async_computation.1 | async-start | bytes 15892480 | tf_op jit(solution)/shard_map/all_gather | solution.py:16
  8.6 787.1 %copy-start.5 = (f32[128]{0:T(128)}, f32[128]{0:T(128)S(1)}, u32[]{:S(2)}) copy-start(f32[128]{0:T(128)S(1)} %add_convert_fusion) | copy-start | bytes 1540
  12.7 373.2 %copy-start.4 = (f32[153]{0:T(256)}, f32[153]{0:T(256)S(1)}, u32[]{:S(2)}) copy-start(f32[153]{0:T(256)S(1)} %pad.12.clone) | copy-start | bytes 1840
  16.6 952.1 %all-gather.20.cloned.1.call-start = ((), (), s32[]{:S(2)}) async-start(), calls=%async_computation.2 | async-start | bytes 15892480 | tf_op jit(solution)/shard_map/all_gather | solution.py:16
  385.2 410.6 %copy-start.7 = (f32[32]{0:T(128)}, f32[32]{0:T(128)S(1)}, u32[]{:S(2)}) copy-start(f32[32]{0:T(128)S(1)} %get-tuple-element.574) | copy-start | bytes 388
  385.2 410.6 %copy-start.8 = (f32[32]{0:T(128)}, f32[32]{0:T(128)S(1)}, u32[]{:S(2)}) copy-start(f32[32]{0:T(128)S(1)} %get-tuple-element.575) | copy-start | bytes 388
  385.2 410.6 %copy-start.9 = (f32[32]{0:T(128)}, f32[32]{0:T(128)S(1)}, u32[]{:S(2)}) copy-start(f32[32]{0:T(128)S(1)} %get-tuple-element.576) | copy-start | bytes 388
  792.7 3.0 copy-start.3
  794.8 6.3 copy-start.6
  798.8 8.2 copy-start.2
  799.5 1.7 copy-start.10
Sparse Core Ops, SparseCore 0:
  10.4 37.4 all-gather.15
  51.6 171.1 all-gather.17
  801.2 161.8 all-gather.19
where the time goes:
time: 1550 us; the launch traced here: 1530 us
  other arithmetic  592 us (38%)
  blocking collectives  509 us (33%)
  loops' own time  203 us (13%)
  local copies, waits for them, and re-layouts  189 us (12%)
  matrix products  17.8 us (1%)
    select_n x768, other arithmetic, step(): return jax.tree.map(lambda a, b: jnp.where(reached, a, b), new, before)  556 us
    all_gather x4, blocking collectives, entering(): everything = jax.tree.map(lambda part: lax.all_gather(part, axis), shard)  285 us
    unnamed x1, blocking collectives  224 us
    another operation x2, loops' own time, entering(): return lax.fori_loop(0, size, step, start)  203 us
    dynamic_slice x192, local copies, waits for them, and re-layouts, step(): new = combine(before, jax.tree.map(lambda part: part[at], everything))  66.9 us
    slice x96, local copies, waits for them, and re-layouts, join_forward(): empty_later = later[0][1] == 0.0  55.8 us
    slice x96, local copies, waits for them, and re-layouts, join_forward(): same_doc = earlier[0][1] == later[0][1]  55.8 us
  transfers between devices with their start and end apart: 3, of which 0 were waited for; matrix products, arithmetic and copies ran while one was open for 2% of the time, Pallas kernels for 0%

commit v1 on v0

--- a/solution.py
+++ b/solution.py
@@ -5,28 +5,30 @@
 from jax.sharding import PartitionSpec as P
 
 FD = 16
+MOST = 2048
 
 
 half_root = 0.7071067811865476
 split_mode = lax.Precision.HIGH
 
 
-def entering(shard, axis, combine, identity, reverse):
-    size, here = (lax.axis_size(axis), lax.axis_index(axis))
-    everything = jax.tree.map(lambda part: lax.all_gather(part, axis), shard)
-    start = jax.tree.map(
-        lambda part, zero: jnp.broadcast_to(jnp.asarray(zero, part.dtype), part.shape),
-        shard,
-        identity,
-    )
+def shifted(piece, axis, step, reverse):
+    size = lax.axis_size(axis)
+    if reverse:
+        pairs = [(source, source - step) for source in range(step, size)]
+    else:
+        pairs = [(source, source + step) for source in range(size - step)]
+    return lax.ppermute(piece, axis, pairs)
 
-    def step(k, before):
-        at = size - 1 - k if reverse else k
-        reached = at > here if reverse else at < here
-        new = combine(before, jax.tree.map(lambda part: part[at], everything))
-        return jax.tree.map(lambda a, b: jnp.where(reached, a, b), new, before)
 
-    return lax.fori_loop(0, size, step, start)
+def entering(shard, axis, combine, reverse, reach):
+    size = lax.axis_size(axis)
+    total = shifted(shard, axis, 1, reverse)
+    step = 1
+    while step < reach and step < size:
+        total = combine(shifted(total, axis, step, reverse), total)
+        step *= 2
+    return total
 
 
 def features(entries):
@@ -83,6 +85,7 @@
     local_heads = queries.shape[0] // FD
     length = queries.shape[1]
     head_width = values.shape[1] // local_heads
+    reach = -(-(MOST - 1) // length)
     grad_attn = lax.dot_general(
         lax.all_gather(out_grad, "head", axis=1, tiled=True),
         out_weight,
@@ -100,9 +103,7 @@
     tail_state = jnp.einsum("hfs,shd->hfd", tail_feat, head_values, precision=split_mode)
     tail_normer = jnp.sum(tail_feat, axis=2)
     forward_piece = (doc_ids[length - 2 :], query_rows[:, length - 2 :], tail_state, tail_normer)
-    before = entering(
-        forward_piece, "ctx", join_forward, jax.tree.map(jnp.zeros_like, forward_piece), False
-    )
+    before = entering(forward_piece, "ctx", join_forward, False, reach)
     query_ext = jnp.concatenate([before[1], query_rows], axis=1)
     ids_before = jnp.concatenate([before[0], doc_ids])
     q_conv = taps[0][:, None] * query_rows
@@ -126,9 +127,7 @@
     _, local_pullback = jax.vjp(local_forward, q_conv, k_feat, head_values, before[2], before[3])
     grad_qconv, grad_kfeat, grad_heads, grad_state, grad_normer = local_pullback(grad_attn)
     backward_piece = (doc_ids[:2], grad_qconv[:, :2], grad_state, grad_normer)
-    after = entering(
-        backward_piece, "ctx", join_backward, jax.tree.map(jnp.zeros_like, backward_piece), True
-    )
+    after = entering(backward_piece, "ctx", join_backward, True, reach)
     head_mask = (doc_ids == after[0][0]).astype(jnp.float32)
     flowing = (
         jnp.einsum("hfd,shd->hfs", after[2], head_values, precision=split_mode)

time: 1550 us -> 359 us (0.23)
  the two profiles are of different devices: /device:TPU:6 before, /device:TPU:108 now
where the time goes in v1:
time: 359 us; the launch traced here: 357 us
  starting transfers between devices  191 us (53%)
  waiting for transfers between devices  89.4 us (25%)
  other arithmetic  29.7 us (8%)
  between operations  26.6 us (7%)
  local copies, waits for them, and re-layouts  11.3 us (3%)
  matrix products  9.89 us (3%)
    ppermute x40, starting transfers between devices, shifted(): return lax.ppermute(piece, axis, pairs)  191 us
    ppermute x40, waiting for transfers between devices, shifted(): return lax.ppermute(piece, axis, pairs)  88.7 us
    scatter-add x2, other arithmetic, features(): jnp.take(scaled, row_index, axis=-2) * jnp.take(scaled, col_index, axis=-2)  10.5 us
    scatter-add x2, other arithmetic, features(): jnp.take(scaled, col_index, axis=-2)  10.1 us
  transfers between devices with their start and end apart: 41, of which 19 were waited for; matrix products, arithmetic and copies ran while one was open for 7% of the time, Pallas kernels for 0%

profile of v1, /device:TPU:108, one launch (start us, length us, event | category | flops | bytes accessed | tf_op | source)
XLA Modules:
  0.0 357.5 jit_solution(10180992036546081674)
XLA Ops:
  10.6 4.3 %collective-permute-start = (f32[2]{0:T(128)S(1)}, f32[2]{0:T(128)S(1)}, u32[]{:S(2)}, u32[]{:S(2)}) collective-permute-start(f32[2]{0:T(128)S(1)} %get-tuple-element.53), channel_id=1, source_target_pairs={{0,8},{8,16},{16,24},{24,32},{32,40},{40,48},{48,56},{56,64},{64,7... | collective-permute-start | bytes 32 | tf_op jit(solution)/shard_map/ppermute | solution.py:21
  15.6 4.3 %collective-permute-start.10 = (f32[32,2]{1,0:T(8,128)S(1)}, f32[32,2]{1,0:T(8,128)S(1)}, u32[]{:S(2)}, u32[]{:S(2)}) collective-permute-start(f32[32,2]{1,0:T(8,128)S(1)} %slice.155), channel_id=1, source_target_pairs={{0,8},{8,16},{16,24},{24,32},{32,40},{40,48},{48,56},{56,64},{64,7... | collective-permute-start | bytes 776 | tf_op jit(solution)/shard_map/ppermute | solution.py:21
  28.3 9.5 %collective-permute-start.21 = (f32[2]{0:T(128)S(1)}, f32[2]{0:T(128)S(1)}, u32[]{:S(2)}, u32[]{:S(2)}) collective-permute-start(f32[2]{0:T(128)S(1)} %collective-permute-done.20), channel_id=1, source_target_pairs={{8,0},{16,8},{24,16},{32,24},{40,32},{48,40},{56,48},{64,56},{72,6... | collective-permute-start | bytes 32 | tf_op jit(solution)/shard_map/ppermute | solution.py:21
  39.8 5.6 %collective-permute-done.1 = f32[2]{0:T(128)S(1)} collective-permute-done((f32[2]{0:T(128)S(1)}, f32[2]{0:T(128)S(1)}, u32[]{:S(2)}, u32[]{:S(2)}) %collective-permute-start.1) | collective-permute-done | bytes 40 | tf_op jit(solution)/shard_map/ppermute | solution.py:21
  48.0 6.9 %collective-permute-start.22 = (f32[2]{0:T(128)S(1)}, f32[2]{0:T(128)S(1)}, u32[]{:S(2)}, u32[]{:S(2)}) collective-permute-start(f32[2]{0:T(128)S(1)} %broadcast_select_fusion.11), channel_id=1, source_target_pairs={{16,0},{24,8},{32,16},{40,24},{48,32},{56,40},{64,48},{72,56},{80,... | collective-permute-start | bytes 32 | tf_op jit(solution)/shard_map/ppermute | solution.py:21
  59.9 8.7 %collective-permute-start.23 = (f32[2]{0:T(128)S(1)}, f32[2]{0:T(128)S(1)}, u32[]{:S(2)}, u32[]{:S(2)}) collective-permute-start(f32[2]{0:T(128)S(1)} %broadcast_select_fusion.10), channel_id=1, source_target_pairs={{32,0},{40,8},{48,16},{56,24},{64,32},{72,40},{80,48},{88,56},{96,... | collective-permute-start | bytes 32 | tf_op jit(solution)/shard_map/ppermute | solution.py:21
  73.6 8.7 %collective-permute-start.29 = (f32[2]{0:T(128)S(1)}, f32[2]{0:T(128)S(1)}, u32[]{:S(2)}, u32[]{:S(2)}) collective-permute-start(f32[2]{0:T(128)S(1)} %broadcast_select_fusion.9), channel_id=1, source_target_pairs={{64,0},{72,8},{80,16},{88,24},{96,32},{104,40},{112,48},{120,56},{... | collective-permute-start | bytes 32 | tf_op jit(solution)/shard_map/ppermute | solution.py:21
  86.2 3.3 collective-permute-start.11
  89.5 2.0 compare_convert_fusion
  91.5 2.4 collective-permute-done.11
  93.9 6.3 %collective-permute-start.12 = (f32[32,2]{1,0:T(8,128)S(1)}, f32[32,2]{1,0:T(8,128)S(1)}, u32[]{:S(2)}, u32[]{:S(2)}) collective-permute-start(f32[32,2]{1,0:T(8,128)S(1)} %broadcast_select_fusion.4), channel_id=1, source_target_pairs={{0,16},{8,24},{16,32},{24,40},{32,48},{40,56},{48,64},{56,72},{64,... | collective-permute-start | bytes 776 | tf_op jit(solution)/shard_map/ppermute | solution.py:21
  100.5 4.8 %collective-permute-start.4 = (f32[2,153]{1,0:T(2,128)S(1)}, f32[2,153]{1,0:T(2,128)S(1)}, u32[]{:S(2)}, u32[]{:S(2)}) collective-permute-start(f32[2,153]{1,0:T(2,128)S(1)} %multiply_reduce_fusion), channel_id=1, source_target_pairs={{0,8},{8,16},{16,24},{24,32},{32,40},{40,48},{48,56},{56,64},{64,7... | collective-permute-start | bytes 3680 | tf_op jit(solution)/shard_map/ppermute | solution.py:21
  105.3 3.2 collective-permute-start.13
  109.6 6.1 %collective-permute-done.13 = f32[32,2]{1,0:T(8,128)S(1)} collective-permute-done((f32[32,2]{1,0:T(8,128)S(1)}, f32[32,2]{1,0:T(8,128)S(1)}, u32[]{:S(2)}, u32[]{:S(2)}) %collective-permute-start.13) | collective-permute-done | bytes 288 | tf_op jit(solution)/shard_map/ppermute | solution.py:21
  115.7 2.9 collective-permute-start.14
  122.5 2.5 collective-permute-start.5
  128.0 7.3 %collective-permute-start.6 = (f32[2,153]{1,0:T(2,128)S(1)}, f32[2,153]{1,0:T(2,128)S(1)}, u32[]{:S(2)}, u32[]{:S(2)}) collective-permute-start(f32[2,153]{1,0:T(2,128)S(1)} %add_select_fusion.19), channel_id=1, source_target_pairs={{0,16},{8,24},{16,32},{24,40},{32,48},{40,56},{48,64},{56,72},{64,... | collective-permute-start | bytes 3680 | tf_op jit(solution)/shard_map/ppermute | solution.py:21
  136.6 5.9 %collective-permute-start.7 = (f32[2,153]{1,0:T(2,128)S(1)}, f32[2,153]{1,0:T(2,128)S(1)}, u32[]{:S(2)}, u32[]{:S(2)}) collective-permute-start(f32[2,153]{1,0:T(2,128)S(1)} %add_select_fusion.18), channel_id=1, source_target_pairs={{0,32},{8,40},{16,48},{24,56},{32,64},{40,72},{48,80},{56,88},{64,... | collective-permute-start | bytes 3680 | tf_op jit(solution)/shard_map/ppermute | solution.py:21
  143.1 3.8 %collective-permute-done.7 = f32[2,153]{1,0:T(2,128)S(1)} collective-permute-done((f32[2,153]{1,0:T(2,128)S(1)}, f32[2,153]{1,0:T(2,128)S(1)}, u32[]{:S(2)}, u32[]{:S(2)}) %collective-permute-start.7) | collective-permute-done | bytes 1256 | tf_op jit(solution)/shard_map/ppermute | solution.py:21
  146.9 4.1 %collective-permute-start.8 = (f32[2,153]{1,0:T(2,128)S(1)}, f32[2,153]{1,0:T(2,128)S(1)}, u32[]{:S(2)}, u32[]{:S(2)}) collective-permute-start(f32[2,153]{1,0:T(2,128)S(1)} %add_select_fusion.17), channel_id=1, source_target_pairs={{0,64},{8,72},{16,80},{24,88},{32,96},{40,104},{48,112},{56,120},{... | collective-permute-start | bytes 3680 | tf_op jit(solution)/shard_map/ppermute | solution.py:21
  151.4 2.7 collective-permute-start.16
  154.1 5.3 %collective-permute-done.8 = f32[2,153]{1,0:T(2,128)S(1)} collective-permute-done((f32[2,153]{1,0:T(2,128)S(1)}, f32[2,153]{1,0:T(2,128)S(1)}, u32[]{:S(2)}, u32[]{:S(2)}) %collective-permute-start.8) | collective-permute-done | bytes 1256 | tf_op jit(solution)/shard_map/ppermute | solution.py:21
  159.4 5.7 %collective-permute-start.17 = (f32[2,153,128]{2,1,0:T(8,128)S(1)}, f32[2,153,128]{2,1,0:T(8,128)S(1)}, u32[]{:S(2)}, u32[]{:S(2)}) collective-permute-start(f32[2,153,128]{2,1,0:T(8,128)S(1)} %add_select_fusion.7), channel_id=1, source_target_pairs={{0,16},{8,24},{16,32},{24,40},{32,48},{40,56},{48,64},{56,72},{64,... | collective-permute-start | bytes 470024 | tf_op jit(solution)/shard_map/ppermute | solution.py:21
  165.3 7.3 %collective-permute-done.17 = f32[2,153,128]{2,1,0:T(8,128)S(1)} collective-permute-done((f32[2,153,128]{2,1,0:T(8,128)S(1)}, f32[2,153,128]{2,1,0:T(8,128)S(1)}, u32[]{:S(2)}, u32[]{:S(2)}) %collective-permute-start.17) | collective-permute-done | bytes 156704 | tf_op jit(solution)/shard_map/ppermute | solution.py:21
  172.7 3.4 collective-permute-start.18
  176.1 11.4 %collective-permute-done.18 = f32[2,153,128]{2,1,0:T(8,128)S(1)} collective-permute-done((f32[2,153,128]{2,1,0:T(8,128)S(1)}, f32[2,153,128]{2,1,0:T(8,128)S(1)}, u32[]{:S(2)}, u32[]{:S(2)}) %collective-permute-start.18) | collective-permute-done | bytes 156704 | tf_op jit(solution)/shard_map/ppermute | solution.py:21
  187.5 5.3 %collective-permute-start.19 = (f32[2,153,128]{2,1,0:T(8,128)S(1)}, f32[2,153,128]{2,1,0:T(8,128)}, u32[]{:S(2)}, u32[]{:S(2)}) collective-permute-start(f32[2,153,128]{2,1,0:T(8,128)S(1)} %add_select_fusion.5), channel_id=1, source_target_pairs={{0,64},{8,72},{16,80},{24,88},{32,96},{40,104},{48,112},{56,120},{... | collective-permute-start | bytes 470024 | tf_op jit(solution)/shard_map/ppermute | solution.py:21
  194.8 15.7 %collective-permute-done.19 = f32[2,153,128]{2,1,0:T(8,128)} collective-permute-done((f32[2,153,128]{2,1,0:T(8,128)S(1)}, f32[2,153,128]{2,1,0:T(8,128)}, u32[]{:S(2)}, u32[]{:S(2)}) %collective-permute-start.19) | collective-permute-done | bytes 156704 | tf_op jit(solution)/shard_map/ppermute | solution.py:21
  213.9 5.1 %scatter_fusion = f32[2,16,128]{2,0,1:T(2,128)S(1)} fusion(f32[2,16,128]{2,0,1:T(2,128)S(1)} %copy.79, s32[120]{0:T(128)S(1)} %copy-done.7, f32[120,2,128]{2,1,0:T(2,128)S(1)} %copy.80), kind=kCustom, calls=%fused_computation.4 | custom fusion | flops 30720 | bytes 369120 | tf_op jit(solution)/shard_map/transpose(jvp(jit(_take)))/scatter-add | solution.py:37
  219.0 5.3 %scatter_fusion.1 = f32[2,16,128]{2,0,1:T(2,128)S(1)} fusion(f32[2,16,128]{2,0,1:T(2,128)S(1)} %broadcast_in_dim.64.clone, s32[120]{0:T(128)S(1)} %copy-done.6, f32[120,2,128]{2,1,0:T(2,128)S(1)} %copy.81), kind=kCustom, calls=%fused_computation.5 | custom fusion | flops 30720 | bytes 369120 | tf_op jit(solution)/shard_map/transpose(jvp(jit(_take)))/scatter-add | solution.py:37
  230.0 2.3 collective-permute-start.25
  233.5 2.2 collective-permute-done.25
  235.6 11.3 %collective-permute-start.26 = (f32[32,2]{1,0:T(8,128)S(1)}, f32[32,2]{1,0:T(8,128)S(1)}, u32[]{:S(2)}, u32[]{:S(2)}) collective-permute-start(f32[32,2]{1,0:T(8,128)S(1)} %broadcast_select_fusion), channel_id=1, source_target_pairs={{16,0},{24,8},{32,16},{40,24},{48,32},{56,40},{64,48},{72,56},{80,... | collective-permute-start | bytes 776 | tf_op jit(solution)/shard_map/ppermute | solution.py:21
  248.4 6.3 %collective-permute-start.27 = (f32[32,2]{1,0:T(8,128)S(1)}, f32[32,2]{1,0:T(8,128)S(1)}, u32[]{:S(2)}, u32[]{:S(2)}) collective-permute-start(f32[32,2]{1,0:T(8,128)S(1)} %broadcast_select_fusion.1), channel_id=1, source_target_pairs={{32,0},{40,8},{48,16},{56,24},{64,32},{72,40},{80,48},{88,56},{96,... | collective-permute-start | bytes 776 | tf_op jit(solution)/shard_map/ppermute | solution.py:21
  255.0 2.7 collective-permute-start.35
  258.0 10.8 %collective-permute-start.28 = (f32[32,2]{1,0:T(8,128)S(1)}, f32[32,2]{1,0:T(8,128)S(1)}, u32[]{:S(2)}, u32[]{:S(2)}) collective-permute-start(f32[32,2]{1,0:T(8,128)S(1)} %broadcast_select_fusion.2), channel_id=1, source_target_pairs={{64,0},{72,8},{80,16},{88,24},{96,32},{104,40},{112,48},{120,56},{... | collective-permute-start | bytes 776 | tf_op jit(solution)/shard_map/ppermute | solution.py:21
  269.2 9.2 %collective-permute-start.30 = (f32[2,153,128]{2,1,0:T(8,128)S(1)}, f32[2,153,128]{2,1,0:T(8,128)S(1)}, u32[]{:S(2)}, u32[]{:S(2)}) collective-permute-start(f32[2,153,128]{2,1,0:T(8,128)S(1)} %fusion.13), channel_id=1, source_target_pairs={{8,0},{16,8},{24,16},{32,24},{40,32},{48,40},{56,48},{64,56},{72,6... | collective-permute-start | bytes 470024 | tf_op jit(solution)/shard_map/ppermute | solution.py:21
  281.3 4.4 %collective-permute-start.31 = (f32[2,153,128]{2,1,0:T(8,128)S(1)}, f32[2,153,128]{2,1,0:T(8,128)S(1)}, u32[]{:S(2)}, u32[]{:S(2)}) collective-permute-start(f32[2,153,128]{2,1,0:T(8,128)S(1)} %collective-permute-done.30), channel_id=1, source_target_pairs={{8,0},{16,8},{24,16},{32,24},{40,32},{48,40},{56,48},{64,56},{72,6... | collective-permute-start | bytes 470024 | tf_op jit(solution)/shard_map/ppermute | solution.py:21
  285.7 3.5 collective-permute-start.37
  289.2 4.7 %collective-permute-done.31 = f32[2,153,128]{2,1,0:T(8,128)S(1)} collective-permute-done((f32[2,153,128]{2,1,0:T(8,128)S(1)}, f32[2,153,128]{2,1,0:T(8,128)S(1)}, u32[]{:S(2)}, u32[]{:S(2)}) %collective-permute-start.31) | collective-permute-done | bytes 156704 | tf_op jit(solution)/shard_map/ppermute | solution.py:21
  293.9 6.5 %collective-permute-start.32 = (f32[2,153,128]{2,1,0:T(8,128)S(1)}, f32[2,153,128]{2,1,0:T(8,128)S(1)}, u32[]{:S(2)}, u32[]{:S(2)}) collective-permute-start(f32[2,153,128]{2,1,0:T(8,128)S(1)} %add_select_fusion.3), channel_id=1, source_target_pairs={{16,0},{24,8},{32,16},{40,24},{48,32},{56,40},{64,48},{72,56},{80,... | collective-permute-start | bytes 470024 | tf_op jit(solution)/shard_map/ppermute | solution.py:21
  300.4 9.0 %collective-permute-start.38 = (f32[2,153]{1,0:T(2,128)S(1)}, f32[2,153]{1,0:T(2,128)S(1)}, u32[]{:S(2)}, u32[]{:S(2)}) collective-permute-start(f32[2,153]{1,0:T(2,128)S(1)} %add_select_fusion.14), channel_id=1, source_target_pairs={{32,0},{40,8},{48,16},{56,24},{64,32},{72,40},{80,48},{88,56},{96,... | collective-permute-start | bytes 3680 | tf_op jit(solution)/shard_map/ppermute | solution.py:21
  309.5 4.1 %collective-permute-start.33 = (f32[2,153,128]{2,1,0:T(8,128)S(1)}, f32[2,153,128]{2,1,0:T(8,128)S(1)}, u32[]{:S(2)}, u32[]{:S(2)}) collective-permute-start(f32[2,153,128]{2,1,0:T(8,128)S(1)} %add_select_fusion.2), channel_id=1, source_target_pairs={{32,0},{40,8},{48,16},{56,24},{64,32},{72,40},{80,48},{88,56},{96,... | collective-permute-start | bytes 470024 | tf_op jit(solution)/shard_map/ppermute | solution.py:21
  313.6 3.4 collective-permute-start.39
  317.0 8.1 %collective-permute-done.33 = f32[2,153,128]{2,1,0:T(8,128)S(1)} collective-permute-done((f32[2,153,128]{2,1,0:T(8,128)S(1)}, f32[2,153,128]{2,1,0:T(8,128)S(1)}, u32[]{:S(2)}, u32[]{:S(2)}) %collective-permute-start.33) | collective-permute-done | bytes 156704 | tf_op jit(solution)/shard_map/ppermute | solution.py:21
  327.1 10.9 %collective-permute-done.34 = f32[2,153,128]{2,1,0:T(8,128)S(1)} collective-permute-done((f32[2,153,128]{2,1,0:T(8,128)S(1)}, f32[2,153,128]{2,1,0:T(8,128)S(1)}, u32[]{:S(2)}, u32[]{:S(2)}) %collective-permute-start.34) | collective-permute-done | bytes 156704 | tf_op jit(solution)/shard_map/ppermute | solution.py:21
  339.6 5.1 %scatter_fusion.2 = f32[2,16,128]{2,0,1:T(2,128)S(1)} fusion(f32[2,16,128]{2,0,1:T(2,128)S(1)} %copy.86, s32[120]{0:T(128)S(1)} %copy-done.7, f32[120,2,128]{2,1,0:T(2,128)S(1)} %copy.87), kind=kCustom, calls=%fused_computation.6 | custom fusion | flops 30720 | bytes 369120 | tf_op jit(solution)/shard_map/transpose(jvp(jit(_take)))/scatter-add | solution.py:37
  344.7 5.3 %scatter_fusion.3 = f32[2,16,128]{2,0,1:T(2,128)S(1)} fusion(f32[2,16,128]{2,0,1:T(2,128)S(1)} %broadcast_in_dim.64.clone.1, s32[120]{0:T(128)S(1)} %copy-done.6, f32[120,2,128]{2,1,0:T(2,128)S(1)} %copy.88), kind=kCustom, calls=%fused_computation.7 | custom fusion | flops 30720 | bytes 369120 | tf_op jit(solution)/shard_map/transpose(jvp(jit(_take)))/scatter-add | solution.py:37
  (174 shorter events, 51.4 us)
Async XLA Ops:
  7.2 185.6 %copy-start = (bf16[256,4096]{1,0:T(8,128)(2,1)S(1)}, bf16[256,4096]{1,0:T(8,128)(2,1)}, u32[]{:S(2)}) copy-start(bf16[256,4096]{1,0:T(8,128)(2,1)} %param.18) | copy-start | bytes 6291460
  7.2 143.9 %copy-start.1 = (bf16[128,256]{1,0:T(8,128)(2,1)S(1)}, bf16[128,256]{1,0:T(8,128)(2,1)}, u32[]{:S(2)}) copy-start(bf16[128,256]{1,0:T(8,128)(2,1)} %param.15) | copy-start | bytes 196612
  7.2 185.6 %all-gather.2.cloned.1.call-start = ((), (), s32[]{:S(2)}) async-start(), calls=%async_computation | async-start | bytes 1179648 | tf_op jit(solution)/shard_map/all_gather | solution.py:90
  8.7 17.6 %collective-permute-start.20 = (f32[2]{0:T(128)S(1)}, f32[2]{0:T(128)S(1)}, u32[]{:S(2)}, u32[]{:S(2)}) collective-permute-start(f32[2]{0:T(128)S(1)} %get-tuple-element.52), channel_id=1, source_target_pairs={{8,0},{16,8},{24,16},{32,24},{40,32},{48,40},{56,48},{64,56},{72,6... | collective-permute-start | bytes 32 | tf_op jit(solution)/shard_map/ppermute | solution.py:21
  10.6 16.5 %collective-permute-start = (f32[2]{0:T(128)S(1)}, f32[2]{0:T(128)S(1)}, u32[]{:S(2)}, u32[]{:S(2)}) collective-permute-start(f32[2]{0:T(128)S(1)} %get-tuple-element.53), channel_id=1, source_target_pairs={{0,8},{8,16},{16,24},{24,32},{32,40},{40,48},{48,56},{56,64},{64,7... | collective-permute-start | bytes 32 | tf_op jit(solution)/shard_map/ppermute | solution.py:21
  15.6 70.5 %collective-permute-start.10 = (f32[32,2]{1,0:T(8,128)S(1)}, f32[32,2]{1,0:T(8,128)S(1)}, u32[]{:S(2)}, u32[]{:S(2)}) collective-permute-start(f32[32,2]{1,0:T(8,128)S(1)} %slice.155), channel_id=1, source_target_pairs={{0,8},{8,16},{16,24},{24,32},{32,40},{40,48},{48,56},{56,64},{64,7... | collective-permute-start | bytes 776 | tf_op jit(solution)/shard_map/ppermute | solution.py:21
  22.7 128.4 %copy-start.4 = (f32[128,128]{0,1:T(8,128)}, f32[128,128]{0,1:T(8,128)S(1)}, u32[]{:S(2)}) copy-start(f32[128,128]{0,1:T(8,128)S(1)} %fusion.34) | copy-start | bytes 196612
  28.3 19.6 %collective-permute-start.21 = (f32[2]{0:T(128)S(1)}, f32[2]{0:T(128)S(1)}, u32[]{:S(2)}, u32[]{:S(2)}) collective-permute-start(f32[2]{0:T(128)S(1)} %collective-permute-done.20), channel_id=1, source_target_pairs={{8,0},{16,8},{24,16},{32,24},{40,32},{48,40},{56,48},{64,56},{72,6... | collective-permute-start | bytes 32 | tf_op jit(solution)/shard_map/ppermute | solution.py:21
  37.9 7.5 %collective-permute-start.1 = (f32[2]{0:T(128)S(1)}, f32[2]{0:T(128)S(1)}, u32[]{:S(2)}, u32[]{:S(2)}) collective-permute-start(f32[2]{0:T(128)S(1)} %collective-permute-done), channel_id=1, source_target_pairs={{0,8},{8,16},{16,24},{24,32},{32,40},{40,48},{48,56},{56,64},{64,7... | collective-permute-start | bytes 32 | tf_op jit(solution)/shard_map/ppermute | solution.py:21
  46.0 11.4 %collective-permute-start.2 = (f32[2]{0:T(128)S(1)}, f32[2]{0:T(128)S(1)}, u32[]{:S(2)}, u32[]{:S(2)}) collective-permute-start(f32[2]{0:T(128)S(1)} %broadcast_select_fusion.15), channel_id=1, source_target_pairs={{0,16},{8,24},{16,32},{24,40},{32,48},{40,56},{48,64},{56,72},{64,... | collective-permute-start | bytes 32 | tf_op jit(solution)/shard_map/ppermute | solution.py:21
  48.0 41.5 %copy-start.8 = (f32[2]{0:T(128)}, f32[2]{0:T(128)S(1)}, u32[]{:S(2)}) copy-start(f32[2]{0:T(128)S(1)} %broadcast_select_fusion.11) | copy-start | bytes 28
  48.0 11.9 %collective-permute-start.22 = (f32[2]{0:T(128)S(1)}, f32[2]{0:T(128)S(1)}, u32[]{:S(2)}, u32[]{:S(2)}) collective-permute-start(f32[2]{0:T(128)S(1)} %broadcast_select_fusion.11), channel_id=1, source_target_pairs={{16,0},{24,8},{32,16},{40,24},{48,32},{56,40},{64,48},{72,56},{80,... | collective-permute-start | bytes 32 | tf_op jit(solution)/shard_map/ppermute | solution.py:21
  58.0 13.1 %collective-permute-start.3 = (f32[2]{0:T(128)S(1)}, f32[2]{0:T(128)S(1)}, u32[]{:S(2)}, u32[]{:S(2)}) collective-permute-start(f32[2]{0:T(128)S(1)} %broadcast_select_fusion.14), channel_id=1, source_target_pairs={{0,32},{8,40},{16,48},{24,56},{32,64},{40,72},{48,80},{56,88},{64,... | collective-permute-start | bytes 32 | tf_op jit(solution)/shard_map/ppermute | solution.py:21
  59.9 13.7 %collective-permute-start.23 = (f32[2]{0:T(128)S(1)}, f32[2]{0:T(128)S(1)}, u32[]{:S(2)}, u32[]{:S(2)}) collective-permute-start(f32[2]{0:T(128)S(1)} %broadcast_select_fusion.10), channel_id=1, source_target_pairs={{32,0},{40,8},{48,16},{56,24},{64,32},{72,40},{80,48},{88,56},{96,... | collective-permute-start | bytes 32 | tf_op jit(solution)/shard_map/ppermute | solution.py:21
  71.7 13.3 %collective-permute-start.9 = (f32[2]{0:T(128)S(1)}, f32[2]{0:T(128)S(1)}, u32[]{:S(2)}, u32[]{:S(2)}) collective-permute-start(f32[2]{0:T(128)S(1)} %broadcast_select_fusion.13), channel_id=1, source_target_pairs={{0,64},{8,72},{16,80},{24,88},{32,96},{40,104},{48,112},{56,120},{... | collective-permute-start | bytes 32 | tf_op jit(solution)/shard_map/ppermute | solution.py:21
  73.6 11.3 %collective-permute-start.29 = (f32[2]{0:T(128)S(1)}, f32[2]{0:T(128)S(1)}, u32[]{:S(2)}, u32[]{:S(2)}) collective-permute-start(f32[2]{0:T(128)S(1)} %broadcast_select_fusion.9), channel_id=1, source_target_pairs={{64,0},{72,8},{80,16},{88,24},{96,32},{104,40},{112,48},{120,56},{... | collective-permute-start | bytes 32 | tf_op jit(solution)/shard_map/ppermute | solution.py:21
  86.2 7.7 %collective-permute-start.11 = (f32[32,2]{1,0:T(8,128)S(1)}, f32[32,2]{1,0:T(8,128)S(1)}, u32[]{:S(2)}, u32[]{:S(2)}) collective-permute-start(f32[32,2]{1,0:T(8,128)S(1)} %collective-permute-done.10), channel_id=1, source_target_pairs={{0,8},{8,16},{16,24},{24,32},{32,40},{40,48},{48,56},{56,64},{64,7... | collective-permute-start | bytes 776 | tf_op jit(solution)/shard_map/ppermute | solution.py:21
  93.9 11.4 %collective-permute-start.12 = (f32[32,2]{1,0:T(8,128)S(1)}, f32[32,2]{1,0:T(8,128)S(1)}, u32[]{:S(2)}, u32[]{:S(2)}) collective-permute-start(f32[32,2]{1,0:T(8,128)S(1)} %broadcast_select_fusion.4), channel_id=1, source_target_pairs={{0,16},{8,24},{16,32},{24,40},{32,48},{40,56},{48,64},{56,72},{64,... | collective-permute-start | bytes 776 | tf_op jit(solution)/shard_map/ppermute | solution.py:21
  100.5 22.0 %collective-permute-start.4 = (f32[2,153]{1,0:T(2,128)S(1)}, f32[2,153]{1,0:T(2,128)S(1)}, u32[]{:S(2)}, u32[]{:S(2)}) collective-permute-start(f32[2,153]{1,0:T(2,128)S(1)} %multiply_reduce_fusion), channel_id=1, source_target_pairs={{0,8},{8,16},{16,24},{24,32},{32,40},{40,48},{48,56},{56,64},{64,7... | collective-permute-start | bytes 3680 | tf_op jit(solution)/shard_map/ppermute | solution.py:21
  105.3 10.5 %collective-permute-start.13 = (f32[32,2]{1,0:T(8,128)S(1)}, f32[32,2]{1,0:T(8,128)S(1)}, u32[]{:S(2)}, u32[]{:S(2)}) collective-permute-start(f32[32,2]{1,0:T(8,128)S(1)} %broadcast_select_fusion.5), channel_id=1, source_target_pairs={{0,32},{8,40},{16,48},{24,56},{32,64},{40,72},{48,80},{56,88},{64,... | collective-permute-start | bytes 776 | tf_op jit(solution)/shard_map/ppermute | solution.py:21
  115.7 10.4 %collective-permute-start.14 = (f32[32,2]{1,0:T(8,128)S(1)}, f32[32,2]{1,0:T(8,128)S(1)}, u32[]{:S(2)}, u32[]{:S(2)}) collective-permute-start(f32[32,2]{1,0:T(8,128)S(1)} %broadcast_select_fusion.6), channel_id=1, source_target_pairs={{0,64},{8,72},{16,80},{24,88},{32,96},{40,104},{48,112},{56,120},{... | collective-permute-start | bytes 776 | tf_op jit(solution)/shard_map/ppermute | solution.py:21
  120.6 30.8 %collective-permute-start.15 = (f32[2,153,128]{2,1,0:T(8,128)S(1)}, f32[2,153,128]{2,1,0:T(8,128)S(1)}, u32[]{:S(2)}, u32[]{:S(2)}) collective-permute-start(f32[2,153,128]{2,1,0:T(8,128)S(1)} %fusion.8), channel_id=1, source_target_pairs={{0,8},{8,16},{16,24},{24,32},{32,40},{40,48},{48,56},{56,64},{64,7... | collective-permute-start | bytes 470024 | tf_op jit(solution)/shard_map/ppermute | solution.py:21
  122.5 5.5 %collective-permute-start.5 = (f32[2,153]{1,0:T(2,128)S(1)}, f32[2,153]{1,0:T(2,128)S(1)}, u32[]{:S(2)}, u32[]{:S(2)}) collective-permute-start(f32[2,153]{1,0:T(2,128)S(1)} %collective-permute-done.4), channel_id=1, source_target_pairs={{0,8},{8,16},{16,24},{24,32},{32,40},{40,48},{48,56},{56,64},{64,7... | collective-permute-start | bytes 3680 | tf_op jit(solution)/shard_map/ppermute | solution.py:21
  128.0 8.6 %collective-permute-start.6 = (f32[2,153]{1,0:T(2,128)S(1)}, f32[2,153]{1,0:T(2,128)S(1)}, u32[]{:S(2)}, u32[]{:S(2)}) collective-permute-start(f32[2,153]{1,0:T(2,128)S(1)} %add_select_fusion.19), channel_id=1, source_target_pairs={{0,16},{8,24},{16,32},{24,40},{32,48},{40,56},{48,64},{56,72},{64,... | collective-permute-start | bytes 3680 | tf_op jit(solution)/shard_map/ppermute | solution.py:21
  136.6 10.3 %collective-permute-start.7 = (f32[2,153]{1,0:T(2,128)S(1)}, f32[2,153]{1,0:T(2,128)S(1)}, u32[]{:S(2)}, u32[]{:S(2)}) collective-permute-start(f32[2,153]{1,0:T(2,128)S(1)} %add_select_fusion.18), channel_id=1, source_target_pairs={{0,32},{8,40},{16,48},{24,56},{32,64},{40,72},{48,80},{56,88},{64,... | collective-permute-start | bytes 3680 | tf_op jit(solution)/shard_map/ppermute | solution.py:21
  146.9 12.4 %collective-permute-start.8 = (f32[2,153]{1,0:T(2,128)S(1)}, f32[2,153]{1,0:T(2,128)S(1)}, u32[]{:S(2)}, u32[]{:S(2)}) collective-permute-start(f32[2,153]{1,0:T(2,128)S(1)} %add_select_fusion.17), channel_id=1, source_target_pairs={{0,64},{8,72},{16,80},{24,88},{32,96},{40,104},{48,112},{56,120},{... | collective-permute-start | bytes 3680 | tf_op jit(solution)/shard_map/ppermute | solution.py:21
  151.4 8.0 %collective-permute-start.16 = (f32[2,153,128]{2,1,0:T(8,128)S(1)}, f32[2,153,128]{2,1,0:T(8,128)S(1)}, u32[]{:S(2)}, u32[]{:S(2)}) collective-permute-start(f32[2,153,128]{2,1,0:T(8,128)S(1)} %collective-permute-done.15), channel_id=1, source_target_pairs={{0,8},{8,16},{16,24},{24,32},{32,40},{40,48},{48,56},{56,64},{64,7... | collective-permute-start | bytes 470024 | tf_op jit(solution)/shard_map/ppermute | solution.py:21
  159.4 13.2 %collective-permute-start.17 = (f32[2,153,128]{2,1,0:T(8,128)S(1)}, f32[2,153,128]{2,1,0:T(8,128)S(1)}, u32[]{:S(2)}, u32[]{:S(2)}) collective-permute-start(f32[2,153,128]{2,1,0:T(8,128)S(1)} %add_select_fusion.7), channel_id=1, source_target_pairs={{0,16},{8,24},{16,32},{24,40},{32,48},{40,56},{48,64},{56,72},{64,... | collective-permute-start | bytes 470024 | tf_op jit(solution)/shard_map/ppermute | solution.py:21
  172.7 14.8 %collective-permute-start.18 = (f32[2,153,128]{2,1,0:T(8,128)S(1)}, f32[2,153,128]{2,1,0:T(8,128)S(1)}, u32[]{:S(2)}, u32[]{:S(2)}) collective-permute-start(f32[2,153,128]{2,1,0:T(8,128)S(1)} %add_select_fusion.6), channel_id=1, source_target_pairs={{0,32},{8,40},{16,48},{24,56},{32,64},{40,72},{48,80},{56,88},{64,... | collective-permute-start | bytes 470024 | tf_op jit(solution)/shard_map/ppermute | solution.py:21
  176.1 36.4 %copy-start.13 = (f32[128,2]{0,1:T(2,128)}, f32[128,2]{0,1:T(2,128)S(1)}, u32[]{:S(2)}) copy-start(f32[128,2]{0,1:T(2,128)S(1)} %get-tuple-element.29) | copy-start | bytes 3076
  187.5 23.0 %collective-permute-start.19 = (f32[2,153,128]{2,1,0:T(8,128)S(1)}, f32[2,153,128]{2,1,0:T(8,128)}, u32[]{:S(2)}, u32[]{:S(2)}) collective-permute-start(f32[2,153,128]{2,1,0:T(8,128)S(1)} %add_select_fusion.5), channel_id=1, source_target_pairs={{0,64},{8,72},{16,80},{24,88},{32,96},{40,104},{48,112},{56,120},{... | collective-permute-start | bytes 470024 | tf_op jit(solution)/shard_map/ppermute | solution.py:21
  213.8 40.9 %copy-start.12 = (f32[2,128]{1,0:T(2,128)S(1)}, f32[2,128]{1,0:T(2,128)}, u32[]{:S(2)}) copy-start(f32[2,128]{1,0:T(2,128)} %copy-done.11) | copy-start | bytes 3076
  224.3 5.7 %collective-permute-start.24 = (f32[32,2]{1,0:T(8,128)S(1)}, f32[32,2]{1,0:T(8,128)S(1)}, u32[]{:S(2)}, u32[]{:S(2)}) collective-permute-start(f32[32,2]{1,0:T(8,128)S(1)} %bitcast.175), channel_id=1, source_target_pairs={{8,0},{16,8},{24,16},{32,24},{40,32},{48,40},{56,48},{64,56},{72,6... | collective-permute-start | bytes 776 | tf_op jit(solution)/shard_map/ppermute | solution.py:21
  230.0 5.6 %collective-permute-start.25 = (f32[32,2]{1,0:T(8,128)S(1)}, f32[32,2]{1,0:T(8,128)S(1)}, u32[]{:S(2)}, u32[]{:S(2)}) collective-permute-start(f32[32,2]{1,0:T(8,128)S(1)} %collective-permute-done.24), channel_id=1, source_target_pairs={{8,0},{16,8},{24,16},{32,24},{40,32},{48,40},{56,48},{64,56},{72,6... | collective-permute-start | bytes 776 | tf_op jit(solution)/shard_map/ppermute | solution.py:21
  235.6 102.6 %copy-start.3 = (bf16[32,128]{1,0:T(8,128)(2,1)S(1)}, bf16[32,128]{1,0:T(8,128)(2,1)}, u32[]{:S(2)}) copy-start(bf16[32,128]{1,0:T(8,128)(2,1)} %param.14) | copy-start | bytes 24580
  235.6 12.7 %collective-permute-start.26 = (f32[32,2]{1,0:T(8,128)S(1)}, f32[32,2]{1,0:T(8,128)S(1)}, u32[]{:S(2)}, u32[]{:S(2)}) collective-permute-start(f32[32,2]{1,0:T(8,128)S(1)} %broadcast_select_fusion), channel_id=1, source_target_pairs={{16,0},{24,8},{32,16},{40,24},{48,32},{56,40},{64,48},{72,56},{80,... | collective-permute-start | bytes 776 | tf_op jit(solution)/shard_map/ppermute | solution.py:21
  248.4 9.7 %collective-permute-start.27 = (f32[32,2]{1,0:T(8,128)S(1)}, f32[32,2]{1,0:T(8,128)S(1)}, u32[]{:S(2)}, u32[]{:S(2)}) collective-permute-start(f32[32,2]{1,0:T(8,128)S(1)} %broadcast_select_fusion.1), channel_id=1, source_target_pairs={{32,0},{40,8},{48,16},{56,24},{64,32},{72,40},{80,48},{88,56},{96,... | collective-permute-start | bytes 776 | tf_op jit(solution)/shard_map/ppermute | solution.py:21
  255.0 23.5 %collective-permute-start.35 = (f32[2,153]{1,0:T(2,128)S(1)}, f32[2,153]{1,0:T(2,128)S(1)}, u32[]{:S(2)}, u32[]{:S(2)}) collective-permute-start(f32[2,153]{1,0:T(2,128)S(1)} %bitcast.180), channel_id=1, source_target_pairs={{8,0},{16,8},{24,16},{32,24},{40,32},{48,40},{56,48},{64,56},{72,6... | collective-permute-start | bytes 3680 | tf_op jit(solution)/shard_map/ppermute | solution.py:21
  258.0 22.3 %collective-permute-start.28 = (f32[32,2]{1,0:T(8,128)S(1)}, f32[32,2]{1,0:T(8,128)S(1)}, u32[]{:S(2)}, u32[]{:S(2)}) collective-permute-start(f32[32,2]{1,0:T(8,128)S(1)} %broadcast_select_fusion.2), channel_id=1, source_target_pairs={{64,0},{72,8},{80,16},{88,24},{96,32},{104,40},{112,48},{120,56},{... | collective-permute-start | bytes 776 | tf_op jit(solution)/shard_map/ppermute | solution.py:21
  269.2 12.1 %collective-permute-start.30 = (f32[2,153,128]{2,1,0:T(8,128)S(1)}, f32[2,153,128]{2,1,0:T(8,128)S(1)}, u32[]{:S(2)}, u32[]{:S(2)}) collective-permute-start(f32[2,153,128]{2,1,0:T(8,128)S(1)} %fusion.13), channel_id=1, source_target_pairs={{8,0},{16,8},{24,16},{32,24},{40,32},{48,40},{56,48},{64,56},{72,6... | collective-permute-start | bytes 470024 | tf_op jit(solution)/shard_map/ppermute | solution.py:21
  278.5 7.2 %collective-permute-start.36 = (f32[2,153]{1,0:T(2,128)S(1)}, f32[2,153]{1,0:T(2,128)S(1)}, u32[]{:S(2)}, u32[]{:S(2)}) collective-permute-start(f32[2,153]{1,0:T(2,128)S(1)} %collective-permute-done.35), channel_id=1, source_target_pairs={{8,0},{16,8},{24,16},{32,24},{40,32},{48,40},{56,48},{64,56},{72,6... | collective-permute-start | bytes 3680 | tf_op jit(solution)/shard_map/ppermute | solution.py:21
  281.3 12.6 %collective-permute-start.31 = (f32[2,153,128]{2,1,0:T(8,128)S(1)}, f32[2,153,128]{2,1,0:T(8,128)S(1)}, u32[]{:S(2)}, u32[]{:S(2)}) collective-permute-start(f32[2,153,128]{2,1,0:T(8,128)S(1)} %collective-permute-done.30), channel_id=1, source_target_pairs={{8,0},{16,8},{24,16},{32,24},{40,32},{48,40},{56,48},{64,56},{72,6... | collective-permute-start | bytes 470024 | tf_op jit(solution)/shard_map/ppermute | solution.py:21
  285.7 14.7 %collective-permute-start.37 = (f32[2,153]{1,0:T(2,128)S(1)}, f32[2,153]{1,0:T(2,128)S(1)}, u32[]{:S(2)}, u32[]{:S(2)}) collective-permute-start(f32[2,153]{1,0:T(2,128)S(1)} %add_select_fusion.15), channel_id=1, source_target_pairs={{16,0},{24,8},{32,16},{40,24},{48,32},{56,40},{64,48},{72,56},{80,... | collective-permute-start | bytes 3680 | tf_op jit(solution)/shard_map/ppermute | solution.py:21
  293.9 15.5 %collective-permute-start.32 = (f32[2,153,128]{2,1,0:T(8,128)S(1)}, f32[2,153,128]{2,1,0:T(8,128)S(1)}, u32[]{:S(2)}, u32[]{:S(2)}) collective-permute-start(f32[2,153,128]{2,1,0:T(8,128)S(1)} %add_select_fusion.3), channel_id=1, source_target_pairs={{16,0},{24,8},{32,16},{40,24},{48,32},{56,40},{64,48},{72,56},{80,... | collective-permute-start | bytes 470024 | tf_op jit(solution)/shard_map/ppermute | solution.py:21
  300.4 13.1 %collective-permute-start.38 = (f32[2,153]{1,0:T(2,128)S(1)}, f32[2,153]{1,0:T(2,128)S(1)}, u32[]{:S(2)}, u32[]{:S(2)}) collective-permute-start(f32[2,153]{1,0:T(2,128)S(1)} %add_select_fusion.14), channel_id=1, source_target_pairs={{32,0},{40,8},{48,16},{56,24},{64,32},{72,40},{80,48},{88,56},{96,... | collective-permute-start | bytes 3680 | tf_op jit(solution)/shard_map/ppermute | solution.py:21
  309.5 15.6 %collective-permute-start.33 = (f32[2,153,128]{2,1,0:T(8,128)S(1)}, f32[2,153,128]{2,1,0:T(8,128)S(1)}, u32[]{:S(2)}, u32[]{:S(2)}) collective-permute-start(f32[2,153,128]{2,1,0:T(8,128)S(1)} %add_select_fusion.2), channel_id=1, source_target_pairs={{32,0},{40,8},{48,16},{56,24},{64,32},{72,40},{80,48},{88,56},{96,... | collective-permute-start | bytes 470024 | tf_op jit(solution)/shard_map/ppermute | solution.py:21
  313.6 13.5 %collective-permute-start.39 = (f32[2,153]{1,0:T(2,128)S(1)}, f32[2,153]{1,0:T(2,128)S(1)}, u32[]{:S(2)}, u32[]{:S(2)}) collective-permute-start(f32[2,153]{1,0:T(2,128)S(1)} %add_select_fusion.13), channel_id=1, source_target_pairs={{64,0},{72,8},{80,16},{88,24},{96,32},{104,40},{112,48},{120,56},{... | collective-permute-start | bytes 3680 | tf_op jit(solution)/shard_map/ppermute | solution.py:21
  325.1 12.8 %collective-permute-start.34 = (f32[2,153,128]{2,1,0:T(8,128)S(1)}, f32[2,153,128]{2,1,0:T(8,128)S(1)}, u32[]{:S(2)}, u32[]{:S(2)}) collective-permute-start(f32[2,153,128]{2,1,0:T(8,128)S(1)} %add_select_fusion.1), channel_id=1, source_target_pairs={{64,0},{72,8},{80,16},{88,24},{96,32},{104,40},{112,48},{120,56},{... | collective-permute-start | bytes 470024 | tf_op jit(solution)/shard_map/ppermute | solution.py:21
  (11 other events, 171.2 us)
Sparse Core Ops, SparseCore 0:
  10.4 35.5 all-gather.1

commit v2 on v1

--- a/solution.py
+++ b/solution.py
@@ -33,8 +33,10 @@
 
 def features(entries):
     scaled = entries * 0.5
-    row_index, col_index = np.triu_indices(scaled.shape[-2], 1)
-    cross = jnp.take(scaled, row_index, axis=-2) * jnp.take(scaled, col_index, axis=-2)
+    width = scaled.shape[-2]
+    cross = jnp.concatenate(
+        [scaled[..., i : i + 1, :] * scaled[..., i + 1 :, :] for i in range(width - 1)], axis=-2
+    )
     return jnp.concatenate(
         [jnp.ones_like(scaled[..., :1, :]), scaled, scaled * scaled * half_root, cross], axis=-2
     )
@@ -55,30 +57,15 @@
     return numerator / denominator[:, :, None]
 
 
-def join_forward(earlier, later):
-    empty_later = later[0][1] == 0.0
-    same_doc = earlier[0][1] == later[0][1]
-    state_out = jnp.where(empty_later, earlier[2], later[2] + jnp.where(same_doc, earlier[2], 0.0))
-    normer_out = jnp.where(empty_later, earlier[3], later[3] + jnp.where(same_doc, earlier[3], 0.0))
-    return (
-        jnp.where(empty_later, earlier[0], later[0]),
-        jnp.where(empty_later, earlier[1], later[1]),
-        state_out,
-        normer_out,
-    )
+def packed_join(key, prefix):
+    def join(earlier, later):
+        empty_later = later[key] == 0.0
+        same_doc = earlier[key] == later[key]
+        position = lax.broadcasted_iota(jnp.int32, later.shape, 0)
+        addend = jnp.where(same_doc & (position >= prefix), earlier, 0.0)
+        return jnp.where(empty_later, earlier, later + addend)
 
-
-def join_backward(earlier, later):
-    empty_later = later[0][0] == 0.0
-    same_doc = earlier[0][0] == later[0][0]
-    state_out = jnp.where(empty_later, earlier[2], later[2] + jnp.where(same_doc, earlier[2], 0.0))
-    normer_out = jnp.where(empty_later, earlier[3], later[3] + jnp.where(same_doc, earlier[3], 0.0))
-    return (
-        jnp.where(empty_later, earlier[0], later[0]),
-        jnp.where(empty_later, earlier[1], later[1]),
-        state_out,
-        normer_out,
-    )
+    return join
 
 
 def body(queries, keys, values, seg_ids, conv_weight, out_weight, out_grad):
@@ -102,8 +89,23 @@
     tail_feat = k_feat * tail_mask[None, None, :]
     tail_state = jnp.einsum("hfs,shd->hfd", tail_feat, head_values, precision=split_mode)
     tail_normer = jnp.sum(tail_feat, axis=2)
-    forward_piece = (doc_ids[length - 2 :], query_rows[:, length - 2 :], tail_state, tail_normer)
-    before = entering(forward_piece, "ctx", join_forward, False, reach)
+    row_count = query_rows.shape[0]
+    prefix = 2 + 2 * row_count
+    forward_piece = jnp.concatenate(
+        [
+            doc_ids[length - 2 :],
+            query_rows[:, length - 2 :].reshape(-1),
+            tail_normer.reshape(-1),
+            tail_state.reshape(-1),
+        ]
+    )
+    packed = entering(forward_piece, "ctx", packed_join(1, prefix), False, reach)
+    before = (
+        packed[:2],
+        packed[2:prefix].reshape(row_count, 2),
+        packed[prefix + tail_normer.size :].reshape(tail_state.shape),
+        packed[prefix : prefix + tail_normer.size].reshape(tail_normer.shape),
+    )
     query_ext = jnp.concatenate([before[1], query_rows], axis=1)
     ids_before = jnp.concatenate([before[0], doc_ids])
     q_conv = taps[0][:, None] * query_rows
@@ -126,8 +128,21 @@
 
     _, local_pullback = jax.vjp(local_forward, q_conv, k_feat, head_values, before[2], before[3])
     grad_qconv, grad_kfeat, grad_heads, grad_state, grad_normer = local_pullback(grad_attn)
-    backward_piece = (doc_ids[:2], grad_qconv[:, :2], grad_state, grad_normer)
-    after = entering(backward_piece, "ctx", join_backward, True, reach)
+    backward_piece = jnp.concatenate(
+        [
+            doc_ids[:2],
+            grad_qconv[:, :2].reshape(-1),
+            grad_normer.reshape(-1),
+            grad_state.reshape(-1),
+        ]
+    )
+    packed = entering(backward_piece, "ctx", packed_join(0, prefix), True, reach)
+    after = (
+        packed[:2],
+        packed[2:prefix].reshape(row_count, 2),
+        packed[prefix + grad_normer.size :].reshape(grad_state.shape),
+        packed[prefix : prefix + grad_normer.size].reshape(grad_normer.shape),
+    )
     head_mask = (doc_ids == after[0][0]).astype(jnp.float32)
     flowing = (
         jnp.einsum("hfd,shd->hfs", after[2], head_values, precision=split_mode)

time: 359 us -> 202 us (0.56)
  the two profiles are of different devices: /device:TPU:108 before, /device:TPU:43 now
where the time goes in v2:
time: 202 us; the launch traced here: 201 us
  waiting for transfers between devices  86.2 us (43%)
  starting transfers between devices  38.9 us (19%)
  between operations  30.8 us (15%)
  other arithmetic  20.1 us (10%)
  local copies, waits for them, and re-layouts  18.6 us (9%)
  matrix products  6.61 us (3%)
    ppermute x10, waiting for transfers between devices, shifted(): return lax.ppermute(piece, axis, pairs)  86.2 us
    ppermute x10, starting transfers between devices, shifted(): return lax.ppermute(piece, axis, pairs)  38.9 us
    mul x60, other arithmetic, features(): scaled[..., i:i + 1, :] * scaled[..., i + 1:, :]  12.2 us
    slice x8, local copies, waits for them, and re-layouts, join(): empty_later = later[key] == 0.0  4.38 us
    slice x8, local copies, waits for them, and re-layouts, join(): same_doc = earlier[key] == later[key]  4.37 us
  transfers between devices with their start and end apart: 11, of which 10 were waited for; matrix products, arithmetic and copies ran while one was open for 6% of the time, Pallas kernels for 0%

profile of v2, /device:TPU:43, one launch (start us, length us, event | category | flops | bytes accessed | tf_op | source)
XLA Modules:
  0.0 201.2 jit_solution(6043887266796252396)
XLA Ops:
  7.2 0.8 add_convert_fusion
  9.2 0.7 multiply_multiply_fusion.1
  9.9 0.7 convert_multiply_fusion
  10.6 1.3 compare_convert_fusion.6
  11.9 0.8 slice.473
  13.5 1.3 concatenate.24
  15.1 1.0 fusion.16
  16.3 4.0 %collective-permute-start = (f32[39540]{0:T(1024)S(1)}, f32[39540]{0:T(1024)S(1)}, u32[]{:S(2)}, u32[]{:S(2)}) collective-permute-start(f32[39540]{0:T(1024)S(1)} %concatenate.25), channel_id=1, source_target_pairs={{0,8},{8,16},{16,24},{24,32},{32,40},{40,48},{48,56},{56,64},{64,7... | collective-permute-start | bytes 474488 | tf_op jit(solution)/shard_map/ppermute | solution.py:21
  20.3 14.9 %collective-permute-done = f32[39540]{0:T(1024)S(1)} collective-permute-done((f32[39540]{0:T(1024)S(1)}, f32[39540]{0:T(1024)S(1)}, u32[]{:S(2)}, u32[]{:S(2)}) %collective-permute-start) | collective-permute-done | bytes 158192 | tf_op jit(solution)/shard_map/ppermute | solution.py:21
  35.2 1.9 collective-permute-start.1
  38.4 5.0 %collective-permute-done.1 = f32[39540]{0:T(1024)S(1)} collective-permute-done((f32[39540]{0:T(1024)S(1)}, f32[39540]{0:T(1024)S(1)}, u32[]{:S(2)}, u32[]{:S(2)}) %collective-permute-start.1) | collective-permute-done | bytes 158192 | tf_op jit(solution)/shard_map/ppermute | solution.py:21
  45.2 1.9 collective-permute-start.2
  48.5 7.8 %collective-permute-done.2 = f32[39540]{0:T(1024)S(1)} collective-permute-done((f32[39540]{0:T(1024)S(1)}, f32[39540]{0:T(1024)S(1)}, u32[]{:S(2)}, u32[]{:S(2)}) %collective-permute-start.2) | collective-permute-done | bytes 158192 | tf_op jit(solution)/shard_map/ppermute | solution.py:21
  58.2 1.9 collective-permute-start.3
  61.4 14.5 %collective-permute-done.3 = f32[39540]{0:T(1024)S(1)} collective-permute-done((f32[39540]{0:T(1024)S(1)}, f32[39540]{0:T(1024)S(1)}, u32[]{:S(2)}, u32[]{:S(2)}) %collective-permute-start.3) | collective-permute-done | bytes 158192 | tf_op jit(solution)/shard_map/ppermute | solution.py:21
  77.9 3.7 %collective-permute-start.4 = (f32[39540]{0:T(1024)S(1)}, f32[39540]{0:T(1024)S(1)}, u32[]{:S(2)}, u32[]{:S(2)}) collective-permute-start(f32[39540]{0:T(1024)S(1)} %add_select_fusion.5), channel_id=1, source_target_pairs={{0,64},{8,72},{16,80},{24,88},{32,96},{40,104},{48,112},{56,120},{... | collective-permute-start | bytes 474488 | tf_op jit(solution)/shard_map/ppermute | solution.py:21
  82.8 11.2 %collective-permute-done.4 = f32[39540]{0:T(1024)S(1)} collective-permute-done((f32[39540]{0:T(1024)S(1)}, f32[39540]{0:T(1024)S(1)}, u32[]{:S(2)}, u32[]{:S(2)}) %collective-permute-start.4) | collective-permute-done | bytes 158192 | tf_op jit(solution)/shard_map/ppermute | solution.py:21
  96.8 0.7 compare_convert_fusion.4
  98.2 1.3 concatenate.28
  100.7 1.9 fusion.111
  103.8 1.2 slice_multiply_fusion.55
  105.0 0.6 slice_multiply_fusion.61
  105.6 1.2 slice_multiply_fusion.48
  106.8 1.2 slice_multiply_fusion.49
  109.1 1.1 slice_multiply_fusion.36
  110.2 1.2 slice_multiply_fusion.37
  111.4 0.6 slice_multiply_fusion.10
  112.0 0.6 slice_multiply_fusion.11
  112.6 0.6 slice_multiply_fusion.12
  114.3 0.6 slice_multiply_fusion.15
  114.9 0.6 slice_multiply_fusion.9
  115.8 0.7 reshape.264
  116.5 0.9 add_multiply_fusion.1
  117.5 0.8 concatenate.29
  118.3 1.9 collective-permute-start.5
  120.3 5.0 %collective-permute-done.5 = f32[39540]{0:T(1024)S(1)} collective-permute-done((f32[39540]{0:T(1024)S(1)}, f32[39540]{0:T(1024)S(1)}, u32[]{:S(2)}, u32[]{:S(2)}) %collective-permute-start.5) | collective-permute-done | bytes 158192 | tf_op jit(solution)/shard_map/ppermute | solution.py:21
  125.3 4.7 %collective-permute-start.6 = (f32[39540]{0:T(1024)S(1)}, f32[39540]{0:T(1024)S(1)}, u32[]{:S(2)}, u32[]{:S(2)}) collective-permute-start(f32[39540]{0:T(1024)S(1)} %collective-permute-done.5), channel_id=1, source_target_pairs={{8,0},{16,8},{24,16},{32,24},{40,32},{48,40},{56,48},{64,56},{72,6... | collective-permute-start | bytes 474488 | tf_op jit(solution)/shard_map/ppermute | solution.py:21
  131.2 1.0 collective-permute-done.6
  134.1 5.7 %collective-permute-start.7 = (f32[39540]{0:T(1024)S(1)}, f32[39540]{0:T(1024)S(1)}, u32[]{:S(2)}, u32[]{:S(2)}) collective-permute-start(f32[39540]{0:T(1024)S(1)} %add_select_fusion.3), channel_id=1, source_target_pairs={{16,0},{24,8},{32,16},{40,24},{48,32},{56,40},{64,48},{72,56},{80,... | collective-permute-start | bytes 474488 | tf_op jit(solution)/shard_map/ppermute | solution.py:21
  141.0 2.2 %collective-permute-done.7 = f32[39540]{0:T(1024)S(1)} collective-permute-done((f32[39540]{0:T(1024)S(1)}, f32[39540]{0:T(1024)S(1)}, u32[]{:S(2)}, u32[]{:S(2)}) %collective-permute-start.7) | collective-permute-done | bytes 158192 | tf_op jit(solution)/shard_map/ppermute | solution.py:21
  145.1 4.3 %collective-permute-start.8 = (f32[39540]{0:T(1024)S(1)}, f32[39540]{0:T(1024)S(1)}, u32[]{:S(2)}, u32[]{:S(2)}) collective-permute-start(f32[39540]{0:T(1024)S(1)} %add_select_fusion.2), channel_id=1, source_target_pairs={{32,0},{40,8},{48,16},{56,24},{64,32},{72,40},{80,48},{88,56},{96,... | collective-permute-start | bytes 474488 | tf_op jit(solution)/shard_map/ppermute | solution.py:21
  150.9 4.1 %collective-permute-done.8 = f32[39540]{0:T(1024)S(1)} collective-permute-done((f32[39540]{0:T(1024)S(1)}, f32[39540]{0:T(1024)S(1)}, u32[]{:S(2)}, u32[]{:S(2)}) %collective-permute-start.8) | collective-permute-done | bytes 158192 | tf_op jit(solution)/shard_map/ppermute | solution.py:21
  156.9 8.7 %collective-permute-start.9 = (f32[39540]{0:T(1024)S(1)}, f32[39540]{0:T(1024)S(1)}, u32[]{:S(2)}, u32[]{:S(2)}) collective-permute-start(f32[39540]{0:T(1024)S(1)} %add_select_fusion.1), channel_id=1, source_target_pairs={{64,0},{72,8},{80,16},{88,24},{96,32},{104,40},{112,48},{120,56},{... | collective-permute-start | bytes 474488 | tf_op jit(solution)/shard_map/ppermute | solution.py:21
  167.1 20.4 %collective-permute-done.9 = f32[39540]{0:T(1024)S(1)} collective-permute-done((f32[39540]{0:T(1024)S(1)}, f32[39540]{0:T(1024)S(1)}, u32[]{:S(2)}, u32[]{:S(2)}) %collective-permute-start.9) | collective-permute-done | bytes 158192 | tf_op jit(solution)/shard_map/ppermute | solution.py:21
  190.2 0.7 compare_convert_fusion.2
  192.1 0.8 copy.35
  193.0 0.7 fusion.95
  193.7 0.7 add_multiply_fusion
  (213 shorter events, 20.1 us)
Async XLA Ops:
  7.2 93.5 %copy-start = (bf16[256,4096]{1,0:T(8,128)(2,1)S(1)}, bf16[256,4096]{1,0:T(8,128)(2,1)}, u32[]{:S(2)}) copy-start(bf16[256,4096]{1,0:T(8,128)(2,1)} %param.12) | copy-start | bytes 6291460
  7.2 40.0 %copy-start.3 = (bf16[32,128]{1,0:T(8,128)(2,1)S(1)}, bf16[32,128]{1,0:T(8,128)(2,1)}, u32[]{:S(2)}) copy-start(bf16[32,128]{1,0:T(8,128)(2,1)} %param.7) | copy-start | bytes 24580
  7.2 40.0 %copy-start.40 = (bf16[3,32]{1,0:T(4,128)(2,1)S(1)}, bf16[3,32]{1,0:T(4,128)(2,1)}, u32[]{:S(2)}) copy-start(bf16[3,32]{1,0:T(4,128)(2,1)} %param.11) | copy-start | bytes 580
  7.2 93.4 %all-gather.2.cloned.1.call-start = ((), (), s32[]{:S(2)}) async-start(), calls=%async_computation | async-start | bytes 1179648 | tf_op jit(solution)/shard_map/all_gather | solution.py:77
  12.8 0.6 copy-start.10
  12.9 0.6 copy-start.12
  12.9 0.6 copy-start.16
  12.9 0.6 copy-start.22
  12.9 0.6 copy-start.24
  12.9 0.6 copy-start.26
  12.9 0.6 copy-start.28
  12.9 0.6 copy-start.30
  13.0 83.8 %copy-start.38 = (s32[128]{0:T(128)S(1)}, s32[128]{0:T(128)}, u32[]{:S(2)}) copy-start(s32[128]{0:T(128)} %param.10) | copy-start | bytes 1540
  16.3 18.9 %collective-permute-start = (f32[39540]{0:T(1024)S(1)}, f32[39540]{0:T(1024)S(1)}, u32[]{:S(2)}, u32[]{:S(2)}) collective-permute-start(f32[39540]{0:T(1024)S(1)} %concatenate.25), channel_id=1, source_target_pairs={{0,8},{8,16},{16,24},{24,32},{32,40},{40,48},{48,56},{56,64},{64,7... | collective-permute-start | bytes 474488 | tf_op jit(solution)/shard_map/ppermute | solution.py:21
  35.2 8.1 %collective-permute-start.1 = (f32[39540]{0:T(1024)S(1)}, f32[39540]{0:T(1024)S(1)}, u32[]{:S(2)}, u32[]{:S(2)}) collective-permute-start(f32[39540]{0:T(1024)S(1)} %collective-permute-done), channel_id=1, source_target_pairs={{0,8},{8,16},{16,24},{24,32},{32,40},{40,48},{48,56},{56,64},{64,7... | collective-permute-start | bytes 474488 | tf_op jit(solution)/shard_map/ppermute | solution.py:21
  45.2 11.0 %collective-permute-start.2 = (f32[39540]{0:T(1024)S(1)}, f32[39540]{0:T(1024)S(1)}, u32[]{:S(2)}, u32[]{:S(2)}) collective-permute-start(f32[39540]{0:T(1024)S(1)} %add_select_fusion.7), channel_id=1, source_target_pairs={{0,16},{8,24},{16,32},{24,40},{32,48},{40,56},{48,64},{56,72},{64,... | collective-permute-start | bytes 474488 | tf_op jit(solution)/shard_map/ppermute | solution.py:21
  58.2 17.8 %collective-permute-start.3 = (f32[39540]{0:T(1024)S(1)}, f32[39540]{0:T(1024)S(1)}, u32[]{:S(2)}, u32[]{:S(2)}) collective-permute-start(f32[39540]{0:T(1024)S(1)} %add_select_fusion.6), channel_id=1, source_target_pairs={{0,32},{8,40},{16,48},{24,56},{32,64},{40,72},{48,80},{56,88},{64,... | collective-permute-start | bytes 474488 | tf_op jit(solution)/shard_map/ppermute | solution.py:21
  77.9 16.1 %collective-permute-start.4 = (f32[39540]{0:T(1024)S(1)}, f32[39540]{0:T(1024)S(1)}, u32[]{:S(2)}, u32[]{:S(2)}) collective-permute-start(f32[39540]{0:T(1024)S(1)} %add_select_fusion.5), channel_id=1, source_target_pairs={{0,64},{8,72},{16,80},{24,88},{32,96},{40,104},{48,112},{56,120},{... | collective-permute-start | bytes 474488 | tf_op jit(solution)/shard_map/ppermute | solution.py:21
  81.6 16.1 %copy-start.32 = (f32[32]{0:T(128)}, f32[32]{0:T(128)S(1)}, u32[]{:S(2)}) copy-start(f32[32]{0:T(128)S(1)} %get-tuple-element.103) | copy-start | bytes 388
  81.6 16.1 %copy-start.34 = (f32[32]{0:T(128)}, f32[32]{0:T(128)S(1)}, u32[]{:S(2)}) copy-start(f32[32]{0:T(128)S(1)} %get-tuple-element.104) | copy-start | bytes 388
  81.6 16.2 %copy-start.36 = (f32[32]{0:T(128)}, f32[32]{0:T(128)S(1)}, u32[]{:S(2)}) copy-start(f32[32]{0:T(128)S(1)} %get-tuple-element.105) | copy-start | bytes 388
  99.7 2.9 %copy-start.1 = (bf16[128,256]{1,0:T(8,128)(2,1)S(1)}, bf16[128,256]{1,0:T(8,128)(2,1)}, u32[]{:S(2)}) copy-start(bf16[128,256]{1,0:T(8,128)(2,1)} %param.9) | copy-start | bytes 196612
  100.2 3.4 %copy-start.41 = (f32[128,2]{0,1:T(2,128)}, f32[128,2]{0,1:T(2,128)S(1)}, u32[]{:S(2)}) copy-start(f32[128,2]{0,1:T(2,128)S(1)} %get-tuple-element.10) | copy-start | bytes 3076
  116.5 49.2 %copy-start.42 = (f32[128,2]{0,1:T(2,128)S(1)}, f32[128,2]{0,1:T(2,128)}, u32[]{:S(2)}) copy-start(f32[128,2]{0,1:T(2,128)} %copy-done.41) | copy-start | bytes 3076
  116.5 73.7 %copy-start.39 = (s32[128]{0:T(128)S(1)}, s32[128]{0:T(128)}, u32[]{:S(2)}) copy-start(s32[128]{0:T(128)} %param.10) | copy-start | bytes 1540
  118.3 72.9 %copy-start.23 = (f32[2,1,128]{2,1,0:T(1,128)S(1)}, f32[2,1,128]{2,1,0:T(1,128)}, u32[]{:S(2)}) copy-start(f32[2,1,128]{2,1,0:T(1,128)} %copy-done.22) | copy-start | bytes 3076
  118.3 72.9 %copy-start.7 = (f32[2,1,128]{2,1,0:T(1,128)S(1)}, f32[2,1,128]{2,1,0:T(1,128)}, u32[]{:S(2)}) copy-start(f32[2,1,128]{2,1,0:T(1,128)} %copy-done.6) | copy-start | bytes 3076
  118.3 72.9 %copy-start.5 = (f32[2,1,128]{2,1,0:T(1,128)S(1)}, f32[2,1,128]{2,1,0:T(1,128)}, u32[]{:S(2)}) copy-start(f32[2,1,128]{2,1,0:T(1,128)} %copy-done.4) | copy-start | bytes 3076
  118.3 72.9 %copy-start.31 = (f32[2,1,128]{2,1,0:T(1,128)S(1)}, f32[2,1,128]{2,1,0:T(1,128)}, u32[]{:S(2)}) copy-start(f32[2,1,128]{2,1,0:T(1,128)} %copy-done.30) | copy-start | bytes 3076
  118.3 73.0 %copy-start.29 = (f32[2,1,128]{2,1,0:T(1,128)S(1)}, f32[2,1,128]{2,1,0:T(1,128)}, u32[]{:S(2)}) copy-start(f32[2,1,128]{2,1,0:T(1,128)} %copy-done.28) | copy-start | bytes 3076
  118.3 6.9 %collective-permute-start.5 = (f32[39540]{0:T(1024)S(1)}, f32[39540]{0:T(1024)S(1)}, u32[]{:S(2)}, u32[]{:S(2)}) collective-permute-start(f32[39540]{0:T(1024)S(1)} %concatenate.29), channel_id=1, source_target_pairs={{8,0},{16,8},{24,16},{32,24},{40,32},{48,40},{56,48},{64,56},{72,6... | collective-permute-start | bytes 474488 | tf_op jit(solution)/shard_map/ppermute | solution.py:21
  125.3 6.9 %collective-permute-start.6 = (f32[39540]{0:T(1024)S(1)}, f32[39540]{0:T(1024)S(1)}, u32[]{:S(2)}, u32[]{:S(2)}) collective-permute-start(f32[39540]{0:T(1024)S(1)} %collective-permute-done.5), channel_id=1, source_target_pairs={{8,0},{16,8},{24,16},{32,24},{40,32},{48,40},{56,48},{64,56},{72,6... | collective-permute-start | bytes 474488 | tf_op jit(solution)/shard_map/ppermute | solution.py:21
  131.2 60.2 %copy-start.27 = (f32[2,1,128]{2,1,0:T(1,128)S(1)}, f32[2,1,128]{2,1,0:T(1,128)}, u32[]{:S(2)}) copy-start(f32[2,1,128]{2,1,0:T(1,128)} %copy-done.26) | copy-start | bytes 3076
  134.0 57.3 %copy-start.25 = (f32[2,1,128]{2,1,0:T(1,128)S(1)}, f32[2,1,128]{2,1,0:T(1,128)}, u32[]{:S(2)}) copy-start(f32[2,1,128]{2,1,0:T(1,128)} %copy-done.24) | copy-start | bytes 3076
  134.0 57.4 %copy-start.21 = (f32[2,1,128]{2,1,0:T(1,128)S(1)}, f32[2,1,128]{2,1,0:T(1,128)}, u32[]{:S(2)}) copy-start(f32[2,1,128]{2,1,0:T(1,128)} %copy-done.20) | copy-start | bytes 3076
  134.0 57.4 %copy-start.19 = (f32[2,1,128]{2,1,0:T(1,128)S(1)}, f32[2,1,128]{2,1,0:T(1,128)}, u32[]{:S(2)}) copy-start(f32[2,1,128]{2,1,0:T(1,128)} %copy-done.18) | copy-start | bytes 3076
  134.0 57.4 %copy-start.17 = (f32[2,1,128]{2,1,0:T(1,128)S(1)}, f32[2,1,128]{2,1,0:T(1,128)}, u32[]{:S(2)}) copy-start(f32[2,1,128]{2,1,0:T(1,128)} %copy-done.16) | copy-start | bytes 3076
  134.1 57.4 %copy-start.15 = (f32[2,1,128]{2,1,0:T(1,128)S(1)}, f32[2,1,128]{2,1,0:T(1,128)}, u32[]{:S(2)}) copy-start(f32[2,1,128]{2,1,0:T(1,128)} %copy-done.14) | copy-start | bytes 3076
  134.1 57.4 %copy-start.13 = (f32[2,1,128]{2,1,0:T(1,128)S(1)}, f32[2,1,128]{2,1,0:T(1,128)}, u32[]{:S(2)}) copy-start(f32[2,1,128]{2,1,0:T(1,128)} %copy-done.12) | copy-start | bytes 3076
  134.1 57.5 %copy-start.11 = (f32[2,1,128]{2,1,0:T(1,128)S(1)}, f32[2,1,128]{2,1,0:T(1,128)}, u32[]{:S(2)}) copy-start(f32[2,1,128]{2,1,0:T(1,128)} %copy-done.10) | copy-start | bytes 3076
  134.1 57.5 %copy-start.9 = (f32[2,1,128]{2,1,0:T(1,128)S(1)}, f32[2,1,128]{2,1,0:T(1,128)}, u32[]{:S(2)}) copy-start(f32[2,1,128]{2,1,0:T(1,128)} %copy-done.8) | copy-start | bytes 3076
  134.1 9.1 %collective-permute-start.7 = (f32[39540]{0:T(1024)S(1)}, f32[39540]{0:T(1024)S(1)}, u32[]{:S(2)}, u32[]{:S(2)}) collective-permute-start(f32[39540]{0:T(1024)S(1)} %add_select_fusion.3), channel_id=1, source_target_pairs={{16,0},{24,8},{32,16},{40,24},{48,32},{56,40},{64,48},{72,56},{80,... | collective-permute-start | bytes 474488 | tf_op jit(solution)/shard_map/ppermute | solution.py:21
  145.1 9.9 %collective-permute-start.8 = (f32[39540]{0:T(1024)S(1)}, f32[39540]{0:T(1024)S(1)}, u32[]{:S(2)}, u32[]{:S(2)}) collective-permute-start(f32[39540]{0:T(1024)S(1)} %add_select_fusion.2), channel_id=1, source_target_pairs={{32,0},{40,8},{48,16},{56,24},{64,32},{72,40},{80,48},{88,56},{96,... | collective-permute-start | bytes 474488 | tf_op jit(solution)/shard_map/ppermute | solution.py:21
  149.7 43.2 %copy-start.33 = (f32[32]{0:T(128)S(1)}, f32[32]{0:T(128)}, u32[]{:S(2)}) copy-start(f32[32]{0:T(128)} %copy-done.32) | copy-start | bytes 388
  149.7 43.2 %copy-start.35 = (f32[32]{0:T(128)S(1)}, f32[32]{0:T(128)}, u32[]{:S(2)}) copy-start(f32[32]{0:T(128)} %copy-done.34) | copy-start | bytes 388
  149.7 43.2 %copy-start.37 = (f32[32]{0:T(128)S(1)}, f32[32]{0:T(128)}, u32[]{:S(2)}) copy-start(f32[32]{0:T(128)} %copy-done.36) | copy-start | bytes 388
  149.7 43.9 %copy-start.2 = (bf16[32,128]{1,0:T(8,128)(2,1)S(1)}, bf16[32,128]{1,0:T(8,128)(2,1)}, u32[]{:S(2)}) copy-start(bf16[32,128]{1,0:T(8,128)(2,1)} %param.8) | copy-start | bytes 24580
  156.9 30.6 %collective-permute-start.9 = (f32[39540]{0:T(1024)S(1)}, f32[39540]{0:T(1024)S(1)}, u32[]{:S(2)}, u32[]{:S(2)}) collective-permute-start(f32[39540]{0:T(1024)S(1)} %add_select_fusion.1), channel_id=1, source_target_pairs={{64,0},{72,8},{80,16},{88,24},{96,32},{104,40},{112,48},{120,56},{... | collective-permute-start | bytes 474488 | tf_op jit(solution)/shard_map/ppermute | solution.py:21
  (6 other events, 3.4 us)
Sparse Core Ops, SparseCore 0:
  47.3 29.0 all-gather.1

commit v3 on v2

--- a/solution.py
+++ b/solution.py
@@ -21,14 +21,23 @@
     return lax.ppermute(piece, axis, pairs)
 
 
+def fold(combine, pieces):
+    total = pieces[0]
+    for piece in pieces[1:]:
+        total = combine(total, piece)
+    return total
+
+
 def entering(shard, axis, combine, reverse, reach):
     size = lax.axis_size(axis)
-    total = shifted(shard, axis, 1, reverse)
-    step = 1
-    while step < reach and step < size:
-        total = combine(shifted(total, axis, step, reverse), total)
-        step *= 2
-    return total
+    fan = 1
+    while fan * fan < reach:
+        fan += 1
+    near = [step for step in range(fan - 1, 0, -1) if step < size]
+    total = fold(combine, [shifted(shard, axis, step, reverse) for step in near] + [shard])
+    far = [1 + fan * k for k in range(-(-reach // fan) - 1, -1, -1)]
+    far = [step for step in far if step < size]
+    return fold(combine, [shifted(total, axis, step, reverse) for step in far])
 
 
 def features(entries):

time: 202 us -> 192 us (0.950)
  the two profiles are of different devices: /device:TPU:43 before, /device:TPU:48 now
where the time goes in v3:
time: 192 us; the launch traced here: 190 us
  starting transfers between devices  64.5 us (34%)
  waiting for transfers between devices  48.1 us (25%)
  between operations  38 us (20%)
  local copies, waits for them, and re-layouts  20.8 us (11%)
  other arithmetic  11 us (6%)
  matrix products  7.96 us (4%)
    ppermute x14, starting transfers between devices, shifted(): return lax.ppermute(piece, axis, pairs)  64.5 us
    ppermute x14, waiting for transfers between devices, shifted(): return lax.ppermute(piece, axis, pairs)  48 us
    slice x12, local copies, waits for them, and re-layouts, join(): same_doc = earlier[key] == later[key]  6.57 us
    slice x11, local copies, waits for them, and re-layouts, join(): empty_later = later[key] == 0.0  6.05 us
  transfers between devices with their start and end apart: 15, of which 7 were waited for; matrix products, arithmetic and copies ran while one was open for 9% of the time, Pallas kernels for 0%

profile of v3, /device:TPU:48, one launch (start us, length us, event | category | flops | bytes accessed | tf_op | source)
XLA Modules:
  0.0 190.4 jit_solution(14633692024320843053)
XLA Ops:
  7.2 0.8 add_convert_fusion
  9.2 0.7 multiply_multiply_fusion.1
  9.9 0.7 convert_multiply_fusion
  10.6 1.3 compare_convert_fusion.6
  11.9 0.8 slice.508
  13.0 1.3 concatenate.24
  14.6 1.0 fusion.20
  15.8 7.9 %collective-permute-start.2 = (f32[39540]{0:T(1024)S(1)}, f32[39540]{0:T(1024)S(1)}, u32[]{:S(2)}, u32[]{:S(2)}) collective-permute-start(f32[39540]{0:T(1024)S(1)} %concatenate.25), channel_id=1, source_target_pairs={{0,24},{8,32},{16,40},{24,48},{32,56},{40,64},{48,72},{56,80},{64,... | collective-permute-start | bytes 474488 | tf_op jit(solution)/shard_map/ppermute | solution.py:21
  23.7 7.3 %collective-permute-start.1 = (f32[39540]{0:T(1024)S(1)}, f32[39540]{0:T(1024)S(1)}, u32[]{:S(2)}, u32[]{:S(2)}) collective-permute-start(f32[39540]{0:T(1024)S(1)} %concatenate.25), channel_id=1, source_target_pairs={{0,16},{8,24},{16,32},{24,40},{32,48},{40,56},{48,64},{56,72},{64,... | collective-permute-start | bytes 474488 | tf_op jit(solution)/shard_map/ppermute | solution.py:21
  31.0 4.3 %collective-permute-start = (f32[39540]{0:T(1024)S(1)}, f32[39540]{0:T(1024)S(1)}, u32[]{:S(2)}, u32[]{:S(2)}) collective-permute-start(f32[39540]{0:T(1024)S(1)} %concatenate.25), channel_id=1, source_target_pairs={{0,8},{8,16},{16,24},{24,32},{32,40},{40,48},{48,56},{56,64},{64,7... | collective-permute-start | bytes 474488 | tf_op jit(solution)/shard_map/ppermute | solution.py:21
  36.7 12.5 %collective-permute-done.1 = f32[39540]{0:T(1024)S(1)} collective-permute-done((f32[39540]{0:T(1024)S(1)}, f32[39540]{0:T(1024)S(1)}, u32[]{:S(2)}, u32[]{:S(2)}) %collective-permute-start.1) | collective-permute-done | bytes 158192 | tf_op jit(solution)/shard_map/ppermute | solution.py:21
  50.4 0.6 slice.541
  52.3 0.6 slice.542
  52.9 0.6 slice.539
  55.4 0.6 slice.543
  57.4 2.4 %collective-permute-start.6 = (f32[39540]{0:T(1024)S(1)}, f32[39540]{0:T(1024)S(1)}, u32[]{:S(2)}, u32[]{:S(2)}) collective-permute-start(f32[39540]{0:T(1024)S(1)} %add_select_fusion.9), channel_id=1, source_target_pairs={{0,104},{8,112},{16,120},{24,128},{32,136},{40,144},{48,152},{56,1... | collective-permute-start | bytes 474488 | tf_op jit(solution)/shard_map/ppermute | solution.py:21
  59.8 6.2 %collective-permute-start.5 = (f32[39540]{0:T(1024)S(1)}, f32[39540]{0:T(1024)S(1)}, u32[]{:S(2)}, u32[]{:S(2)}) collective-permute-start(f32[39540]{0:T(1024)S(1)} %add_select_fusion.9), channel_id=1, source_target_pairs={{0,72},{8,80},{16,88},{24,96},{32,104},{40,112},{48,120},{56,128},... | collective-permute-start | bytes 474488 | tf_op jit(solution)/shard_map/ppermute | solution.py:21
  66.0 1.9 %collective-permute-start.4 = (f32[39540]{0:T(1024)S(1)}, f32[39540]{0:T(1024)S(1)}, u32[]{:S(2)}, u32[]{:S(2)}) collective-permute-start(f32[39540]{0:T(1024)S(1)} %add_select_fusion.9), channel_id=1, source_target_pairs={{0,40},{8,48},{16,56},{24,64},{32,72},{40,80},{48,88},{56,96},{64,... | collective-permute-start | bytes 474488 | tf_op jit(solution)/shard_map/ppermute | solution.py:21
  67.9 2.5 %collective-permute-start.3 = (f32[39540]{0:T(1024)S(1)}, f32[39540]{0:T(1024)S(1)}, u32[]{:S(2)}, u32[]{:S(2)}) collective-permute-start(f32[39540]{0:T(1024)S(1)} %add_select_fusion.9), channel_id=1, source_target_pairs={{0,8},{8,16},{16,24},{24,32},{32,40},{40,48},{48,56},{56,64},{64,7... | collective-permute-start | bytes 474488 | tf_op jit(solution)/shard_map/ppermute | solution.py:21
  70.4 6.5 %collective-permute-done.5 = f32[39540]{0:T(1024)S(1)} collective-permute-done((f32[39540]{0:T(1024)S(1)}, f32[39540]{0:T(1024)S(1)}, u32[]{:S(2)}, u32[]{:S(2)}) %collective-permute-start.5) | collective-permute-done | bytes 158192 | tf_op jit(solution)/shard_map/ppermute | solution.py:21
  78.2 0.6 slice.547
  80.1 0.6 slice.548
  80.7 5.5 %collective-permute-done.4 = f32[39540]{0:T(1024)S(1)} collective-permute-done((f32[39540]{0:T(1024)S(1)}, f32[39540]{0:T(1024)S(1)}, u32[]{:S(2)}, u32[]{:S(2)}) %collective-permute-start.4) | collective-permute-done | bytes 158192 | tf_op jit(solution)/shard_map/ppermute | solution.py:21
  88.7 0.6 slice.549
  89.3 1.6 collective-permute-done.3
  93.5 0.6 slice.551
  94.3 0.7 compare_convert_fusion.4
  95.7 1.3 concatenate.28
  98.2 1.9 %fusion.113 = f32[128,256]{0,1:T(8,128)S(1)} fusion(bf16[128,4096]{1,0:T(8,128)(2,1)} %all-gather.2.cloned.1.call-done, bf16[256,4096]{1,0:T(8,128)(2,1)S(1)} %copy-done), kind=kOutput, calls=%fused_computation.259 | convolution fusion | flops 268435456 | bytes 3276800 | tf_op jit(solution)/shard_map/transpose(jvp())/reshape | solution.py:136
  102.9 0.6 slice_multiply_fusion.37
  103.7 0.9 fusion.25
  105.0 0.8 add_multiply_fusion.1
  105.9 0.8 concatenate.29
  106.7 7.5 %collective-permute-start.9 = (f32[39540]{0:T(1024)S(1)}, f32[39540]{0:T(1024)S(1)}, u32[]{:S(2)}, u32[]{:S(2)}) collective-permute-start(f32[39540]{0:T(1024)S(1)} %concatenate.29), channel_id=1, source_target_pairs={{24,0},{32,8},{40,16},{48,24},{56,32},{64,40},{72,48},{80,56},{88,... | collective-permute-start | bytes 474488 | tf_op jit(solution)/shard_map/ppermute | solution.py:21
  114.3 3.5 %collective-permute-start.8 = (f32[39540]{0:T(1024)S(1)}, f32[39540]{0:T(1024)S(1)}, u32[]{:S(2)}, u32[]{:S(2)}) collective-permute-start(f32[39540]{0:T(1024)S(1)} %concatenate.29), channel_id=1, source_target_pairs={{16,0},{24,8},{32,16},{40,24},{48,32},{56,40},{64,48},{72,56},{80,... | collective-permute-start | bytes 474488 | tf_op jit(solution)/shard_map/ppermute | solution.py:21
  117.8 2.2 %collective-permute-start.7 = (f32[39540]{0:T(1024)S(1)}, f32[39540]{0:T(1024)S(1)}, u32[]{:S(2)}, u32[]{:S(2)}) collective-permute-start(f32[39540]{0:T(1024)S(1)} %concatenate.29), channel_id=1, source_target_pairs={{8,0},{16,8},{24,16},{32,24},{40,32},{48,40},{56,48},{64,56},{72,6... | collective-permute-start | bytes 474488 | tf_op jit(solution)/shard_map/ppermute | solution.py:21
  120.3 13.1 %collective-permute-done.8 = f32[39540]{0:T(1024)S(1)} collective-permute-done((f32[39540]{0:T(1024)S(1)}, f32[39540]{0:T(1024)S(1)}, u32[]{:S(2)}, u32[]{:S(2)}) %collective-permute-start.8) | collective-permute-done | bytes 158192 | tf_op jit(solution)/shard_map/ppermute | solution.py:21
  141.2 4.6 %collective-permute-start.13 = (f32[39540]{0:T(1024)S(1)}, f32[39540]{0:T(1024)S(1)}, u32[]{:S(2)}, u32[]{:S(2)}) collective-permute-start(f32[39540]{0:T(1024)S(1)} %add_select_fusion.3), channel_id=1, source_target_pairs={{104,0},{112,8},{120,16},{128,24},{136,32},{144,40},{152,48},{160,... | collective-permute-start | bytes 474488 | tf_op jit(solution)/shard_map/ppermute | solution.py:21
  145.8 2.9 %collective-permute-start.12 = (f32[39540]{0:T(1024)S(1)}, f32[39540]{0:T(1024)S(1)}, u32[]{:S(2)}, u32[]{:S(2)}) collective-permute-start(f32[39540]{0:T(1024)S(1)} %add_select_fusion.3), channel_id=1, source_target_pairs={{72,0},{80,8},{88,16},{96,24},{104,32},{112,40},{120,48},{128,56},... | collective-permute-start | bytes 474488 | tf_op jit(solution)/shard_map/ppermute | solution.py:21
  148.7 0.9 fusion.22
  149.7 7.4 %collective-permute-start.11 = (f32[39540]{0:T(1024)S(1)}, f32[39540]{0:T(1024)S(1)}, u32[]{:S(2)}, u32[]{:S(2)}) collective-permute-start(f32[39540]{0:T(1024)S(1)} %add_select_fusion.3), channel_id=1, source_target_pairs={{40,0},{48,8},{56,16},{64,24},{72,32},{80,40},{88,48},{96,56},{104... | collective-permute-start | bytes 474488 | tf_op jit(solution)/shard_map/ppermute | solution.py:21
  157.1 3.8 %collective-permute-start.10 = (f32[39540]{0:T(1024)S(1)}, f32[39540]{0:T(1024)S(1)}, u32[]{:S(2)}, u32[]{:S(2)}) collective-permute-start(f32[39540]{0:T(1024)S(1)} %add_select_fusion.3), channel_id=1, source_target_pairs={{8,0},{16,8},{24,16},{32,24},{40,32},{48,40},{56,48},{64,56},{72,6... | collective-permute-start | bytes 474488 | tf_op jit(solution)/shard_map/ppermute | solution.py:21
  164.5 4.9 %collective-permute-done.11 = f32[39540]{0:T(1024)S(1)} collective-permute-done((f32[39540]{0:T(1024)S(1)}, f32[39540]{0:T(1024)S(1)}, u32[]{:S(2)}, u32[]{:S(2)}) %collective-permute-start.11) | collective-permute-done | bytes 158192 | tf_op jit(solution)/shard_map/ppermute | solution.py:21
  172.4 3.8 %collective-permute-done.10 = f32[39540]{0:T(1024)S(1)} collective-permute-done((f32[39540]{0:T(1024)S(1)}, f32[39540]{0:T(1024)S(1)}, u32[]{:S(2)}, u32[]{:S(2)}) %collective-permute-start.10) | collective-permute-done | bytes 158192 | tf_op jit(solution)/shard_map/ppermute | solution.py:21
  179.6 0.7 compare_convert_fusion.2
  181.3 0.8 copy.35
  182.2 0.7 fusion.96
  182.9 0.7 add_multiply_fusion
  (161 shorter events, 17.7 us)
Async XLA Ops:
  7.2 91.0 %copy-start = (bf16[256,4096]{1,0:T(8,128)(2,1)S(1)}, bf16[256,4096]{1,0:T(8,128)(2,1)}, u32[]{:S(2)}) copy-start(bf16[256,4096]{1,0:T(8,128)(2,1)} %param.12) | copy-start | bytes 6291460
  7.2 28.1 %copy-start.3 = (bf16[32,128]{1,0:T(8,128)(2,1)S(1)}, bf16[32,128]{1,0:T(8,128)(2,1)}, u32[]{:S(2)}) copy-start(bf16[32,128]{1,0:T(8,128)(2,1)} %param.7) | copy-start | bytes 24580
  7.2 28.8 %copy-start.6 = (bf16[3,32]{1,0:T(4,128)(2,1)S(1)}, bf16[3,32]{1,0:T(4,128)(2,1)}, u32[]{:S(2)}) copy-start(bf16[3,32]{1,0:T(4,128)(2,1)} %param.11) | copy-start | bytes 580
  7.2 91.0 %all-gather.2.cloned.1.call-start = ((), (), s32[]{:S(2)}) async-start(), calls=%async_computation | async-start | bytes 1179648 | tf_op jit(solution)/shard_map/all_gather | solution.py:86
  14.6 79.7 %copy-start.4 = (s32[128]{0:T(128)S(1)}, s32[128]{0:T(128)}, u32[]{:S(2)}) copy-start(s32[128]{0:T(128)} %param.10) | copy-start | bytes 1540
  15.8 34.6 %collective-permute-start.2 = (f32[39540]{0:T(1024)S(1)}, f32[39540]{0:T(1024)S(1)}, u32[]{:S(2)}, u32[]{:S(2)}) collective-permute-start(f32[39540]{0:T(1024)S(1)} %concatenate.25), channel_id=1, source_target_pairs={{0,24},{8,32},{16,40},{24,48},{32,56},{40,64},{48,72},{56,80},{64,... | collective-permute-start | bytes 474488 | tf_op jit(solution)/shard_map/ppermute | solution.py:21
  23.7 25.4 %collective-permute-start.1 = (f32[39540]{0:T(1024)S(1)}, f32[39540]{0:T(1024)S(1)}, u32[]{:S(2)}, u32[]{:S(2)}) collective-permute-start(f32[39540]{0:T(1024)S(1)} %concatenate.25), channel_id=1, source_target_pairs={{0,16},{8,24},{16,32},{24,40},{32,48},{40,56},{48,64},{56,72},{64,... | collective-permute-start | bytes 474488 | tf_op jit(solution)/shard_map/ppermute | solution.py:21
  31.0 21.9 %collective-permute-start = (f32[39540]{0:T(1024)S(1)}, f32[39540]{0:T(1024)S(1)}, u32[]{:S(2)}, u32[]{:S(2)}) collective-permute-start(f32[39540]{0:T(1024)S(1)} %concatenate.25), channel_id=1, source_target_pairs={{0,8},{8,16},{16,24},{24,32},{32,40},{40,48},{48,56},{56,64},{64,7... | collective-permute-start | bytes 474488 | tf_op jit(solution)/shard_map/ppermute | solution.py:21
  57.4 20.8 %collective-permute-start.6 = (f32[39540]{0:T(1024)S(1)}, f32[39540]{0:T(1024)S(1)}, u32[]{:S(2)}, u32[]{:S(2)}) collective-permute-start(f32[39540]{0:T(1024)S(1)} %add_select_fusion.9), channel_id=1, source_target_pairs={{0,104},{8,112},{16,120},{24,128},{32,136},{40,144},{48,152},{56,1... | collective-permute-start | bytes 474488 | tf_op jit(solution)/shard_map/ppermute | solution.py:21
  59.8 17.2 %collective-permute-start.5 = (f32[39540]{0:T(1024)S(1)}, f32[39540]{0:T(1024)S(1)}, u32[]{:S(2)}, u32[]{:S(2)}) collective-permute-start(f32[39540]{0:T(1024)S(1)} %add_select_fusion.9), channel_id=1, source_target_pairs={{0,72},{8,80},{16,88},{24,96},{32,104},{40,112},{48,120},{56,128},... | collective-permute-start | bytes 474488 | tf_op jit(solution)/shard_map/ppermute | solution.py:21
  66.0 20.1 %collective-permute-start.4 = (f32[39540]{0:T(1024)S(1)}, f32[39540]{0:T(1024)S(1)}, u32[]{:S(2)}, u32[]{:S(2)}) collective-permute-start(f32[39540]{0:T(1024)S(1)} %add_select_fusion.9), channel_id=1, source_target_pairs={{0,40},{8,48},{16,56},{24,64},{32,72},{40,80},{48,88},{56,96},{64,... | collective-permute-start | bytes 474488 | tf_op jit(solution)/shard_map/ppermute | solution.py:21
  67.9 23.0 %collective-permute-start.3 = (f32[39540]{0:T(1024)S(1)}, f32[39540]{0:T(1024)S(1)}, u32[]{:S(2)}, u32[]{:S(2)}) collective-permute-start(f32[39540]{0:T(1024)S(1)} %add_select_fusion.9), channel_id=1, source_target_pairs={{0,8},{8,16},{16,24},{24,32},{32,40},{40,48},{48,56},{56,64},{64,7... | collective-permute-start | bytes 474488 | tf_op jit(solution)/shard_map/ppermute | solution.py:21
  97.2 2.9 %copy-start.1 = (bf16[128,256]{1,0:T(8,128)(2,1)S(1)}, bf16[128,256]{1,0:T(8,128)(2,1)}, u32[]{:S(2)}) copy-start(bf16[128,256]{1,0:T(8,128)(2,1)} %param.9) | copy-start | bytes 196612
  97.7 2.9 %copy-start.7 = (f32[128,2]{0,1:T(2,128)}, f32[128,2]{0,1:T(2,128)S(1)}, u32[]{:S(2)}) copy-start(f32[128,2]{0,1:T(2,128)S(1)} %get-tuple-element.10) | copy-start | bytes 3076
  106.7 27.9 %collective-permute-start.9 = (f32[39540]{0:T(1024)S(1)}, f32[39540]{0:T(1024)S(1)}, u32[]{:S(2)}, u32[]{:S(2)}) collective-permute-start(f32[39540]{0:T(1024)S(1)} %concatenate.29), channel_id=1, source_target_pairs={{24,0},{32,8},{40,16},{48,24},{56,32},{64,40},{72,48},{80,56},{88,... | collective-permute-start | bytes 474488 | tf_op jit(solution)/shard_map/ppermute | solution.py:21
  114.3 19.2 %collective-permute-start.8 = (f32[39540]{0:T(1024)S(1)}, f32[39540]{0:T(1024)S(1)}, u32[]{:S(2)}, u32[]{:S(2)}) collective-permute-start(f32[39540]{0:T(1024)S(1)} %concatenate.29), channel_id=1, source_target_pairs={{16,0},{24,8},{32,16},{40,24},{48,32},{56,40},{64,48},{72,56},{80,... | collective-permute-start | bytes 474488 | tf_op jit(solution)/shard_map/ppermute | solution.py:21
  117.8 19.2 %collective-permute-start.7 = (f32[39540]{0:T(1024)S(1)}, f32[39540]{0:T(1024)S(1)}, u32[]{:S(2)}, u32[]{:S(2)}) collective-permute-start(f32[39540]{0:T(1024)S(1)} %concatenate.29), channel_id=1, source_target_pairs={{8,0},{16,8},{24,16},{32,24},{40,32},{48,40},{56,48},{64,56},{72,6... | collective-permute-start | bytes 474488 | tf_op jit(solution)/shard_map/ppermute | solution.py:21
  120.3 59.3 %copy-start.5 = (s32[128]{0:T(128)S(1)}, s32[128]{0:T(128)}, u32[]{:S(2)}) copy-start(s32[128]{0:T(128)} %param.10) | copy-start | bytes 1540
  141.2 20.9 %collective-permute-start.13 = (f32[39540]{0:T(1024)S(1)}, f32[39540]{0:T(1024)S(1)}, u32[]{:S(2)}, u32[]{:S(2)}) collective-permute-start(f32[39540]{0:T(1024)S(1)} %add_select_fusion.3), channel_id=1, source_target_pairs={{104,0},{112,8},{120,16},{128,24},{136,32},{144,40},{152,48},{160,... | collective-permute-start | bytes 474488 | tf_op jit(solution)/shard_map/ppermute | solution.py:21
  145.8 15.1 %collective-permute-start.12 = (f32[39540]{0:T(1024)S(1)}, f32[39540]{0:T(1024)S(1)}, u32[]{:S(2)}, u32[]{:S(2)}) collective-permute-start(f32[39540]{0:T(1024)S(1)} %add_select_fusion.3), channel_id=1, source_target_pairs={{72,0},{80,8},{88,16},{96,24},{104,32},{112,40},{120,48},{128,56},... | collective-permute-start | bytes 474488 | tf_op jit(solution)/shard_map/ppermute | solution.py:21
  149.7 19.7 %collective-permute-start.11 = (f32[39540]{0:T(1024)S(1)}, f32[39540]{0:T(1024)S(1)}, u32[]{:S(2)}, u32[]{:S(2)}) collective-permute-start(f32[39540]{0:T(1024)S(1)} %add_select_fusion.3), channel_id=1, source_target_pairs={{40,0},{48,8},{56,16},{64,24},{72,32},{80,40},{88,48},{96,56},{104... | collective-permute-start | bytes 474488 | tf_op jit(solution)/shard_map/ppermute | solution.py:21
  157.1 19.1 %collective-permute-start.10 = (f32[39540]{0:T(1024)S(1)}, f32[39540]{0:T(1024)S(1)}, u32[]{:S(2)}, u32[]{:S(2)}) collective-permute-start(f32[39540]{0:T(1024)S(1)} %add_select_fusion.3), channel_id=1, source_target_pairs={{8,0},{16,8},{24,16},{32,24},{40,32},{48,40},{56,48},{64,56},{72,6... | collective-permute-start | bytes 474488 | tf_op jit(solution)/shard_map/ppermute | solution.py:21
  163.9 19.0 %copy-start.2 = (bf16[32,128]{1,0:T(8,128)(2,1)S(1)}, bf16[32,128]{1,0:T(8,128)(2,1)}, u32[]{:S(2)}) copy-start(bf16[32,128]{1,0:T(8,128)(2,1)} %param.8) | copy-start | bytes 24580
Sparse Core Ops, SparseCore 0:
  35.4 29.5 all-gather.1

commit v4 on v3

--- a/solution.py
+++ b/solution.py
@@ -66,15 +66,49 @@
     return numerator / denominator[:, :, None]
 
 
-def packed_join(key, prefix):
+def packed_join(key_row):
     def join(earlier, later):
-        empty_later = later[key] == 0.0
-        same_doc = earlier[key] == later[key]
-        position = lax.broadcasted_iota(jnp.int32, later.shape, 0)
-        addend = jnp.where(same_doc & (position >= prefix), earlier, 0.0)
+        empty_later = later[key_row : key_row + 1] == 0.0
+        same_doc = earlier[key_row : key_row + 1] == later[key_row : key_row + 1]
+        row = lax.broadcasted_iota(jnp.int32, later.shape, 0)
+        addend = jnp.where(same_doc & (row < key_row), earlier, 0.0)
         return jnp.where(empty_later, earlier, later + addend)
 
     return join
+
+
+def pack(state, normer, key, edge):
+    lanes = state.shape[-1]
+    state_rows = state.reshape(-1, lanes)
+    normer_flat = normer.reshape(-1)
+    normer_rows = -(-normer_flat.size // lanes)
+    normer_part = jnp.pad(normer_flat, (0, normer_rows * lanes - normer_flat.size))
+    key_part = jnp.broadcast_to(key, (1, lanes))
+    edge_rows = -(-edge.size // lanes)
+    edge_part = jnp.pad(edge, (0, edge_rows * lanes - edge.size)).reshape(edge_rows, lanes)
+    rows = state_rows.shape[0] + normer_rows + 1 + edge_rows
+    tail = -rows % 8
+    return jnp.concatenate(
+        [
+            state_rows,
+            normer_part.reshape(normer_rows, lanes),
+            key_part,
+            edge_part,
+            jnp.zeros((tail, lanes), state.dtype),
+        ]
+    )
+
+
+def unpack(packed, state_shape, normer_shape, edge_size):
+    lanes = state_shape[-1]
+    state_rows = int(np.prod(state_shape[:-1]))
+    normer_size = int(np.prod(normer_shape))
+    key_row = state_rows + -(-normer_size // lanes)
+    state = packed[:state_rows].reshape(state_shape)
+    normer = packed[state_rows:key_row].reshape(-1)[:normer_size].reshape(normer_shape)
+    edge_rows = -(-edge_size // lanes)
+    edge = packed[key_row + 1 : key_row + 1 + edge_rows].reshape(-1)[:edge_size]
+    return state, normer, edge
 
 
 def body(queries, keys, values, seg_ids, conv_weight, out_weight, out_grad):
@@ -99,22 +133,16 @@
     tail_state = jnp.einsum("hfs,shd->hfd", tail_feat, head_values, precision=split_mode)
     tail_normer = jnp.sum(tail_feat, axis=2)
     row_count = query_rows.shape[0]
-    prefix = 2 + 2 * row_count
-    forward_piece = jnp.concatenate(
-        [
-            doc_ids[length - 2 :],
-            query_rows[:, length - 2 :].reshape(-1),
-            tail_normer.reshape(-1),
-            tail_state.reshape(-1),
-        ]
-    )
-    packed = entering(forward_piece, "ctx", packed_join(1, prefix), False, reach)
-    before = (
-        packed[:2],
-        packed[2:prefix].reshape(row_count, 2),
-        packed[prefix + tail_normer.size :].reshape(tail_state.shape),
-        packed[prefix : prefix + tail_normer.size].reshape(tail_normer.shape),
-    )
+    key_row = tail_state.size // head_width + -(-tail_normer.size // head_width)
+    forward_piece = pack(
+        tail_state,
+        tail_normer,
+        doc_ids[length - 1],
+        jnp.concatenate([doc_ids[length - 2 :], query_rows[:, length - 2 :].reshape(-1)]),
+    )
+    packed = entering(forward_piece, "ctx", packed_join(key_row), False, reach)
+    state_in, normer_in, edge = unpack(packed, tail_state.shape, tail_normer.shape, 2 + 2 * row_count)
+    before = (edge[:2], edge[2:].reshape(row_count, 2), state_in, normer_in)
     query_ext = jnp.concatenate([before[1], query_rows], axis=1)
     ids_before = jnp.concatenate([before[0], doc_ids])
     q_conv = taps[0][:, None] * query_rows
@@ -137,21 +165,15 @@
 
     _, local_pullback = jax.vjp(local_forward, q_conv, k_feat, head_values, before[2], before[3])
     grad_qconv, grad_kfeat, grad_heads, grad_state, grad_normer = local_pullback(grad_attn)
-    backward_piece = jnp.concatenate(
-        [
-            doc_ids[:2],
-            grad_qconv[:, :2].reshape(-1),
-            grad_normer.reshape(-1),
-            grad_state.reshape(-1),
-        ]
-    )
-    packed = entering(backward_piece, "ctx", packed_join(0, prefix), True, reach)
-    after = (
-        packed[:2],
-        packed[2:prefix].reshape(row_count, 2),
-        packed[prefix + grad_normer.size :].reshape(grad_state.shape),
-        packed[prefix : prefix + grad_normer.size].reshape(grad_normer.shape),
-    )
+    backward_piece = pack(
+        grad_state,
+        grad_normer,
+        doc_ids[0],
+        jnp.concatenate([doc_ids[:2], grad_qconv[:, :2].reshape(-1)]),
+    )
+    packed = entering(backward_piece, "ctx", packed_join(key_row), True, reach)
+    state_out, normer_out, edge = unpack(packed, grad_state.shape, grad_normer.shape, 2 + 2 * row_count)
+    after = (edge[:2], edge[2:].reshape(row_count, 2), state_out, normer_out)
     head_mask = (doc_ids == after[0][0]).astype(jnp.float32)
     flowing = (
         jnp.einsum("hfd,shd->hfs", after[2], head_values, precision=split_mode)

time: 192 us -> 178 us (0.927)
  the two profiles are of different devices: /device:TPU:48 before, /device:TPU:52 now
where the time goes in v4:
time: 178 us; the launch traced here: 177 us
  starting transfers between devices  65.1 us (37%)
  waiting for transfers between devices  65.1 us (37%)
  between operations  16.1 us (9%)
  other arithmetic  13.5 us (8%)
  local copies, waits for them, and re-layouts  9.46 us (5%)
  matrix products  7.96 us (4%)
    ppermute x14, starting transfers between devices, shifted(): return lax.ppermute(piece, axis, pairs)  65.1 us
    ppermute x14, waiting for transfers between devices, shifted(): return lax.ppermute(piece, axis, pairs)  65.1 us
  transfers between devices with their start and end apart: 15, of which 13 were waited for; matrix products, arithmetic and copies ran while one was open for 4% of the time, Pallas kernels for 0%

profile of v4, /device:TPU:52, one launch (start us, length us, event | category | flops | bytes accessed | tf_op | source)
XLA Modules:
  0.0 177.2 jit_solution(10070764309765300539)
XLA Ops:
  7.2 0.8 add_convert_fusion
  9.2 0.7 multiply_multiply_fusion.1
  9.9 0.7 convert_multiply_fusion
  10.6 1.3 compare_convert_fusion.6
  11.9 0.8 slice.544
  13.0 1.3 concatenate.30
  14.5 1.0 fusion.8
  15.7 0.6 broadcast_in_dim.126
  16.4 7.9 %collective-permute-start.2 = (f32[312,128]{1,0:T(8,128)S(1)}, f32[312,128]{1,0:T(8,128)S(1)}, u32[]{:S(2)}, u32[]{:S(2)}) collective-permute-start(f32[312,128]{1,0:T(8,128)S(1)} %concatenate.32), channel_id=1, source_target_pairs={{0,24},{8,32},{16,40},{24,48},{32,56},{40,64},{48,72},{56,80},{64,... | collective-permute-start | bytes 479240 | tf_op jit(solution)/shard_map/ppermute | solution.py:21
  24.3 7.3 %collective-permute-start.1 = (f32[312,128]{1,0:T(8,128)S(1)}, f32[312,128]{1,0:T(8,128)S(1)}, u32[]{:S(2)}, u32[]{:S(2)}) collective-permute-start(f32[312,128]{1,0:T(8,128)S(1)} %concatenate.32), channel_id=1, source_target_pairs={{0,16},{8,24},{16,32},{24,40},{32,48},{40,56},{48,64},{56,72},{64,... | collective-permute-start | bytes 479240 | tf_op jit(solution)/shard_map/ppermute | solution.py:21
  31.6 4.3 %collective-permute-start = (f32[312,128]{1,0:T(8,128)S(1)}, f32[312,128]{1,0:T(8,128)S(1)}, u32[]{:S(2)}, u32[]{:S(2)}) collective-permute-start(f32[312,128]{1,0:T(8,128)S(1)} %concatenate.32), channel_id=1, source_target_pairs={{0,8},{8,16},{16,24},{24,32},{32,40},{40,48},{48,56},{56,64},{64,7... | collective-permute-start | bytes 479240 | tf_op jit(solution)/shard_map/ppermute | solution.py:21
  37.3 6.7 %collective-permute-done.2 = f32[312,128]{1,0:T(8,128)S(1)} collective-permute-done((f32[312,128]{1,0:T(8,128)S(1)}, f32[312,128]{1,0:T(8,128)S(1)}, u32[]{:S(2)}, u32[]{:S(2)}) %collective-permute-start.2) | collective-permute-done | bytes 159776 | tf_op jit(solution)/shard_map/ppermute | solution.py:21
  44.0 5.8 %collective-permute-done.1 = f32[312,128]{1,0:T(8,128)S(1)} collective-permute-done((f32[312,128]{1,0:T(8,128)S(1)}, f32[312,128]{1,0:T(8,128)S(1)}, u32[]{:S(2)}, u32[]{:S(2)}) %collective-permute-start.1) | collective-permute-done | bytes 159776 | tf_op jit(solution)/shard_map/ppermute | solution.py:21
  49.9 3.1 %collective-permute-done = f32[312,128]{1,0:T(8,128)S(1)} collective-permute-done((f32[312,128]{1,0:T(8,128)S(1)}, f32[312,128]{1,0:T(8,128)S(1)}, u32[]{:S(2)}, u32[]{:S(2)}) %collective-permute-start) | collective-permute-done | bytes 159776 | tf_op jit(solution)/shard_map/ppermute | solution.py:21
  53.1 0.7 compare_bitcast_fusion.17
  53.9 1.9 %collective-permute-start.6 = (f32[312,128]{1,0:T(8,128)S(1)}, f32[312,128]{1,0:T(8,128)S(1)}, u32[]{:S(2)}, u32[]{:S(2)}) collective-permute-start(f32[312,128]{1,0:T(8,128)S(1)} %add_select_fusion.9), channel_id=1, source_target_pairs={{0,104},{8,112},{16,120},{24,128},{32,136},{40,144},{48,152},{56,1... | collective-permute-start | bytes 479240 | tf_op jit(solution)/shard_map/ppermute | solution.py:21
  55.8 4.7 %collective-permute-start.5 = (f32[312,128]{1,0:T(8,128)S(1)}, f32[312,128]{1,0:T(8,128)S(1)}, u32[]{:S(2)}, u32[]{:S(2)}) collective-permute-start(f32[312,128]{1,0:T(8,128)S(1)} %add_select_fusion.9), channel_id=1, source_target_pairs={{0,72},{8,80},{16,88},{24,96},{32,104},{40,112},{48,120},{56,128},... | collective-permute-start | bytes 479240 | tf_op jit(solution)/shard_map/ppermute | solution.py:21
  60.6 3.1 %collective-permute-start.4 = (f32[312,128]{1,0:T(8,128)S(1)}, f32[312,128]{1,0:T(8,128)S(1)}, u32[]{:S(2)}, u32[]{:S(2)}) collective-permute-start(f32[312,128]{1,0:T(8,128)S(1)} %add_select_fusion.9), channel_id=1, source_target_pairs={{0,40},{8,48},{16,56},{24,64},{32,72},{40,80},{48,88},{56,96},{64,... | collective-permute-start | bytes 479240 | tf_op jit(solution)/shard_map/ppermute | solution.py:21
  63.7 3.4 %collective-permute-start.3 = (f32[312,128]{1,0:T(8,128)S(1)}, f32[312,128]{1,0:T(8,128)S(1)}, u32[]{:S(2)}, u32[]{:S(2)}) collective-permute-start(f32[312,128]{1,0:T(8,128)S(1)} %add_select_fusion.9), channel_id=1, source_target_pairs={{0,8},{8,16},{16,24},{24,32},{32,40},{40,48},{48,56},{56,64},{64,7... | collective-permute-start | bytes 479240 | tf_op jit(solution)/shard_map/ppermute | solution.py:21
  67.6 5.4 %collective-permute-done.5 = f32[312,128]{1,0:T(8,128)S(1)} collective-permute-done((f32[312,128]{1,0:T(8,128)S(1)}, f32[312,128]{1,0:T(8,128)S(1)}, u32[]{:S(2)}, u32[]{:S(2)}) %collective-permute-start.5) | collective-permute-done | bytes 159776 | tf_op jit(solution)/shard_map/ppermute | solution.py:21
  73.1 11.1 %collective-permute-done.4 = f32[312,128]{1,0:T(8,128)S(1)} collective-permute-done((f32[312,128]{1,0:T(8,128)S(1)}, f32[312,128]{1,0:T(8,128)S(1)}, u32[]{:S(2)}, u32[]{:S(2)}) %collective-permute-start.4) | collective-permute-done | bytes 159776 | tf_op jit(solution)/shard_map/ppermute | solution.py:21
  84.3 3.1 %collective-permute-done.3 = f32[312,128]{1,0:T(8,128)S(1)} collective-permute-done((f32[312,128]{1,0:T(8,128)S(1)}, f32[312,128]{1,0:T(8,128)S(1)}, u32[]{:S(2)}, u32[]{:S(2)}) %collective-permute-start.3) | collective-permute-done | bytes 159776 | tf_op jit(solution)/shard_map/ppermute | solution.py:21
  87.6 0.6 slice.557
  88.5 0.7 compare_convert_fusion.4
  89.7 1.3 concatenate.35
  92.2 1.9 %fusion.103 = f32[128,256]{0,1:T(8,128)S(1)} fusion(bf16[128,4096]{1,0:T(8,128)(2,1)} %all-gather.2.cloned.1.call-done, bf16[256,4096]{1,0:T(8,128)(2,1)S(1)} %copy-done), kind=kOutput, calls=%fused_computation.281 | convolution fusion | flops 268435456 | bytes 3276800 | tf_op jit(solution)/shard_map/transpose(jvp())/reshape | solution.py:164
  97.1 0.9 fusion.13
  98.3 0.8 add_multiply_fusion.1
  99.3 0.7 fusion.97
  100.5 0.7 concatenate.37
  101.2 5.1 %collective-permute-start.9 = (f32[312,128]{1,0:T(8,128)S(1)}, f32[312,128]{1,0:T(8,128)S(1)}, u32[]{:S(2)}, u32[]{:S(2)}) collective-permute-start(f32[312,128]{1,0:T(8,128)S(1)} %concatenate.37), channel_id=1, source_target_pairs={{24,0},{32,8},{40,16},{48,24},{56,32},{64,40},{72,48},{80,56},{88,... | collective-permute-start | bytes 479240 | tf_op jit(solution)/shard_map/ppermute | solution.py:21
  106.4 4.5 %collective-permute-start.8 = (f32[312,128]{1,0:T(8,128)S(1)}, f32[312,128]{1,0:T(8,128)S(1)}, u32[]{:S(2)}, u32[]{:S(2)}) collective-permute-start(f32[312,128]{1,0:T(8,128)S(1)} %concatenate.37), channel_id=1, source_target_pairs={{16,0},{24,8},{32,16},{40,24},{48,32},{56,40},{64,48},{72,56},{80,... | collective-permute-start | bytes 479240 | tf_op jit(solution)/shard_map/ppermute | solution.py:21
  110.9 4.2 %collective-permute-start.7 = (f32[312,128]{1,0:T(8,128)S(1)}, f32[312,128]{1,0:T(8,128)S(1)}, u32[]{:S(2)}, u32[]{:S(2)}) collective-permute-start(f32[312,128]{1,0:T(8,128)S(1)} %concatenate.37), channel_id=1, source_target_pairs={{8,0},{16,8},{24,16},{32,24},{40,32},{48,40},{56,48},{64,56},{72,6... | collective-permute-start | bytes 479240 | tf_op jit(solution)/shard_map/ppermute | solution.py:21
  115.4 1.9 %collective-permute-done.9 = f32[312,128]{1,0:T(8,128)S(1)} collective-permute-done((f32[312,128]{1,0:T(8,128)S(1)}, f32[312,128]{1,0:T(8,128)S(1)}, u32[]{:S(2)}, u32[]{:S(2)}) %collective-permute-start.9) | collective-permute-done | bytes 159776 | tf_op jit(solution)/shard_map/ppermute | solution.py:21
  117.3 6.5 %collective-permute-done.8 = f32[312,128]{1,0:T(8,128)S(1)} collective-permute-done((f32[312,128]{1,0:T(8,128)S(1)}, f32[312,128]{1,0:T(8,128)S(1)}, u32[]{:S(2)}, u32[]{:S(2)}) %collective-permute-start.8) | collective-permute-done | bytes 159776 | tf_op jit(solution)/shard_map/ppermute | solution.py:21
  124.0 3.3 %collective-permute-done.7 = f32[312,128]{1,0:T(8,128)S(1)} collective-permute-done((f32[312,128]{1,0:T(8,128)S(1)}, f32[312,128]{1,0:T(8,128)S(1)}, u32[]{:S(2)}, u32[]{:S(2)}) %collective-permute-start.7) | collective-permute-done | bytes 159776 | tf_op jit(solution)/shard_map/ppermute | solution.py:21
  128.1 5.0 %collective-permute-start.13 = (f32[312,128]{1,0:T(8,128)S(1)}, f32[312,128]{1,0:T(8,128)S(1)}, u32[]{:S(2)}, u32[]{:S(2)}) collective-permute-start(f32[312,128]{1,0:T(8,128)S(1)} %add_select_fusion.3), channel_id=1, source_target_pairs={{104,0},{112,8},{120,16},{128,24},{136,32},{144,40},{152,48},{160,... | collective-permute-start | bytes 479240 | tf_op jit(solution)/shard_map/ppermute | solution.py:21
  133.1 2.9 %collective-permute-start.12 = (f32[312,128]{1,0:T(8,128)S(1)}, f32[312,128]{1,0:T(8,128)S(1)}, u32[]{:S(2)}, u32[]{:S(2)}) collective-permute-start(f32[312,128]{1,0:T(8,128)S(1)} %add_select_fusion.3), channel_id=1, source_target_pairs={{72,0},{80,8},{88,16},{96,24},{104,32},{112,40},{120,48},{128,56},... | collective-permute-start | bytes 479240 | tf_op jit(solution)/shard_map/ppermute | solution.py:21
  136.0 0.9 fusion.10
  136.9 7.5 %collective-permute-start.11 = (f32[312,128]{1,0:T(8,128)S(1)}, f32[312,128]{1,0:T(8,128)S(1)}, u32[]{:S(2)}, u32[]{:S(2)}) collective-permute-start(f32[312,128]{1,0:T(8,128)S(1)} %add_select_fusion.3), channel_id=1, source_target_pairs={{40,0},{48,8},{56,16},{64,24},{72,32},{80,40},{88,48},{96,56},{104... | collective-permute-start | bytes 479240 | tf_op jit(solution)/shard_map/ppermute | solution.py:21
  144.4 3.3 %collective-permute-start.10 = (f32[312,128]{1,0:T(8,128)S(1)}, f32[312,128]{1,0:T(8,128)S(1)}, u32[]{:S(2)}, u32[]{:S(2)}) collective-permute-start(f32[312,128]{1,0:T(8,128)S(1)} %add_select_fusion.3), channel_id=1, source_target_pairs={{8,0},{16,8},{24,16},{32,24},{40,32},{48,40},{56,48},{64,56},{72,6... | collective-permute-start | bytes 479240 | tf_op jit(solution)/shard_map/ppermute | solution.py:21
  147.8 1.5 collective-permute-done.12
  149.4 12.5 %collective-permute-done.11 = f32[312,128]{1,0:T(8,128)S(1)} collective-permute-done((f32[312,128]{1,0:T(8,128)S(1)}, f32[312,128]{1,0:T(8,128)S(1)}, u32[]{:S(2)}, u32[]{:S(2)}) %collective-permute-start.11) | collective-permute-done | bytes 159776 | tf_op jit(solution)/shard_map/ppermute | solution.py:21
  161.9 3.6 %collective-permute-done.10 = f32[312,128]{1,0:T(8,128)S(1)} collective-permute-done((f32[312,128]{1,0:T(8,128)S(1)}, f32[312,128]{1,0:T(8,128)S(1)}, u32[]{:S(2)}, u32[]{:S(2)}) %collective-permute-start.10) | collective-permute-done | bytes 159776 | tf_op jit(solution)/shard_map/ppermute | solution.py:21
  166.4 0.7 compare_convert_fusion.2
  168.3 0.8 copy.35
  169.0 0.7 fusion.84
  169.7 0.7 add_multiply_fusion
  (159 shorter events, 12.1 us)
Async XLA Ops:
  7.2 85.0 %copy-start = (bf16[256,4096]{1,0:T(8,128)(2,1)S(1)}, bf16[256,4096]{1,0:T(8,128)(2,1)}, u32[]{:S(2)}) copy-start(bf16[256,4096]{1,0:T(8,128)(2,1)} %param.12) | copy-start | bytes 6291460
  7.2 29.5 %copy-start.3 = (bf16[32,128]{1,0:T(8,128)(2,1)S(1)}, bf16[32,128]{1,0:T(8,128)(2,1)}, u32[]{:S(2)}) copy-start(bf16[32,128]{1,0:T(8,128)(2,1)} %param.7) | copy-start | bytes 24580
  7.2 30.1 %copy-start.7 = (bf16[3,32]{1,0:T(4,128)(2,1)S(1)}, bf16[3,32]{1,0:T(4,128)(2,1)}, u32[]{:S(2)}) copy-start(bf16[3,32]{1,0:T(4,128)(2,1)} %param.11) | copy-start | bytes 580
  7.2 84.9 %all-gather.2.cloned.1.call-start = ((), (), s32[]{:S(2)}) async-start(), calls=%async_computation | async-start | bytes 1179648 | tf_op jit(solution)/shard_map/all_gather | solution.py:120
  14.5 73.9 %copy-start.5 = (s32[128]{0:T(128)S(1)}, s32[128]{0:T(128)}, u32[]{:S(2)}) copy-start(s32[128]{0:T(128)} %param.10) | copy-start | bytes 1540
  16.4 8.0 %copy-start.4 = (f32[1,128]{1,0:T(1,128)}, f32[1,128]{1,0:T(1,128)S(1)}, u32[]{:S(2)}) copy-start(f32[1,128]{1,0:T(1,128)S(1)} %broadcast.205) | copy-start | bytes 1540
  16.4 27.6 %collective-permute-start.2 = (f32[312,128]{1,0:T(8,128)S(1)}, f32[312,128]{1,0:T(8,128)S(1)}, u32[]{:S(2)}, u32[]{:S(2)}) collective-permute-start(f32[312,128]{1,0:T(8,128)S(1)} %concatenate.32), channel_id=1, source_target_pairs={{0,24},{8,32},{16,40},{24,48},{32,56},{40,64},{48,72},{56,80},{64,... | collective-permute-start | bytes 479240 | tf_op jit(solution)/shard_map/ppermute | solution.py:21
  24.3 25.4 %collective-permute-start.1 = (f32[312,128]{1,0:T(8,128)S(1)}, f32[312,128]{1,0:T(8,128)S(1)}, u32[]{:S(2)}, u32[]{:S(2)}) collective-permute-start(f32[312,128]{1,0:T(8,128)S(1)} %concatenate.32), channel_id=1, source_target_pairs={{0,16},{8,24},{16,32},{24,40},{32,48},{40,56},{48,64},{56,72},{64,... | collective-permute-start | bytes 479240 | tf_op jit(solution)/shard_map/ppermute | solution.py:21
  31.6 21.4 %collective-permute-start = (f32[312,128]{1,0:T(8,128)S(1)}, f32[312,128]{1,0:T(8,128)S(1)}, u32[]{:S(2)}, u32[]{:S(2)}) collective-permute-start(f32[312,128]{1,0:T(8,128)S(1)} %concatenate.32), channel_id=1, source_target_pairs={{0,8},{8,16},{16,24},{24,32},{32,40},{40,48},{48,56},{56,64},{64,7... | collective-permute-start | bytes 479240 | tf_op jit(solution)/shard_map/ppermute | solution.py:21
  53.9 13.7 %collective-permute-start.6 = (f32[312,128]{1,0:T(8,128)S(1)}, f32[312,128]{1,0:T(8,128)S(1)}, u32[]{:S(2)}, u32[]{:S(2)}) collective-permute-start(f32[312,128]{1,0:T(8,128)S(1)} %add_select_fusion.9), channel_id=1, source_target_pairs={{0,104},{8,112},{16,120},{24,128},{32,136},{40,144},{48,152},{56,1... | collective-permute-start | bytes 479240 | tf_op jit(solution)/shard_map/ppermute | solution.py:21
  55.8 17.1 %collective-permute-start.5 = (f32[312,128]{1,0:T(8,128)S(1)}, f32[312,128]{1,0:T(8,128)S(1)}, u32[]{:S(2)}, u32[]{:S(2)}) collective-permute-start(f32[312,128]{1,0:T(8,128)S(1)} %add_select_fusion.9), channel_id=1, source_target_pairs={{0,72},{8,80},{16,88},{24,96},{32,104},{40,112},{48,120},{56,128},... | collective-permute-start | bytes 479240 | tf_op jit(solution)/shard_map/ppermute | solution.py:21
  60.6 23.6 %collective-permute-start.4 = (f32[312,128]{1,0:T(8,128)S(1)}, f32[312,128]{1,0:T(8,128)S(1)}, u32[]{:S(2)}, u32[]{:S(2)}) collective-permute-start(f32[312,128]{1,0:T(8,128)S(1)} %add_select_fusion.9), channel_id=1, source_target_pairs={{0,40},{8,48},{16,56},{24,64},{32,72},{40,80},{48,88},{56,96},{64,... | collective-permute-start | bytes 479240 | tf_op jit(solution)/shard_map/ppermute | solution.py:21
  63.7 23.8 %collective-permute-start.3 = (f32[312,128]{1,0:T(8,128)S(1)}, f32[312,128]{1,0:T(8,128)S(1)}, u32[]{:S(2)}, u32[]{:S(2)}) collective-permute-start(f32[312,128]{1,0:T(8,128)S(1)} %add_select_fusion.9), channel_id=1, source_target_pairs={{0,8},{8,16},{16,24},{24,32},{32,40},{40,48},{48,56},{56,64},{64,7... | collective-permute-start | bytes 479240 | tf_op jit(solution)/shard_map/ppermute | solution.py:21
  91.2 2.9 %copy-start.1 = (bf16[128,256]{1,0:T(8,128)(2,1)S(1)}, bf16[128,256]{1,0:T(8,128)(2,1)}, u32[]{:S(2)}) copy-start(bf16[128,256]{1,0:T(8,128)(2,1)} %param.9) | copy-start | bytes 196612
  91.7 2.9 %copy-start.8 = (f32[128,2]{0,1:T(2,128)}, f32[128,2]{0,1:T(2,128)S(1)}, u32[]{:S(2)}) copy-start(f32[128,2]{0,1:T(2,128)S(1)} %get-tuple-element.10) | copy-start | bytes 3076
  101.2 65.2 %copy-start.6 = (s32[128]{0:T(128)S(1)}, s32[128]{0:T(128)}, u32[]{:S(2)}) copy-start(s32[128]{0:T(128)} %param.10) | copy-start | bytes 1540
  101.2 16.0 %collective-permute-start.9 = (f32[312,128]{1,0:T(8,128)S(1)}, f32[312,128]{1,0:T(8,128)S(1)}, u32[]{:S(2)}, u32[]{:S(2)}) collective-permute-start(f32[312,128]{1,0:T(8,128)S(1)} %concatenate.37), channel_id=1, source_target_pairs={{24,0},{32,8},{40,16},{48,24},{56,32},{64,40},{72,48},{80,56},{88,... | collective-permute-start | bytes 479240 | tf_op jit(solution)/shard_map/ppermute | solution.py:21
  106.4 17.4 %collective-permute-start.8 = (f32[312,128]{1,0:T(8,128)S(1)}, f32[312,128]{1,0:T(8,128)S(1)}, u32[]{:S(2)}, u32[]{:S(2)}) collective-permute-start(f32[312,128]{1,0:T(8,128)S(1)} %concatenate.37), channel_id=1, source_target_pairs={{16,0},{24,8},{32,16},{40,24},{48,32},{56,40},{64,48},{72,56},{80,... | collective-permute-start | bytes 479240 | tf_op jit(solution)/shard_map/ppermute | solution.py:21
  110.9 16.4 %collective-permute-start.7 = (f32[312,128]{1,0:T(8,128)S(1)}, f32[312,128]{1,0:T(8,128)S(1)}, u32[]{:S(2)}, u32[]{:S(2)}) collective-permute-start(f32[312,128]{1,0:T(8,128)S(1)} %concatenate.37), channel_id=1, source_target_pairs={{8,0},{16,8},{24,16},{32,24},{40,32},{48,40},{56,48},{64,56},{72,6... | collective-permute-start | bytes 479240 | tf_op jit(solution)/shard_map/ppermute | solution.py:21
  128.1 41.7 %copy-start.2 = (bf16[32,128]{1,0:T(8,128)(2,1)S(1)}, bf16[32,128]{1,0:T(8,128)(2,1)}, u32[]{:S(2)}) copy-start(bf16[32,128]{1,0:T(8,128)(2,1)} %param.8) | copy-start | bytes 24580
  128.1 19.7 %collective-permute-start.13 = (f32[312,128]{1,0:T(8,128)S(1)}, f32[312,128]{1,0:T(8,128)S(1)}, u32[]{:S(2)}, u32[]{:S(2)}) collective-permute-start(f32[312,128]{1,0:T(8,128)S(1)} %add_select_fusion.3), channel_id=1, source_target_pairs={{104,0},{112,8},{120,16},{128,24},{136,32},{144,40},{152,48},{160,... | collective-permute-start | bytes 479240 | tf_op jit(solution)/shard_map/ppermute | solution.py:21
  133.1 16.1 %collective-permute-start.12 = (f32[312,128]{1,0:T(8,128)S(1)}, f32[312,128]{1,0:T(8,128)S(1)}, u32[]{:S(2)}, u32[]{:S(2)}) collective-permute-start(f32[312,128]{1,0:T(8,128)S(1)} %add_select_fusion.3), channel_id=1, source_target_pairs={{72,0},{80,8},{88,16},{96,24},{104,32},{112,40},{120,48},{128,56},... | collective-permute-start | bytes 479240 | tf_op jit(solution)/shard_map/ppermute | solution.py:21
  136.9 24.9 %collective-permute-start.11 = (f32[312,128]{1,0:T(8,128)S(1)}, f32[312,128]{1,0:T(8,128)S(1)}, u32[]{:S(2)}, u32[]{:S(2)}) collective-permute-start(f32[312,128]{1,0:T(8,128)S(1)} %add_select_fusion.3), channel_id=1, source_target_pairs={{40,0},{48,8},{56,16},{64,24},{72,32},{80,40},{88,48},{96,56},{104... | collective-permute-start | bytes 479240 | tf_op jit(solution)/shard_map/ppermute | solution.py:21
  144.4 21.1 %collective-permute-start.10 = (f32[312,128]{1,0:T(8,128)S(1)}, f32[312,128]{1,0:T(8,128)S(1)}, u32[]{:S(2)}, u32[]{:S(2)}) collective-permute-start(f32[312,128]{1,0:T(8,128)S(1)} %add_select_fusion.3), channel_id=1, source_target_pairs={{8,0},{16,8},{24,16},{32,24},{40,32},{48,40},{56,48},{64,56},{72,6... | collective-permute-start | bytes 479240 | tf_op jit(solution)/shard_map/ppermute | solution.py:21
Sparse Core Ops, SparseCore 0:
  36.1 28.0 all-gather.1

commit v5 on v4

--- a/solution.py
+++ b/solution.py
@@ -28,16 +28,44 @@
     return total
 
 
-def entering(shard, axis, combine, reverse, reach):
-    size = lax.axis_size(axis)
+def window_steps(reach, size):
     fan = 1
     while fan * fan < reach:
         fan += 1
     near = [step for step in range(fan - 1, 0, -1) if step < size]
+    far = [1 + fan * k for k in range(-(-reach // fan) - 1, -1, -1)]
+    return near, [step for step in far if step < size]
+
+
+def entering(shard, axis, combine, reverse, reach):
+    near, far = window_steps(reach, lax.axis_size(axis))
     total = fold(combine, [shifted(shard, axis, step, reverse) for step in near] + [shard])
-    far = [1 + fan * k for k in range(-(-reach // fan) - 1, -1, -1)]
-    far = [step for step in far if step < size]
     return fold(combine, [shifted(total, axis, step, reverse) for step in far])
+
+
+def rows_of(flat, lanes):
+    count = -(-flat.size // lanes)
+    return jnp.pad(flat, (0, count * lanes - flat.size)).reshape(count, lanes)
+
+
+def raw_pack(keys, values, doc_ids, edge):
+    lanes = keys.shape[1]
+    parts = [values.T, keys, doc_ids.astype(keys.dtype)[None, :], rows_of(edge, lanes)]
+    rows = sum(part.shape[0] for part in parts)
+    parts.append(jnp.zeros((-rows % 16, lanes), keys.dtype))
+    return jnp.concatenate(parts)
+
+
+def raw_unpack(packed, value_rows, key_rows, edge_size):
+    lanes = packed.shape[1]
+    ids_row = value_rows + key_rows
+    edge_rows = -(-edge_size // lanes)
+    return (
+        packed[:value_rows],
+        packed[value_rows:ids_row],
+        packed[ids_row].astype(jnp.float32),
+        packed[ids_row + 1 : ids_row + 1 + edge_rows].reshape(-1)[:edge_size],
+    )
 
 
 def features(entries):
@@ -128,21 +156,42 @@
     head_values = values.astype(jnp.float32).reshape(length, local_heads, head_width)
     taps = conv_weight.astype(jnp.float32)
     k_feat, feature_pullback = jax.vjp(features, key_heads)
-    tail_mask = (doc_ids == doc_ids[length - 1]).astype(jnp.float32)
-    tail_feat = k_feat * tail_mask[None, None, :]
-    tail_state = jnp.einsum("hfs,shd->hfd", tail_feat, head_values, precision=split_mode)
+    row_count = query_rows.shape[0]
+    near, far = window_steps(reach, lax.axis_size("ctx"))
+    raw = raw_pack(keys, values, doc_ids, queries[:, length - 2 :].reshape(-1))
+    received = [
+        raw_unpack(shifted(raw, "ctx", step, False), values.shape[1], row_count, 2 * row_count)
+        for step in near
+    ]
+    window_keys = jnp.concatenate([part[1] for part in received], axis=1).astype(jnp.float32)
+    window_feat = jnp.concatenate(
+        [features(window_keys.reshape(local_heads, FD, -1)), k_feat], axis=2
+    )
+    window_values = jnp.concatenate(
+        [part[0] for part in received] + [values.T], axis=1
+    ).astype(jnp.float32)
+    window_ids = jnp.concatenate([part[2] for part in received] + [doc_ids])
+    tail_mask = (window_ids == doc_ids[length - 1]).astype(jnp.float32)
+    tail_feat = window_feat * tail_mask[None, None, :]
+    tail_state = jnp.einsum(
+        "hft,hdt->hfd",
+        tail_feat,
+        window_values.reshape(local_heads, head_width, -1),
+        precision=split_mode,
+    )
     tail_normer = jnp.sum(tail_feat, axis=2)
-    row_count = query_rows.shape[0]
     key_row = tail_state.size // head_width + -(-tail_normer.size // head_width)
-    forward_piece = pack(
-        tail_state,
-        tail_normer,
-        doc_ids[length - 1],
-        jnp.concatenate([doc_ids[length - 2 :], query_rows[:, length - 2 :].reshape(-1)]),
-    )
-    packed = entering(forward_piece, "ctx", packed_join(key_row), False, reach)
-    state_in, normer_in, edge = unpack(packed, tail_state.shape, tail_normer.shape, 2 + 2 * row_count)
-    before = (edge[:2], edge[2:].reshape(row_count, 2), state_in, normer_in)
+    forward_piece = pack(tail_state, tail_normer, doc_ids[length - 1], jnp.zeros((1,), jnp.float32))
+    join = packed_join(key_row)
+    packed = fold(join, [shifted(forward_piece, "ctx", step, False) for step in far])
+    state_in, normer_in, _ = unpack(packed, tail_state.shape, tail_normer.shape, 1)
+    previous = received[-1] if near else raw_unpack(jnp.zeros_like(raw), values.shape[1], row_count, 2 * row_count)
+    before = (
+        previous[2][length - 2 :],
+        previous[3].astype(jnp.float32).reshape(row_count, 2),
+        state_in,
+        normer_in,
+    )
     query_ext = jnp.concatenate([before[1], query_rows], axis=1)
     ids_before = jnp.concatenate([before[0], doc_ids])
     q_conv = taps[0][:, None] * query_rows

time: 178 us -> 171 us (0.961)
  the two profiles are of different devices: /device:TPU:52 before, /device:TPU:124 now
where the time goes in v5:
time: 171 us; the launch traced here: 170 us
  starting transfers between devices  64.1 us (37%)
  waiting for transfers between devices  44.4 us (26%)
  local copies, waits for them, and re-layouts  20.3 us (12%)
  other arithmetic  18.8 us (11%)
  between operations  16.3 us (10%)
  matrix products  5.91 us (3%)
    ppermute x14, starting transfers between devices, shifted(): return lax.ppermute(piece, axis, pairs)  64.1 us
    ppermute x14, waiting for transfers between devices, shifted(): return lax.ppermute(piece, axis, pairs)  44.4 us
    concatenate x3, local copies, waits for them, and re-layouts, features(): jnp.concatenate([jnp.ones_like(scaled[..., :1, :]), scaled, scaled * scal...  10.6 us
    mul x75, other arithmetic, features(): scaled[..., i:i + 1, :] * scaled[..., i + 1:, :]  5.83 us
  transfers between devices with their start and end apart: 15, of which 7 were waited for; matrix products, arithmetic and copies ran while one was open for 18% of the time, Pallas kernels for 0%

profile of v5, /device:TPU:124, one launch (start us, length us, event | category | flops | bytes accessed | tf_op | source)
XLA Modules:
  0.0 169.9 jit_solution(2892355029640660244)
XLA Ops:
  7.2 0.8 add_convert_fusion
  8.0 0.8 slice.495
  8.9 1.0 copy.29
  9.9 0.9 concatenate.56
  10.8 4.3 %collective-permute-start.2 = (bf16[304,128]{1,0:T(8,128)(2,1)S(1)}, bf16[304,128]{1,0:T(8,128)(2,1)S(1)}, u32[]{:S(2)}, u32[]{:S(2)}) collective-permute-start(bf16[304,128]{1,0:T(8,128)(2,1)S(1)} %concatenate.56), channel_id=1, source_target_pairs={{0,8},{8,16},{16,24},{24,32},{32,40},{40,48},{48,56},{56,64},{64,7... | collective-permute-start | bytes 233480 | tf_op jit(solution)/shard_map/ppermute | solution.py:21
  15.0 7.3 %collective-permute-start.1 = (bf16[304,128]{1,0:T(8,128)(2,1)S(1)}, bf16[304,128]{1,0:T(8,128)(2,1)S(1)}, u32[]{:S(2)}, u32[]{:S(2)}) collective-permute-start(bf16[304,128]{1,0:T(8,128)(2,1)S(1)} %concatenate.56), channel_id=1, source_target_pairs={{0,16},{8,24},{16,32},{24,40},{32,48},{40,56},{48,64},{56,72},{64,... | collective-permute-start | bytes 233480 | tf_op jit(solution)/shard_map/ppermute | solution.py:21
  22.4 7.6 %collective-permute-start = (bf16[304,128]{1,0:T(8,128)(2,1)S(1)}, bf16[304,128]{1,0:T(8,128)(2,1)S(1)}, u32[]{:S(2)}, u32[]{:S(2)}) collective-permute-start(bf16[304,128]{1,0:T(8,128)(2,1)S(1)} %concatenate.56), channel_id=1, source_target_pairs={{0,24},{8,32},{16,40},{24,48},{32,56},{40,64},{48,72},{56,80},{64,... | collective-permute-start | bytes 233480 | tf_op jit(solution)/shard_map/ppermute | solution.py:21
  30.0 0.7 convert_element_type.106
  30.7 0.7 multiply_multiply_fusion.2
  31.4 0.7 convert_multiply_fusion.1
  32.8 0.7 convert_element_type.93
  35.4 1.3 concatenate.62
  38.0 0.6 multiply_multiply_fusion
  38.6 0.6 slice_multiply_fusion.68
  41.1 0.6 slice_multiply_fusion.8
  42.3 0.6 slice_multiply_fusion.7
  43.0 0.6 slice_multiply_fusion
  43.8 0.6 fusion.95
  44.5 7.3 %concatenate.61 = f32[2,153,384]{2,1,0:T(8,128)S(1)} concatenate(f32[2,1,384]{2,1,0:T(1,128)S(1)} %broadcast_in_dim.112, f32[2,16,384]{2,1,0:T(8,128)S(1)} %get-tuple-element.107, f32[2,16,384]{2,1,0:T(8,128)} %get-tuple-element.106, f32[2,15,384]{2,1,0:T(8,128)S(1)} %slice_multiply_fusion.6, f32[2,14,384]{2,1,0:T(8,128)S(1)} %slice_multiply_fusion.5, ...), dimensions={1} | concatenate | bytes 940032 | tf_op jit(solution)/shard_map/concatenate | solution.py:77
  52.4 0.6 broadcast_in_dim.115
  53.1 1.3 collective-permute-start.6
  54.4 3.1 %collective-permute-start.5 = (f32[312,128]{1,0:T(8,128)S(1)}, f32[312,128]{1,0:T(8,128)S(1)}, u32[]{:S(2)}, u32[]{:S(2)}) collective-permute-start(f32[312,128]{1,0:T(8,128)S(1)} %concatenate.66), channel_id=1, source_target_pairs={{0,72},{8,80},{16,88},{24,96},{32,104},{40,112},{48,120},{56,128},... | collective-permute-start | bytes 479240 | tf_op jit(solution)/shard_map/ppermute | solution.py:21
  57.5 3.7 %collective-permute-start.4 = (f32[312,128]{1,0:T(8,128)S(1)}, f32[312,128]{1,0:T(8,128)S(1)}, u32[]{:S(2)}, u32[]{:S(2)}) collective-permute-start(f32[312,128]{1,0:T(8,128)S(1)} %concatenate.66), channel_id=1, source_target_pairs={{0,40},{8,48},{16,56},{24,64},{32,72},{40,80},{48,88},{56,96},{64,... | collective-permute-start | bytes 479240 | tf_op jit(solution)/shard_map/ppermute | solution.py:21
  61.3 2.1 %collective-permute-start.3 = (f32[312,128]{1,0:T(8,128)S(1)}, f32[312,128]{1,0:T(8,128)S(1)}, u32[]{:S(2)}, u32[]{:S(2)}) collective-permute-start(f32[312,128]{1,0:T(8,128)S(1)} %concatenate.66), channel_id=1, source_target_pairs={{0,8},{8,16},{16,24},{24,32},{32,40},{40,48},{48,56},{56,64},{64,7... | collective-permute-start | bytes 479240 | tf_op jit(solution)/shard_map/ppermute | solution.py:21
  63.4 0.7 pad_maximum_fusion.3
  64.1 0.7 fusion.97
  64.9 1.8 %compare_convert_fusion.4 = (f32[128]{0:T(128)S(1)}, f32[128]{0:T(128)S(1)}, f32[128]{0:T(128)}) fusion(f32[130]{0:T(256)S(1)} %pad_maximum_fusion.3, s32[128]{0:T(128)} %param.10, f32[]{:T(128)} %bitcast.35), kind=kLoop, calls=%fused_computation.265 | loop fusion | flops 1024 | bytes 3076 | tf_op jit(solution)/shard_map/convert_element_type | solution.py:199
  66.7 0.8 multiply_multiply_fusion.1
  68.3 1.9 %concatenate.69 = f32[2,153,128]{2,1,0:T(8,128)S(1)} concatenate(f32[2,1,128]{2,1,0:T(1,128)} %copy-done.66, f32[2,16,128]{2,1,0:T(8,128)S(1)} %bitcast.282, f32[2,16,128]{2,1,0:T(8,128)S(1)} %get-tuple-element.11, f32[2,15,128]{2,1,0:T(8,128)S(1)} %slice_multiply_fusion.33, f32[2,14,128]{2,1,0:T(8,128)S(1)} %slice_multiply_fusion.32, f32[2,13,128]{2,1,0:T(8,128)S(1)} %slice_multiply_fusion.31, ...), dimensions={1} | concatenate | bytes 313344 | tf_op jit(solution)/shard_map/jvp()/concatenate | solution.py:77
  70.7 1.1 collective-permute-done.5
  71.9 10.2 %collective-permute-done.4 = f32[312,128]{1,0:T(8,128)S(1)} collective-permute-done((f32[312,128]{1,0:T(8,128)S(1)}, f32[312,128]{1,0:T(8,128)S(1)}, u32[]{:S(2)}, u32[]{:S(2)}) %collective-permute-start.4) | collective-permute-done | bytes 159776 | tf_op jit(solution)/shard_map/ppermute | solution.py:21
  83.3 1.9 %fusion.106 = f32[128,256]{0,1:T(8,128)S(1)} fusion(bf16[128,4096]{1,0:T(8,128)(2,1)} %all-gather.2.cloned.1.call-done, bf16[256,4096]{1,0:T(8,128)(2,1)S(1)} %copy-done), kind=kOutput, calls=%fused_computation.313 | convolution fusion | flops 268435456 | bytes 3276800 | tf_op jit(solution)/shard_map/transpose(jvp())/reshape | solution.py:213
  88.3 7.0 %collective-permute-start.9 = (f32[312,128]{1,0:T(8,128)S(1)}, f32[312,128]{1,0:T(8,128)S(1)}, u32[]{:S(2)}, u32[]{:S(2)}) collective-permute-start(f32[312,128]{1,0:T(8,128)S(1)} %concatenate.71), channel_id=1, source_target_pairs={{24,0},{32,8},{40,16},{48,24},{56,32},{64,40},{72,48},{80,56},{88,... | collective-permute-start | bytes 479240 | tf_op jit(solution)/shard_map/ppermute | solution.py:21
  95.3 5.9 %collective-permute-start.8 = (f32[312,128]{1,0:T(8,128)S(1)}, f32[312,128]{1,0:T(8,128)S(1)}, u32[]{:S(2)}, u32[]{:S(2)}) collective-permute-start(f32[312,128]{1,0:T(8,128)S(1)} %concatenate.71), channel_id=1, source_target_pairs={{16,0},{24,8},{32,16},{40,24},{48,32},{56,40},{64,48},{72,56},{80,... | collective-permute-start | bytes 479240 | tf_op jit(solution)/shard_map/ppermute | solution.py:21
  101.2 1.9 %collective-permute-start.7 = (f32[312,128]{1,0:T(8,128)S(1)}, f32[312,128]{1,0:T(8,128)S(1)}, u32[]{:S(2)}, u32[]{:S(2)}) collective-permute-start(f32[312,128]{1,0:T(8,128)S(1)} %concatenate.71), channel_id=1, source_target_pairs={{8,0},{16,8},{24,16},{32,24},{40,32},{48,40},{56,48},{64,56},{72,6... | collective-permute-start | bytes 479240 | tf_op jit(solution)/shard_map/ppermute | solution.py:21
  103.4 5.0 %collective-permute-done.9 = f32[312,128]{1,0:T(8,128)S(1)} collective-permute-done((f32[312,128]{1,0:T(8,128)S(1)}, f32[312,128]{1,0:T(8,128)S(1)}, u32[]{:S(2)}, u32[]{:S(2)}) %collective-permute-start.9) | collective-permute-done | bytes 159776 | tf_op jit(solution)/shard_map/ppermute | solution.py:21
  108.4 3.6 %collective-permute-done.8 = f32[312,128]{1,0:T(8,128)S(1)} collective-permute-done((f32[312,128]{1,0:T(8,128)S(1)}, f32[312,128]{1,0:T(8,128)S(1)}, u32[]{:S(2)}, u32[]{:S(2)}) %collective-permute-start.8) | collective-permute-done | bytes 159776 | tf_op jit(solution)/shard_map/ppermute | solution.py:21
  112.3 3.1 %collective-permute-done.7 = f32[312,128]{1,0:T(8,128)S(1)} collective-permute-done((f32[312,128]{1,0:T(8,128)S(1)}, f32[312,128]{1,0:T(8,128)S(1)}, u32[]{:S(2)}, u32[]{:S(2)}) %collective-permute-start.7) | collective-permute-done | bytes 159776 | tf_op jit(solution)/shard_map/ppermute | solution.py:21
  116.2 6.3 %collective-permute-start.13 = (f32[312,128]{1,0:T(8,128)S(1)}, f32[312,128]{1,0:T(8,128)S(1)}, u32[]{:S(2)}, u32[]{:S(2)}) collective-permute-start(f32[312,128]{1,0:T(8,128)S(1)} %add_select_fusion.3), channel_id=1, source_target_pairs={{104,0},{112,8},{120,16},{128,24},{136,32},{144,40},{152,48},{160,... | collective-permute-start | bytes 479240 | tf_op jit(solution)/shard_map/ppermute | solution.py:21
  122.5 8.2 %collective-permute-start.12 = (f32[312,128]{1,0:T(8,128)S(1)}, f32[312,128]{1,0:T(8,128)S(1)}, u32[]{:S(2)}, u32[]{:S(2)}) collective-permute-start(f32[312,128]{1,0:T(8,128)S(1)} %add_select_fusion.3), channel_id=1, source_target_pairs={{72,0},{80,8},{88,16},{96,24},{104,32},{112,40},{120,48},{128,56},... | collective-permute-start | bytes 479240 | tf_op jit(solution)/shard_map/ppermute | solution.py:21
  131.0 3.3 %collective-permute-start.11 = (f32[312,128]{1,0:T(8,128)S(1)}, f32[312,128]{1,0:T(8,128)S(1)}, u32[]{:S(2)}, u32[]{:S(2)}) collective-permute-start(f32[312,128]{1,0:T(8,128)S(1)} %add_select_fusion.3), channel_id=1, source_target_pairs={{40,0},{48,8},{56,16},{64,24},{72,32},{80,40},{88,48},{96,56},{104... | collective-permute-start | bytes 479240 | tf_op jit(solution)/shard_map/ppermute | solution.py:21
  134.4 1.9 %collective-permute-start.10 = (f32[312,128]{1,0:T(8,128)S(1)}, f32[312,128]{1,0:T(8,128)S(1)}, u32[]{:S(2)}, u32[]{:S(2)}) collective-permute-start(f32[312,128]{1,0:T(8,128)S(1)} %add_select_fusion.3), channel_id=1, source_target_pairs={{8,0},{16,8},{24,16},{32,24},{40,32},{48,40},{56,48},{64,56},{72,6... | collective-permute-start | bytes 479240 | tf_op jit(solution)/shard_map/ppermute | solution.py:21
  136.3 3.9 %collective-permute-done.12 = f32[312,128]{1,0:T(8,128)S(1)} collective-permute-done((f32[312,128]{1,0:T(8,128)S(1)}, f32[312,128]{1,0:T(8,128)S(1)}, u32[]{:S(2)}, u32[]{:S(2)}) %collective-permute-start.12) | collective-permute-done | bytes 159776 | tf_op jit(solution)/shard_map/ppermute | solution.py:21
  140.3 17.6 %collective-permute-done.11 = f32[312,128]{1,0:T(8,128)S(1)} collective-permute-done((f32[312,128]{1,0:T(8,128)S(1)}, f32[312,128]{1,0:T(8,128)S(1)}, u32[]{:S(2)}, u32[]{:S(2)}) %collective-permute-start.11) | collective-permute-done | bytes 159776 | tf_op jit(solution)/shard_map/ppermute | solution.py:21
  158.9 0.7 compare_convert_fusion.2
  160.9 0.8 copy.41
  161.6 0.7 fusion.82
  162.3 0.7 add_multiply_fusion
  (308 shorter events, 15.2 us)
Async XLA Ops:
  7.2 76.2 %copy-start = (bf16[256,4096]{1,0:T(8,128)(2,1)S(1)}, bf16[256,4096]{1,0:T(8,128)(2,1)}, u32[]{:S(2)}) copy-start(bf16[256,4096]{1,0:T(8,128)(2,1)} %param.12) | copy-start | bytes 6291460
  7.2 76.1 %all-gather.2.cloned.1.call-start = ((), (), s32[]{:S(2)}) async-start(), calls=%async_computation | async-start | bytes 1179648 | tf_op jit(solution)/shard_map/all_gather | solution.py:148
  10.8 26.0 %collective-permute-start.2 = (bf16[304,128]{1,0:T(8,128)(2,1)S(1)}, bf16[304,128]{1,0:T(8,128)(2,1)S(1)}, u32[]{:S(2)}, u32[]{:S(2)}) collective-permute-start(bf16[304,128]{1,0:T(8,128)(2,1)S(1)} %concatenate.56), channel_id=1, source_target_pairs={{0,8},{8,16},{16,24},{24,32},{32,40},{40,48},{48,56},{56,64},{64,7... | collective-permute-start | bytes 233480 | tf_op jit(solution)/shard_map/ppermute | solution.py:21
  15.0 22.9 %collective-permute-start.1 = (bf16[304,128]{1,0:T(8,128)(2,1)S(1)}, bf16[304,128]{1,0:T(8,128)(2,1)S(1)}, u32[]{:S(2)}, u32[]{:S(2)}) collective-permute-start(bf16[304,128]{1,0:T(8,128)(2,1)S(1)} %concatenate.56), channel_id=1, source_target_pairs={{0,16},{8,24},{16,32},{24,40},{32,48},{40,56},{48,64},{56,72},{64,... | collective-permute-start | bytes 233480 | tf_op jit(solution)/shard_map/ppermute | solution.py:21
  22.4 15.6 %collective-permute-start = (bf16[304,128]{1,0:T(8,128)(2,1)S(1)}, bf16[304,128]{1,0:T(8,128)(2,1)S(1)}, u32[]{:S(2)}, u32[]{:S(2)}) collective-permute-start(bf16[304,128]{1,0:T(8,128)(2,1)S(1)} %concatenate.56), channel_id=1, source_target_pairs={{0,24},{8,32},{16,40},{24,48},{32,56},{40,64},{48,72},{56,80},{64,... | collective-permute-start | bytes 233480 | tf_op jit(solution)/shard_map/ppermute | solution.py:21
  34.2 9.5 %copy-start.12 = (f32[2,1,128]{2,1,0:T(1,128)}, f32[2,1,128]{2,1,0:T(1,128)S(1)}, u32[]{:S(2)}) copy-start(f32[2,1,128]{2,1,0:T(1,128)S(1)} %get-tuple-element.137) | copy-start | bytes 3076
  34.2 9.5 %copy-start.16 = (f32[2,1,128]{2,1,0:T(1,128)}, f32[2,1,128]{2,1,0:T(1,128)S(1)}, u32[]{:S(2)}) copy-start(f32[2,1,128]{2,1,0:T(1,128)S(1)} %get-tuple-element.132) | copy-start | bytes 3076
  34.2 9.5 %copy-start.18 = (f32[2,1,128]{2,1,0:T(1,128)}, f32[2,1,128]{2,1,0:T(1,128)S(1)}, u32[]{:S(2)}) copy-start(f32[2,1,128]{2,1,0:T(1,128)S(1)} %get-tuple-element.133) | copy-start | bytes 3076
  35.4 8.3 %copy-start.66 = (f32[2,1,128]{2,1,0:T(1,128)}, f32[2,1,128]{2,1,0:T(1,128)S(1)}, u32[]{:S(2)}) copy-start(f32[2,1,128]{2,1,0:T(1,128)S(1)} %broadcast.198) | copy-start | bytes 3076
  36.7 7.0 %copy-start.3 = (bf16[304,128]{1,0:T(8,128)(2,1)}, bf16[304,128]{1,0:T(8,128)(2,1)S(1)}, u32[]{:S(2)}) copy-start(bf16[304,128]{1,0:T(8,128)(2,1)S(1)} %collective-permute-done.2) | copy-start | bytes 233476
  53.1 14.6 %copy-start.61 = (f32[1,128]{1,0:T(1,128)}, f32[1,128]{1,0:T(1,128)S(1)}, u32[]{:S(2)}) copy-start(f32[1,128]{1,0:T(1,128)S(1)} %reshape.286) | copy-start | bytes 1540
  53.1 17.6 %collective-permute-start.6 = (f32[312,128]{1,0:T(8,128)S(1)}, f32[312,128]{1,0:T(8,128)S(1)}, u32[]{:S(2)}, u32[]{:S(2)}) collective-permute-start(f32[312,128]{1,0:T(8,128)S(1)} %concatenate.66), channel_id=1, source_target_pairs={{0,104},{8,112},{16,120},{24,128},{32,136},{40,144},{48,152},{56,1... | collective-permute-start | bytes 479240 | tf_op jit(solution)/shard_map/ppermute | solution.py:21
  54.4 17.4 %collective-permute-start.5 = (f32[312,128]{1,0:T(8,128)S(1)}, f32[312,128]{1,0:T(8,128)S(1)}, u32[]{:S(2)}, u32[]{:S(2)}) collective-permute-start(f32[312,128]{1,0:T(8,128)S(1)} %concatenate.66), channel_id=1, source_target_pairs={{0,72},{8,80},{16,88},{24,96},{32,104},{40,112},{48,120},{56,128},... | collective-permute-start | bytes 479240 | tf_op jit(solution)/shard_map/ppermute | solution.py:21
  57.5 24.6 %collective-permute-start.4 = (f32[312,128]{1,0:T(8,128)S(1)}, f32[312,128]{1,0:T(8,128)S(1)}, u32[]{:S(2)}, u32[]{:S(2)}) collective-permute-start(f32[312,128]{1,0:T(8,128)S(1)} %concatenate.66), channel_id=1, source_target_pairs={{0,40},{8,48},{16,56},{24,64},{32,72},{40,80},{48,88},{56,96},{64,... | collective-permute-start | bytes 479240 | tf_op jit(solution)/shard_map/ppermute | solution.py:21
  61.3 20.9 %collective-permute-start.3 = (f32[312,128]{1,0:T(8,128)S(1)}, f32[312,128]{1,0:T(8,128)S(1)}, u32[]{:S(2)}, u32[]{:S(2)}) collective-permute-start(f32[312,128]{1,0:T(8,128)S(1)} %concatenate.66), channel_id=1, source_target_pairs={{0,8},{8,16},{16,24},{24,32},{32,40},{40,48},{48,56},{56,64},{64,7... | collective-permute-start | bytes 479240 | tf_op jit(solution)/shard_map/ppermute | solution.py:21
  70.3 12.5 %copy-start.60 = (f32[128]{0:T(128)S(1)}, f32[128]{0:T(128)}, u32[]{:S(2)}) copy-start(f32[128]{0:T(128)} %get-tuple-element.148) | copy-start | bytes 1540
  83.2 3.2 %copy-start.57 = (f32[2,1,128]{2,1,0:T(1,128)S(1)}, f32[2,1,128]{2,1,0:T(1,128)}, u32[]{:S(2)}) copy-start(f32[2,1,128]{2,1,0:T(1,128)} %copy-done.56) | copy-start | bytes 3076
  83.3 3.2 %copy-start.55 = (f32[2,1,128]{2,1,0:T(1,128)S(1)}, f32[2,1,128]{2,1,0:T(1,128)}, u32[]{:S(2)}) copy-start(f32[2,1,128]{2,1,0:T(1,128)} %copy-done.54) | copy-start | bytes 3076
  83.3 3.2 %copy-start.53 = (f32[2,1,128]{2,1,0:T(1,128)S(1)}, f32[2,1,128]{2,1,0:T(1,128)}, u32[]{:S(2)}) copy-start(f32[2,1,128]{2,1,0:T(1,128)} %copy-done.52) | copy-start | bytes 3076
  83.3 3.2 %copy-start.39 = (f32[2,1,128]{2,1,0:T(1,128)S(1)}, f32[2,1,128]{2,1,0:T(1,128)}, u32[]{:S(2)}) copy-start(f32[2,1,128]{2,1,0:T(1,128)} %copy-done.38) | copy-start | bytes 3076
  83.3 3.3 %copy-start.37 = (f32[2,1,128]{2,1,0:T(1,128)S(1)}, f32[2,1,128]{2,1,0:T(1,128)}, u32[]{:S(2)}) copy-start(f32[2,1,128]{2,1,0:T(1,128)} %copy-done.36) | copy-start | bytes 3076
  83.3 3.3 %copy-start.35 = (f32[2,1,128]{2,1,0:T(1,128)S(1)}, f32[2,1,128]{2,1,0:T(1,128)}, u32[]{:S(2)}) copy-start(f32[2,1,128]{2,1,0:T(1,128)} %copy-done.34) | copy-start | bytes 3076
  88.3 70.6 %copy-start.67 = (s32[128]{0:T(128)S(1)}, s32[128]{0:T(128)}, u32[]{:S(2)}) copy-start(s32[128]{0:T(128)} %param.10) | copy-start | bytes 1540
  88.3 20.2 %collective-permute-start.9 = (f32[312,128]{1,0:T(8,128)S(1)}, f32[312,128]{1,0:T(8,128)S(1)}, u32[]{:S(2)}, u32[]{:S(2)}) collective-permute-start(f32[312,128]{1,0:T(8,128)S(1)} %concatenate.71), channel_id=1, source_target_pairs={{24,0},{32,8},{40,16},{48,24},{56,32},{64,40},{72,48},{80,56},{88,... | collective-permute-start | bytes 479240 | tf_op jit(solution)/shard_map/ppermute | solution.py:21
  95.3 16.7 %collective-permute-start.8 = (f32[312,128]{1,0:T(8,128)S(1)}, f32[312,128]{1,0:T(8,128)S(1)}, u32[]{:S(2)}, u32[]{:S(2)}) collective-permute-start(f32[312,128]{1,0:T(8,128)S(1)} %concatenate.71), channel_id=1, source_target_pairs={{16,0},{24,8},{32,16},{40,24},{48,32},{56,40},{64,48},{72,56},{80,... | collective-permute-start | bytes 479240 | tf_op jit(solution)/shard_map/ppermute | solution.py:21
  101.2 14.1 %collective-permute-start.7 = (f32[312,128]{1,0:T(8,128)S(1)}, f32[312,128]{1,0:T(8,128)S(1)}, u32[]{:S(2)}, u32[]{:S(2)}) collective-permute-start(f32[312,128]{1,0:T(8,128)S(1)} %concatenate.71), channel_id=1, source_target_pairs={{8,0},{16,8},{24,16},{32,24},{40,32},{48,40},{56,48},{64,56},{72,6... | collective-permute-start | bytes 479240 | tf_op jit(solution)/shard_map/ppermute | solution.py:21
  112.0 47.8 %copy-start.41 = (f32[2,1,128]{2,1,0:T(1,128)S(1)}, f32[2,1,128]{2,1,0:T(1,128)}, u32[]{:S(2)}) copy-start(f32[2,1,128]{2,1,0:T(1,128)} %copy-done.40) | copy-start | bytes 3076
  112.0 47.9 %copy-start.7 = (f32[2,1,128]{2,1,0:T(1,128)S(1)}, f32[2,1,128]{2,1,0:T(1,128)}, u32[]{:S(2)}) copy-start(f32[2,1,128]{2,1,0:T(1,128)} %copy-done.6) | copy-start | bytes 3076
  112.0 47.9 %copy-start.5 = (f32[2,1,128]{2,1,0:T(1,128)S(1)}, f32[2,1,128]{2,1,0:T(1,128)}, u32[]{:S(2)}) copy-start(f32[2,1,128]{2,1,0:T(1,128)} %copy-done.4) | copy-start | bytes 3076
  112.0 47.9 %copy-start.51 = (f32[2,1,128]{2,1,0:T(1,128)S(1)}, f32[2,1,128]{2,1,0:T(1,128)}, u32[]{:S(2)}) copy-start(f32[2,1,128]{2,1,0:T(1,128)} %copy-done.50) | copy-start | bytes 3076
  112.0 47.9 %copy-start.49 = (f32[2,1,128]{2,1,0:T(1,128)S(1)}, f32[2,1,128]{2,1,0:T(1,128)}, u32[]{:S(2)}) copy-start(f32[2,1,128]{2,1,0:T(1,128)} %copy-done.48) | copy-start | bytes 3076
  112.1 47.9 %copy-start.47 = (f32[2,1,128]{2,1,0:T(1,128)S(1)}, f32[2,1,128]{2,1,0:T(1,128)}, u32[]{:S(2)}) copy-start(f32[2,1,128]{2,1,0:T(1,128)} %copy-done.46) | copy-start | bytes 3076
  112.1 48.0 %copy-start.45 = (f32[2,1,128]{2,1,0:T(1,128)S(1)}, f32[2,1,128]{2,1,0:T(1,128)}, u32[]{:S(2)}) copy-start(f32[2,1,128]{2,1,0:T(1,128)} %copy-done.44) | copy-start | bytes 3076
  112.1 48.0 %copy-start.25 = (f32[2,1,128]{2,1,0:T(1,128)S(1)}, f32[2,1,128]{2,1,0:T(1,128)}, u32[]{:S(2)}) copy-start(f32[2,1,128]{2,1,0:T(1,128)} %copy-done.24) | copy-start | bytes 3076
  112.2 47.9 %copy-start.23 = (f32[2,1,128]{2,1,0:T(1,128)S(1)}, f32[2,1,128]{2,1,0:T(1,128)}, u32[]{:S(2)}) copy-start(f32[2,1,128]{2,1,0:T(1,128)} %copy-done.22) | copy-start | bytes 3076
  112.2 47.9 %copy-start.21 = (f32[2,1,128]{2,1,0:T(1,128)S(1)}, f32[2,1,128]{2,1,0:T(1,128)}, u32[]{:S(2)}) copy-start(f32[2,1,128]{2,1,0:T(1,128)} %copy-done.20) | copy-start | bytes 3076
  112.2 47.9 %copy-start.19 = (f32[2,1,128]{2,1,0:T(1,128)S(1)}, f32[2,1,128]{2,1,0:T(1,128)}, u32[]{:S(2)}) copy-start(f32[2,1,128]{2,1,0:T(1,128)} %copy-done.18) | copy-start | bytes 3076
  112.2 48.0 %copy-start.17 = (f32[2,1,128]{2,1,0:T(1,128)S(1)}, f32[2,1,128]{2,1,0:T(1,128)}, u32[]{:S(2)}) copy-start(f32[2,1,128]{2,1,0:T(1,128)} %copy-done.16) | copy-start | bytes 3076
  112.2 48.0 %copy-start.15 = (f32[2,1,128]{2,1,0:T(1,128)S(1)}, f32[2,1,128]{2,1,0:T(1,128)}, u32[]{:S(2)}) copy-start(f32[2,1,128]{2,1,0:T(1,128)} %copy-done.14) | copy-start | bytes 3076
  115.4 44.9 %copy-start.13 = (f32[2,1,128]{2,1,0:T(1,128)S(1)}, f32[2,1,128]{2,1,0:T(1,128)}, u32[]{:S(2)}) copy-start(f32[2,1,128]{2,1,0:T(1,128)} %copy-done.12) | copy-start | bytes 3076
  116.1 45.5 %copy-start.63 = (f32[32]{0:T(128)S(1)}, f32[32]{0:T(128)}, u32[]{:S(2)}) copy-start(f32[32]{0:T(128)} %get-tuple-element.138) | copy-start | bytes 388
  116.2 45.5 %copy-start.64 = (f32[32]{0:T(128)S(1)}, f32[32]{0:T(128)}, u32[]{:S(2)}) copy-start(f32[32]{0:T(128)} %get-tuple-element.139) | copy-start | bytes 388
  116.2 45.5 %copy-start.65 = (f32[32]{0:T(128)S(1)}, f32[32]{0:T(128)}, u32[]{:S(2)}) copy-start(f32[32]{0:T(128)} %get-tuple-element.140) | copy-start | bytes 388
  116.2 46.2 %copy-start.2 = (bf16[32,128]{1,0:T(8,128)(2,1)S(1)}, bf16[32,128]{1,0:T(8,128)(2,1)}, u32[]{:S(2)}) copy-start(bf16[32,128]{1,0:T(8,128)(2,1)} %param.8) | copy-start | bytes 24580
  116.2 20.1 %collective-permute-start.13 = (f32[312,128]{1,0:T(8,128)S(1)}, f32[312,128]{1,0:T(8,128)S(1)}, u32[]{:S(2)}, u32[]{:S(2)}) collective-permute-start(f32[312,128]{1,0:T(8,128)S(1)} %add_select_fusion.3), channel_id=1, source_target_pairs={{104,0},{112,8},{120,16},{128,24},{136,32},{144,40},{152,48},{160,... | collective-permute-start | bytes 479240 | tf_op jit(solution)/shard_map/ppermute | solution.py:21
  122.5 17.6 %collective-permute-start.12 = (f32[312,128]{1,0:T(8,128)S(1)}, f32[312,128]{1,0:T(8,128)S(1)}, u32[]{:S(2)}, u32[]{:S(2)}) collective-permute-start(f32[312,128]{1,0:T(8,128)S(1)} %add_select_fusion.3), channel_id=1, source_target_pairs={{72,0},{80,8},{88,16},{96,24},{104,32},{112,40},{120,48},{128,56},... | collective-permute-start | bytes 479240 | tf_op jit(solution)/shard_map/ppermute | solution.py:21
  131.0 26.8 %collective-permute-start.11 = (f32[312,128]{1,0:T(8,128)S(1)}, f32[312,128]{1,0:T(8,128)S(1)}, u32[]{:S(2)}, u32[]{:S(2)}) collective-permute-start(f32[312,128]{1,0:T(8,128)S(1)} %add_select_fusion.3), channel_id=1, source_target_pairs={{40,0},{48,8},{56,16},{64,24},{72,32},{80,40},{88,48},{96,56},{104... | collective-permute-start | bytes 479240 | tf_op jit(solution)/shard_map/ppermute | solution.py:21
  134.4 23.6 %collective-permute-start.10 = (f32[312,128]{1,0:T(8,128)S(1)}, f32[312,128]{1,0:T(8,128)S(1)}, u32[]{:S(2)}, u32[]{:S(2)}) collective-permute-start(f32[312,128]{1,0:T(8,128)S(1)} %add_select_fusion.3), channel_id=1, source_target_pairs={{8,0},{16,8},{24,16},{32,24},{40,32},{48,40},{56,48},{64,56},{72,6... | collective-permute-start | bytes 479240 | tf_op jit(solution)/shard_map/ppermute | solution.py:21
  (35 other events, 39.3 us)
Sparse Core Ops, SparseCore 0:
  30.1 27.5 all-gather.1

commit v6 on v5

--- a/solution.py
+++ b/solution.py
@@ -10,6 +10,7 @@
 
 half_root = 0.7071067811865476
 split_mode = lax.Precision.HIGH
+exact_mode = lax.Precision.HIGHEST
 
 
 def shifted(piece, axis, step, reverse):
@@ -68,15 +69,34 @@
     )
 
 
+def feature_tables(width):
+    count = 1 + 2 * width + width * (width - 1) // 2
+    left = np.zeros((count, width), np.float32)
+    right = np.zeros((count, width), np.float32)
+    left_one = np.zeros((count, 1), np.float32)
+    right_one = np.zeros((count, 1), np.float32)
+    weight = np.ones((count, 1), np.float32)
+    left_one[0] = 1.0
+    right_one[0] = 1.0
+    for i in range(width):
+        left[1 + i, i] = 1.0
+        right_one[1 + i] = 1.0
+        left[1 + width + i, i] = 1.0
+        right[1 + width + i, i] = 1.0
+        weight[1 + width + i] = half_root
+    row_index, col_index = np.triu_indices(width, 1)
+    for n, (i, j) in enumerate(zip(row_index, col_index)):
+        left[1 + 2 * width + n, i] = 1.0
+        right[1 + 2 * width + n, j] = 1.0
+    return left, right, left_one, right_one, weight
+
+
 def features(entries):
     scaled = entries * 0.5
-    width = scaled.shape[-2]
-    cross = jnp.concatenate(
-        [scaled[..., i : i + 1, :] * scaled[..., i + 1 :, :] for i in range(width - 1)], axis=-2
-    )
-    return jnp.concatenate(
-        [jnp.ones_like(scaled[..., :1, :]), scaled, scaled * scaled * half_root, cross], axis=-2
-    )
+    left, right, left_one, right_one, weight = feature_tables(scaled.shape[-2])
+    first = jnp.einsum("rk,...kt->...rt", left, scaled, precision=exact_mode) + left_one
+    second = jnp.einsum("rk,...kt->...rt", right, scaled, precision=exact_mode) + right_one
+    return first * second * weight
 
 
 def block_output(q_feat, k_feat, head_values, doc_ids, carry_mask, state_in, normer_in):

time: 171 us -> 175 us (1.023)
  the two profiles are of different devices: /device:TPU:124 before, /device:TPU:45 now
where the time goes in v6:
time: 175 us; the launch traced here: 174 us
  starting transfers between devices  62.2 us (36%)
  waiting for transfers between devices  52.7 us (30%)
  matrix products  20.1 us (11%)
  between operations  15.5 us (9%)
  other arithmetic  12.2 us (7%)
  local copies, waits for them, and re-layouts  11.1 us (6%)
    ppermute x14, starting transfers between devices, shifted(): return lax.ppermute(piece, axis, pairs)  62.1 us
    ppermute x14, waiting for transfers between devices, shifted(): return lax.ppermute(piece, axis, pairs)  52.7 us
    dot_general x3, matrix products, block_output(): jnp.einsum('hft,hfs->hts', q_feat, k_feat, precision=split_mode)  4.29 us
  transfers between devices with their start and end apart: 15, of which 10 were waited for; matrix products, arithmetic and copies ran while one was open for 14% of the time, Pallas kernels for 0%

profile of v6, /device:TPU:45, one launch (start us, length us, event | category | flops | bytes accessed | tf_op | source)
XLA Modules:
  0.0 173.7 jit_solution(384033567400674891)
XLA Ops:
  7.3 0.8 add_convert_fusion
  8.1 0.8 slice.196
  9.3 0.8 copy.44
  10.1 1.0 concatenate.47
  11.0 5.8 %collective-permute-start.2 = (bf16[304,128]{0,1:T(8,128)(2,1)S(1)}, bf16[304,128]{0,1:T(8,128)(2,1)S(1)}, u32[]{:S(2)}, u32[]{:S(2)}) collective-permute-start(bf16[304,128]{0,1:T(8,128)(2,1)S(1)} %concatenate.47), channel_id=1, source_target_pairs={{0,16},{8,24},{16,32},{24,40},{32,48},{40,56},{48,64},{56,72},{64,... | collective-permute-start | bytes 233480 | tf_op jit(solution)/shard_map/ppermute | solution.py:22
  16.9 8.8 %collective-permute-start.1 = (bf16[304,128]{0,1:T(8,128)(2,1)S(1)}, bf16[304,128]{0,1:T(8,128)(2,1)S(1)}, u32[]{:S(2)}, u32[]{:S(2)}) collective-permute-start(bf16[304,128]{0,1:T(8,128)(2,1)S(1)} %concatenate.47), channel_id=1, source_target_pairs={{0,24},{8,32},{16,40},{24,48},{32,56},{40,64},{48,72},{56,80},{64,... | collective-permute-start | bytes 233480 | tf_op jit(solution)/shard_map/ppermute | solution.py:22
  25.7 4.0 %collective-permute-start = (bf16[304,128]{0,1:T(8,128)(2,1)S(1)}, bf16[304,128]{0,1:T(8,128)(2,1)S(1)}, u32[]{:S(2)}, u32[]{:S(2)}) collective-permute-start(bf16[304,128]{0,1:T(8,128)(2,1)S(1)} %concatenate.47), channel_id=1, source_target_pairs={{0,8},{8,16},{16,24},{24,32},{32,40},{40,48},{48,56},{56,64},{64,7... | collective-permute-start | bytes 233480 | tf_op jit(solution)/shard_map/ppermute | solution.py:22
  33.8 1.1 convolution_add_fusion.5
  34.9 1.1 convolution_add_fusion.6
  36.1 2.8 %collective-permute-done = bf16[304,128]{0,1:T(8,128)(2,1)S(1)} collective-permute-done((bf16[304,128]{0,1:T(8,128)(2,1)S(1)}, bf16[304,128]{0,1:T(8,128)(2,1)S(1)}, u32[]{:S(2)}, u32[]{:S(2)}) %collective-permute-start) | collective-permute-done | bytes 77856 | tf_op jit(solution)/shard_map/ppermute | solution.py:22
  40.5 0.9 pad_maximum_fusion
  41.6 1.2 compare_convert_fusion.5
  44.8 0.9 convert_reduce_fusion
  45.8 0.9 convert_reduce_fusion.1
  48.8 1.9 %concatenate.57 = f32[312,128]{1,0:T(8,128)} concatenate(f32[306,128]{1,0:T(8,128)S(1)} %reshape.209, f32[3,128]{1,0:T(4,128)S(1)} %pad_bitcast_fusion.1, f32[1,128]{1,0:T(1,128)S(1)} %broadcast_in_dim.121, f32[1,128]{1,0:T(1,128)S(1)} %reshape.212, f32[1,128]{1,0:T(1,128)S(1)} %reshape.212), dimensions={0} | concatenate | bytes 319488 | tf_op jit(solution)/shard_map/concatenate | solution.py:139
  50.8 1.9 %collective-permute-start.6 = (f32[312,128]{1,0:T(8,128)}, f32[312,128]{1,0:T(8,128)S(1)}, u32[]{:S(2)}, u32[]{:S(2)}) collective-permute-start(f32[312,128]{1,0:T(8,128)} %concatenate.57), channel_id=1, source_target_pairs={{0,104},{8,112},{16,120},{24,128},{32,136},{40,144},{48,152},{56,1... | collective-permute-start | bytes 479240 | tf_op jit(solution)/shard_map/ppermute | solution.py:22
  52.7 5.5 %collective-permute-start.5 = (f32[312,128]{1,0:T(8,128)}, f32[312,128]{1,0:T(8,128)S(1)}, u32[]{:S(2)}, u32[]{:S(2)}) collective-permute-start(f32[312,128]{1,0:T(8,128)} %concatenate.57), channel_id=1, source_target_pairs={{0,72},{8,80},{16,88},{24,96},{32,104},{40,112},{48,120},{56,128},... | collective-permute-start | bytes 479240 | tf_op jit(solution)/shard_map/ppermute | solution.py:22
  58.2 3.5 %collective-permute-start.4 = (f32[312,128]{1,0:T(8,128)}, f32[312,128]{1,0:T(8,128)S(1)}, u32[]{:S(2)}, u32[]{:S(2)}) collective-permute-start(f32[312,128]{1,0:T(8,128)} %concatenate.57), channel_id=1, source_target_pairs={{0,40},{8,48},{16,56},{24,64},{32,72},{40,80},{48,88},{56,96},{64,... | collective-permute-start | bytes 479240 | tf_op jit(solution)/shard_map/ppermute | solution.py:22
  61.8 3.1 %collective-permute-start.3 = (f32[312,128]{1,0:T(8,128)}, f32[312,128]{1,0:T(8,128)S(1)}, u32[]{:S(2)}, u32[]{:S(2)}) collective-permute-start(f32[312,128]{1,0:T(8,128)} %concatenate.57), channel_id=1, source_target_pairs={{0,8},{8,16},{16,24},{24,32},{32,40},{40,48},{48,56},{56,64},{64,7... | collective-permute-start | bytes 479240 | tf_op jit(solution)/shard_map/ppermute | solution.py:22
  64.9 1.9 %fusion.72 = (f32[2,128]{1,0:T(2,128)S(1)}, f32[2,128,128]{1,2,0:T(8,128)}) fusion(f32[128,128]{0,1:T(8,128)} %fusion.40, f32[2,128,153]{1,2,0:T(8,128)S(1)} %get-tuple-element.34, f32[2,128,153]{1,2,0:T(8,128)S(1)} %get-tuple-element.35), kind=kOutput, calls=%fused_computation.163 | convolution fusion | flops 30146304 | bytes 510976 | tf_op jit(solution)/shard_map/jvp(hft,hfs->hts)/dot_general | solution.py:106
  66.8 2.6 %collective-permute-done.5 = f32[312,128]{1,0:T(8,128)S(1)} collective-permute-done((f32[312,128]{1,0:T(8,128)}, f32[312,128]{1,0:T(8,128)S(1)}, u32[]{:S(2)}, u32[]{:S(2)}) %collective-permute-start.5) | collective-permute-done | bytes 159776 | tf_op jit(solution)/shard_map/ppermute | solution.py:22
  69.6 11.7 %collective-permute-done.4 = f32[312,128]{1,0:T(8,128)S(1)} collective-permute-done((f32[312,128]{1,0:T(8,128)}, f32[312,128]{1,0:T(8,128)S(1)}, u32[]{:S(2)}, u32[]{:S(2)}) %collective-permute-start.4) | collective-permute-done | bytes 159776 | tf_op jit(solution)/shard_map/ppermute | solution.py:22
  81.4 4.7 %collective-permute-done.3 = f32[312,128]{1,0:T(8,128)S(1)} collective-permute-done((f32[312,128]{1,0:T(8,128)}, f32[312,128]{1,0:T(8,128)S(1)}, u32[]{:S(2)}, u32[]{:S(2)}) %collective-permute-start.3) | collective-permute-done | bytes 159776 | tf_op jit(solution)/shard_map/ppermute | solution.py:22
  86.6 1.1 fusion.11
  87.7 2.0 %fusion.73 = f32[128,256]{0,1:T(8,128)S(1)} fusion(bf16[128,4096]{1,0:T(8,128)(2,1)} %all-gather.2.cloned.1.call-done, bf16[256,4096]{1,0:T(8,128)(2,1)S(1)} %copy-done), kind=kOutput, calls=%fused_computation.164 | convolution fusion | flops 268435456 | bytes 3276800 | tf_op jit(solution)/shard_map/transpose(jvp())/reshape | solution.py:233
  90.0 0.9 fusion.28
  91.0 0.9 convolution_add_fusion.4
  92.2 1.0 fusion.10
  93.2 1.2 fusion.7
  95.0 0.9 reshape.218
  96.7 2.6 %collective-permute-start.9 = (f32[312,128]{1,0:T(8,128)S(1)}, f32[312,128]{1,0:T(8,128)S(1)}, u32[]{:S(2)}, u32[]{:S(2)}) collective-permute-start(f32[312,128]{1,0:T(8,128)S(1)} %concatenate.59), channel_id=1, source_target_pairs={{24,0},{32,8},{40,16},{48,24},{56,32},{64,40},{72,48},{80,56},{88,... | collective-permute-start | bytes 479240 | tf_op jit(solution)/shard_map/ppermute | solution.py:22
  99.3 3.0 %collective-permute-start.8 = (f32[312,128]{1,0:T(8,128)S(1)}, f32[312,128]{1,0:T(8,128)S(1)}, u32[]{:S(2)}, u32[]{:S(2)}) collective-permute-start(f32[312,128]{1,0:T(8,128)S(1)} %concatenate.59), channel_id=1, source_target_pairs={{16,0},{24,8},{32,16},{40,24},{48,32},{56,40},{64,48},{72,56},{80,... | collective-permute-start | bytes 479240 | tf_op jit(solution)/shard_map/ppermute | solution.py:22
  102.3 5.1 %collective-permute-start.7 = (f32[312,128]{1,0:T(8,128)S(1)}, f32[312,128]{1,0:T(8,128)S(1)}, u32[]{:S(2)}, u32[]{:S(2)}) collective-permute-start(f32[312,128]{1,0:T(8,128)S(1)} %concatenate.59), channel_id=1, source_target_pairs={{8,0},{16,8},{24,16},{32,24},{40,32},{48,40},{56,48},{64,56},{72,6... | collective-permute-start | bytes 479240 | tf_op jit(solution)/shard_map/ppermute | solution.py:22
  107.4 1.2 fusion.76
  108.6 2.5 %collective-permute-done.9 = f32[312,128]{1,0:T(8,128)S(1)} collective-permute-done((f32[312,128]{1,0:T(8,128)S(1)}, f32[312,128]{1,0:T(8,128)S(1)}, u32[]{:S(2)}, u32[]{:S(2)}) %collective-permute-start.9) | collective-permute-done | bytes 159776 | tf_op jit(solution)/shard_map/ppermute | solution.py:22
  111.1 2.5 %collective-permute-done.8 = f32[312,128]{1,0:T(8,128)S(1)} collective-permute-done((f32[312,128]{1,0:T(8,128)S(1)}, f32[312,128]{1,0:T(8,128)S(1)}, u32[]{:S(2)}, u32[]{:S(2)}) %collective-permute-start.8) | collective-permute-done | bytes 159776 | tf_op jit(solution)/shard_map/ppermute | solution.py:22
  113.7 8.1 %collective-permute-done.7 = f32[312,128]{1,0:T(8,128)S(1)} collective-permute-done((f32[312,128]{1,0:T(8,128)S(1)}, f32[312,128]{1,0:T(8,128)S(1)}, u32[]{:S(2)}, u32[]{:S(2)}) %collective-permute-start.7) | collective-permute-done | bytes 159776 | tf_op jit(solution)/shard_map/ppermute | solution.py:22
  122.7 6.7 %collective-permute-start.13 = (f32[312,128]{1,0:T(8,128)S(1)}, f32[312,128]{1,0:T(8,128)S(1)}, u32[]{:S(2)}, u32[]{:S(2)}) collective-permute-start(f32[312,128]{1,0:T(8,128)S(1)} %add_select_fusion.3), channel_id=1, source_target_pairs={{104,0},{112,8},{120,16},{128,24},{136,32},{144,40},{152,48},{160,... | collective-permute-start | bytes 479240 | tf_op jit(solution)/shard_map/ppermute | solution.py:22
  129.4 2.4 %collective-permute-start.12 = (f32[312,128]{1,0:T(8,128)S(1)}, f32[312,128]{1,0:T(8,128)S(1)}, u32[]{:S(2)}, u32[]{:S(2)}) collective-permute-start(f32[312,128]{1,0:T(8,128)S(1)} %add_select_fusion.3), channel_id=1, source_target_pairs={{72,0},{80,8},{88,16},{96,24},{104,32},{112,40},{120,48},{128,56},... | collective-permute-start | bytes 479240 | tf_op jit(solution)/shard_map/ppermute | solution.py:22
  131.8 1.8 %fusion.25 = f32[2,128,128]{2,1,0:T(8,128)} fusion(f32[2,128,128]{1,2,0:T(8,128)} %get-tuple-element.44, f32[128,2]{0,1:T(2,128)S(1)} %get-tuple-element.10, f32[128,256]{0,1:T(8,128)S(1)} %fusion.73), kind=kOutput, calls=%fused_computation.54 | convolution fusion | flops 25198592 | bytes 394240 | tf_op jit(solution)/shard_map/transpose(jvp(hts,shd->thd))/dot_general | solution.py:107
  133.6 5.6 %collective-permute-start.11 = (f32[312,128]{1,0:T(8,128)S(1)}, f32[312,128]{1,0:T(8,128)S(1)}, u32[]{:S(2)}, u32[]{:S(2)}) collective-permute-start(f32[312,128]{1,0:T(8,128)S(1)} %add_select_fusion.3), channel_id=1, source_target_pairs={{40,0},{48,8},{56,16},{64,24},{72,32},{80,40},{88,48},{96,56},{104... | collective-permute-start | bytes 479240 | tf_op jit(solution)/shard_map/ppermute | solution.py:22
  139.2 4.1 %collective-permute-start.10 = (f32[312,128]{1,0:T(8,128)S(1)}, f32[312,128]{1,0:T(8,128)S(1)}, u32[]{:S(2)}, u32[]{:S(2)}) collective-permute-start(f32[312,128]{1,0:T(8,128)S(1)} %add_select_fusion.3), channel_id=1, source_target_pairs={{8,0},{16,8},{24,16},{32,24},{40,32},{48,40},{56,48},{64,56},{72,6... | collective-permute-start | bytes 479240 | tf_op jit(solution)/shard_map/ppermute | solution.py:22
  143.5 5.4 %collective-permute-done.11 = f32[312,128]{1,0:T(8,128)S(1)} collective-permute-done((f32[312,128]{1,0:T(8,128)S(1)}, f32[312,128]{1,0:T(8,128)S(1)}, u32[]{:S(2)}, u32[]{:S(2)}) %collective-permute-start.11) | collective-permute-done | bytes 159776 | tf_op jit(solution)/shard_map/ppermute | solution.py:22
  149.0 12.1 %collective-permute-done.10 = f32[312,128]{1,0:T(8,128)S(1)} collective-permute-done((f32[312,128]{1,0:T(8,128)S(1)}, f32[312,128]{1,0:T(8,128)S(1)}, u32[]{:S(2)}, u32[]{:S(2)}) %collective-permute-start.10) | collective-permute-done | bytes 159776 | tf_op jit(solution)/shard_map/ppermute | solution.py:22
  162.0 0.7 compare_convert_fusion.2
  162.8 1.3 convolution_add_fusion.10
  164.5 0.8 fusion.13
  165.4 0.8 copy.62
  (140 shorter events, 15.8 us)
Async XLA Ops:
  7.2 80.6 %copy-start = (bf16[256,4096]{1,0:T(8,128)(2,1)S(1)}, bf16[256,4096]{1,0:T(8,128)(2,1)}, u32[]{:S(2)}) copy-start(bf16[256,4096]{1,0:T(8,128)(2,1)} %param.27) | copy-start | bytes 6291460
  7.2 35.7 %copy-start.6 = (f32[153,16,1]{0,1,2:T(8,128)S(1)}, f32[153,16,1]{0,1,2:T(8,128)}, u32[]{:S(2)}) copy-start(f32[153,16,1]{0,1,2:T(8,128)} %constant.53) | copy-start | bytes 29380
  7.2 35.7 %copy-start.10 = (f32[153]{0:T(256)S(1)}, f32[153]{0:T(256)}, u32[]{:S(2)}) copy-start(f32[153]{0:T(256)} %constant.50) | copy-start | bytes 1840
  7.2 36.6 %copy-start.5 = (f32[153,16,1]{0,1,2:T(8,128)S(1)}, f32[153,16,1]{0,1,2:T(8,128)}, u32[]{:S(2)}) copy-start(f32[153,16,1]{0,1,2:T(8,128)} %constant.52) | copy-start | bytes 29380
  7.2 36.6 %copy-start.11 = (f32[153]{0:T(256)S(1)}, f32[153]{0:T(256)}, u32[]{:S(2)}) copy-start(f32[153]{0:T(256)} %constant.49) | copy-start | bytes 1840
  7.2 36.6 %copy-start.9 = (f32[153]{0:T(256)S(1)}, f32[153]{0:T(256)}, u32[]{:S(2)}) copy-start(f32[153]{0:T(256)} %constant.51) | copy-start | bytes 1840
  7.2 34.3 %copy-start.19 = (s32[128]{0:T(128)S(1)}, s32[128]{0:T(128)}, u32[]{:S(2)}) copy-start(s32[128]{0:T(128)} %param.25) | copy-start | bytes 1540
  7.3 80.5 %all-gather.2.cloned.1.call-start = ((), (), s32[]{:S(2)}) async-start(), calls=%async_computation | async-start | bytes 1179648 | tf_op jit(solution)/shard_map/all_gather | solution.py:168
  11.0 24.9 %collective-permute-start.2 = (bf16[304,128]{0,1:T(8,128)(2,1)S(1)}, bf16[304,128]{0,1:T(8,128)(2,1)S(1)}, u32[]{:S(2)}, u32[]{:S(2)}) collective-permute-start(bf16[304,128]{0,1:T(8,128)(2,1)S(1)} %concatenate.47), channel_id=1, source_target_pairs={{0,16},{8,24},{16,32},{24,40},{32,48},{40,56},{48,64},{56,72},{64,... | collective-permute-start | bytes 233480 | tf_op jit(solution)/shard_map/ppermute | solution.py:22
  16.9 23.1 %collective-permute-start.1 = (bf16[304,128]{0,1:T(8,128)(2,1)S(1)}, bf16[304,128]{0,1:T(8,128)(2,1)S(1)}, u32[]{:S(2)}, u32[]{:S(2)}) collective-permute-start(bf16[304,128]{0,1:T(8,128)(2,1)S(1)} %concatenate.47), channel_id=1, source_target_pairs={{0,24},{8,32},{16,40},{24,48},{32,56},{40,64},{48,72},{56,80},{64,... | collective-permute-start | bytes 233480 | tf_op jit(solution)/shard_map/ppermute | solution.py:22
  25.7 13.2 %collective-permute-start = (bf16[304,128]{0,1:T(8,128)(2,1)S(1)}, bf16[304,128]{0,1:T(8,128)(2,1)S(1)}, u32[]{:S(2)}, u32[]{:S(2)}) collective-permute-start(bf16[304,128]{0,1:T(8,128)(2,1)S(1)} %concatenate.47), channel_id=1, source_target_pairs={{0,8},{8,16},{16,24},{24,32},{32,40},{40,48},{48,56},{56,64},{64,7... | collective-permute-start | bytes 233480 | tf_op jit(solution)/shard_map/ppermute | solution.py:22
  33.1 9.7 %copy-start.13 = (f32[32]{0:T(128)}, f32[32]{0:T(128)S(1)}, u32[]{:S(2)}) copy-start(f32[32]{0:T(128)S(1)} %get-tuple-element.27) | copy-start | bytes 388
  33.1 9.7 %copy-start.15 = (f32[32]{0:T(128)}, f32[32]{0:T(128)S(1)}, u32[]{:S(2)}) copy-start(f32[32]{0:T(128)S(1)} %get-tuple-element.28) | copy-start | bytes 388
  33.1 9.7 %copy-start.17 = (f32[32]{0:T(128)}, f32[32]{0:T(128)S(1)}, u32[]{:S(2)}) copy-start(f32[32]{0:T(128)S(1)} %get-tuple-element.29) | copy-start | bytes 388
  36.0 4.5 %copy-start.7 = (bf16[304,128]{0,1:T(8,128)(2,1)}, bf16[304,128]{0,1:T(8,128)(2,1)S(1)}, u32[]{:S(2)}) copy-start(bf16[304,128]{0,1:T(8,128)(2,1)S(1)} %collective-permute-done.2) | copy-start | bytes 233476
  39.9 0.6 copy-start.8
  48.1 38.5 %copy-start.12 = (f32[128]{0:T(128)S(1)}, f32[128]{0:T(128)}, u32[]{:S(2)}) copy-start(f32[128]{0:T(128)} %get-tuple-element.39) | copy-start | bytes 1540
  50.8 16.0 %collective-permute-start.6 = (f32[312,128]{1,0:T(8,128)}, f32[312,128]{1,0:T(8,128)S(1)}, u32[]{:S(2)}, u32[]{:S(2)}) collective-permute-start(f32[312,128]{1,0:T(8,128)} %concatenate.57), channel_id=1, source_target_pairs={{0,104},{8,112},{16,120},{24,128},{32,136},{40,144},{48,152},{56,1... | collective-permute-start | bytes 479240 | tf_op jit(solution)/shard_map/ppermute | solution.py:22
  52.7 16.7 %collective-permute-start.5 = (f32[312,128]{1,0:T(8,128)}, f32[312,128]{1,0:T(8,128)S(1)}, u32[]{:S(2)}, u32[]{:S(2)}) collective-permute-start(f32[312,128]{1,0:T(8,128)} %concatenate.57), channel_id=1, source_target_pairs={{0,72},{8,80},{16,88},{24,96},{32,104},{40,112},{48,120},{56,128},... | collective-permute-start | bytes 479240 | tf_op jit(solution)/shard_map/ppermute | solution.py:22
  58.2 23.0 %collective-permute-start.4 = (f32[312,128]{1,0:T(8,128)}, f32[312,128]{1,0:T(8,128)S(1)}, u32[]{:S(2)}, u32[]{:S(2)}) collective-permute-start(f32[312,128]{1,0:T(8,128)} %concatenate.57), channel_id=1, source_target_pairs={{0,40},{8,48},{16,56},{24,64},{32,72},{40,80},{48,88},{56,96},{64,... | collective-permute-start | bytes 479240 | tf_op jit(solution)/shard_map/ppermute | solution.py:22
  61.8 24.3 %collective-permute-start.3 = (f32[312,128]{1,0:T(8,128)}, f32[312,128]{1,0:T(8,128)S(1)}, u32[]{:S(2)}, u32[]{:S(2)}) collective-permute-start(f32[312,128]{1,0:T(8,128)} %concatenate.57), channel_id=1, source_target_pairs={{0,8},{8,16},{16,24},{24,32},{32,40},{40,48},{48,56},{56,64},{64,7... | collective-permute-start | bytes 479240 | tf_op jit(solution)/shard_map/ppermute | solution.py:22
  86.4 3.3 %copy-start.1 = (bf16[128,256]{1,0:T(8,128)(2,1)S(1)}, bf16[128,256]{1,0:T(8,128)(2,1)}, u32[]{:S(2)}) copy-start(bf16[128,256]{1,0:T(8,128)(2,1)} %param.24) | copy-start | bytes 196612
  87.7 2.0 %copy-start.3 = (f32[2,128,128]{1,2,0:T(8,128)S(1)}, f32[2,128,128]{1,2,0:T(8,128)}, u32[]{:S(2)}) copy-start(f32[2,128,128]{1,2,0:T(8,128)} %get-tuple-element.44) | copy-start | bytes 393220
  87.7 2.0 %copy-start.4 = (f32[128,2,128]{0,2,1:T(8,128)S(1)}, f32[128,2,128]{0,2,1:T(8,128)}, u32[]{:S(2)}) copy-start(f32[128,2,128]{0,2,1:T(8,128)} %fusion.11) | copy-start | bytes 393220
  93.2 2.7 %copy-start.2 = (f32[2,128,128]{1,2,0:T(8,128)}, f32[2,128,128]{1,2,0:T(8,128)S(1)}, u32[]{:S(2)}) copy-start(f32[2,128,128]{1,2,0:T(8,128)S(1)} %fusion.10) | copy-start | bytes 393220
  96.7 65.3 %copy-start.20 = (s32[128]{0:T(128)S(1)}, s32[128]{0:T(128)}, u32[]{:S(2)}) copy-start(s32[128]{0:T(128)} %param.25) | copy-start | bytes 1540
  96.7 14.3 %collective-permute-start.9 = (f32[312,128]{1,0:T(8,128)S(1)}, f32[312,128]{1,0:T(8,128)S(1)}, u32[]{:S(2)}, u32[]{:S(2)}) collective-permute-start(f32[312,128]{1,0:T(8,128)S(1)} %concatenate.59), channel_id=1, source_target_pairs={{24,0},{32,8},{40,16},{48,24},{56,32},{64,40},{72,48},{80,56},{88,... | collective-permute-start | bytes 479240 | tf_op jit(solution)/shard_map/ppermute | solution.py:22
  99.3 14.2 %collective-permute-start.8 = (f32[312,128]{1,0:T(8,128)S(1)}, f32[312,128]{1,0:T(8,128)S(1)}, u32[]{:S(2)}, u32[]{:S(2)}) collective-permute-start(f32[312,128]{1,0:T(8,128)S(1)} %concatenate.59), channel_id=1, source_target_pairs={{16,0},{24,8},{32,16},{40,24},{48,32},{56,40},{64,48},{72,56},{80,... | collective-permute-start | bytes 479240 | tf_op jit(solution)/shard_map/ppermute | solution.py:22
  102.3 19.4 %collective-permute-start.7 = (f32[312,128]{1,0:T(8,128)S(1)}, f32[312,128]{1,0:T(8,128)S(1)}, u32[]{:S(2)}, u32[]{:S(2)}) collective-permute-start(f32[312,128]{1,0:T(8,128)S(1)} %concatenate.59), channel_id=1, source_target_pairs={{8,0},{16,8},{24,16},{32,24},{40,32},{48,40},{56,48},{64,56},{72,6... | collective-permute-start | bytes 479240 | tf_op jit(solution)/shard_map/ppermute | solution.py:22
  122.7 20.6 %collective-permute-start.13 = (f32[312,128]{1,0:T(8,128)S(1)}, f32[312,128]{1,0:T(8,128)S(1)}, u32[]{:S(2)}, u32[]{:S(2)}) collective-permute-start(f32[312,128]{1,0:T(8,128)S(1)} %add_select_fusion.3), channel_id=1, source_target_pairs={{104,0},{112,8},{120,16},{128,24},{136,32},{144,40},{152,48},{160,... | collective-permute-start | bytes 479240 | tf_op jit(solution)/shard_map/ppermute | solution.py:22
  129.4 13.9 %collective-permute-start.12 = (f32[312,128]{1,0:T(8,128)S(1)}, f32[312,128]{1,0:T(8,128)S(1)}, u32[]{:S(2)}, u32[]{:S(2)}) collective-permute-start(f32[312,128]{1,0:T(8,128)S(1)} %add_select_fusion.3), channel_id=1, source_target_pairs={{72,0},{80,8},{88,16},{96,24},{104,32},{112,40},{120,48},{128,56},... | collective-permute-start | bytes 479240 | tf_op jit(solution)/shard_map/ppermute | solution.py:22
  133.6 32.5 %copy-start.14 = (f32[32]{0:T(128)S(1)}, f32[32]{0:T(128)}, u32[]{:S(2)}) copy-start(f32[32]{0:T(128)} %copy-done.13) | copy-start | bytes 388
  133.6 32.5 %copy-start.16 = (f32[32]{0:T(128)S(1)}, f32[32]{0:T(128)}, u32[]{:S(2)}) copy-start(f32[32]{0:T(128)} %copy-done.15) | copy-start | bytes 388
  133.6 32.5 %copy-start.18 = (f32[32]{0:T(128)S(1)}, f32[32]{0:T(128)}, u32[]{:S(2)}) copy-start(f32[32]{0:T(128)} %copy-done.17) | copy-start | bytes 388
  133.6 15.2 %collective-permute-start.11 = (f32[312,128]{1,0:T(8,128)S(1)}, f32[312,128]{1,0:T(8,128)S(1)}, u32[]{:S(2)}, u32[]{:S(2)}) collective-permute-start(f32[312,128]{1,0:T(8,128)S(1)} %add_select_fusion.3), channel_id=1, source_target_pairs={{40,0},{48,8},{56,16},{64,24},{72,32},{80,40},{88,48},{96,56},{104... | collective-permute-start | bytes 479240 | tf_op jit(solution)/shard_map/ppermute | solution.py:22
  139.2 21.9 %collective-permute-start.10 = (f32[312,128]{1,0:T(8,128)S(1)}, f32[312,128]{1,0:T(8,128)S(1)}, u32[]{:S(2)}, u32[]{:S(2)}) collective-permute-start(f32[312,128]{1,0:T(8,128)S(1)} %add_select_fusion.3), channel_id=1, source_target_pairs={{8,0},{16,8},{24,16},{32,24},{40,32},{48,40},{56,48},{64,56},{72,6... | collective-permute-start | bytes 479240 | tf_op jit(solution)/shard_map/ppermute | solution.py:22
Sparse Core Ops, SparseCore 0:
  29.8 29.4 all-gather.1

commit v7 on v6

--- a/solution.py
+++ b/solution.py
@@ -3,9 +3,12 @@
 import numpy as np
 from jax import lax
 from jax.sharding import PartitionSpec as P
+from jax.experimental import pallas as pl
+from jax.experimental.pallas import tpu as pltpu
 
 FD = 16
 MOST = 2048
+INTERPRET = False
 
 
 half_root = 0.7071067811865476
@@ -91,6 +94,80 @@
     return left, right, left_one, right_one, weight
 
 
+def window_tables(heads, width):
+    left, right, left_one, right_one, weight = feature_tables(width)
+    count = left.shape[0]
+    big_left = np.zeros((heads * count, heads * width), np.float32)
+    big_right = np.zeros((heads * count, heads * width), np.float32)
+    aux = np.zeros((heads * count, 128), np.float32)
+    for h in range(heads):
+        rows = slice(h * count, (h + 1) * count)
+        big_left[rows, h * width : (h + 1) * width] = left
+        big_right[rows, h * width : (h + 1) * width] = right
+        aux[rows, 0:1] = left_one
+        aux[rows, 1:2] = right_one
+        aux[rows, 2:3] = weight
+        aux[rows, 3] = h
+    return big_left, big_right, aux
+
+
+def window_state(pieces, heads, width, value_rows, out_rows):
+    big_left, big_right, aux = window_tables(heads, width)
+    feature_rows = big_left.shape[0]
+    head_width = value_rows // heads
+    key_rows = heads * width
+    ids_row = value_rows + key_rows
+    normer_rows = -(-feature_rows // head_width)
+    key_row = feature_rows + normer_rows
+    dims = (((1,), (1,)), ((), ()))
+
+    def kernel(*refs):
+        piece_refs = refs[: len(pieces)]
+        left_ref, right_ref, aux_ref, out_ref = refs[len(pieces) :]
+        own_ids = piece_refs[-1][ids_row : ids_row + 1, :].astype(jnp.float32)
+        last = jnp.max(own_ids, axis=1, keepdims=True)
+        block = aux_ref[...]
+        left_one = block[:, 0:1]
+        right_one = block[:, 1:2]
+        weight = block[:, 2:3]
+        head_of = block[:, 3:4]
+        state = jnp.zeros((feature_rows, value_rows), jnp.float32)
+        normer = jnp.zeros((8, feature_rows), jnp.float32)
+        ones = jnp.ones((8, piece_refs[0].shape[1]), jnp.float32)
+        for ref in piece_refs:
+            ids = ref[ids_row : ids_row + 1, :].astype(jnp.float32)
+            mask = (ids == last).astype(jnp.float32)
+            scaled = ref[value_rows:ids_row, :].astype(jnp.float32) * 0.5
+            first = jnp.dot(left_ref[...], scaled, precision=exact_mode, preferred_element_type=jnp.float32)
+            second = jnp.dot(right_ref[...], scaled, precision=exact_mode, preferred_element_type=jnp.float32)
+            feat = (first + left_one) * (second + right_one) * weight * mask
+            high = feat.astype(jnp.bfloat16)
+            low = (feat - high.astype(jnp.float32)).astype(jnp.bfloat16)
+            vals = ref[0:value_rows, :]
+            state = state + lax.dot_general(high, vals, dims, preferred_element_type=jnp.float32)
+            state = state + lax.dot_general(low, vals, dims, preferred_element_type=jnp.float32)
+            normer = normer + lax.dot_general(
+                ones, feat, dims, precision=exact_mode, preferred_element_type=jnp.float32
+            )
+        chosen = jnp.zeros((feature_rows, head_width), jnp.float32)
+        for h in range(heads):
+            chosen = jnp.where(head_of == h, state[:, h * head_width : (h + 1) * head_width], chosen)
+        out_ref[...] = jnp.zeros(out_ref.shape, jnp.float32)
+        out_ref[0:feature_rows, :] = chosen
+        for k in range(normer_rows):
+            stop = min(feature_rows, (k + 1) * head_width)
+            out_ref[feature_rows + k : feature_rows + k + 1, 0 : stop - k * head_width] = normer[
+                0:1, k * head_width : stop
+            ]
+        out_ref[key_row : key_row + 1, :] = jnp.broadcast_to(last, (1, head_width))
+
+    return pl.pallas_call(
+        kernel,
+        out_shape=jax.ShapeDtypeStruct((out_rows, head_width), jnp.float32),
+        interpret=INTERPRET,
+    )(*pieces, jnp.asarray(big_left), jnp.asarray(big_right), jnp.asarray(aux))
+
+
 def features(entries):
     scaled = entries * 0.5
     left, right, left_one, right_one, weight = feature_tables(scaled.shape[-2])
@@ -179,33 +256,23 @@
     row_count = query_rows.shape[0]
     near, far = window_steps(reach, lax.axis_size("ctx"))
     raw = raw_pack(keys, values, doc_ids, queries[:, length - 2 :].reshape(-1))
-    received = [
-        raw_unpack(shifted(raw, "ctx", step, False), values.shape[1], row_count, 2 * row_count)
-        for step in near
-    ]
-    window_keys = jnp.concatenate([part[1] for part in received], axis=1).astype(jnp.float32)
-    window_feat = jnp.concatenate(
-        [features(window_keys.reshape(local_heads, FD, -1)), k_feat], axis=2
-    )
-    window_values = jnp.concatenate(
-        [part[0] for part in received] + [values.T], axis=1
-    ).astype(jnp.float32)
-    window_ids = jnp.concatenate([part[2] for part in received] + [doc_ids])
-    tail_mask = (window_ids == doc_ids[length - 1]).astype(jnp.float32)
-    tail_feat = window_feat * tail_mask[None, None, :]
-    tail_state = jnp.einsum(
-        "hft,hdt->hfd",
-        tail_feat,
-        window_values.reshape(local_heads, head_width, -1),
-        precision=split_mode,
-    )
-    tail_normer = jnp.sum(tail_feat, axis=2)
-    key_row = tail_state.size // head_width + -(-tail_normer.size // head_width)
-    forward_piece = pack(tail_state, tail_normer, doc_ids[length - 1], jnp.zeros((1,), jnp.float32))
+    feature_count = 1 + 2 * FD + FD * (FD - 1) // 2
+    state_shape = (local_heads, feature_count, head_width)
+    normer_shape = (local_heads, feature_count)
+    key_row = local_heads * feature_count + -(-local_heads * feature_count // head_width)
+    out_rows = key_row + 2 + (-(key_row + 2) % 8)
+    received = [shifted(raw, "ctx", step, False) for step in near]
+    forward_piece = window_state(
+        received + [raw],
+        local_heads,
+        FD,
+        values.shape[1],
+        out_rows,
+    )
     join = packed_join(key_row)
     packed = fold(join, [shifted(forward_piece, "ctx", step, False) for step in far])
-    state_in, normer_in, _ = unpack(packed, tail_state.shape, tail_normer.shape, 1)
-    previous = received[-1] if near else raw_unpack(jnp.zeros_like(raw), values.shape[1], row_count, 2 * row_count)
+    state_in, normer_in, _ = unpack(packed, state_shape, normer_shape, 1)
+    previous = raw_unpack(received[-1], values.shape[1], row_count, 2 * row_count)
     before = (
         previous[2][length - 2 :],
         previous[3].astype(jnp.float32).reshape(row_count, 2),

time: 175 us -> 169 us (0.966)
  the two profiles are of different devices: /device:TPU:45 before, /device:TPU:46 now
where the time goes in v7:
time: 169 us; the launch traced here: 167 us
  starting transfers between devices  69 us (41%)
  waiting for transfers between devices  43.5 us (26%)
  matrix products  15.2 us (9%)
  between operations  14.7 us (9%)
  other arithmetic  11.6 us (7%)
  local copies, waits for them, and re-layouts  7.66 us (5%)
  Pallas kernels  5.87 us (3%)
    ppermute x14, starting transfers between devices, shifted(): return lax.ppermute(piece, axis, pairs)  68.9 us
    ppermute x14, waiting for transfers between devices, shifted(): return lax.ppermute(piece, axis, pairs)  43.5 us
    pallas_call x1, Pallas kernels, window_state(): pl.pallas_call(kernel, out_shape=jax.ShapeDtypeStruct((out_rows, head_wid...  5.87 us
  transfers between devices with their start and end apart: 15, of which 9 were waited for; matrix products, arithmetic and copies ran while one was open for 10% of the time, Pallas kernels for 4%

profile of v7, /device:TPU:46, one launch (start us, length us, event | category | flops | bytes accessed | tf_op | source)
XLA Modules:
  0.0 167.5 jit_solution(2099125721616924499)
XLA Ops:
  7.3 0.8 add_convert_fusion
  8.1 0.8 slice.168
  9.0 1.0 copy.36
  9.9 0.9 concatenate.21.refs_3_
  10.8 6.1 %collective-permute-start.2 = (bf16[304,128]{1,0:T(8,128)(2,1)S(1)}, bf16[304,128]{1,0:T(8,128)(2,1)S(1)}, u32[]{:S(2)}, u32[]{:S(2)}) collective-permute-start(bf16[304,128]{1,0:T(8,128)(2,1)S(1)} %concatenate.21.refs_3_), channel_id=1, source_target_pairs={{0,16},{8,24},{16,32},{24,40},{32,48},{40,56},{48,64},{56,72},{64,... | collective-permute-start | bytes 233480 | tf_op jit(solution)/shard_map/ppermute | solution.py:25
  16.9 9.1 %collective-permute-start.1 = (bf16[304,128]{1,0:T(8,128)(2,1)S(1)}, bf16[304,128]{1,0:T(8,128)(2,1)S(1)}, u32[]{:S(2)}, u32[]{:S(2)}) collective-permute-start(bf16[304,128]{1,0:T(8,128)(2,1)S(1)} %concatenate.21.refs_3_), channel_id=1, source_target_pairs={{0,24},{8,32},{16,40},{24,48},{32,56},{40,64},{48,72},{56,80},{64,... | collective-permute-start | bytes 233480 | tf_op jit(solution)/shard_map/ppermute | solution.py:25
  26.0 4.3 %collective-permute-start = (bf16[304,128]{1,0:T(8,128)(2,1)S(1)}, bf16[304,128]{1,0:T(8,128)(2,1)S(1)}, u32[]{:S(2)}, u32[]{:S(2)}) collective-permute-start(bf16[304,128]{1,0:T(8,128)(2,1)S(1)} %concatenate.21.refs_3_), channel_id=1, source_target_pairs={{0,8},{8,16},{16,24},{24,32},{32,40},{40,48},{48,56},{56,64},{64,7... | collective-permute-start | bytes 233480 | tf_op jit(solution)/shard_map/ppermute | solution.py:25
  30.3 0.7 convert_element_type.59
  31.0 0.7 convert_multiply_fusion
  32.5 1.1 convolution_add_fusion.3
  33.6 1.1 convolution_add_fusion.4
  34.7 0.9 collective-permute-done.refs_2_
  36.3 1.3 collective-permute-done.1.refs_0_
  38.2 5.9 %shard_map.211 = f32[312,128]{1,0:T(8,128)} custom-call(bf16[304,128]{1,0:T(8,128)(2,1)} %copy-done.8, bf16[304,128]{1,0:T(8,128)(2,1)} %copy-done.7, bf16[304,128]{1,0:T(8,128)(2,1)} %copy-done.6, bf16[304,128]{1,0:T(8,128)(2,1)} %copy-done.3, f32[306,32]{1,0:T(8,128)} %constant.37.clone.refs_4_, f32[306,32]{1,0:T(8,128)} %constant.38.clone.refs_5_, ...), custom_call_target="tpu_custom_call" | custom-call | tf_op jit(solution)/shard_map/pallas_call | solution.py:164
  44.1 2.6 %collective-permute-start.6 = (f32[312,128]{1,0:T(8,128)}, f32[312,128]{1,0:T(8,128)S(1)}, u32[]{:S(2)}, u32[]{:S(2)}) collective-permute-start(f32[312,128]{1,0:T(8,128)} %shard_map.211), channel_id=1, source_target_pairs={{0,104},{8,112},{16,120},{24,128},{32,136},{40,144},{48,152},{56,1... | collective-permute-start | bytes 479240 | tf_op jit(solution)/shard_map/ppermute | solution.py:25
  46.6 5.3 %collective-permute-start.5 = (f32[312,128]{1,0:T(8,128)}, f32[312,128]{1,0:T(8,128)}, u32[]{:S(2)}, u32[]{:S(2)}) collective-permute-start(f32[312,128]{1,0:T(8,128)} %shard_map.211), channel_id=1, source_target_pairs={{0,72},{8,80},{16,88},{24,96},{32,104},{40,112},{48,120},{56,128},... | collective-permute-start | bytes 479240 | tf_op jit(solution)/shard_map/ppermute | solution.py:25
  51.9 5.5 %collective-permute-start.4 = (f32[312,128]{1,0:T(8,128)}, f32[312,128]{1,0:T(8,128)S(1)}, u32[]{:S(2)}, u32[]{:S(2)}) collective-permute-start(f32[312,128]{1,0:T(8,128)} %shard_map.211), channel_id=1, source_target_pairs={{0,40},{8,48},{16,56},{24,64},{32,72},{40,80},{48,88},{56,96},{64,... | collective-permute-start | bytes 479240 | tf_op jit(solution)/shard_map/ppermute | solution.py:25
  57.4 3.5 %collective-permute-start.3 = (f32[312,128]{1,0:T(8,128)}, f32[312,128]{1,0:T(8,128)}, u32[]{:S(2)}, u32[]{:S(2)}) collective-permute-start(f32[312,128]{1,0:T(8,128)} %shard_map.211), channel_id=1, source_target_pairs={{0,8},{8,16},{16,24},{24,32},{32,40},{40,48},{48,56},{56,64},{64,7... | collective-permute-start | bytes 479240 | tf_op jit(solution)/shard_map/ppermute | solution.py:25
  61.8 1.4 compare_convert_fusion.5
  63.3 1.1 convolution_add_fusion.5
  65.9 1.0 add_select_fusion.8
  67.0 10.4 %collective-permute-done.4 = f32[312,128]{1,0:T(8,128)S(1)} collective-permute-done((f32[312,128]{1,0:T(8,128)}, f32[312,128]{1,0:T(8,128)S(1)}, u32[]{:S(2)}, u32[]{:S(2)}) %collective-permute-start.4) | collective-permute-done | bytes 159776 | tf_op jit(solution)/shard_map/ppermute | solution.py:25
  77.5 2.0 %collective-permute-done.3 = f32[312,128]{1,0:T(8,128)} collective-permute-done((f32[312,128]{1,0:T(8,128)}, f32[312,128]{1,0:T(8,128)}, u32[]{:S(2)}, u32[]{:S(2)}) %collective-permute-start.3) | collective-permute-done | bytes 159776 | tf_op jit(solution)/shard_map/ppermute | solution.py:25
  80.2 1.0 add_select_fusion.6
  82.8 1.1 fusion.8
  83.9 2.0 %fusion.57 = f32[128,256]{0,1:T(8,128)S(1)} fusion(bf16[128,4096]{1,0:T(8,128)(2,1)} %all-gather.2.cloned.1.call-done, bf16[256,4096]{1,0:T(8,128)(2,1)S(1)} %copy-done), kind=kOutput, calls=%fused_computation.138 | convolution fusion | flops 268435456 | bytes 3276800 | tf_op jit(solution)/shard_map/transpose(jvp())/reshape | solution.py:300
  86.1 0.9 fusion.22
  87.1 0.9 convolution_add_fusion.2
  88.5 1.2 fusion.4
  90.3 0.9 reshape.157
  91.4 3.8 %collective-permute-start.9 = (f32[312,128]{1,0:T(8,128)S(1)}, f32[312,128]{1,0:T(8,128)S(1)}, u32[]{:S(2)}, u32[]{:S(2)}) collective-permute-start(f32[312,128]{1,0:T(8,128)S(1)} %concatenate.25), channel_id=1, source_target_pairs={{24,0},{32,8},{40,16},{48,24},{56,32},{64,40},{72,48},{80,56},{88,... | collective-permute-start | bytes 479240 | tf_op jit(solution)/shard_map/ppermute | solution.py:25
  95.2 3.4 %collective-permute-start.8 = (f32[312,128]{1,0:T(8,128)S(1)}, f32[312,128]{1,0:T(8,128)S(1)}, u32[]{:S(2)}, u32[]{:S(2)}) collective-permute-start(f32[312,128]{1,0:T(8,128)S(1)} %concatenate.25), channel_id=1, source_target_pairs={{16,0},{24,8},{32,16},{40,24},{48,32},{56,40},{64,48},{72,56},{80,... | collective-permute-start | bytes 479240 | tf_op jit(solution)/shard_map/ppermute | solution.py:25
  98.6 5.8 %collective-permute-start.7 = (f32[312,128]{1,0:T(8,128)S(1)}, f32[312,128]{1,0:T(8,128)S(1)}, u32[]{:S(2)}, u32[]{:S(2)}) collective-permute-start(f32[312,128]{1,0:T(8,128)S(1)} %concatenate.25), channel_id=1, source_target_pairs={{8,0},{16,8},{24,16},{32,24},{40,32},{48,40},{56,48},{64,56},{72,6... | collective-permute-start | bytes 479240 | tf_op jit(solution)/shard_map/ppermute | solution.py:25
  104.7 5.6 %collective-permute-done.9 = f32[312,128]{1,0:T(8,128)S(1)} collective-permute-done((f32[312,128]{1,0:T(8,128)S(1)}, f32[312,128]{1,0:T(8,128)S(1)}, u32[]{:S(2)}, u32[]{:S(2)}) %collective-permute-start.9) | collective-permute-done | bytes 159776 | tf_op jit(solution)/shard_map/ppermute | solution.py:25
  110.2 2.0 %collective-permute-done.8 = f32[312,128]{1,0:T(8,128)S(1)} collective-permute-done((f32[312,128]{1,0:T(8,128)S(1)}, f32[312,128]{1,0:T(8,128)S(1)}, u32[]{:S(2)}, u32[]{:S(2)}) %collective-permute-start.8) | collective-permute-done | bytes 159776 | tf_op jit(solution)/shard_map/ppermute | solution.py:25
  112.4 3.8 %collective-permute-done.7 = f32[312,128]{1,0:T(8,128)S(1)} collective-permute-done((f32[312,128]{1,0:T(8,128)S(1)}, f32[312,128]{1,0:T(8,128)S(1)}, u32[]{:S(2)}, u32[]{:S(2)}) %collective-permute-start.7) | collective-permute-done | bytes 159776 | tf_op jit(solution)/shard_map/ppermute | solution.py:25
  116.5 8.1 %collective-permute-start.13 = (f32[312,128]{1,0:T(8,128)S(1)}, f32[312,128]{1,0:T(8,128)S(1)}, u32[]{:S(2)}, u32[]{:S(2)}) collective-permute-start(f32[312,128]{1,0:T(8,128)S(1)} %add_select_fusion.3), channel_id=1, source_target_pairs={{104,0},{112,8},{120,16},{128,24},{136,32},{144,40},{152,48},{160,... | collective-permute-start | bytes 479240 | tf_op jit(solution)/shard_map/ppermute | solution.py:25
  124.6 2.2 %collective-permute-start.12 = (f32[312,128]{1,0:T(8,128)S(1)}, f32[312,128]{1,0:T(8,128)S(1)}, u32[]{:S(2)}, u32[]{:S(2)}) collective-permute-start(f32[312,128]{1,0:T(8,128)S(1)} %add_select_fusion.3), channel_id=1, source_target_pairs={{72,0},{80,8},{88,16},{96,24},{104,32},{112,40},{120,48},{128,56},... | collective-permute-start | bytes 479240 | tf_op jit(solution)/shard_map/ppermute | solution.py:25
  126.8 0.9 fusion.19
  127.7 5.9 %collective-permute-start.11 = (f32[312,128]{1,0:T(8,128)S(1)}, f32[312,128]{1,0:T(8,128)S(1)}, u32[]{:S(2)}, u32[]{:S(2)}) collective-permute-start(f32[312,128]{1,0:T(8,128)S(1)} %add_select_fusion.3), channel_id=1, source_target_pairs={{40,0},{48,8},{56,16},{64,24},{72,32},{80,40},{88,48},{96,56},{104... | collective-permute-start | bytes 479240 | tf_op jit(solution)/shard_map/ppermute | solution.py:25
  133.6 3.4 %collective-permute-start.10 = (f32[312,128]{1,0:T(8,128)S(1)}, f32[312,128]{1,0:T(8,128)S(1)}, u32[]{:S(2)}, u32[]{:S(2)}) collective-permute-start(f32[312,128]{1,0:T(8,128)S(1)} %add_select_fusion.3), channel_id=1, source_target_pairs={{8,0},{16,8},{24,16},{32,24},{40,32},{48,40},{56,48},{64,56},{72,6... | collective-permute-start | bytes 479240 | tf_op jit(solution)/shard_map/ppermute | solution.py:25
  137.1 2.1 %collective-permute-done.12 = f32[312,128]{1,0:T(8,128)S(1)} collective-permute-done((f32[312,128]{1,0:T(8,128)S(1)}, f32[312,128]{1,0:T(8,128)S(1)}, u32[]{:S(2)}, u32[]{:S(2)}) %collective-permute-start.12) | collective-permute-done | bytes 159776 | tf_op jit(solution)/shard_map/ppermute | solution.py:25
  139.3 15.3 %collective-permute-done.11 = f32[312,128]{1,0:T(8,128)S(1)} collective-permute-done((f32[312,128]{1,0:T(8,128)S(1)}, f32[312,128]{1,0:T(8,128)S(1)}, u32[]{:S(2)}, u32[]{:S(2)}) %collective-permute-start.11) | collective-permute-done | bytes 159776 | tf_op jit(solution)/shard_map/ppermute | solution.py:25
  155.8 0.7 compare_convert_fusion.2
  156.5 1.4 convolution_add_fusion.8
  158.3 0.8 fusion.10
  159.2 0.8 copy.48
  159.9 0.7 fusion.42
  (100 shorter events, 10.8 us)
Async XLA Ops:
  7.2 76.7 %copy-start = (bf16[256,4096]{1,0:T(8,128)(2,1)S(1)}, bf16[256,4096]{1,0:T(8,128)(2,1)}, u32[]{:S(2)}) copy-start(bf16[256,4096]{1,0:T(8,128)(2,1)} %param.25) | copy-start | bytes 6291460
  7.2 57.2 %copy-start.4 = (f32[153,16,1]{0,1,2:T(8,128)S(1)}, f32[153,16,1]{0,1,2:T(8,128)}, u32[]{:S(2)}) copy-start(f32[153,16,1]{0,1,2:T(8,128)} %constant.54) | copy-start | bytes 29380
  7.2 57.2 %copy-start.10 = (f32[153]{0:T(256)S(1)}, f32[153]{0:T(256)}, u32[]{:S(2)}) copy-start(f32[153]{0:T(256)} %constant.51) | copy-start | bytes 1840
  7.2 57.2 %copy-start.9 = (f32[153]{0:T(256)S(1)}, f32[153]{0:T(256)}, u32[]{:S(2)}) copy-start(f32[153]{0:T(256)} %constant.53) | copy-start | bytes 1840
  7.2 76.6 %all-gather.2.cloned.1.call-start = ((), (), s32[]{:S(2)}) async-start(), calls=%async_computation | async-start | bytes 1179648 | tf_op jit(solution)/shard_map/all_gather | solution.py:245
  10.8 26.8 %copy-start.3 = (bf16[304,128]{1,0:T(8,128)(2,1)}, bf16[304,128]{1,0:T(8,128)(2,1)S(1)}, u32[]{:S(2)}) copy-start(bf16[304,128]{1,0:T(8,128)(2,1)S(1)} %concatenate.21.refs_3_) | copy-start | bytes 233476
  10.8 25.5 %collective-permute-start.2 = (bf16[304,128]{1,0:T(8,128)(2,1)S(1)}, bf16[304,128]{1,0:T(8,128)(2,1)S(1)}, u32[]{:S(2)}, u32[]{:S(2)}) collective-permute-start(bf16[304,128]{1,0:T(8,128)(2,1)S(1)} %concatenate.21.refs_3_), channel_id=1, source_target_pairs={{0,16},{8,24},{16,32},{24,40},{32,48},{40,56},{48,64},{56,72},{64,... | collective-permute-start | bytes 233480 | tf_op jit(solution)/shard_map/ppermute | solution.py:25
  16.9 20.6 %collective-permute-start.1 = (bf16[304,128]{1,0:T(8,128)(2,1)S(1)}, bf16[304,128]{1,0:T(8,128)(2,1)S(1)}, u32[]{:S(2)}, u32[]{:S(2)}) collective-permute-start(bf16[304,128]{1,0:T(8,128)(2,1)S(1)} %concatenate.21.refs_3_), channel_id=1, source_target_pairs={{0,24},{8,32},{16,40},{24,48},{32,56},{40,64},{48,72},{56,80},{64,... | collective-permute-start | bytes 233480 | tf_op jit(solution)/shard_map/ppermute | solution.py:25
  26.0 9.6 %collective-permute-start = (bf16[304,128]{1,0:T(8,128)(2,1)S(1)}, bf16[304,128]{1,0:T(8,128)(2,1)S(1)}, u32[]{:S(2)}, u32[]{:S(2)}) collective-permute-start(bf16[304,128]{1,0:T(8,128)(2,1)S(1)} %concatenate.21.refs_3_), channel_id=1, source_target_pairs={{0,8},{8,16},{16,24},{24,32},{32,40},{40,48},{48,56},{56,64},{64,7... | collective-permute-start | bytes 233480 | tf_op jit(solution)/shard_map/ppermute | solution.py:25
  35.6 1.9 %copy-start.6 = (bf16[304,128]{1,0:T(8,128)(2,1)}, bf16[304,128]{1,0:T(8,128)(2,1)S(1)}, u32[]{:S(2)}) copy-start(bf16[304,128]{1,0:T(8,128)(2,1)S(1)} %collective-permute-done.refs_2_) | copy-start | bytes 233476
  36.3 1.3 copy-start.7
  37.6 0.6 copy-start.8
  44.1 21.2 %collective-permute-start.6 = (f32[312,128]{1,0:T(8,128)}, f32[312,128]{1,0:T(8,128)S(1)}, u32[]{:S(2)}, u32[]{:S(2)}) collective-permute-start(f32[312,128]{1,0:T(8,128)} %shard_map.211), channel_id=1, source_target_pairs={{0,104},{8,112},{16,120},{24,128},{32,136},{40,144},{48,152},{56,1... | collective-permute-start | bytes 479240 | tf_op jit(solution)/shard_map/ppermute | solution.py:25
  46.6 18.6 %collective-permute-start.5 = (f32[312,128]{1,0:T(8,128)}, f32[312,128]{1,0:T(8,128)}, u32[]{:S(2)}, u32[]{:S(2)}) collective-permute-start(f32[312,128]{1,0:T(8,128)} %shard_map.211), channel_id=1, source_target_pairs={{0,72},{8,80},{16,88},{24,96},{32,104},{40,112},{48,120},{56,128},... | collective-permute-start | bytes 479240 | tf_op jit(solution)/shard_map/ppermute | solution.py:25
  51.9 25.5 %collective-permute-start.4 = (f32[312,128]{1,0:T(8,128)}, f32[312,128]{1,0:T(8,128)S(1)}, u32[]{:S(2)}, u32[]{:S(2)}) collective-permute-start(f32[312,128]{1,0:T(8,128)} %shard_map.211), channel_id=1, source_target_pairs={{0,40},{8,48},{16,56},{24,64},{32,72},{40,80},{48,88},{56,96},{64,... | collective-permute-start | bytes 479240 | tf_op jit(solution)/shard_map/ppermute | solution.py:25
  57.4 22.1 %collective-permute-start.3 = (f32[312,128]{1,0:T(8,128)}, f32[312,128]{1,0:T(8,128)}, u32[]{:S(2)}, u32[]{:S(2)}) collective-permute-start(f32[312,128]{1,0:T(8,128)} %shard_map.211), channel_id=1, source_target_pairs={{0,8},{8,16},{16,24},{24,32},{32,40},{40,48},{48,56},{56,64},{64,7... | collective-permute-start | bytes 479240 | tf_op jit(solution)/shard_map/ppermute | solution.py:25
  82.0 3.9 %copy-start.1 = (bf16[128,256]{1,0:T(8,128)(2,1)S(1)}, bf16[128,256]{1,0:T(8,128)(2,1)}, u32[]{:S(2)}) copy-start(bf16[128,256]{1,0:T(8,128)(2,1)} %param.22) | copy-start | bytes 196612
  82.8 3.4 %copy-start.13 = (f32[128,2]{0,1:T(2,128)S(1)}, f32[128,2]{0,1:T(2,128)}, u32[]{:S(2)}) copy-start(f32[128,2]{0,1:T(2,128)} %get-tuple-element.10) | copy-start | bytes 3076
  83.9 3.2 %copy-start.12 = (f32[2,153]{1,0:T(2,128)S(1)}, f32[2,153]{1,0:T(2,128)}, u32[]{:S(2)}) copy-start(f32[2,153]{1,0:T(2,128)} %reshape.153) | copy-start | bytes 3676
  83.9 2.0 %copy-start.2 = (f32[128,2,128]{0,2,1:T(8,128)S(1)}, f32[128,2,128]{0,2,1:T(8,128)}, u32[]{:S(2)}) copy-start(f32[128,2,128]{0,2,1:T(8,128)} %fusion.8) | copy-start | bytes 393220
  85.8 3.9 %copy-start.5 = (f32[153,16,1]{0,1,2:T(8,128)S(1)}, f32[153,16,1]{0,1,2:T(8,128)}, u32[]{:S(2)}) copy-start(f32[153,16,1]{0,1,2:T(8,128)} %constant.55) | copy-start | bytes 29380
  91.4 64.4 %copy-start.11 = (s32[128]{0:T(128)S(1)}, s32[128]{0:T(128)}, u32[]{:S(2)}) copy-start(s32[128]{0:T(128)} %param.23) | copy-start | bytes 1540
  91.4 18.9 %collective-permute-start.9 = (f32[312,128]{1,0:T(8,128)S(1)}, f32[312,128]{1,0:T(8,128)S(1)}, u32[]{:S(2)}, u32[]{:S(2)}) collective-permute-start(f32[312,128]{1,0:T(8,128)S(1)} %concatenate.25), channel_id=1, source_target_pairs={{24,0},{32,8},{40,16},{48,24},{56,32},{64,40},{72,48},{80,56},{88,... | collective-permute-start | bytes 479240 | tf_op jit(solution)/shard_map/ppermute | solution.py:25
  95.2 17.1 %collective-permute-start.8 = (f32[312,128]{1,0:T(8,128)S(1)}, f32[312,128]{1,0:T(8,128)S(1)}, u32[]{:S(2)}, u32[]{:S(2)}) collective-permute-start(f32[312,128]{1,0:T(8,128)S(1)} %concatenate.25), channel_id=1, source_target_pairs={{16,0},{24,8},{32,16},{40,24},{48,32},{56,40},{64,48},{72,56},{80,... | collective-permute-start | bytes 479240 | tf_op jit(solution)/shard_map/ppermute | solution.py:25
  98.6 17.6 %collective-permute-start.7 = (f32[312,128]{1,0:T(8,128)S(1)}, f32[312,128]{1,0:T(8,128)S(1)}, u32[]{:S(2)}, u32[]{:S(2)}) collective-permute-start(f32[312,128]{1,0:T(8,128)S(1)} %concatenate.25), channel_id=1, source_target_pairs={{8,0},{16,8},{24,16},{32,24},{40,32},{48,40},{56,48},{64,56},{72,6... | collective-permute-start | bytes 479240 | tf_op jit(solution)/shard_map/ppermute | solution.py:25
  116.5 20.6 %collective-permute-start.13 = (f32[312,128]{1,0:T(8,128)S(1)}, f32[312,128]{1,0:T(8,128)S(1)}, u32[]{:S(2)}, u32[]{:S(2)}) collective-permute-start(f32[312,128]{1,0:T(8,128)S(1)} %add_select_fusion.3), channel_id=1, source_target_pairs={{104,0},{112,8},{120,16},{128,24},{136,32},{144,40},{152,48},{160,... | collective-permute-start | bytes 479240 | tf_op jit(solution)/shard_map/ppermute | solution.py:25
  124.6 14.6 %collective-permute-start.12 = (f32[312,128]{1,0:T(8,128)S(1)}, f32[312,128]{1,0:T(8,128)S(1)}, u32[]{:S(2)}, u32[]{:S(2)}) collective-permute-start(f32[312,128]{1,0:T(8,128)S(1)} %add_select_fusion.3), channel_id=1, source_target_pairs={{72,0},{80,8},{88,16},{96,24},{104,32},{112,40},{120,48},{128,56},... | collective-permute-start | bytes 479240 | tf_op jit(solution)/shard_map/ppermute | solution.py:25
  127.7 26.9 %collective-permute-start.11 = (f32[312,128]{1,0:T(8,128)S(1)}, f32[312,128]{1,0:T(8,128)S(1)}, u32[]{:S(2)}, u32[]{:S(2)}) collective-permute-start(f32[312,128]{1,0:T(8,128)S(1)} %add_select_fusion.3), channel_id=1, source_target_pairs={{40,0},{48,8},{56,16},{64,24},{72,32},{80,40},{88,48},{96,56},{104... | collective-permute-start | bytes 479240 | tf_op jit(solution)/shard_map/ppermute | solution.py:25
  133.6 21.2 %collective-permute-start.10 = (f32[312,128]{1,0:T(8,128)S(1)}, f32[312,128]{1,0:T(8,128)S(1)}, u32[]{:S(2)}, u32[]{:S(2)}) collective-permute-start(f32[312,128]{1,0:T(8,128)S(1)} %add_select_fusion.3), channel_id=1, source_target_pairs={{8,0},{16,8},{24,16},{32,24},{40,32},{48,40},{56,48},{64,56},{72,6... | collective-permute-start | bytes 479240 | tf_op jit(solution)/shard_map/ppermute | solution.py:25
Sparse Core Ops, SparseCore 0:
  30.4 27.8 all-gather.1

commit v8 on v7

--- a/solution.py
+++ b/solution.py
@@ -137,9 +137,9 @@
         for ref in piece_refs:
             ids = ref[ids_row : ids_row + 1, :].astype(jnp.float32)
             mask = (ids == last).astype(jnp.float32)
-            scaled = ref[value_rows:ids_row, :].astype(jnp.float32) * 0.5
-            first = jnp.dot(left_ref[...], scaled, precision=exact_mode, preferred_element_type=jnp.float32)
-            second = jnp.dot(right_ref[...], scaled, precision=exact_mode, preferred_element_type=jnp.float32)
+            scaled = ref[value_rows:ids_row, :] * jnp.asarray(0.5, ref.dtype)
+            first = jnp.dot(left_ref[...], scaled, preferred_element_type=jnp.float32)
+            second = jnp.dot(right_ref[...], scaled, preferred_element_type=jnp.float32)
             feat = (first + left_one) * (second + right_one) * weight * mask
             high = feat.astype(jnp.bfloat16)
             low = (feat - high.astype(jnp.float32)).astype(jnp.bfloat16)
@@ -165,7 +165,12 @@
         kernel,
         out_shape=jax.ShapeDtypeStruct((out_rows, head_width), jnp.float32),
         interpret=INTERPRET,
-    )(*pieces, jnp.asarray(big_left), jnp.asarray(big_right), jnp.asarray(aux))
+    )(
+        *pieces,
+        jnp.asarray(big_left, jnp.bfloat16),
+        jnp.asarray(big_right, jnp.bfloat16),
+        jnp.asarray(aux),
+    )
 
 
 def features(entries):

time: 169 us -> 166 us (0.982)
  the two profiles are of different devices: /device:TPU:46 before, /device:TPU:40 now
where the time goes in v8:
time: 166 us; the launch traced here: 165 us
  starting transfers between devices  69 us (42%)
  waiting for transfers between devices  42.8 us (26%)
  matrix products  16.6 us (10%)
  between operations  14.7 us (9%)
  other arithmetic  11.6 us (7%)
  local copies, waits for them, and re-layouts  7.09 us (4%)
  Pallas kernels  3.49 us (2%)
    ppermute x14, starting transfers between devices, shifted(): return lax.ppermute(piece, axis, pairs)  68.9 us
    ppermute x14, waiting for transfers between devices, shifted(): return lax.ppermute(piece, axis, pairs)  42.8 us
    pallas_call x1, Pallas kernels, window_state(): pl.pallas_call(kernel, out_shape=jax.ShapeDtypeStruct((out_rows, head_wid...  3.49 us
  transfers between devices with their start and end apart: 15, of which 9 were waited for; matrix products, arithmetic and copies ran while one was open for 10% of the time, Pallas kernels for 2%

profile of v8, /device:TPU:40, one launch (start us, length us, event | category | flops | bytes accessed | tf_op | source)
XLA Modules:
  0.0 165.2 jit_solution(12990985286504638365)
XLA Ops:
  7.2 0.8 add_convert_fusion
  8.0 0.8 slice.168
  8.9 1.0 copy.36
  9.9 0.9 concatenate.21.refs_3_
  10.8 6.1 %collective-permute-start.2 = (bf16[304,128]{1,0:T(8,128)(2,1)S(1)}, bf16[304,128]{1,0:T(8,128)(2,1)S(1)}, u32[]{:S(2)}, u32[]{:S(2)}) collective-permute-start(bf16[304,128]{1,0:T(8,128)(2,1)S(1)} %concatenate.21.refs_3_), channel_id=1, source_target_pairs={{0,16},{8,24},{16,32},{24,40},{32,48},{40,56},{48,64},{56,72},{64,... | collective-permute-start | bytes 233480 | tf_op jit(solution)/shard_map/ppermute | solution.py:25
  16.9 9.1 %collective-permute-start.1 = (bf16[304,128]{1,0:T(8,128)(2,1)S(1)}, bf16[304,128]{1,0:T(8,128)(2,1)S(1)}, u32[]{:S(2)}, u32[]{:S(2)}) collective-permute-start(bf16[304,128]{1,0:T(8,128)(2,1)S(1)} %concatenate.21.refs_3_), channel_id=1, source_target_pairs={{0,24},{8,32},{16,40},{24,48},{32,56},{40,64},{48,72},{56,80},{64,... | collective-permute-start | bytes 233480 | tf_op jit(solution)/shard_map/ppermute | solution.py:25
  26.0 4.3 %collective-permute-start = (bf16[304,128]{1,0:T(8,128)(2,1)S(1)}, bf16[304,128]{1,0:T(8,128)(2,1)S(1)}, u32[]{:S(2)}, u32[]{:S(2)}) collective-permute-start(bf16[304,128]{1,0:T(8,128)(2,1)S(1)} %concatenate.21.refs_3_), channel_id=1, source_target_pairs={{0,8},{8,16},{16,24},{24,32},{32,40},{40,48},{48,56},{56,64},{64,7... | collective-permute-start | bytes 233480 | tf_op jit(solution)/shard_map/ppermute | solution.py:25
  32.5 1.1 convolution_add_fusion.3
  33.6 1.1 convolution_add_fusion.4
  34.7 0.9 collective-permute-done.refs_2_
  36.3 1.3 collective-permute-done.1.refs_0_
  38.2 3.5 %shard_map.211 = f32[312,128]{1,0:T(8,128)} custom-call(bf16[304,128]{1,0:T(8,128)(2,1)} %copy-done.8, bf16[304,128]{1,0:T(8,128)(2,1)} %copy-done.7, bf16[304,128]{1,0:T(8,128)(2,1)} %copy-done.6, bf16[304,128]{1,0:T(8,128)(2,1)} %copy-done.3, bf16[306,32]{1,0:T(8,128)(2,1)} %constant.37.clone.refs_4_, bf16[306,32]{1,0:T(8,128)(2,1)} %constant.38.clone.refs_5_, ...), custom_call_target="tpu_custom_call" | custom-call | tf_op jit(solution)/shard_map/pallas_call | solution.py:164
  41.6 2.6 %collective-permute-start.6 = (f32[312,128]{1,0:T(8,128)}, f32[312,128]{1,0:T(8,128)S(1)}, u32[]{:S(2)}, u32[]{:S(2)}) collective-permute-start(f32[312,128]{1,0:T(8,128)} %shard_map.211), channel_id=1, source_target_pairs={{0,104},{8,112},{16,120},{24,128},{32,136},{40,144},{48,152},{56,1... | collective-permute-start | bytes 479240 | tf_op jit(solution)/shard_map/ppermute | solution.py:25
  44.2 5.3 %collective-permute-start.5 = (f32[312,128]{1,0:T(8,128)}, f32[312,128]{1,0:T(8,128)}, u32[]{:S(2)}, u32[]{:S(2)}) collective-permute-start(f32[312,128]{1,0:T(8,128)} %shard_map.211), channel_id=1, source_target_pairs={{0,72},{8,80},{16,88},{24,96},{32,104},{40,112},{48,120},{56,128},... | collective-permute-start | bytes 479240 | tf_op jit(solution)/shard_map/ppermute | solution.py:25
  49.5 5.5 %collective-permute-start.4 = (f32[312,128]{1,0:T(8,128)}, f32[312,128]{1,0:T(8,128)S(1)}, u32[]{:S(2)}, u32[]{:S(2)}) collective-permute-start(f32[312,128]{1,0:T(8,128)} %shard_map.211), channel_id=1, source_target_pairs={{0,40},{8,48},{16,56},{24,64},{32,72},{40,80},{48,88},{56,96},{64,... | collective-permute-start | bytes 479240 | tf_op jit(solution)/shard_map/ppermute | solution.py:25
  55.0 3.5 %collective-permute-start.3 = (f32[312,128]{1,0:T(8,128)}, f32[312,128]{1,0:T(8,128)}, u32[]{:S(2)}, u32[]{:S(2)}) collective-permute-start(f32[312,128]{1,0:T(8,128)} %shard_map.211), channel_id=1, source_target_pairs={{0,8},{8,16},{16,24},{24,32},{32,40},{40,48},{48,56},{56,64},{64,7... | collective-permute-start | bytes 479240 | tf_op jit(solution)/shard_map/ppermute | solution.py:25
  59.4 1.4 compare_convert_fusion.5
  60.9 1.1 convolution_add_fusion.5
  61.9 1.1 multiply_multiply_fusion.1
  64.3 1.0 add_select_fusion.8
  65.3 9.7 %collective-permute-done.4 = f32[312,128]{1,0:T(8,128)S(1)} collective-permute-done((f32[312,128]{1,0:T(8,128)}, f32[312,128]{1,0:T(8,128)S(1)}, u32[]{:S(2)}, u32[]{:S(2)}) %collective-permute-start.4) | collective-permute-done | bytes 159776 | tf_op jit(solution)/shard_map/ppermute | solution.py:25
  75.1 2.0 %collective-permute-done.3 = f32[312,128]{1,0:T(8,128)} collective-permute-done((f32[312,128]{1,0:T(8,128)}, f32[312,128]{1,0:T(8,128)}, u32[]{:S(2)}, u32[]{:S(2)}) %collective-permute-start.3) | collective-permute-done | bytes 159776 | tf_op jit(solution)/shard_map/ppermute | solution.py:25
  77.8 1.0 add_select_fusion.6
  79.8 1.1 fusion.8
  80.9 2.0 %fusion.57 = f32[128,256]{0,1:T(8,128)S(1)} fusion(bf16[128,4096]{1,0:T(8,128)(2,1)} %all-gather.2.cloned.1.call-done, bf16[256,4096]{1,0:T(8,128)(2,1)S(1)} %copy-done), kind=kOutput, calls=%fused_computation.138 | convolution fusion | flops 268435456 | bytes 3276800 | tf_op jit(solution)/shard_map/transpose(jvp())/reshape | solution.py:305
  83.2 0.9 fusion.22
  84.1 0.9 convolution_add_fusion.2
  85.3 0.9 fusion.7
  86.2 1.2 fusion.4
  88.0 0.9 reshape.157
  89.1 3.8 %collective-permute-start.9 = (f32[312,128]{1,0:T(8,128)S(1)}, f32[312,128]{1,0:T(8,128)S(1)}, u32[]{:S(2)}, u32[]{:S(2)}) collective-permute-start(f32[312,128]{1,0:T(8,128)S(1)} %concatenate.25), channel_id=1, source_target_pairs={{24,0},{32,8},{40,16},{48,24},{56,32},{64,40},{72,48},{80,56},{88,... | collective-permute-start | bytes 479240 | tf_op jit(solution)/shard_map/ppermute | solution.py:25
  92.9 3.4 %collective-permute-start.8 = (f32[312,128]{1,0:T(8,128)S(1)}, f32[312,128]{1,0:T(8,128)S(1)}, u32[]{:S(2)}, u32[]{:S(2)}) collective-permute-start(f32[312,128]{1,0:T(8,128)S(1)} %concatenate.25), channel_id=1, source_target_pairs={{16,0},{24,8},{32,16},{40,24},{48,32},{56,40},{64,48},{72,56},{80,... | collective-permute-start | bytes 479240 | tf_op jit(solution)/shard_map/ppermute | solution.py:25
  96.3 5.8 %collective-permute-start.7 = (f32[312,128]{1,0:T(8,128)S(1)}, f32[312,128]{1,0:T(8,128)S(1)}, u32[]{:S(2)}, u32[]{:S(2)}) collective-permute-start(f32[312,128]{1,0:T(8,128)S(1)} %concatenate.25), channel_id=1, source_target_pairs={{8,0},{16,8},{24,16},{32,24},{40,32},{48,40},{56,48},{64,56},{72,6... | collective-permute-start | bytes 479240 | tf_op jit(solution)/shard_map/ppermute | solution.py:25
  102.4 5.6 %collective-permute-done.9 = f32[312,128]{1,0:T(8,128)S(1)} collective-permute-done((f32[312,128]{1,0:T(8,128)S(1)}, f32[312,128]{1,0:T(8,128)S(1)}, u32[]{:S(2)}, u32[]{:S(2)}) %collective-permute-start.9) | collective-permute-done | bytes 159776 | tf_op jit(solution)/shard_map/ppermute | solution.py:25
  107.9 2.1 %collective-permute-done.8 = f32[312,128]{1,0:T(8,128)S(1)} collective-permute-done((f32[312,128]{1,0:T(8,128)S(1)}, f32[312,128]{1,0:T(8,128)S(1)}, u32[]{:S(2)}, u32[]{:S(2)}) %collective-permute-start.8) | collective-permute-done | bytes 159776 | tf_op jit(solution)/shard_map/ppermute | solution.py:25
  110.2 3.8 %collective-permute-done.7 = f32[312,128]{1,0:T(8,128)S(1)} collective-permute-done((f32[312,128]{1,0:T(8,128)S(1)}, f32[312,128]{1,0:T(8,128)S(1)}, u32[]{:S(2)}, u32[]{:S(2)}) %collective-permute-start.7) | collective-permute-done | bytes 159776 | tf_op jit(solution)/shard_map/ppermute | solution.py:25
  114.2 8.1 %collective-permute-start.13 = (f32[312,128]{1,0:T(8,128)S(1)}, f32[312,128]{1,0:T(8,128)S(1)}, u32[]{:S(2)}, u32[]{:S(2)}) collective-permute-start(f32[312,128]{1,0:T(8,128)S(1)} %add_select_fusion.3), channel_id=1, source_target_pairs={{104,0},{112,8},{120,16},{128,24},{136,32},{144,40},{152,48},{160,... | collective-permute-start | bytes 479240 | tf_op jit(solution)/shard_map/ppermute | solution.py:25
  122.3 2.2 %collective-permute-start.12 = (f32[312,128]{1,0:T(8,128)S(1)}, f32[312,128]{1,0:T(8,128)S(1)}, u32[]{:S(2)}, u32[]{:S(2)}) collective-permute-start(f32[312,128]{1,0:T(8,128)S(1)} %add_select_fusion.3), channel_id=1, source_target_pairs={{72,0},{80,8},{88,16},{96,24},{104,32},{112,40},{120,48},{128,56},... | collective-permute-start | bytes 479240 | tf_op jit(solution)/shard_map/ppermute | solution.py:25
  124.5 0.9 fusion.19
  125.4 5.9 %collective-permute-start.11 = (f32[312,128]{1,0:T(8,128)S(1)}, f32[312,128]{1,0:T(8,128)S(1)}, u32[]{:S(2)}, u32[]{:S(2)}) collective-permute-start(f32[312,128]{1,0:T(8,128)S(1)} %add_select_fusion.3), channel_id=1, source_target_pairs={{40,0},{48,8},{56,16},{64,24},{72,32},{80,40},{88,48},{96,56},{104... | collective-permute-start | bytes 479240 | tf_op jit(solution)/shard_map/ppermute | solution.py:25
  131.3 3.5 %collective-permute-start.10 = (f32[312,128]{1,0:T(8,128)S(1)}, f32[312,128]{1,0:T(8,128)S(1)}, u32[]{:S(2)}, u32[]{:S(2)}) collective-permute-start(f32[312,128]{1,0:T(8,128)S(1)} %add_select_fusion.3), channel_id=1, source_target_pairs={{8,0},{16,8},{24,16},{32,24},{40,32},{48,40},{56,48},{64,56},{72,6... | collective-permute-start | bytes 479240 | tf_op jit(solution)/shard_map/ppermute | solution.py:25
  134.8 2.1 %collective-permute-done.12 = f32[312,128]{1,0:T(8,128)S(1)} collective-permute-done((f32[312,128]{1,0:T(8,128)S(1)}, f32[312,128]{1,0:T(8,128)S(1)}, u32[]{:S(2)}, u32[]{:S(2)}) %collective-permute-start.12) | collective-permute-done | bytes 159776 | tf_op jit(solution)/shard_map/ppermute | solution.py:25
  137.0 15.4 %collective-permute-done.11 = f32[312,128]{1,0:T(8,128)S(1)} collective-permute-done((f32[312,128]{1,0:T(8,128)S(1)}, f32[312,128]{1,0:T(8,128)S(1)}, u32[]{:S(2)}, u32[]{:S(2)}) %collective-permute-start.11) | collective-permute-done | bytes 159776 | tf_op jit(solution)/shard_map/ppermute | solution.py:25
  153.5 0.7 compare_convert_fusion.2
  154.2 1.4 convolution_add_fusion.8
  156.1 0.8 fusion.10
  156.9 0.8 copy.48
  157.6 0.7 fusion.42
  (98 shorter events, 11.1 us)
Async XLA Ops:
  7.2 73.7 %copy-start = (bf16[256,4096]{1,0:T(8,128)(2,1)S(1)}, bf16[256,4096]{1,0:T(8,128)(2,1)}, u32[]{:S(2)}) copy-start(bf16[256,4096]{1,0:T(8,128)(2,1)} %param.25) | copy-start | bytes 6291460
  7.2 55.9 %copy-start.9 = (f32[153]{0:T(256)S(1)}, f32[153]{0:T(256)}, u32[]{:S(2)}) copy-start(f32[153]{0:T(256)} %constant.53) | copy-start | bytes 1840
  7.2 73.7 %all-gather.2.cloned.1.call-start = ((), (), s32[]{:S(2)}) async-start(), calls=%async_computation | async-start | bytes 1179648 | tf_op jit(solution)/shard_map/all_gather | solution.py:250
  10.8 26.8 %copy-start.3 = (bf16[304,128]{1,0:T(8,128)(2,1)}, bf16[304,128]{1,0:T(8,128)(2,1)S(1)}, u32[]{:S(2)}) copy-start(bf16[304,128]{1,0:T(8,128)(2,1)S(1)} %concatenate.21.refs_3_) | copy-start | bytes 233476
  10.8 25.5 %collective-permute-start.2 = (bf16[304,128]{1,0:T(8,128)(2,1)S(1)}, bf16[304,128]{1,0:T(8,128)(2,1)S(1)}, u32[]{:S(2)}, u32[]{:S(2)}) collective-permute-start(bf16[304,128]{1,0:T(8,128)(2,1)S(1)} %concatenate.21.refs_3_), channel_id=1, source_target_pairs={{0,16},{8,24},{16,32},{24,40},{32,48},{40,56},{48,64},{56,72},{64,... | collective-permute-start | bytes 233480 | tf_op jit(solution)/shard_map/ppermute | solution.py:25
  16.9 20.6 %collective-permute-start.1 = (bf16[304,128]{1,0:T(8,128)(2,1)S(1)}, bf16[304,128]{1,0:T(8,128)(2,1)S(1)}, u32[]{:S(2)}, u32[]{:S(2)}) collective-permute-start(bf16[304,128]{1,0:T(8,128)(2,1)S(1)} %concatenate.21.refs_3_), channel_id=1, source_target_pairs={{0,24},{8,32},{16,40},{24,48},{32,56},{40,64},{48,72},{56,80},{64,... | collective-permute-start | bytes 233480 | tf_op jit(solution)/shard_map/ppermute | solution.py:25
  26.0 9.6 %collective-permute-start = (bf16[304,128]{1,0:T(8,128)(2,1)S(1)}, bf16[304,128]{1,0:T(8,128)(2,1)S(1)}, u32[]{:S(2)}, u32[]{:S(2)}) collective-permute-start(bf16[304,128]{1,0:T(8,128)(2,1)S(1)} %concatenate.21.refs_3_), channel_id=1, source_target_pairs={{0,8},{8,16},{16,24},{24,32},{32,40},{40,48},{48,56},{56,64},{64,7... | collective-permute-start | bytes 233480 | tf_op jit(solution)/shard_map/ppermute | solution.py:25
  35.6 1.9 %copy-start.6 = (bf16[304,128]{1,0:T(8,128)(2,1)}, bf16[304,128]{1,0:T(8,128)(2,1)S(1)}, u32[]{:S(2)}) copy-start(bf16[304,128]{1,0:T(8,128)(2,1)S(1)} %collective-permute-done.refs_2_) | copy-start | bytes 233476
  36.3 1.3 copy-start.7
  37.5 0.6 copy-start.8
  41.6 21.9 %collective-permute-start.6 = (f32[312,128]{1,0:T(8,128)}, f32[312,128]{1,0:T(8,128)S(1)}, u32[]{:S(2)}, u32[]{:S(2)}) collective-permute-start(f32[312,128]{1,0:T(8,128)} %shard_map.211), channel_id=1, source_target_pairs={{0,104},{8,112},{16,120},{24,128},{32,136},{40,144},{48,152},{56,1... | collective-permute-start | bytes 479240 | tf_op jit(solution)/shard_map/ppermute | solution.py:25
  44.2 19.4 %collective-permute-start.5 = (f32[312,128]{1,0:T(8,128)}, f32[312,128]{1,0:T(8,128)}, u32[]{:S(2)}, u32[]{:S(2)}) collective-permute-start(f32[312,128]{1,0:T(8,128)} %shard_map.211), channel_id=1, source_target_pairs={{0,72},{8,80},{16,88},{24,96},{32,104},{40,112},{48,120},{56,128},... | collective-permute-start | bytes 479240 | tf_op jit(solution)/shard_map/ppermute | solution.py:25
  49.5 25.5 %collective-permute-start.4 = (f32[312,128]{1,0:T(8,128)}, f32[312,128]{1,0:T(8,128)S(1)}, u32[]{:S(2)}, u32[]{:S(2)}) collective-permute-start(f32[312,128]{1,0:T(8,128)} %shard_map.211), channel_id=1, source_target_pairs={{0,40},{8,48},{16,56},{24,64},{32,72},{40,80},{48,88},{56,96},{64,... | collective-permute-start | bytes 479240 | tf_op jit(solution)/shard_map/ppermute | solution.py:25
  55.0 22.1 %collective-permute-start.3 = (f32[312,128]{1,0:T(8,128)}, f32[312,128]{1,0:T(8,128)}, u32[]{:S(2)}, u32[]{:S(2)}) collective-permute-start(f32[312,128]{1,0:T(8,128)} %shard_map.211), channel_id=1, source_target_pairs={{0,8},{8,16},{16,24},{24,32},{32,40},{40,48},{48,56},{56,64},{64,7... | collective-permute-start | bytes 479240 | tf_op jit(solution)/shard_map/ppermute | solution.py:25
  79.0 3.9 %copy-start.1 = (bf16[128,256]{1,0:T(8,128)(2,1)S(1)}, bf16[128,256]{1,0:T(8,128)(2,1)}, u32[]{:S(2)}) copy-start(bf16[128,256]{1,0:T(8,128)(2,1)} %param.22) | copy-start | bytes 196612
  80.9 2.0 %copy-start.2 = (f32[128,2,128]{0,2,1:T(8,128)S(1)}, f32[128,2,128]{0,2,1:T(8,128)}, u32[]{:S(2)}) copy-start(f32[128,2,128]{0,2,1:T(8,128)} %fusion.8) | copy-start | bytes 393220
  80.9 2.3 %copy-start.11 = (f32[128,2]{0,1:T(2,128)S(1)}, f32[128,2]{0,1:T(2,128)}, u32[]{:S(2)}) copy-start(f32[128,2]{0,1:T(2,128)} %get-tuple-element.10) | copy-start | bytes 3076
  82.9 4.6 %copy-start.5 = (f32[153,16,1]{0,1,2:T(8,128)S(1)}, f32[153,16,1]{0,1,2:T(8,128)}, u32[]{:S(2)}) copy-start(f32[153,16,1]{0,1,2:T(8,128)} %constant.55) | copy-start | bytes 29380
  82.9 4.8 %copy-start.4 = (f32[153,16,1]{0,1,2:T(8,128)S(1)}, f32[153,16,1]{0,1,2:T(8,128)}, u32[]{:S(2)}) copy-start(f32[153,16,1]{0,1,2:T(8,128)} %constant.54) | copy-start | bytes 29380
  86.2 38.3 %copy-start.12 = (f32[128,2]{0,1:T(2,128)S(1)}, f32[128,2]{0,1:T(2,128)}, u32[]{:S(2)}) copy-start(f32[128,2]{0,1:T(2,128)} %get-tuple-element.10) | copy-start | bytes 3076
  89.1 64.4 %copy-start.10 = (s32[128]{0:T(128)S(1)}, s32[128]{0:T(128)}, u32[]{:S(2)}) copy-start(s32[128]{0:T(128)} %param.23) | copy-start | bytes 1540
  89.1 18.8 %collective-permute-start.9 = (f32[312,128]{1,0:T(8,128)S(1)}, f32[312,128]{1,0:T(8,128)S(1)}, u32[]{:S(2)}, u32[]{:S(2)}) collective-permute-start(f32[312,128]{1,0:T(8,128)S(1)} %concatenate.25), channel_id=1, source_target_pairs={{24,0},{32,8},{40,16},{48,24},{56,32},{64,40},{72,48},{80,56},{88,... | collective-permute-start | bytes 479240 | tf_op jit(solution)/shard_map/ppermute | solution.py:25
  92.9 17.2 %collective-permute-start.8 = (f32[312,128]{1,0:T(8,128)S(1)}, f32[312,128]{1,0:T(8,128)S(1)}, u32[]{:S(2)}, u32[]{:S(2)}) collective-permute-start(f32[312,128]{1,0:T(8,128)S(1)} %concatenate.25), channel_id=1, source_target_pairs={{16,0},{24,8},{32,16},{40,24},{48,32},{56,40},{64,48},{72,56},{80,... | collective-permute-start | bytes 479240 | tf_op jit(solution)/shard_map/ppermute | solution.py:25
  96.3 17.6 %collective-permute-start.7 = (f32[312,128]{1,0:T(8,128)S(1)}, f32[312,128]{1,0:T(8,128)S(1)}, u32[]{:S(2)}, u32[]{:S(2)}) collective-permute-start(f32[312,128]{1,0:T(8,128)S(1)} %concatenate.25), channel_id=1, source_target_pairs={{8,0},{16,8},{24,16},{32,24},{40,32},{48,40},{56,48},{64,56},{72,6... | collective-permute-start | bytes 479240 | tf_op jit(solution)/shard_map/ppermute | solution.py:25
  114.2 20.6 %collective-permute-start.13 = (f32[312,128]{1,0:T(8,128)S(1)}, f32[312,128]{1,0:T(8,128)S(1)}, u32[]{:S(2)}, u32[]{:S(2)}) collective-permute-start(f32[312,128]{1,0:T(8,128)S(1)} %add_select_fusion.3), channel_id=1, source_target_pairs={{104,0},{112,8},{120,16},{128,24},{136,32},{144,40},{152,48},{160,... | collective-permute-start | bytes 479240 | tf_op jit(solution)/shard_map/ppermute | solution.py:25
  122.3 14.6 %collective-permute-start.12 = (f32[312,128]{1,0:T(8,128)S(1)}, f32[312,128]{1,0:T(8,128)S(1)}, u32[]{:S(2)}, u32[]{:S(2)}) collective-permute-start(f32[312,128]{1,0:T(8,128)S(1)} %add_select_fusion.3), channel_id=1, source_target_pairs={{72,0},{80,8},{88,16},{96,24},{104,32},{112,40},{120,48},{128,56},... | collective-permute-start | bytes 479240 | tf_op jit(solution)/shard_map/ppermute | solution.py:25
  125.4 27.0 %collective-permute-start.11 = (f32[312,128]{1,0:T(8,128)S(1)}, f32[312,128]{1,0:T(8,128)S(1)}, u32[]{:S(2)}, u32[]{:S(2)}) collective-permute-start(f32[312,128]{1,0:T(8,128)S(1)} %add_select_fusion.3), channel_id=1, source_target_pairs={{40,0},{48,8},{56,16},{64,24},{72,32},{80,40},{88,48},{96,56},{104... | collective-permute-start | bytes 479240 | tf_op jit(solution)/shard_map/ppermute | solution.py:25
  131.3 21.2 %collective-permute-start.10 = (f32[312,128]{1,0:T(8,128)S(1)}, f32[312,128]{1,0:T(8,128)S(1)}, u32[]{:S(2)}, u32[]{:S(2)}) collective-permute-start(f32[312,128]{1,0:T(8,128)S(1)} %add_select_fusion.3), channel_id=1, source_target_pairs={{8,0},{16,8},{24,16},{32,24},{40,32},{48,40},{56,48},{64,56},{72,6... | collective-permute-start | bytes 479240 | tf_op jit(solution)/shard_map/ppermute | solution.py:25
Sparse Core Ops, SparseCore 0:
  30.4 29.6 all-gather.1

commit v9 on v8

--- a/solution.py
+++ b/solution.py
@@ -257,7 +257,6 @@
     key_heads = keys.astype(jnp.float32).reshape(local_heads, FD, length)
     head_values = values.astype(jnp.float32).reshape(length, local_heads, head_width)
     taps = conv_weight.astype(jnp.float32)
-    k_feat, feature_pullback = jax.vjp(features, key_heads)
     row_count = query_rows.shape[0]
     near, far = window_steps(reach, lax.axis_size("ctx"))
     raw = raw_pack(keys, values, doc_ids, queries[:, length - 2 :].reshape(-1))
@@ -274,6 +273,8 @@
         values.shape[1],
         out_rows,
     )
+    key_late, forward_piece = lax.optimization_barrier((key_heads, forward_piece))
+    k_feat, feature_pullback = jax.vjp(features, key_late)
     join = packed_join(key_row)
     packed = fold(join, [shifted(forward_piece, "ctx", step, False) for step in far])
     state_in, normer_in, _ = unpack(packed, state_shape, normer_shape, 1)

time: 166 us -> 166 us (level)
  the two profiles are of different devices: /device:TPU:40 before, /device:TPU:54 now
where the time goes in v9:
time: 166 us; the launch traced here: 165 us
  starting transfers between devices  66 us (40%)
  waiting for transfers between devices  45.1 us (27%)
  matrix products  16.6 us (10%)
  between operations  14.7 us (9%)
  other arithmetic  11.6 us (7%)
  local copies, waits for them, and re-layouts  7.09 us (4%)
  Pallas kernels  3.49 us (2%)
    ppermute x14, starting transfers between devices, shifted(): return lax.ppermute(piece, axis, pairs)  66 us
    ppermute x14, waiting for transfers between devices, shifted(): return lax.ppermute(piece, axis, pairs)  45.1 us
    pallas_call x1, Pallas kernels, window_state(): pl.pallas_call(kernel, out_shape=jax.ShapeDtypeStruct((out_rows, head_wid...  3.49 us
  transfers between devices with their start and end apart: 15, of which 10 were waited for; matrix products, arithmetic and copies ran while one was open for 10% of the time, Pallas kernels for 2%

profile of v9, /device:TPU:54, one launch (start us, length us, event | category | flops | bytes accessed | tf_op | source)
XLA Modules:
  0.0 164.6 jit_solution(5307594144639698783)
XLA Ops:
  7.2 0.8 add_convert_fusion
  8.0 0.8 slice.168
  8.9 1.0 copy.36
  9.9 0.9 concatenate.21.refs_3_
  10.8 6.1 %collective-permute-start.2 = (bf16[304,128]{1,0:T(8,128)(2,1)S(1)}, bf16[304,128]{1,0:T(8,128)(2,1)S(1)}, u32[]{:S(2)}, u32[]{:S(2)}) collective-permute-start(bf16[304,128]{1,0:T(8,128)(2,1)S(1)} %concatenate.21.refs_3_), channel_id=1, source_target_pairs={{0,16},{8,24},{16,32},{24,40},{32,48},{40,56},{48,64},{56,72},{64,... | collective-permute-start | bytes 233480 | tf_op jit(solution)/shard_map/ppermute | solution.py:25
  16.9 9.1 %collective-permute-start.1 = (bf16[304,128]{1,0:T(8,128)(2,1)S(1)}, bf16[304,128]{1,0:T(8,128)(2,1)S(1)}, u32[]{:S(2)}, u32[]{:S(2)}) collective-permute-start(bf16[304,128]{1,0:T(8,128)(2,1)S(1)} %concatenate.21.refs_3_), channel_id=1, source_target_pairs={{0,24},{8,32},{16,40},{24,48},{32,56},{40,64},{48,72},{56,80},{64,... | collective-permute-start | bytes 233480 | tf_op jit(solution)/shard_map/ppermute | solution.py:25
  26.0 4.3 %collective-permute-start = (bf16[304,128]{1,0:T(8,128)(2,1)S(1)}, bf16[304,128]{1,0:T(8,128)(2,1)S(1)}, u32[]{:S(2)}, u32[]{:S(2)}) collective-permute-start(bf16[304,128]{1,0:T(8,128)(2,1)S(1)} %concatenate.21.refs_3_), channel_id=1, source_target_pairs={{0,8},{8,16},{16,24},{24,32},{32,40},{40,48},{48,56},{56,64},{64,7... | collective-permute-start | bytes 233480 | tf_op jit(solution)/shard_map/ppermute | solution.py:25
  32.5 3.1 %collective-permute-done.refs_2_ = bf16[304,128]{1,0:T(8,128)(2,1)S(1)} collective-permute-done((bf16[304,128]{1,0:T(8,128)(2,1)S(1)}, bf16[304,128]{1,0:T(8,128)(2,1)S(1)}, u32[]{:S(2)}, u32[]{:S(2)}) %collective-permute-start) | collective-permute-done | bytes 77856 | tf_op jit(solution)/shard_map/ppermute | solution.py:25
  36.3 1.3 collective-permute-done.1.refs_0_
  38.2 3.5 %shard_map.211 = f32[312,128]{1,0:T(8,128)} custom-call(bf16[304,128]{1,0:T(8,128)(2,1)} %copy-done.8, bf16[304,128]{1,0:T(8,128)(2,1)} %copy-done.7, bf16[304,128]{1,0:T(8,128)(2,1)} %copy-done.6, bf16[304,128]{1,0:T(8,128)(2,1)} %copy-done.3, bf16[306,32]{1,0:T(8,128)(2,1)} %constant.32.clone.refs_4_, bf16[306,32]{1,0:T(8,128)(2,1)} %constant.33.clone.refs_5_, ...), custom_call_target="tpu_custom_call" | custom-call | tf_op jit(solution)/shard_map/pallas_call | solution.py:164
  41.6 1.9 %collective-permute-start.6 = (f32[312,128]{1,0:T(8,128)}, f32[312,128]{1,0:T(8,128)S(1)}, u32[]{:S(2)}, u32[]{:S(2)}) collective-permute-start(f32[312,128]{1,0:T(8,128)} %shard_map.211), channel_id=1, source_target_pairs={{0,104},{8,112},{16,120},{24,128},{32,136},{40,144},{48,152},{56,1... | collective-permute-start | bytes 479240 | tf_op jit(solution)/shard_map/ppermute | solution.py:25
  43.6 4.3 %collective-permute-start.5 = (f32[312,128]{1,0:T(8,128)}, f32[312,128]{1,0:T(8,128)}, u32[]{:S(2)}, u32[]{:S(2)}) collective-permute-start(f32[312,128]{1,0:T(8,128)} %shard_map.211), channel_id=1, source_target_pairs={{0,72},{8,80},{16,88},{24,96},{32,104},{40,112},{48,120},{56,128},... | collective-permute-start | bytes 479240 | tf_op jit(solution)/shard_map/ppermute | solution.py:25
  47.8 4.8 %collective-permute-start.4 = (f32[312,128]{1,0:T(8,128)}, f32[312,128]{1,0:T(8,128)S(1)}, u32[]{:S(2)}, u32[]{:S(2)}) collective-permute-start(f32[312,128]{1,0:T(8,128)} %shard_map.211), channel_id=1, source_target_pairs={{0,40},{8,48},{16,56},{24,64},{32,72},{40,80},{48,88},{56,96},{64,... | collective-permute-start | bytes 479240 | tf_op jit(solution)/shard_map/ppermute | solution.py:25
  52.7 3.4 %collective-permute-start.3 = (f32[312,128]{1,0:T(8,128)}, f32[312,128]{1,0:T(8,128)}, u32[]{:S(2)}, u32[]{:S(2)}) collective-permute-start(f32[312,128]{1,0:T(8,128)} %shard_map.211), channel_id=1, source_target_pairs={{0,8},{8,16},{16,24},{24,32},{32,40},{40,48},{48,56},{56,64},{64,7... | collective-permute-start | bytes 479240 | tf_op jit(solution)/shard_map/ppermute | solution.py:25
  56.9 1.4 compare_convert_fusion.5
  58.3 1.1 convolution_add_fusion.3
  59.5 1.1 convolution_add_fusion.5
  60.5 1.1 convolution_add_fusion.4
  61.6 1.1 multiply_multiply_fusion.1
  63.9 1.0 add_select_fusion.8
  65.0 7.8 %collective-permute-done.4 = f32[312,128]{1,0:T(8,128)S(1)} collective-permute-done((f32[312,128]{1,0:T(8,128)}, f32[312,128]{1,0:T(8,128)S(1)}, u32[]{:S(2)}, u32[]{:S(2)}) %collective-permute-start.4) | collective-permute-done | bytes 159776 | tf_op jit(solution)/shard_map/ppermute | solution.py:25
  72.9 3.7 %collective-permute-done.3 = f32[312,128]{1,0:T(8,128)} collective-permute-done((f32[312,128]{1,0:T(8,128)}, f32[312,128]{1,0:T(8,128)}, u32[]{:S(2)}, u32[]{:S(2)}) %collective-permute-start.3) | collective-permute-done | bytes 159776 | tf_op jit(solution)/shard_map/ppermute | solution.py:25
  77.2 1.0 add_select_fusion.6
  79.2 1.1 fusion.8
  80.3 2.0 %fusion.63 = f32[128,256]{0,1:T(8,128)S(1)} fusion(bf16[128,4096]{1,0:T(8,128)(2,1)} %all-gather.2.cloned.1.call-done, bf16[256,4096]{1,0:T(8,128)(2,1)S(1)} %copy-done), kind=kOutput, calls=%fused_computation.143 | convolution fusion | flops 268435456 | bytes 3276800 | tf_op jit(solution)/shard_map/transpose(jvp())/reshape | solution.py:306
  82.6 0.9 fusion.22
  83.5 0.9 convolution_add_fusion.2
  84.8 0.9 fusion.7
  85.7 1.2 fusion.4
  87.4 0.9 reshape.162
  88.5 5.3 %collective-permute-start.9 = (f32[312,128]{1,0:T(8,128)S(1)}, f32[312,128]{1,0:T(8,128)S(1)}, u32[]{:S(2)}, u32[]{:S(2)}) collective-permute-start(f32[312,128]{1,0:T(8,128)S(1)} %concatenate.25), channel_id=1, source_target_pairs={{24,0},{32,8},{40,16},{48,24},{56,32},{64,40},{72,48},{80,56},{88,... | collective-permute-start | bytes 479240 | tf_op jit(solution)/shard_map/ppermute | solution.py:25
  93.8 3.3 %collective-permute-start.8 = (f32[312,128]{1,0:T(8,128)S(1)}, f32[312,128]{1,0:T(8,128)S(1)}, u32[]{:S(2)}, u32[]{:S(2)}) collective-permute-start(f32[312,128]{1,0:T(8,128)S(1)} %concatenate.25), channel_id=1, source_target_pairs={{16,0},{24,8},{32,16},{40,24},{48,32},{56,40},{64,48},{72,56},{80,... | collective-permute-start | bytes 479240 | tf_op jit(solution)/shard_map/ppermute | solution.py:25
  97.2 3.7 %collective-permute-start.7 = (f32[312,128]{1,0:T(8,128)S(1)}, f32[312,128]{1,0:T(8,128)S(1)}, u32[]{:S(2)}, u32[]{:S(2)}) collective-permute-start(f32[312,128]{1,0:T(8,128)S(1)} %concatenate.25), channel_id=1, source_target_pairs={{8,0},{16,8},{24,16},{32,24},{40,32},{48,40},{56,48},{64,56},{72,6... | collective-permute-start | bytes 479240 | tf_op jit(solution)/shard_map/ppermute | solution.py:25
  101.2 6.7 %collective-permute-done.9 = f32[312,128]{1,0:T(8,128)S(1)} collective-permute-done((f32[312,128]{1,0:T(8,128)S(1)}, f32[312,128]{1,0:T(8,128)S(1)}, u32[]{:S(2)}, u32[]{:S(2)}) %collective-permute-start.9) | collective-permute-done | bytes 159776 | tf_op jit(solution)/shard_map/ppermute | solution.py:25
  107.8 2.8 %collective-permute-done.8 = f32[312,128]{1,0:T(8,128)S(1)} collective-permute-done((f32[312,128]{1,0:T(8,128)S(1)}, f32[312,128]{1,0:T(8,128)S(1)}, u32[]{:S(2)}, u32[]{:S(2)}) %collective-permute-start.8) | collective-permute-done | bytes 159776 | tf_op jit(solution)/shard_map/ppermute | solution.py:25
  110.8 2.6 %collective-permute-done.7 = f32[312,128]{1,0:T(8,128)S(1)} collective-permute-done((f32[312,128]{1,0:T(8,128)S(1)}, f32[312,128]{1,0:T(8,128)S(1)}, u32[]{:S(2)}, u32[]{:S(2)}) %collective-permute-start.7) | collective-permute-done | bytes 159776 | tf_op jit(solution)/shard_map/ppermute | solution.py:25
  113.6 5.9 %collective-permute-start.13 = (f32[312,128]{1,0:T(8,128)S(1)}, f32[312,128]{1,0:T(8,128)S(1)}, u32[]{:S(2)}, u32[]{:S(2)}) collective-permute-start(f32[312,128]{1,0:T(8,128)S(1)} %add_select_fusion.3), channel_id=1, source_target_pairs={{104,0},{112,8},{120,16},{128,24},{136,32},{144,40},{152,48},{160,... | collective-permute-start | bytes 479240 | tf_op jit(solution)/shard_map/ppermute | solution.py:25
  119.6 3.2 %collective-permute-start.12 = (f32[312,128]{1,0:T(8,128)S(1)}, f32[312,128]{1,0:T(8,128)S(1)}, u32[]{:S(2)}, u32[]{:S(2)}) collective-permute-start(f32[312,128]{1,0:T(8,128)S(1)} %add_select_fusion.3), channel_id=1, source_target_pairs={{72,0},{80,8},{88,16},{96,24},{104,32},{112,40},{120,48},{128,56},... | collective-permute-start | bytes 479240 | tf_op jit(solution)/shard_map/ppermute | solution.py:25
  122.8 0.9 fusion.19
  123.7 7.1 %collective-permute-start.11 = (f32[312,128]{1,0:T(8,128)S(1)}, f32[312,128]{1,0:T(8,128)S(1)}, u32[]{:S(2)}, u32[]{:S(2)}) collective-permute-start(f32[312,128]{1,0:T(8,128)S(1)} %add_select_fusion.3), channel_id=1, source_target_pairs={{40,0},{48,8},{56,16},{64,24},{72,32},{80,40},{88,48},{96,56},{104... | collective-permute-start | bytes 479240 | tf_op jit(solution)/shard_map/ppermute | solution.py:25
  130.8 3.6 %collective-permute-start.10 = (f32[312,128]{1,0:T(8,128)S(1)}, f32[312,128]{1,0:T(8,128)S(1)}, u32[]{:S(2)}, u32[]{:S(2)}) collective-permute-start(f32[312,128]{1,0:T(8,128)S(1)} %add_select_fusion.3), channel_id=1, source_target_pairs={{8,0},{16,8},{24,16},{32,24},{40,32},{48,40},{56,48},{64,56},{72,6... | collective-permute-start | bytes 479240 | tf_op jit(solution)/shard_map/ppermute | solution.py:25
  134.4 0.9 collective-permute-done.12
  135.4 13.5 %collective-permute-done.11 = f32[312,128]{1,0:T(8,128)S(1)} collective-permute-done((f32[312,128]{1,0:T(8,128)S(1)}, f32[312,128]{1,0:T(8,128)S(1)}, u32[]{:S(2)}, u32[]{:S(2)}) %collective-permute-start.11) | collective-permute-done | bytes 159776 | tf_op jit(solution)/shard_map/ppermute | solution.py:25
  149.0 2.9 %collective-permute-done.10 = f32[312,128]{1,0:T(8,128)S(1)} collective-permute-done((f32[312,128]{1,0:T(8,128)S(1)}, f32[312,128]{1,0:T(8,128)S(1)}, u32[]{:S(2)}, u32[]{:S(2)}) %collective-permute-start.10) | collective-permute-done | bytes 159776 | tf_op jit(solution)/shard_map/ppermute | solution.py:25
  152.9 0.7 compare_convert_fusion.2
  153.6 1.4 convolution_add_fusion.8
  155.5 0.8 fusion.10
  156.3 0.8 copy.48
  (98 shorter events, 11.8 us)
Async XLA Ops:
  7.2 73.1 %copy-start = (bf16[256,4096]{1,0:T(8,128)(2,1)S(1)}, bf16[256,4096]{1,0:T(8,128)(2,1)}, u32[]{:S(2)}) copy-start(bf16[256,4096]{1,0:T(8,128)(2,1)} %param.25) | copy-start | bytes 6291460
  7.2 55.5 %copy-start.9 = (f32[153]{0:T(256)S(1)}, f32[153]{0:T(256)}, u32[]{:S(2)}) copy-start(f32[153]{0:T(256)} %constant.53) | copy-start | bytes 1840
  7.2 73.1 %all-gather.2.cloned.1.call-start = ((), (), s32[]{:S(2)}) async-start(), calls=%async_computation | async-start | bytes 1179648 | tf_op jit(solution)/shard_map/all_gather | solution.py:250
  10.8 26.8 %copy-start.3 = (bf16[304,128]{1,0:T(8,128)(2,1)}, bf16[304,128]{1,0:T(8,128)(2,1)S(1)}, u32[]{:S(2)}) copy-start(bf16[304,128]{1,0:T(8,128)(2,1)S(1)} %concatenate.21.refs_3_) | copy-start | bytes 233476
  10.8 25.5 %collective-permute-start.2 = (bf16[304,128]{1,0:T(8,128)(2,1)S(1)}, bf16[304,128]{1,0:T(8,128)(2,1)S(1)}, u32[]{:S(2)}, u32[]{:S(2)}) collective-permute-start(bf16[304,128]{1,0:T(8,128)(2,1)S(1)} %concatenate.21.refs_3_), channel_id=1, source_target_pairs={{0,16},{8,24},{16,32},{24,40},{32,48},{40,56},{48,64},{56,72},{64,... | collective-permute-start | bytes 233480 | tf_op jit(solution)/shard_map/ppermute | solution.py:25
  16.9 20.6 %collective-permute-start.1 = (bf16[304,128]{1,0:T(8,128)(2,1)S(1)}, bf16[304,128]{1,0:T(8,128)(2,1)S(1)}, u32[]{:S(2)}, u32[]{:S(2)}) collective-permute-start(bf16[304,128]{1,0:T(8,128)(2,1)S(1)} %concatenate.21.refs_3_), channel_id=1, source_target_pairs={{0,24},{8,32},{16,40},{24,48},{32,56},{40,64},{48,72},{56,80},{64,... | collective-permute-start | bytes 233480 | tf_op jit(solution)/shard_map/ppermute | solution.py:25
  26.0 9.6 %collective-permute-start = (bf16[304,128]{1,0:T(8,128)(2,1)S(1)}, bf16[304,128]{1,0:T(8,128)(2,1)S(1)}, u32[]{:S(2)}, u32[]{:S(2)}) collective-permute-start(bf16[304,128]{1,0:T(8,128)(2,1)S(1)} %concatenate.21.refs_3_), channel_id=1, source_target_pairs={{0,8},{8,16},{16,24},{24,32},{32,40},{40,48},{48,56},{56,64},{64,7... | collective-permute-start | bytes 233480 | tf_op jit(solution)/shard_map/ppermute | solution.py:25
  35.6 1.9 %copy-start.6 = (bf16[304,128]{1,0:T(8,128)(2,1)}, bf16[304,128]{1,0:T(8,128)(2,1)S(1)}, u32[]{:S(2)}) copy-start(bf16[304,128]{1,0:T(8,128)(2,1)S(1)} %collective-permute-done.refs_2_) | copy-start | bytes 233476
  36.3 1.3 copy-start.7
  37.5 0.6 copy-start.8
  41.6 21.6 %collective-permute-start.6 = (f32[312,128]{1,0:T(8,128)}, f32[312,128]{1,0:T(8,128)S(1)}, u32[]{:S(2)}, u32[]{:S(2)}) collective-permute-start(f32[312,128]{1,0:T(8,128)} %shard_map.211), channel_id=1, source_target_pairs={{0,104},{8,112},{16,120},{24,128},{32,136},{40,144},{48,152},{56,1... | collective-permute-start | bytes 479240 | tf_op jit(solution)/shard_map/ppermute | solution.py:25
  43.6 19.7 %collective-permute-start.5 = (f32[312,128]{1,0:T(8,128)}, f32[312,128]{1,0:T(8,128)}, u32[]{:S(2)}, u32[]{:S(2)}) collective-permute-start(f32[312,128]{1,0:T(8,128)} %shard_map.211), channel_id=1, source_target_pairs={{0,72},{8,80},{16,88},{24,96},{32,104},{40,112},{48,120},{56,128},... | collective-permute-start | bytes 479240 | tf_op jit(solution)/shard_map/ppermute | solution.py:25
  47.8 24.9 %collective-permute-start.4 = (f32[312,128]{1,0:T(8,128)}, f32[312,128]{1,0:T(8,128)S(1)}, u32[]{:S(2)}, u32[]{:S(2)}) collective-permute-start(f32[312,128]{1,0:T(8,128)} %shard_map.211), channel_id=1, source_target_pairs={{0,40},{8,48},{16,56},{24,64},{32,72},{40,80},{48,88},{56,96},{64,... | collective-permute-start | bytes 479240 | tf_op jit(solution)/shard_map/ppermute | solution.py:25
  52.7 23.9 %collective-permute-start.3 = (f32[312,128]{1,0:T(8,128)}, f32[312,128]{1,0:T(8,128)}, u32[]{:S(2)}, u32[]{:S(2)}) collective-permute-start(f32[312,128]{1,0:T(8,128)} %shard_map.211), channel_id=1, source_target_pairs={{0,8},{8,16},{16,24},{24,32},{32,40},{40,48},{48,56},{56,64},{64,7... | collective-permute-start | bytes 479240 | tf_op jit(solution)/shard_map/ppermute | solution.py:25
  78.4 3.9 %copy-start.1 = (bf16[128,256]{1,0:T(8,128)(2,1)S(1)}, bf16[128,256]{1,0:T(8,128)(2,1)}, u32[]{:S(2)}) copy-start(bf16[128,256]{1,0:T(8,128)(2,1)} %param.22) | copy-start | bytes 196612
  80.3 2.0 %copy-start.2 = (f32[128,2,128]{0,2,1:T(8,128)S(1)}, f32[128,2,128]{0,2,1:T(8,128)}, u32[]{:S(2)}) copy-start(f32[128,2,128]{0,2,1:T(8,128)} %fusion.8) | copy-start | bytes 393220
  80.3 2.3 %copy-start.11 = (f32[128,2]{0,1:T(2,128)S(1)}, f32[128,2]{0,1:T(2,128)}, u32[]{:S(2)}) copy-start(f32[128,2]{0,1:T(2,128)} %get-tuple-element.14) | copy-start | bytes 3076
  82.3 4.6 %copy-start.5 = (f32[153,16,1]{0,1,2:T(8,128)S(1)}, f32[153,16,1]{0,1,2:T(8,128)}, u32[]{:S(2)}) copy-start(f32[153,16,1]{0,1,2:T(8,128)} %constant.55) | copy-start | bytes 29380
  82.3 4.8 %copy-start.4 = (f32[153,16,1]{0,1,2:T(8,128)S(1)}, f32[153,16,1]{0,1,2:T(8,128)}, u32[]{:S(2)}) copy-start(f32[153,16,1]{0,1,2:T(8,128)} %constant.54) | copy-start | bytes 29380
  85.6 37.1 %copy-start.12 = (f32[128,2]{0,1:T(2,128)S(1)}, f32[128,2]{0,1:T(2,128)}, u32[]{:S(2)}) copy-start(f32[128,2]{0,1:T(2,128)} %get-tuple-element.14) | copy-start | bytes 3076
  88.5 64.4 %copy-start.10 = (s32[128]{0:T(128)S(1)}, s32[128]{0:T(128)}, u32[]{:S(2)}) copy-start(s32[128]{0:T(128)} %param.23) | copy-start | bytes 1540
  88.5 19.3 %collective-permute-start.9 = (f32[312,128]{1,0:T(8,128)S(1)}, f32[312,128]{1,0:T(8,128)S(1)}, u32[]{:S(2)}, u32[]{:S(2)}) collective-permute-start(f32[312,128]{1,0:T(8,128)S(1)} %concatenate.25), channel_id=1, source_target_pairs={{24,0},{32,8},{40,16},{48,24},{56,32},{64,40},{72,48},{80,56},{88,... | collective-permute-start | bytes 479240 | tf_op jit(solution)/shard_map/ppermute | solution.py:25
  93.8 16.8 %collective-permute-start.8 = (f32[312,128]{1,0:T(8,128)S(1)}, f32[312,128]{1,0:T(8,128)S(1)}, u32[]{:S(2)}, u32[]{:S(2)}) collective-permute-start(f32[312,128]{1,0:T(8,128)S(1)} %concatenate.25), channel_id=1, source_target_pairs={{16,0},{24,8},{32,16},{40,24},{48,32},{56,40},{64,48},{72,56},{80,... | collective-permute-start | bytes 479240 | tf_op jit(solution)/shard_map/ppermute | solution.py:25
  97.2 16.2 %collective-permute-start.7 = (f32[312,128]{1,0:T(8,128)S(1)}, f32[312,128]{1,0:T(8,128)S(1)}, u32[]{:S(2)}, u32[]{:S(2)}) collective-permute-start(f32[312,128]{1,0:T(8,128)S(1)} %concatenate.25), channel_id=1, source_target_pairs={{8,0},{16,8},{24,16},{32,24},{40,32},{48,40},{56,48},{64,56},{72,6... | collective-permute-start | bytes 479240 | tf_op jit(solution)/shard_map/ppermute | solution.py:25
  113.6 20.7 %collective-permute-start.13 = (f32[312,128]{1,0:T(8,128)S(1)}, f32[312,128]{1,0:T(8,128)S(1)}, u32[]{:S(2)}, u32[]{:S(2)}) collective-permute-start(f32[312,128]{1,0:T(8,128)S(1)} %add_select_fusion.3), channel_id=1, source_target_pairs={{104,0},{112,8},{120,16},{128,24},{136,32},{144,40},{152,48},{160,... | collective-permute-start | bytes 479240 | tf_op jit(solution)/shard_map/ppermute | solution.py:25
  119.6 15.7 %collective-permute-start.12 = (f32[312,128]{1,0:T(8,128)S(1)}, f32[312,128]{1,0:T(8,128)S(1)}, u32[]{:S(2)}, u32[]{:S(2)}) collective-permute-start(f32[312,128]{1,0:T(8,128)S(1)} %add_select_fusion.3), channel_id=1, source_target_pairs={{72,0},{80,8},{88,16},{96,24},{104,32},{112,40},{120,48},{128,56},... | collective-permute-start | bytes 479240 | tf_op jit(solution)/shard_map/ppermute | solution.py:25
  123.7 25.2 %collective-permute-start.11 = (f32[312,128]{1,0:T(8,128)S(1)}, f32[312,128]{1,0:T(8,128)S(1)}, u32[]{:S(2)}, u32[]{:S(2)}) collective-permute-start(f32[312,128]{1,0:T(8,128)S(1)} %add_select_fusion.3), channel_id=1, source_target_pairs={{40,0},{48,8},{56,16},{64,24},{72,32},{80,40},{88,48},{96,56},{104... | collective-permute-start | bytes 479240 | tf_op jit(solution)/shard_map/ppermute | solution.py:25
  130.8 21.2 %collective-permute-start.10 = (f32[312,128]{1,0:T(8,128)S(1)}, f32[312,128]{1,0:T(8,128)S(1)}, u32[]{:S(2)}, u32[]{:S(2)}) collective-permute-start(f32[312,128]{1,0:T(8,128)S(1)} %add_select_fusion.3), channel_id=1, source_target_pairs={{8,0},{16,8},{24,16},{32,24},{40,32},{48,40},{56,48},{64,56},{72,6... | collective-permute-start | bytes 479240 | tf_op jit(solution)/shard_map/ppermute | solution.py:25
Sparse Core Ops, SparseCore 0:
  30.4 27.7 all-gather.1

commit v10 on v9

--- a/solution.py
+++ b/solution.py
@@ -23,6 +23,20 @@
     else:
         pairs = [(source, source + step) for source in range(size - step)]
     return lax.ppermute(piece, axis, pairs)
+
+
+def gather_columns(block, axis):
+    size, here = (lax.axis_size(axis), lax.axis_index(axis))
+    held = block[None]
+    step = 1
+    while step < size:
+        pairs = [(source, (source + step) % size) for source in range(size)]
+        held = jnp.concatenate([held, lax.ppermute(held, axis, pairs)], axis=0)
+        step *= 2
+    turned = held[:size][::-1]
+    doubled = jnp.concatenate([turned, turned], axis=0)
+    ordered = lax.dynamic_slice_in_dim(doubled, size - 1 - here, size, axis=0)
+    return ordered.transpose(1, 0, 2).reshape(block.shape[0], size * block.shape[1])
 
 
 def fold(combine, pieces):
@@ -247,7 +261,7 @@
     head_width = values.shape[1] // local_heads
     reach = -(-(MOST - 1) // length)
     grad_attn = lax.dot_general(
-        lax.all_gather(out_grad, "head", axis=1, tiled=True),
+        gather_columns(out_grad, "head"),
         out_weight,
         (((1,), (1,)), ((), ())),
         preferred_element_type=jnp.float32,

time: 166 us -> 175 us (1.054)
  the two profiles are of different devices: /device:TPU:54 before, /device:TPU:46 now
where the time goes in v10:
time: 175 us; the launch traced here: 174 us
  starting transfers between devices  74.6 us (43%)
  waiting for transfers between devices  45.9 us (26%)
  other arithmetic  18.1 us (10%)
  matrix products  17.6 us (10%)
  local copies, waits for them, and re-layouts  12.5 us (7%)
  Pallas kernels  3.51 us (2%)
    ppermute x14, starting transfers between devices, shifted(): return lax.ppermute(piece, axis, pairs)  69 us
    ppermute x14, waiting for transfers between devices, shifted(): return lax.ppermute(piece, axis, pairs)  37 us
    ppermute x3, waiting for transfers between devices, gather_columns(): held = jnp.concatenate([held, lax.ppermute(held, axis, pairs)], axis=0)  8.86 us
    ppermute x3, starting transfers between devices, gather_columns(): held = jnp.concatenate([held, lax.ppermute(held, axis, pairs)], axis=0)  5.65 us
    dot_general x4, matrix products, features(): jnp.einsum('rk,...kt->...rt', left, scaled, precision=exact_mode) + left_one  3.9 us
    select_n x9, other arithmetic, join(): return jnp.where(empty_later, earlier, later + addend)  3.8 us
    concatenate x3, other arithmetic, gather_columns(): held = jnp.concatenate([held, lax.ppermute(held, axis, pairs)], axis=0)  3.71 us
    pallas_call x1, Pallas kernels, window_state(): pl.pallas_call(kernel, out_shape=jax.ShapeDtypeStruct((out_rows, head_wid...  3.51 us
  transfers between devices with their start and end apart: 17, of which 9 were waited for; matrix products, arithmetic and copies ran while one was open for 14% of the time, Pallas kernels for 2%

profile of v10, /device:TPU:46, one launch (start us, length us, event | category | flops | bytes accessed | tf_op | source)
XLA Modules:
  0.0 173.8 jit_solution(73993130068045731)
XLA Ops:
  1.5 0.9 copy.35
  3.4 0.9 concatenate.35.refs_3_
  4.2 4.3 %collective-permute-start = (bf16[304,128]{1,0:T(8,128)(2,1)S(1)}, bf16[304,128]{1,0:T(8,128)(2,1)S(1)}, u32[]{:S(2)}, u32[]{:S(2)}) collective-permute-start(bf16[304,128]{1,0:T(8,128)(2,1)S(1)} %concatenate.35.refs_3_), channel_id=1, source_target_pairs={{0,8},{8,16},{16,24},{24,32},{32,40},{40,48},{48,56},{56,64},{64,7... | collective-permute-start | bytes 233480 | tf_op jit(solution)/shard_map/ppermute | solution.py:25
  8.5 9.1 %collective-permute-start.4 = (bf16[304,128]{1,0:T(8,128)(2,1)S(1)}, bf16[304,128]{1,0:T(8,128)(2,1)S(1)}, u32[]{:S(2)}, u32[]{:S(2)}) collective-permute-start(bf16[304,128]{1,0:T(8,128)(2,1)S(1)} %concatenate.35.refs_3_), channel_id=1, source_target_pairs={{0,24},{8,32},{16,40},{24,48},{32,56},{40,64},{48,72},{56,80},{64,... | collective-permute-start | bytes 233480 | tf_op jit(solution)/shard_map/ppermute | solution.py:25
  17.6 6.1 %collective-permute-start.5 = (bf16[304,128]{1,0:T(8,128)(2,1)S(1)}, bf16[304,128]{1,0:T(8,128)(2,1)S(1)}, u32[]{:S(2)}, u32[]{:S(2)}) collective-permute-start(bf16[304,128]{1,0:T(8,128)(2,1)S(1)} %concatenate.35.refs_3_), channel_id=1, source_target_pairs={{0,16},{8,24},{16,32},{24,40},{32,48},{40,56},{48,64},{56,72},{64,... | collective-permute-start | bytes 233480 | tf_op jit(solution)/shard_map/ppermute | solution.py:25
  26.2 4.5 %collective-permute-done.5.refs_1_ = bf16[304,128]{1,0:T(8,128)(2,1)S(1)} collective-permute-done((bf16[304,128]{1,0:T(8,128)(2,1)S(1)}, bf16[304,128]{1,0:T(8,128)(2,1)S(1)}, u32[]{:S(2)}, u32[]{:S(2)}) %collective-permute-start.5) | collective-permute-done | bytes 77856 | tf_op jit(solution)/shard_map/ppermute | solution.py:25
  31.3 3.5 %shard_map.211 = f32[312,128]{1,0:T(8,128)} custom-call(bf16[304,128]{1,0:T(8,128)(2,1)} %copy-done.21, bf16[304,128]{1,0:T(8,128)(2,1)} %copy-done.22, bf16[304,128]{1,0:T(8,128)(2,1)} %copy-done.20, bf16[304,128]{1,0:T(8,128)(2,1)} %copy-done.15, bf16[306,32]{1,0:T(8,128)(2,1)} %constant.42.clone.refs_4_, bf16[306,32]{1,0:T(8,128)(2,1)} %constant.43.clone.refs_5_, ...), custom_call_target="tpu_custom_call" | custom-call | tf_op jit(solution)/shard_map/pallas_call | solution.py:178
  34.9 6.9 %collective-permute-start.8 = (f32[312,128]{1,0:T(8,128)}, f32[312,128]{1,0:T(8,128)S(1)}, u32[]{:S(2)}, u32[]{:S(2)}) collective-permute-start(f32[312,128]{1,0:T(8,128)} %shard_map.211), channel_id=1, source_target_pairs={{0,72},{8,80},{16,88},{24,96},{32,104},{40,112},{48,120},{56,128},... | collective-permute-start | bytes 479240 | tf_op jit(solution)/shard_map/ppermute | solution.py:25
  41.7 2.2 %collective-permute-start.9 = (f32[312,128]{1,0:T(8,128)}, f32[312,128]{1,0:T(8,128)}, u32[]{:S(2)}, u32[]{:S(2)}) collective-permute-start(f32[312,128]{1,0:T(8,128)} %shard_map.211), channel_id=1, source_target_pairs={{0,104},{8,112},{16,120},{24,128},{32,136},{40,144},{48,152},{56,1... | collective-permute-start | bytes 479240 | tf_op jit(solution)/shard_map/ppermute | solution.py:25
  44.0 2.0 %collective-permute-start.7 = (f32[312,128]{1,0:T(8,128)}, f32[312,128]{1,0:T(8,128)}, u32[]{:S(2)}, u32[]{:S(2)}) collective-permute-start(f32[312,128]{1,0:T(8,128)} %shard_map.211), channel_id=1, source_target_pairs={{0,40},{8,48},{16,56},{24,64},{32,72},{40,80},{48,88},{56,96},{64,... | collective-permute-start | bytes 479240 | tf_op jit(solution)/shard_map/ppermute | solution.py:25
  46.0 3.9 %collective-permute-start.6 = (f32[312,128]{1,0:T(8,128)}, f32[312,128]{1,0:T(8,128)}, u32[]{:S(2)}, u32[]{:S(2)}) collective-permute-start(f32[312,128]{1,0:T(8,128)} %shard_map.211), channel_id=1, source_target_pairs={{0,8},{8,16},{16,24},{24,32},{32,40},{40,48},{48,56},{56,64},{64,7... | collective-permute-start | bytes 479240 | tf_op jit(solution)/shard_map/ppermute | solution.py:25
  52.1 1.4 compare_convert_fusion.5
  53.6 1.1 convolution_add_fusion.5
  54.7 1.1 convolution_add_fusion.3
  55.8 1.1 convolution_add_fusion.4
  56.9 1.8 %multiply_multiply_fusion.1 = (f32[2,128,153]{1,2,0:T(8,128)S(1)}, f32[2,128,153]{1,2,0:T(8,128)}) fusion(f32[2,128,153]{1,2,0:T(8,128)S(1)} %convolution_add_fusion.5, f32[153]{0:T(256)} %constant.63, f32[153]{0:T(256)} %constant.61, f32[2,16,128]{2,1,0:T(8,128)S(1)} %bitcast.180, f32[153,16,1]{0,1,2:T(8,128)} %constant.64), kind=kOutput, calls=%fused_computation.41 | convolution fusion | flops 7637760 | bytes 497416 | tf_op jit(solution)/shard_map/jvp(rk,...kt->...rt)/dot_general | solution.py:193
  58.7 1.2 fusion.60
  60.6 2.4 %collective-permute-start.2 = (bf16[2,128,512]{2,1,0:T(8,128)(2,1)}, bf16[2,128,512]{2,1,0:T(8,128)(2,1)S(1)}, u32[]{:S(2)}, u32[]{:S(2)}) collective-permute-start(bf16[2,128,512]{2,1,0:T(8,128)(2,1)} %pad_maximum_fusion.2), channel_id=1, source_target_pairs={{0,2},{1,3},{2,4},{3,5},{4,6},{5,7},{6,0},{7,1},{8,10},{9,11},{10,... | collective-permute-start | bytes 786440 | tf_op jit(solution)/shard_map/ppermute | solution.py:34
  63.7 1.1 add_select_fusion.8
  64.8 4.6 %collective-permute-done.7 = f32[312,128]{1,0:T(8,128)} collective-permute-done((f32[312,128]{1,0:T(8,128)}, f32[312,128]{1,0:T(8,128)}, u32[]{:S(2)}, u32[]{:S(2)}) %collective-permute-start.7) | collective-permute-done | bytes 159776 | tf_op jit(solution)/shard_map/ppermute | solution.py:25
  70.1 1.0 add_select_fusion.7
  71.1 0.9 collective-permute-done.6
  72.7 1.0 add_select_fusion.6
  73.9 0.9 pad_maximum_fusion.1
  74.7 3.3 %collective-permute-start.3 = (bf16[4,128,512]{2,1,0:T(8,128)(2,1)}, bf16[4,128,512]{2,1,0:T(8,128)(2,1)}, u32[]{:S(2)}, u32[]{:S(2)}) collective-permute-start(bf16[4,128,512]{2,1,0:T(8,128)(2,1)} %pad_maximum_fusion.1), channel_id=1, source_target_pairs={{0,4},{1,5},{2,6},{3,7},{4,0},{5,1},{6,2},{7,3},{8,12},{9,13},{10,... | collective-permute-start | bytes 1572872 | tf_op jit(solution)/shard_map/ppermute | solution.py:34
  78.8 0.9 reshape.162
  80.4 1.1 fusion.8
  81.5 8.9 %collective-permute-done.3 = bf16[4,128,512]{2,1,0:T(8,128)(2,1)} collective-permute-done((bf16[4,128,512]{2,1,0:T(8,128)(2,1)}, bf16[4,128,512]{2,1,0:T(8,128)(2,1)}, u32[]{:S(2)}, u32[]{:S(2)}) %collective-permute-start.3) | collective-permute-done | bytes 524320 | tf_op jit(solution)/shard_map/ppermute | solution.py:34
  90.3 2.1 %pad_maximum_fusion = bf16[8,128,512]{2,1,0:T(8,128)(2,1)} fusion(bf16[4,128,512]{2,1,0:T(8,128)(2,1)} %collective-permute-done.3, bf16[2,128,512]{2,1,0:T(8,128)(2,1)S(1)} %collective-permute-done.2, bf16[1,128,512]{2,1,0:T(8,128)(2,1)S(1)} %collective-permute-done.1, bf16[1,128,512]{2,1,0:T(8,128)(2,1)S(1)} %bitcast.174), kind=kLoop, calls=%fused_computation.30 | loop fusion | flops 1572864 | bytes 2097152 | tf_op jit(solution)/shard_map/concatenate | solution.py:34
  92.5 1.3 rev.3
  94.2 1.6 copy.36
  95.8 1.6 reshape.178
  99.4 1.1 fusion.7
  100.5 1.3 convolution_add_fusion.2
  102.9 3.3 %collective-permute-start.11 = (f32[312,128]{1,0:T(8,128)S(1)}, f32[312,128]{1,0:T(8,128)S(1)}, u32[]{:S(2)}, u32[]{:S(2)}) collective-permute-start(f32[312,128]{1,0:T(8,128)S(1)} %concatenate.43), channel_id=1, source_target_pairs={{16,0},{24,8},{32,16},{40,24},{48,32},{56,40},{64,48},{72,56},{80,... | collective-permute-start | bytes 479240 | tf_op jit(solution)/shard_map/ppermute | solution.py:25
  106.2 6.6 %collective-permute-start.12 = (f32[312,128]{1,0:T(8,128)S(1)}, f32[312,128]{1,0:T(8,128)S(1)}, u32[]{:S(2)}, u32[]{:S(2)}) collective-permute-start(f32[312,128]{1,0:T(8,128)S(1)} %concatenate.43), channel_id=1, source_target_pairs={{24,0},{32,8},{40,16},{48,24},{56,32},{64,40},{72,48},{80,56},{88,... | collective-permute-start | bytes 479240 | tf_op jit(solution)/shard_map/ppermute | solution.py:25
  112.8 2.2 %collective-permute-start.10 = (f32[312,128]{1,0:T(8,128)S(1)}, f32[312,128]{1,0:T(8,128)S(1)}, u32[]{:S(2)}, u32[]{:S(2)}) collective-permute-start(f32[312,128]{1,0:T(8,128)S(1)} %concatenate.43), channel_id=1, source_target_pairs={{8,0},{16,8},{24,16},{32,24},{40,32},{48,40},{56,48},{64,56},{72,6... | collective-permute-start | bytes 479240 | tf_op jit(solution)/shard_map/ppermute | solution.py:25
  114.9 1.2 fusion.64
  116.1 7.6 %collective-permute-done.12 = f32[312,128]{1,0:T(8,128)S(1)} collective-permute-done((f32[312,128]{1,0:T(8,128)S(1)}, f32[312,128]{1,0:T(8,128)S(1)}, u32[]{:S(2)}, u32[]{:S(2)}) %collective-permute-start.12) | collective-permute-done | bytes 159776 | tf_op jit(solution)/shard_map/ppermute | solution.py:25
  123.9 2.3 %collective-permute-done.10 = f32[312,128]{1,0:T(8,128)S(1)} collective-permute-done((f32[312,128]{1,0:T(8,128)S(1)}, f32[312,128]{1,0:T(8,128)S(1)}, u32[]{:S(2)}, u32[]{:S(2)}) %collective-permute-start.10) | collective-permute-done | bytes 159776 | tf_op jit(solution)/shard_map/ppermute | solution.py:25
  126.5 5.4 %collective-permute-start.15 = (f32[312,128]{1,0:T(8,128)S(1)}, f32[312,128]{1,0:T(8,128)S(1)}, u32[]{:S(2)}, u32[]{:S(2)}) collective-permute-start(f32[312,128]{1,0:T(8,128)S(1)} %add_select_fusion.3), channel_id=1, source_target_pairs={{72,0},{80,8},{88,16},{96,24},{104,32},{112,40},{120,48},{128,56},... | collective-permute-start | bytes 479240 | tf_op jit(solution)/shard_map/ppermute | solution.py:25
  131.8 6.1 %collective-permute-start.16 = (f32[312,128]{1,0:T(8,128)S(1)}, f32[312,128]{1,0:T(8,128)S(1)}, u32[]{:S(2)}, u32[]{:S(2)}) collective-permute-start(f32[312,128]{1,0:T(8,128)S(1)} %add_select_fusion.3), channel_id=1, source_target_pairs={{104,0},{112,8},{120,16},{128,24},{136,32},{144,40},{152,48},{160,... | collective-permute-start | bytes 479240 | tf_op jit(solution)/shard_map/ppermute | solution.py:25
  137.9 1.8 %fusion.59 = f32[2,128,128]{2,1,0:T(8,128)} fusion(f32[2,128,128]{1,2,0:T(8,128)} %get-tuple-element.45, f32[128,2,128]{0,2,1:T(8,128)S(1)} %copy-done.11, f32[2,128]{1,0:T(2,128)S(1)} %copy-done.33), kind=kOutput, calls=%fused_computation.144 | convolution fusion | flops 25198592 | bytes 394240 | tf_op jit(solution)/shard_map/transpose(jvp(hts,shd->thd))/dot_general | solution.py:203
  139.8 9.1 %collective-permute-start.14 = (f32[312,128]{1,0:T(8,128)S(1)}, f32[312,128]{1,0:T(8,128)S(1)}, u32[]{:S(2)}, u32[]{:S(2)}) collective-permute-start(f32[312,128]{1,0:T(8,128)S(1)} %add_select_fusion.3), channel_id=1, source_target_pairs={{40,0},{48,8},{56,16},{64,24},{72,32},{80,40},{88,48},{96,56},{104... | collective-permute-start | bytes 479240 | tf_op jit(solution)/shard_map/ppermute | solution.py:25
  148.8 1.9 %collective-permute-start.13 = (f32[312,128]{1,0:T(8,128)S(1)}, f32[312,128]{1,0:T(8,128)S(1)}, u32[]{:S(2)}, u32[]{:S(2)}) collective-permute-start(f32[312,128]{1,0:T(8,128)S(1)} %add_select_fusion.3), channel_id=1, source_target_pairs={{8,0},{16,8},{24,16},{32,24},{40,32},{48,40},{56,48},{64,56},{72,6... | collective-permute-start | bytes 479240 | tf_op jit(solution)/shard_map/ppermute | solution.py:25
  150.9 7.7 %collective-permute-done.14 = f32[312,128]{1,0:T(8,128)S(1)} collective-permute-done((f32[312,128]{1,0:T(8,128)S(1)}, f32[312,128]{1,0:T(8,128)S(1)}, u32[]{:S(2)}, u32[]{:S(2)}) %collective-permute-start.14) | collective-permute-done | bytes 159776 | tf_op jit(solution)/shard_map/ppermute | solution.py:25
  158.8 9.2 %collective-permute-done.13 = f32[312,128]{1,0:T(8,128)S(1)} collective-permute-done((f32[312,128]{1,0:T(8,128)S(1)}, f32[312,128]{1,0:T(8,128)S(1)}, u32[]{:S(2)}, u32[]{:S(2)}) %collective-permute-start.13) | collective-permute-done | bytes 159776 | tf_op jit(solution)/shard_map/ppermute | solution.py:25
  169.5 1.4 convolution_add_fusion.8
  (150 shorter events, 19.6 us)
Async XLA Ops:
  0.6 96.7 %copy-start = (bf16[256,4096]{1,0:T(8,128)(2,1)S(1)}, bf16[256,4096]{1,0:T(8,128)(2,1)}, u32[]{:S(2)}) copy-start(bf16[256,4096]{1,0:T(8,128)(2,1)} %param.25) | copy-start | bytes 6291460
  0.6 58.1 %copy-start.23 = (f32[153]{0:T(256)S(1)}, f32[153]{0:T(256)}, u32[]{:S(2)}) copy-start(f32[153]{0:T(256)} %constant.63) | copy-start | bytes 1840
  0.7 59.2 %copy-start.5 = (bf16[128,512]{1,0:T(8,128)(2,1)S(1)}, bf16[128,512]{1,0:T(8,128)(2,1)}, u32[]{:S(2)}) copy-start(bf16[128,512]{1,0:T(8,128)(2,1)} %param.26) | copy-start | bytes 393220
  4.2 26.5 %copy-start.15 = (bf16[304,128]{1,0:T(8,128)(2,1)}, bf16[304,128]{1,0:T(8,128)(2,1)S(1)}, u32[]{:S(2)}) copy-start(bf16[304,128]{1,0:T(8,128)(2,1)S(1)} %concatenate.35.refs_3_) | copy-start | bytes 233476
  4.2 21.8 %collective-permute-start = (bf16[304,128]{1,0:T(8,128)(2,1)S(1)}, bf16[304,128]{1,0:T(8,128)(2,1)S(1)}, u32[]{:S(2)}, u32[]{:S(2)}) collective-permute-start(bf16[304,128]{1,0:T(8,128)(2,1)S(1)} %concatenate.35.refs_3_), channel_id=1, source_target_pairs={{0,8},{8,16},{16,24},{24,32},{32,40},{40,48},{48,56},{56,64},{64,7... | collective-permute-start | bytes 233480 | tf_op jit(solution)/shard_map/ppermute | solution.py:25
  8.5 17.7 %collective-permute-start.4 = (bf16[304,128]{1,0:T(8,128)(2,1)S(1)}, bf16[304,128]{1,0:T(8,128)(2,1)S(1)}, u32[]{:S(2)}, u32[]{:S(2)}) collective-permute-start(bf16[304,128]{1,0:T(8,128)(2,1)S(1)} %concatenate.35.refs_3_), channel_id=1, source_target_pairs={{0,24},{8,32},{16,40},{24,48},{32,56},{40,64},{48,72},{56,80},{64,... | collective-permute-start | bytes 233480 | tf_op jit(solution)/shard_map/ppermute | solution.py:25
  17.6 13.1 %collective-permute-start.5 = (bf16[304,128]{1,0:T(8,128)(2,1)S(1)}, bf16[304,128]{1,0:T(8,128)(2,1)S(1)}, u32[]{:S(2)}, u32[]{:S(2)}) collective-permute-start(bf16[304,128]{1,0:T(8,128)(2,1)S(1)} %concatenate.35.refs_3_), channel_id=1, source_target_pairs={{0,16},{8,24},{16,32},{24,40},{32,48},{40,56},{48,64},{56,72},{64,... | collective-permute-start | bytes 233480 | tf_op jit(solution)/shard_map/ppermute | solution.py:25
  23.7 36.1 %collective-permute-start.1 = (bf16[1,128,512]{2,1,0:T(8,128)(2,1)}, bf16[1,128,512]{2,1,0:T(8,128)(2,1)S(1)}, u32[]{:S(2)}, u32[]{:S(2)}) collective-permute-start(bf16[1,128,512]{2,1,0:T(8,128)(2,1)} %bitcast.171), channel_id=1, source_target_pairs={{0,1},{1,2},{2,3},{3,4},{4,5},{5,6},{6,7},{7,0},{8,9},{9,10},{10,1... | collective-permute-start | bytes 393224 | tf_op jit(solution)/shard_map/ppermute | solution.py:34
  25.8 27.8 %copy-start.26 = (f32[32]{0:T(128)}, f32[32]{0:T(128)S(1)}, u32[]{:S(2)}) copy-start(f32[32]{0:T(128)S(1)} %get-tuple-element.32) | copy-start | bytes 388
  25.8 27.8 %copy-start.28 = (f32[32]{0:T(128)}, f32[32]{0:T(128)S(1)}, u32[]{:S(2)}) copy-start(f32[32]{0:T(128)S(1)} %get-tuple-element.33) | copy-start | bytes 388
  25.9 45.2 %copy-start.24 = (f32[32]{0:T(128)}, f32[32]{0:T(128)S(1)}, u32[]{:S(2)}) copy-start(f32[32]{0:T(128)S(1)} %get-tuple-element.31) | copy-start | bytes 388
  25.9 33.9 %copy-start.18 = (f32[128,128]{0,1:T(8,128)}, f32[128,128]{0,1:T(8,128)S(1)}, u32[]{:S(2)}) copy-start(f32[128,128]{0,1:T(8,128)S(1)} %fusion.31) | copy-start | bytes 196612
  26.0 4.7 %copy-start.20 = (bf16[304,128]{1,0:T(8,128)(2,1)}, bf16[304,128]{1,0:T(8,128)(2,1)S(1)}, u32[]{:S(2)}) copy-start(bf16[304,128]{1,0:T(8,128)(2,1)S(1)} %collective-permute-done.refs_2_) | copy-start | bytes 233476
  26.2 4.5 %copy-start.21 = (bf16[304,128]{1,0:T(8,128)(2,1)}, bf16[304,128]{1,0:T(8,128)(2,1)S(1)}, u32[]{:S(2)}) copy-start(bf16[304,128]{1,0:T(8,128)(2,1)S(1)} %collective-permute-done.4.refs_0_) | copy-start | bytes 233476
  34.9 28.1 %collective-permute-start.8 = (f32[312,128]{1,0:T(8,128)}, f32[312,128]{1,0:T(8,128)S(1)}, u32[]{:S(2)}, u32[]{:S(2)}) collective-permute-start(f32[312,128]{1,0:T(8,128)} %shard_map.211), channel_id=1, source_target_pairs={{0,72},{8,80},{16,88},{24,96},{32,104},{40,112},{48,120},{56,128},... | collective-permute-start | bytes 479240 | tf_op jit(solution)/shard_map/ppermute | solution.py:25
  41.7 21.3 %collective-permute-start.9 = (f32[312,128]{1,0:T(8,128)}, f32[312,128]{1,0:T(8,128)}, u32[]{:S(2)}, u32[]{:S(2)}) collective-permute-start(f32[312,128]{1,0:T(8,128)} %shard_map.211), channel_id=1, source_target_pairs={{0,104},{8,112},{16,120},{24,128},{32,136},{40,144},{48,152},{56,1... | collective-permute-start | bytes 479240 | tf_op jit(solution)/shard_map/ppermute | solution.py:25
  44.0 25.4 %collective-permute-start.7 = (f32[312,128]{1,0:T(8,128)}, f32[312,128]{1,0:T(8,128)}, u32[]{:S(2)}, u32[]{:S(2)}) collective-permute-start(f32[312,128]{1,0:T(8,128)} %shard_map.211), channel_id=1, source_target_pairs={{0,40},{8,48},{16,56},{24,64},{32,72},{40,80},{48,88},{56,96},{64,... | collective-permute-start | bytes 479240 | tf_op jit(solution)/shard_map/ppermute | solution.py:25
  46.0 26.0 %collective-permute-start.6 = (f32[312,128]{1,0:T(8,128)}, f32[312,128]{1,0:T(8,128)}, u32[]{:S(2)}, u32[]{:S(2)}) collective-permute-start(f32[312,128]{1,0:T(8,128)} %shard_map.211), channel_id=1, source_target_pairs={{0,8},{8,16},{16,24},{24,32},{32,40},{40,48},{48,56},{56,64},{64,7... | collective-permute-start | bytes 479240 | tf_op jit(solution)/shard_map/ppermute | solution.py:25
  54.7 20.0 %copy-start.3 = (f32[2,128,153]{1,2,0:T(8,128)}, f32[2,128,153]{1,2,0:T(8,128)S(1)}, u32[]{:S(2)}) copy-start(f32[2,128,153]{1,2,0:T(8,128)S(1)} %convolution_add_fusion.5) | copy-start | bytes 470020
  56.9 17.8 %copy-start.1 = (f32[2,128,153]{1,2,0:T(8,128)}, f32[2,128,153]{1,2,0:T(8,128)S(1)}, u32[]{:S(2)}) copy-start(f32[2,128,153]{1,2,0:T(8,128)S(1)} %convolution_add_fusion.4) | copy-start | bytes 470020
  60.6 13.3 %collective-permute-start.2 = (bf16[2,128,512]{2,1,0:T(8,128)(2,1)}, bf16[2,128,512]{2,1,0:T(8,128)(2,1)S(1)}, u32[]{:S(2)}, u32[]{:S(2)}) collective-permute-start(bf16[2,128,512]{2,1,0:T(8,128)(2,1)} %pad_maximum_fusion.2), channel_id=1, source_target_pairs={{0,2},{1,3},{2,4},{3,5},{4,6},{5,7},{6,0},{7,1},{8,10},{9,11},{10,... | collective-permute-start | bytes 786440 | tf_op jit(solution)/shard_map/ppermute | solution.py:34
  73.7 5.1 %copy-start.8 = (f32[312,128]{1,0:T(8,128)}, f32[312,128]{1,0:T(8,128)S(1)}, u32[]{:S(2)}) copy-start(f32[312,128]{1,0:T(8,128)S(1)} %add_select_fusion.6) | copy-start | bytes 479236
  74.7 15.6 %collective-permute-start.3 = (bf16[4,128,512]{2,1,0:T(8,128)(2,1)}, bf16[4,128,512]{2,1,0:T(8,128)(2,1)}, u32[]{:S(2)}, u32[]{:S(2)}) collective-permute-start(bf16[4,128,512]{2,1,0:T(8,128)(2,1)} %pad_maximum_fusion.1), channel_id=1, source_target_pairs={{0,4},{1,5},{2,6},{3,7},{4,0},{5,1},{6,2},{7,3},{8,12},{9,13},{10,... | collective-permute-start | bytes 1572872 | tf_op jit(solution)/shard_map/ppermute | solution.py:34
  79.7 10.6 %copy-start.7 = (f32[2,153,128]{2,1,0:T(8,128)}, f32[2,153,128]{2,1,0:T(8,128)S(1)}, u32[]{:S(2)}) copy-start(f32[2,153,128]{2,1,0:T(8,128)S(1)} %reshape.162) | copy-start | bytes 470020
  97.3 0.8 copy-start.9
  97.3 0.9 copy-start.12
  97.3 1.0 copy-start.14
  97.4 1.0 copy-start.30
  97.4 1.4 copy-start.32
  98.1 3.7 %copy-start.2 = (f32[2,128,153]{1,2,0:T(8,128)S(1)}, f32[2,128,153]{1,2,0:T(8,128)}, u32[]{:S(2)}) copy-start(f32[2,128,153]{1,2,0:T(8,128)} %copy-done.1) | copy-start | bytes 470020
  98.1 4.0 %copy-start.6 = (f32[2,128,153]{1,2,0:T(8,128)S(1)}, f32[2,128,153]{1,2,0:T(8,128)}, u32[]{:S(2)}) copy-start(f32[2,128,153]{1,2,0:T(8,128)} %get-tuple-element.43) | copy-start | bytes 470020
  98.1 4.0 %copy-start.17 = (f32[153,16,1]{0,1,2:T(8,128)S(1)}, f32[153,16,1]{0,1,2:T(8,128)}, u32[]{:S(2)}) copy-start(f32[153,16,1]{0,1,2:T(8,128)} %constant.65) | copy-start | bytes 29380
  98.1 4.2 %copy-start.4 = (f32[2,128,153]{1,2,0:T(8,128)S(1)}, f32[2,128,153]{1,2,0:T(8,128)}, u32[]{:S(2)}) copy-start(f32[2,128,153]{1,2,0:T(8,128)} %copy-done.3) | copy-start | bytes 470020
  98.1 4.2 %copy-start.16 = (f32[153,16,1]{0,1,2:T(8,128)S(1)}, f32[153,16,1]{0,1,2:T(8,128)}, u32[]{:S(2)}) copy-start(f32[153,16,1]{0,1,2:T(8,128)} %constant.64) | copy-start | bytes 29380
  100.5 2.1 %copy-start.13 = (f32[2,128,128]{1,2,0:T(8,128)}, f32[2,128,128]{1,2,0:T(8,128)S(1)}, u32[]{:S(2)}) copy-start(f32[2,128,128]{1,2,0:T(8,128)S(1)} %fusion.7) | copy-start | bytes 393220
  100.5 37.4 %copy-start.11 = (f32[128,2,128]{0,2,1:T(8,128)S(1)}, f32[128,2,128]{0,2,1:T(8,128)}, u32[]{:S(2)}) copy-start(f32[128,2,128]{0,2,1:T(8,128)} %copy-done.10) | copy-start | bytes 393220
  100.5 37.4 %copy-start.33 = (f32[2,128]{1,0:T(2,128)S(1)}, f32[2,128]{1,0:T(2,128)}, u32[]{:S(2)}) copy-start(f32[2,128]{1,0:T(2,128)} %get-tuple-element.14) | copy-start | bytes 3076
  102.9 65.9 %copy-start.31 = (s32[128]{0:T(128)S(1)}, s32[128]{0:T(128)}, u32[]{:S(2)}) copy-start(s32[128]{0:T(128)} %param.23) | copy-start | bytes 1540
  102.9 13.3 %collective-permute-start.11 = (f32[312,128]{1,0:T(8,128)S(1)}, f32[312,128]{1,0:T(8,128)S(1)}, u32[]{:S(2)}, u32[]{:S(2)}) collective-permute-start(f32[312,128]{1,0:T(8,128)S(1)} %concatenate.43), channel_id=1, source_target_pairs={{16,0},{24,8},{32,16},{40,24},{48,32},{56,40},{64,48},{72,56},{80,... | collective-permute-start | bytes 479240 | tf_op jit(solution)/shard_map/ppermute | solution.py:25
  106.2 17.6 %collective-permute-start.12 = (f32[312,128]{1,0:T(8,128)S(1)}, f32[312,128]{1,0:T(8,128)S(1)}, u32[]{:S(2)}, u32[]{:S(2)}) collective-permute-start(f32[312,128]{1,0:T(8,128)S(1)} %concatenate.43), channel_id=1, source_target_pairs={{24,0},{32,8},{40,16},{48,24},{56,32},{64,40},{72,48},{80,56},{88,... | collective-permute-start | bytes 479240 | tf_op jit(solution)/shard_map/ppermute | solution.py:25
  112.8 13.4 %collective-permute-start.10 = (f32[312,128]{1,0:T(8,128)S(1)}, f32[312,128]{1,0:T(8,128)S(1)}, u32[]{:S(2)}, u32[]{:S(2)}) collective-permute-start(f32[312,128]{1,0:T(8,128)S(1)} %concatenate.43), channel_id=1, source_target_pairs={{8,0},{16,8},{24,16},{32,24},{40,32},{48,40},{56,48},{64,56},{72,6... | collective-permute-start | bytes 479240 | tf_op jit(solution)/shard_map/ppermute | solution.py:25
  126.5 24.3 %collective-permute-start.15 = (f32[312,128]{1,0:T(8,128)S(1)}, f32[312,128]{1,0:T(8,128)S(1)}, u32[]{:S(2)}, u32[]{:S(2)}) collective-permute-start(f32[312,128]{1,0:T(8,128)S(1)} %add_select_fusion.3), channel_id=1, source_target_pairs={{72,0},{80,8},{88,16},{96,24},{104,32},{112,40},{120,48},{128,56},... | collective-permute-start | bytes 479240 | tf_op jit(solution)/shard_map/ppermute | solution.py:25
  131.8 19.0 %collective-permute-start.16 = (f32[312,128]{1,0:T(8,128)S(1)}, f32[312,128]{1,0:T(8,128)S(1)}, u32[]{:S(2)}, u32[]{:S(2)}) collective-permute-start(f32[312,128]{1,0:T(8,128)S(1)} %add_select_fusion.3), channel_id=1, source_target_pairs={{104,0},{112,8},{120,16},{128,24},{136,32},{144,40},{152,48},{160,... | collective-permute-start | bytes 479240 | tf_op jit(solution)/shard_map/ppermute | solution.py:25
  139.8 33.3 %copy-start.25 = (f32[32]{0:T(128)S(1)}, f32[32]{0:T(128)}, u32[]{:S(2)}) copy-start(f32[32]{0:T(128)} %copy-done.24) | copy-start | bytes 388
  139.8 33.3 %copy-start.27 = (f32[32]{0:T(128)S(1)}, f32[32]{0:T(128)}, u32[]{:S(2)}) copy-start(f32[32]{0:T(128)} %copy-done.26) | copy-start | bytes 388
  139.8 33.3 %copy-start.29 = (f32[32]{0:T(128)S(1)}, f32[32]{0:T(128)}, u32[]{:S(2)}) copy-start(f32[32]{0:T(128)} %copy-done.28) | copy-start | bytes 388
  139.8 18.9 %collective-permute-start.14 = (f32[312,128]{1,0:T(8,128)S(1)}, f32[312,128]{1,0:T(8,128)S(1)}, u32[]{:S(2)}, u32[]{:S(2)}) collective-permute-start(f32[312,128]{1,0:T(8,128)S(1)} %add_select_fusion.3), channel_id=1, source_target_pairs={{40,0},{48,8},{56,16},{64,24},{72,32},{80,40},{88,48},{96,56},{104... | collective-permute-start | bytes 479240 | tf_op jit(solution)/shard_map/ppermute | solution.py:25
  148.8 19.1 %collective-permute-start.13 = (f32[312,128]{1,0:T(8,128)S(1)}, f32[312,128]{1,0:T(8,128)S(1)}, u32[]{:S(2)}, u32[]{:S(2)}) collective-permute-start(f32[312,128]{1,0:T(8,128)S(1)} %add_select_fusion.3), channel_id=1, source_target_pairs={{8,0},{16,8},{24,16},{32,24},{40,32},{48,40},{56,48},{64,56},{72,6... | collective-permute-start | bytes 479240 | tf_op jit(solution)/shard_map/ppermute | solution.py:25
  (3 other events, 2.0 us)

commit v11 on v9

--- a/solution.py
+++ b/solution.py
@@ -42,8 +42,13 @@
 
 
 def entering(shard, axis, combine, reverse, reach):
-    near, far = window_steps(reach, lax.axis_size(axis))
-    total = fold(combine, [shifted(shard, axis, step, reverse) for step in near] + [shard])
+    size = lax.axis_size(axis)
+    near, far = window_steps(reach, size)
+    total = shard
+    step = 1
+    while step <= len(near):
+        total = combine(shifted(total, axis, step, reverse), total)
+        step *= 2
     return fold(combine, [shifted(total, axis, step, reverse) for step in far])
 
 

time: 166 us -> 160 us (0.964)
  the two profiles are of different devices: /device:TPU:54 before, /device:TPU:44 now
where the time goes in v11:
time: 160 us; the launch traced here: 159 us
  starting transfers between devices  64.4 us (40%)
  waiting for transfers between devices  40.8 us (25%)
  matrix products  16.7 us (10%)
  between operations  14.6 us (9%)
  other arithmetic  11.5 us (7%)
  local copies, waits for them, and re-layouts  7.1 us (4%)
  Pallas kernels  3.5 us (2%)
    ppermute x13, starting transfers between devices, shifted(): return lax.ppermute(piece, axis, pairs)  64.4 us
    ppermute x13, waiting for transfers between devices, shifted(): return lax.ppermute(piece, axis, pairs)  40.8 us
    pallas_call x1, Pallas kernels, window_state(): pl.pallas_call(kernel, out_shape=jax.ShapeDtypeStruct((out_rows, head_wid...  3.5 us
  transfers between devices with their start and end apart: 14, of which 9 were waited for; matrix products, arithmetic and copies ran while one was open for 11% of the time, Pallas kernels for 2%

profile of v11, /device:TPU:44, one launch (start us, length us, event | category | flops | bytes accessed | tf_op | source)
XLA Modules:
  0.0 158.6 jit_solution(13051390132644038206)
XLA Ops:
  7.2 0.8 add_convert_fusion
  8.0 0.8 slice.161
  8.9 1.0 copy.36
  9.9 0.9 concatenate.21.refs_3_
  10.8 6.1 %collective-permute-start.2 = (bf16[304,128]{1,0:T(8,128)(2,1)S(1)}, bf16[304,128]{1,0:T(8,128)(2,1)S(1)}, u32[]{:S(2)}, u32[]{:S(2)}) collective-permute-start(bf16[304,128]{1,0:T(8,128)(2,1)S(1)} %concatenate.21.refs_3_), channel_id=1, source_target_pairs={{0,16},{8,24},{16,32},{24,40},{32,48},{40,56},{48,64},{56,72},{64,... | collective-permute-start | bytes 233480 | tf_op jit(solution)/shard_map/ppermute | solution.py:25
  16.9 9.1 %collective-permute-start.1 = (bf16[304,128]{1,0:T(8,128)(2,1)S(1)}, bf16[304,128]{1,0:T(8,128)(2,1)S(1)}, u32[]{:S(2)}, u32[]{:S(2)}) collective-permute-start(bf16[304,128]{1,0:T(8,128)(2,1)S(1)} %concatenate.21.refs_3_), channel_id=1, source_target_pairs={{0,24},{8,32},{16,40},{24,48},{32,56},{40,64},{48,72},{56,80},{64,... | collective-permute-start | bytes 233480 | tf_op jit(solution)/shard_map/ppermute | solution.py:25
  26.0 4.3 %collective-permute-start = (bf16[304,128]{1,0:T(8,128)(2,1)S(1)}, bf16[304,128]{1,0:T(8,128)(2,1)S(1)}, u32[]{:S(2)}, u32[]{:S(2)}) collective-permute-start(bf16[304,128]{1,0:T(8,128)(2,1)S(1)} %concatenate.21.refs_3_), channel_id=1, source_target_pairs={{0,8},{8,16},{16,24},{24,32},{32,40},{40,48},{48,56},{56,64},{64,7... | collective-permute-start | bytes 233480 | tf_op jit(solution)/shard_map/ppermute | solution.py:25
  30.3 0.7 convert_element_type.57
  32.5 3.1 %collective-permute-done.refs_2_ = bf16[304,128]{1,0:T(8,128)(2,1)S(1)} collective-permute-done((bf16[304,128]{1,0:T(8,128)(2,1)S(1)}, bf16[304,128]{1,0:T(8,128)(2,1)S(1)}, u32[]{:S(2)}, u32[]{:S(2)}) %collective-permute-start) | collective-permute-done | bytes 77856 | tf_op jit(solution)/shard_map/ppermute | solution.py:25
  36.3 1.3 collective-permute-done.1.refs_0_
  38.2 3.5 %shard_map.211 = f32[312,128]{1,0:T(8,128)} custom-call(bf16[304,128]{1,0:T(8,128)(2,1)} %copy-done.8, bf16[304,128]{1,0:T(8,128)(2,1)} %copy-done.7, bf16[304,128]{1,0:T(8,128)(2,1)} %copy-done.6, bf16[304,128]{1,0:T(8,128)(2,1)} %copy-done.3, bf16[306,32]{1,0:T(8,128)(2,1)} %constant.32.clone.refs_4_, bf16[306,32]{1,0:T(8,128)(2,1)} %constant.33.clone.refs_5_, ...), custom_call_target="tpu_custom_call" | custom-call | tf_op jit(solution)/shard_map/pallas_call | solution.py:169
  41.7 2.4 %collective-permute-start.6 = (f32[312,128]{1,0:T(8,128)}, f32[312,128]{1,0:T(8,128)S(1)}, u32[]{:S(2)}, u32[]{:S(2)}) collective-permute-start(f32[312,128]{1,0:T(8,128)} %shard_map.211), channel_id=1, source_target_pairs={{0,104},{8,112},{16,120},{24,128},{32,136},{40,144},{48,152},{56,1... | collective-permute-start | bytes 479240 | tf_op jit(solution)/shard_map/ppermute | solution.py:25
  44.1 5.4 %collective-permute-start.5 = (f32[312,128]{1,0:T(8,128)}, f32[312,128]{1,0:T(8,128)}, u32[]{:S(2)}, u32[]{:S(2)}) collective-permute-start(f32[312,128]{1,0:T(8,128)} %shard_map.211), channel_id=1, source_target_pairs={{0,72},{8,80},{16,88},{24,96},{32,104},{40,112},{48,120},{56,128},... | collective-permute-start | bytes 479240 | tf_op jit(solution)/shard_map/ppermute | solution.py:25
  49.5 4.0 %collective-permute-start.4 = (f32[312,128]{1,0:T(8,128)}, f32[312,128]{1,0:T(8,128)S(1)}, u32[]{:S(2)}, u32[]{:S(2)}) collective-permute-start(f32[312,128]{1,0:T(8,128)} %shard_map.211), channel_id=1, source_target_pairs={{0,40},{8,48},{16,56},{24,64},{32,72},{40,80},{48,88},{56,96},{64,... | collective-permute-start | bytes 479240 | tf_op jit(solution)/shard_map/ppermute | solution.py:25
  53.5 5.0 %collective-permute-start.3 = (f32[312,128]{1,0:T(8,128)}, f32[312,128]{1,0:T(8,128)}, u32[]{:S(2)}, u32[]{:S(2)}) collective-permute-start(f32[312,128]{1,0:T(8,128)} %shard_map.211), channel_id=1, source_target_pairs={{0,8},{8,16},{16,24},{24,32},{32,40},{40,48},{48,56},{56,64},{64,7... | collective-permute-start | bytes 479240 | tf_op jit(solution)/shard_map/ppermute | solution.py:25
  58.6 0.7 fusion.58
  59.4 1.4 compare_convert_fusion.5
  60.8 1.1 convolution_add_fusion.3
  62.0 1.1 convolution_add_fusion.5
  63.0 1.1 convolution_add_fusion.4
  64.1 1.1 multiply_multiply_fusion.1
  66.4 1.0 add_select_fusion.7
  67.4 7.7 %collective-permute-done.4 = f32[312,128]{1,0:T(8,128)S(1)} collective-permute-done((f32[312,128]{1,0:T(8,128)}, f32[312,128]{1,0:T(8,128)S(1)}, u32[]{:S(2)}, u32[]{:S(2)}) %collective-permute-start.4) | collective-permute-done | bytes 159776 | tf_op jit(solution)/shard_map/ppermute | solution.py:25
  75.2 1.9 %collective-permute-done.3 = f32[312,128]{1,0:T(8,128)} collective-permute-done((f32[312,128]{1,0:T(8,128)}, f32[312,128]{1,0:T(8,128)}, u32[]{:S(2)}, u32[]{:S(2)}) %collective-permute-start.3) | collective-permute-done | bytes 159776 | tf_op jit(solution)/shard_map/ppermute | solution.py:25
  77.9 1.0 add_select_fusion.5
  79.8 1.1 fusion.8
  80.9 2.0 %fusion.63 = f32[128,256]{0,1:T(8,128)S(1)} fusion(bf16[128,4096]{1,0:T(8,128)(2,1)} %all-gather.2.cloned.1.call-done, bf16[256,4096]{1,0:T(8,128)(2,1)S(1)} %copy-done), kind=kOutput, calls=%fused_computation.140 | convolution fusion | flops 268435456 | bytes 3276800 | tf_op jit(solution)/shard_map/transpose(jvp())/reshape | solution.py:311
  83.2 0.9 fusion.22
  84.2 0.9 convolution_add_fusion.2
  85.4 0.9 fusion.7
  86.4 1.2 fusion.4
  88.1 0.9 reshape.162
  89.2 2.1 %collective-permute-start.7 = (f32[312,128]{1,0:T(8,128)S(1)}, f32[312,128]{1,0:T(8,128)S(1)}, u32[]{:S(2)}, u32[]{:S(2)}) collective-permute-start(f32[312,128]{1,0:T(8,128)S(1)} %concatenate.25), channel_id=1, source_target_pairs={{8,0},{16,8},{24,16},{32,24},{40,32},{48,40},{56,48},{64,56},{72,6... | collective-permute-start | bytes 479240 | tf_op jit(solution)/shard_map/ppermute | solution.py:25
  91.4 5.8 %collective-permute-done.7 = f32[312,128]{1,0:T(8,128)S(1)} collective-permute-done((f32[312,128]{1,0:T(8,128)S(1)}, f32[312,128]{1,0:T(8,128)S(1)}, u32[]{:S(2)}, u32[]{:S(2)}) %collective-permute-start.7) | collective-permute-done | bytes 159776 | tf_op jit(solution)/shard_map/ppermute | solution.py:25
  97.3 4.9 %collective-permute-start.8 = (f32[312,128]{1,0:T(8,128)S(1)}, f32[312,128]{1,0:T(8,128)S(1)}, u32[]{:S(2)}, u32[]{:S(2)}) collective-permute-start(f32[312,128]{1,0:T(8,128)S(1)} %add_select_fusion.4), channel_id=1, source_target_pairs={{16,0},{24,8},{32,16},{40,24},{48,32},{56,40},{64,48},{72,56},{80,... | collective-permute-start | bytes 479240 | tf_op jit(solution)/shard_map/ppermute | solution.py:25
  102.5 5.3 %collective-permute-done.8 = f32[312,128]{1,0:T(8,128)S(1)} collective-permute-done((f32[312,128]{1,0:T(8,128)S(1)}, f32[312,128]{1,0:T(8,128)S(1)}, u32[]{:S(2)}, u32[]{:S(2)}) %collective-permute-start.8) | collective-permute-done | bytes 159776 | tf_op jit(solution)/shard_map/ppermute | solution.py:25
  107.9 9.4 %collective-permute-start.12 = (f32[312,128]{1,0:T(8,128)S(1)}, f32[312,128]{1,0:T(8,128)S(1)}, u32[]{:S(2)}, u32[]{:S(2)}) collective-permute-start(f32[312,128]{1,0:T(8,128)S(1)} %add_select_fusion.3), channel_id=1, source_target_pairs={{104,0},{112,8},{120,16},{128,24},{136,32},{144,40},{152,48},{160,... | collective-permute-start | bytes 479240 | tf_op jit(solution)/shard_map/ppermute | solution.py:25
  117.3 1.9 %collective-permute-start.11 = (f32[312,128]{1,0:T(8,128)S(1)}, f32[312,128]{1,0:T(8,128)S(1)}, u32[]{:S(2)}, u32[]{:S(2)}) collective-permute-start(f32[312,128]{1,0:T(8,128)S(1)} %add_select_fusion.3), channel_id=1, source_target_pairs={{72,0},{80,8},{88,16},{96,24},{104,32},{112,40},{120,48},{128,56},... | collective-permute-start | bytes 479240 | tf_op jit(solution)/shard_map/ppermute | solution.py:25
  119.3 0.9 fusion.19
  120.2 7.8 %collective-permute-start.10 = (f32[312,128]{1,0:T(8,128)S(1)}, f32[312,128]{1,0:T(8,128)S(1)}, u32[]{:S(2)}, u32[]{:S(2)}) collective-permute-start(f32[312,128]{1,0:T(8,128)S(1)} %add_select_fusion.3), channel_id=1, source_target_pairs={{40,0},{48,8},{56,16},{64,24},{72,32},{80,40},{88,48},{96,56},{104... | collective-permute-start | bytes 479240 | tf_op jit(solution)/shard_map/ppermute | solution.py:25
  128.0 1.9 %collective-permute-start.9 = (f32[312,128]{1,0:T(8,128)S(1)}, f32[312,128]{1,0:T(8,128)S(1)}, u32[]{:S(2)}, u32[]{:S(2)}) collective-permute-start(f32[312,128]{1,0:T(8,128)S(1)} %add_select_fusion.3), channel_id=1, source_target_pairs={{8,0},{16,8},{24,16},{32,24},{40,32},{48,40},{56,48},{64,56},{72,6... | collective-permute-start | bytes 479240 | tf_op jit(solution)/shard_map/ppermute | solution.py:25
  130.0 1.2 collective-permute-done.11
  131.3 14.3 %collective-permute-done.10 = f32[312,128]{1,0:T(8,128)S(1)} collective-permute-done((f32[312,128]{1,0:T(8,128)S(1)}, f32[312,128]{1,0:T(8,128)S(1)}, u32[]{:S(2)}, u32[]{:S(2)}) %collective-permute-start.10) | collective-permute-done | bytes 159776 | tf_op jit(solution)/shard_map/ppermute | solution.py:25
  147.0 0.7 compare_convert_fusion.2
  147.7 1.4 convolution_add_fusion.8
  149.5 0.8 fusion.10
  150.3 0.8 copy.48
  151.1 0.7 fusion.42
  (94 shorter events, 9.9 us)
Async XLA Ops:
  7.2 73.8 %copy-start = (bf16[256,4096]{1,0:T(8,128)(2,1)S(1)}, bf16[256,4096]{1,0:T(8,128)(2,1)}, u32[]{:S(2)}) copy-start(bf16[256,4096]{1,0:T(8,128)(2,1)} %param.25) | copy-start | bytes 6291460
  7.2 58.0 %copy-start.9 = (f32[153]{0:T(256)S(1)}, f32[153]{0:T(256)}, u32[]{:S(2)}) copy-start(f32[153]{0:T(256)} %constant.53) | copy-start | bytes 1840
  7.2 73.7 %all-gather.2.cloned.1.call-start = ((), (), s32[]{:S(2)}) async-start(), calls=%async_computation | async-start | bytes 1179648 | tf_op jit(solution)/shard_map/all_gather | solution.py:255
  10.8 26.8 %copy-start.3 = (bf16[304,128]{1,0:T(8,128)(2,1)}, bf16[304,128]{1,0:T(8,128)(2,1)S(1)}, u32[]{:S(2)}) copy-start(bf16[304,128]{1,0:T(8,128)(2,1)S(1)} %concatenate.21.refs_3_) | copy-start | bytes 233476
  10.8 25.5 %collective-permute-start.2 = (bf16[304,128]{1,0:T(8,128)(2,1)S(1)}, bf16[304,128]{1,0:T(8,128)(2,1)S(1)}, u32[]{:S(2)}, u32[]{:S(2)}) collective-permute-start(bf16[304,128]{1,0:T(8,128)(2,1)S(1)} %concatenate.21.refs_3_), channel_id=1, source_target_pairs={{0,16},{8,24},{16,32},{24,40},{32,48},{40,56},{48,64},{56,72},{64,... | collective-permute-start | bytes 233480 | tf_op jit(solution)/shard_map/ppermute | solution.py:25
  16.9 20.6 %collective-permute-start.1 = (bf16[304,128]{1,0:T(8,128)(2,1)S(1)}, bf16[304,128]{1,0:T(8,128)(2,1)S(1)}, u32[]{:S(2)}, u32[]{:S(2)}) collective-permute-start(bf16[304,128]{1,0:T(8,128)(2,1)S(1)} %concatenate.21.refs_3_), channel_id=1, source_target_pairs={{0,24},{8,32},{16,40},{24,48},{32,56},{40,64},{48,72},{56,80},{64,... | collective-permute-start | bytes 233480 | tf_op jit(solution)/shard_map/ppermute | solution.py:25
  26.0 9.6 %collective-permute-start = (bf16[304,128]{1,0:T(8,128)(2,1)S(1)}, bf16[304,128]{1,0:T(8,128)(2,1)S(1)}, u32[]{:S(2)}, u32[]{:S(2)}) collective-permute-start(bf16[304,128]{1,0:T(8,128)(2,1)S(1)} %concatenate.21.refs_3_), channel_id=1, source_target_pairs={{0,8},{8,16},{16,24},{24,32},{32,40},{40,48},{48,56},{56,64},{64,7... | collective-permute-start | bytes 233480 | tf_op jit(solution)/shard_map/ppermute | solution.py:25
  35.6 1.9 %copy-start.6 = (bf16[304,128]{1,0:T(8,128)(2,1)}, bf16[304,128]{1,0:T(8,128)(2,1)S(1)}, u32[]{:S(2)}) copy-start(bf16[304,128]{1,0:T(8,128)(2,1)S(1)} %collective-permute-done.refs_2_) | copy-start | bytes 233476
  36.3 1.3 copy-start.7
  37.5 0.6 copy-start.8
  41.7 24.1 %collective-permute-start.6 = (f32[312,128]{1,0:T(8,128)}, f32[312,128]{1,0:T(8,128)S(1)}, u32[]{:S(2)}, u32[]{:S(2)}) collective-permute-start(f32[312,128]{1,0:T(8,128)} %shard_map.211), channel_id=1, source_target_pairs={{0,104},{8,112},{16,120},{24,128},{32,136},{40,144},{48,152},{56,1... | collective-permute-start | bytes 479240 | tf_op jit(solution)/shard_map/ppermute | solution.py:25
  44.1 21.6 %collective-permute-start.5 = (f32[312,128]{1,0:T(8,128)}, f32[312,128]{1,0:T(8,128)}, u32[]{:S(2)}, u32[]{:S(2)}) collective-permute-start(f32[312,128]{1,0:T(8,128)} %shard_map.211), channel_id=1, source_target_pairs={{0,72},{8,80},{16,88},{24,96},{32,104},{40,112},{48,120},{56,128},... | collective-permute-start | bytes 479240 | tf_op jit(solution)/shard_map/ppermute | solution.py:25
  49.5 25.6 %collective-permute-start.4 = (f32[312,128]{1,0:T(8,128)}, f32[312,128]{1,0:T(8,128)S(1)}, u32[]{:S(2)}, u32[]{:S(2)}) collective-permute-start(f32[312,128]{1,0:T(8,128)} %shard_map.211), channel_id=1, source_target_pairs={{0,40},{8,48},{16,56},{24,64},{32,72},{40,80},{48,88},{56,96},{64,... | collective-permute-start | bytes 479240 | tf_op jit(solution)/shard_map/ppermute | solution.py:25
  53.5 23.7 %collective-permute-start.3 = (f32[312,128]{1,0:T(8,128)}, f32[312,128]{1,0:T(8,128)}, u32[]{:S(2)}, u32[]{:S(2)}) collective-permute-start(f32[312,128]{1,0:T(8,128)} %shard_map.211), channel_id=1, source_target_pairs={{0,8},{8,16},{16,24},{24,32},{32,40},{40,48},{48,56},{56,64},{64,7... | collective-permute-start | bytes 479240 | tf_op jit(solution)/shard_map/ppermute | solution.py:25
  79.1 3.9 %copy-start.1 = (bf16[128,256]{1,0:T(8,128)(2,1)S(1)}, bf16[128,256]{1,0:T(8,128)(2,1)}, u32[]{:S(2)}) copy-start(bf16[128,256]{1,0:T(8,128)(2,1)} %param.22) | copy-start | bytes 196612
  80.9 2.0 %copy-start.2 = (f32[128,2,128]{0,2,1:T(8,128)S(1)}, f32[128,2,128]{0,2,1:T(8,128)}, u32[]{:S(2)}) copy-start(f32[128,2,128]{0,2,1:T(8,128)} %fusion.8) | copy-start | bytes 393220
  80.9 2.3 %copy-start.11 = (f32[128,2]{0,1:T(2,128)S(1)}, f32[128,2]{0,1:T(2,128)}, u32[]{:S(2)}) copy-start(f32[128,2]{0,1:T(2,128)} %get-tuple-element.14) | copy-start | bytes 3076
  82.9 4.7 %copy-start.5 = (f32[153,16,1]{0,1,2:T(8,128)S(1)}, f32[153,16,1]{0,1,2:T(8,128)}, u32[]{:S(2)}) copy-start(f32[153,16,1]{0,1,2:T(8,128)} %constant.55) | copy-start | bytes 29380
  82.9 4.9 %copy-start.4 = (f32[153,16,1]{0,1,2:T(8,128)S(1)}, f32[153,16,1]{0,1,2:T(8,128)}, u32[]{:S(2)}) copy-start(f32[153,16,1]{0,1,2:T(8,128)} %constant.54) | copy-start | bytes 29380
  85.4 33.9 %copy-start.12 = (f32[128,2]{0,1:T(2,128)S(1)}, f32[128,2]{0,1:T(2,128)}, u32[]{:S(2)}) copy-start(f32[128,2]{0,1:T(2,128)} %get-tuple-element.14) | copy-start | bytes 3076
  89.1 57.9 %copy-start.10 = (s32[128]{0:T(128)S(1)}, s32[128]{0:T(128)}, u32[]{:S(2)}) copy-start(s32[128]{0:T(128)} %param.23) | copy-start | bytes 1540
  89.2 7.9 %collective-permute-start.7 = (f32[312,128]{1,0:T(8,128)S(1)}, f32[312,128]{1,0:T(8,128)S(1)}, u32[]{:S(2)}, u32[]{:S(2)}) collective-permute-start(f32[312,128]{1,0:T(8,128)S(1)} %concatenate.25), channel_id=1, source_target_pairs={{8,0},{16,8},{24,16},{32,24},{40,32},{48,40},{56,48},{64,56},{72,6... | collective-permute-start | bytes 479240 | tf_op jit(solution)/shard_map/ppermute | solution.py:25
  97.3 10.5 %collective-permute-start.8 = (f32[312,128]{1,0:T(8,128)S(1)}, f32[312,128]{1,0:T(8,128)S(1)}, u32[]{:S(2)}, u32[]{:S(2)}) collective-permute-start(f32[312,128]{1,0:T(8,128)S(1)} %add_select_fusion.4), channel_id=1, source_target_pairs={{16,0},{24,8},{32,16},{40,24},{48,32},{56,40},{64,48},{72,56},{80,... | collective-permute-start | bytes 479240 | tf_op jit(solution)/shard_map/ppermute | solution.py:25
  107.9 22.0 %collective-permute-start.12 = (f32[312,128]{1,0:T(8,128)S(1)}, f32[312,128]{1,0:T(8,128)S(1)}, u32[]{:S(2)}, u32[]{:S(2)}) collective-permute-start(f32[312,128]{1,0:T(8,128)S(1)} %add_select_fusion.3), channel_id=1, source_target_pairs={{104,0},{112,8},{120,16},{128,24},{136,32},{144,40},{152,48},{160,... | collective-permute-start | bytes 479240 | tf_op jit(solution)/shard_map/ppermute | solution.py:25
  117.3 13.8 %collective-permute-start.11 = (f32[312,128]{1,0:T(8,128)S(1)}, f32[312,128]{1,0:T(8,128)S(1)}, u32[]{:S(2)}, u32[]{:S(2)}) collective-permute-start(f32[312,128]{1,0:T(8,128)S(1)} %add_select_fusion.3), channel_id=1, source_target_pairs={{72,0},{80,8},{88,16},{96,24},{104,32},{112,40},{120,48},{128,56},... | collective-permute-start | bytes 479240 | tf_op jit(solution)/shard_map/ppermute | solution.py:25
  120.2 25.4 %collective-permute-start.10 = (f32[312,128]{1,0:T(8,128)S(1)}, f32[312,128]{1,0:T(8,128)S(1)}, u32[]{:S(2)}, u32[]{:S(2)}) collective-permute-start(f32[312,128]{1,0:T(8,128)S(1)} %add_select_fusion.3), channel_id=1, source_target_pairs={{40,0},{48,8},{56,16},{64,24},{72,32},{80,40},{88,48},{96,56},{104... | collective-permute-start | bytes 479240 | tf_op jit(solution)/shard_map/ppermute | solution.py:25
  128.0 18.0 %collective-permute-start.9 = (f32[312,128]{1,0:T(8,128)S(1)}, f32[312,128]{1,0:T(8,128)S(1)}, u32[]{:S(2)}, u32[]{:S(2)}) collective-permute-start(f32[312,128]{1,0:T(8,128)S(1)} %add_select_fusion.3), channel_id=1, source_target_pairs={{8,0},{16,8},{24,16},{32,24},{40,32},{48,40},{56,48},{64,56},{72,6... | collective-permute-start | bytes 479240 | tf_op jit(solution)/shard_map/ppermute | solution.py:25
Sparse Core Ops, SparseCore 0:
  30.4 28.1 all-gather.1

commit v12 on v11

--- a/solution.py
+++ b/solution.py
@@ -41,15 +41,35 @@
     return near, [step for step in far if step < size]
 
 
-def entering(shard, axis, combine, reverse, reach):
+def fold_kernel(key_row, pieces):
+    def kernel(*refs):
+        out_ref = refs[-1]
+        total = refs[0][...]
+        row = lax.broadcasted_iota(jnp.int32, total.shape, 0)
+        for ref in refs[1:-1]:
+            later = ref[...]
+            empty_later = later[key_row : key_row + 1, :] == 0.0
+            same_doc = total[key_row : key_row + 1, :] == later[key_row : key_row + 1, :]
+            addend = jnp.where(same_doc & (row < key_row), total, 0.0)
+            total = jnp.where(empty_later, total, later + addend)
+        out_ref[...] = total
+
+    return pl.pallas_call(
+        kernel,
+        out_shape=jax.ShapeDtypeStruct(pieces[0].shape, pieces[0].dtype),
+        interpret=INTERPRET,
+    )(*pieces)
+
+
+def entering(shard, axis, key_row, reverse, reach):
     size = lax.axis_size(axis)
     near, far = window_steps(reach, size)
     total = shard
     step = 1
     while step <= len(near):
-        total = combine(shifted(total, axis, step, reverse), total)
+        total = fold_kernel(key_row, [shifted(total, axis, step, reverse), total])
         step *= 2
-    return fold(combine, [shifted(total, axis, step, reverse) for step in far])
+    return fold_kernel(key_row, [shifted(total, axis, step, reverse) for step in far])
 
 
 def rows_of(flat, lanes):
@@ -280,8 +300,7 @@
     )
     key_late, forward_piece = lax.optimization_barrier((key_heads, forward_piece))
     k_feat, feature_pullback = jax.vjp(features, key_late)
-    join = packed_join(key_row)
-    packed = fold(join, [shifted(forward_piece, "ctx", step, False) for step in far])
+    packed = fold_kernel(key_row, [shifted(forward_piece, "ctx", step, False) for step in far])
     state_in, normer_in, _ = unpack(packed, state_shape, normer_shape, 1)
     previous = raw_unpack(received[-1], values.shape[1], row_count, 2 * row_count)
     before = (
@@ -318,7 +337,7 @@
         doc_ids[0],
         jnp.concatenate([doc_ids[:2], grad_qconv[:, :2].reshape(-1)]),
     )
-    packed = entering(backward_piece, "ctx", packed_join(key_row), True, reach)
+    packed = entering(backward_piece, "ctx", key_row, True, reach)
     state_out, normer_out, edge = unpack(packed, grad_state.shape, grad_normer.shape, 2 + 2 * row_count)
     after = (edge[:2], edge[2:].reshape(row_count, 2), state_out, normer_out)
     head_mask = (doc_ids == after[0][0]).astype(jnp.float32)

time: 160 us -> 166 us (1.038)
  the two profiles are of different devices: /device:TPU:44 before, /device:TPU:39 now
where the time goes in v12:
time: 166 us; the launch traced here: 165 us
  starting transfers between devices  53.5 us (32%)
  waiting for transfers between devices  47.4 us (29%)
  matrix products  17.5 us (11%)
  local copies, waits for them, and re-layouts  14.8 us (9%)
  between operations  14.6 us (9%)
  Pallas kernels  10.6 us (6%)
  other arithmetic  6.75 us (4%)
    ppermute x13, starting transfers between devices, shifted(): return lax.ppermute(piece, axis, pairs)  53.5 us
    ppermute x13, waiting for transfers between devices, shifted(): return lax.ppermute(piece, axis, pairs)  47.3 us
    pallas_call x4, Pallas kernels, fold_kernel(): pl.pallas_call(kernel, out_shape=jax.ShapeDtypeStruct(pieces[0].shape, pi...  7.06 us
    unnamed x58, local copies, waits for them, and re-layouts  4.32 us
    pallas_call x1, Pallas kernels, window_state(): pl.pallas_call(kernel, out_shape=jax.ShapeDtypeStruct((out_rows, head_wid...  3.51 us
  transfers between devices with their start and end apart: 14, of which 9 were waited for; matrix products, arithmetic and copies ran while one was open for 10% of the time, Pallas kernels for 3%

profile of v12, /device:TPU:39, one launch (start us, length us, event | category | flops | bytes accessed | tf_op | source)
XLA Modules:
  0.0 165.2 jit_solution(5964819543592607424)
XLA Ops:
  8.9 1.0 copy.36
  9.9 0.9 concatenate.21.refs_3_
  10.8 5.8 %collective-permute-start.2 = (bf16[304,128]{1,0:T(8,128)(2,1)S(1)}, bf16[304,128]{1,0:T(8,128)(2,1)S(1)}, u32[]{:S(2)}, u32[]{:S(2)}) collective-permute-start(bf16[304,128]{1,0:T(8,128)(2,1)S(1)} %concatenate.21.refs_3_), channel_id=1, source_target_pairs={{0,16},{8,24},{16,32},{24,40},{32,48},{40,56},{48,64},{56,72},{64,... | collective-permute-start | bytes 233480 | tf_op jit(solution)/shard_map/ppermute | solution.py:25
  16.6 8.8 %collective-permute-start.1 = (bf16[304,128]{1,0:T(8,128)(2,1)S(1)}, bf16[304,128]{1,0:T(8,128)(2,1)S(1)}, u32[]{:S(2)}, u32[]{:S(2)}) collective-permute-start(bf16[304,128]{1,0:T(8,128)(2,1)S(1)} %concatenate.21.refs_3_), channel_id=1, source_target_pairs={{0,24},{8,32},{16,40},{24,48},{32,56},{40,64},{48,72},{56,80},{64,... | collective-permute-start | bytes 233480 | tf_op jit(solution)/shard_map/ppermute | solution.py:25
  25.4 4.0 %collective-permute-start = (bf16[304,128]{1,0:T(8,128)(2,1)S(1)}, bf16[304,128]{1,0:T(8,128)(2,1)S(1)}, u32[]{:S(2)}, u32[]{:S(2)}) collective-permute-start(bf16[304,128]{1,0:T(8,128)(2,1)S(1)} %concatenate.21.refs_3_), channel_id=1, source_target_pairs={{0,8},{8,16},{16,24},{24,32},{32,40},{40,48},{48,56},{56,64},{64,7... | collective-permute-start | bytes 233480 | tf_op jit(solution)/shard_map/ppermute | solution.py:25
  31.7 2.5 %collective-permute-done.refs_2_ = bf16[304,128]{1,0:T(8,128)(2,1)S(1)} collective-permute-done((bf16[304,128]{1,0:T(8,128)(2,1)S(1)}, bf16[304,128]{1,0:T(8,128)(2,1)S(1)}, u32[]{:S(2)}, u32[]{:S(2)}) %collective-permute-start) | collective-permute-done | bytes 77856 | tf_op jit(solution)/shard_map/ppermute | solution.py:25
  34.9 1.5 collective-permute-done.1.refs_0_
  37.0 3.5 %shard_map.211 = f32[312,128]{1,0:T(8,128)} custom-call(bf16[304,128]{1,0:T(8,128)(2,1)} %copy-done.18, bf16[304,128]{1,0:T(8,128)(2,1)} %copy-done.17, bf16[304,128]{1,0:T(8,128)(2,1)} %copy-done.16, bf16[304,128]{1,0:T(8,128)(2,1)} %copy-done.6, bf16[306,32]{1,0:T(8,128)(2,1)} %constant.30.clone.refs_4_, bf16[306,32]{1,0:T(8,128)(2,1)} %constant.31.clone.refs_5_, ...), custom_call_target="tpu_custom_call" | custom-call | tf_op jit(solution)/shard_map/pallas_call | solution.py:189
  40.5 2.7 %collective-permute-start.6 = (f32[312,128]{1,0:T(8,128)}, f32[312,128]{1,0:T(8,128)S(1)}, u32[]{:S(2)}, u32[]{:S(2)}) collective-permute-start(f32[312,128]{1,0:T(8,128)} %shard_map.211), channel_id=1, source_target_pairs={{0,8},{8,16},{16,24},{24,32},{32,40},{40,48},{48,56},{56,64},{64,7... | collective-permute-start | bytes 479240 | tf_op jit(solution)/shard_map/ppermute | solution.py:25
  43.3 6.4 %collective-permute-start.5 = (f32[312,128]{1,0:T(8,128)}, f32[312,128]{1,0:T(8,128)S(1)}, u32[]{:S(2)}, u32[]{:S(2)}) collective-permute-start(f32[312,128]{1,0:T(8,128)} %shard_map.211), channel_id=1, source_target_pairs={{0,40},{8,48},{16,56},{24,64},{32,72},{40,80},{48,88},{56,96},{64,... | collective-permute-start | bytes 479240 | tf_op jit(solution)/shard_map/ppermute | solution.py:25
  49.7 3.2 %collective-permute-start.4 = (f32[312,128]{1,0:T(8,128)}, f32[312,128]{1,0:T(8,128)}, u32[]{:S(2)}, u32[]{:S(2)}) collective-permute-start(f32[312,128]{1,0:T(8,128)} %shard_map.211), channel_id=1, source_target_pairs={{0,72},{8,80},{16,88},{24,96},{32,104},{40,112},{48,120},{56,128},... | collective-permute-start | bytes 479240 | tf_op jit(solution)/shard_map/ppermute | solution.py:25
  52.8 4.3 %collective-permute-start.3 = (f32[312,128]{1,0:T(8,128)}, f32[312,128]{1,0:T(8,128)}, u32[]{:S(2)}, u32[]{:S(2)}) collective-permute-start(f32[312,128]{1,0:T(8,128)} %shard_map.211), channel_id=1, source_target_pairs={{0,104},{8,112},{16,120},{24,128},{32,136},{40,144},{48,152},{56,1... | collective-permute-start | bytes 479240 | tf_op jit(solution)/shard_map/ppermute | solution.py:25
  58.1 1.4 compare_convert_fusion.5
  59.4 1.1 convolution_add_fusion.2
  60.6 1.1 convolution_add_fusion.4
  61.7 1.1 convolution_add_fusion.3
  62.8 1.1 multiply_multiply_fusion.1
  64.4 7.2 %collective-permute-done.5.refs_2_ = f32[312,128]{1,0:T(8,128)S(1)} collective-permute-done((f32[312,128]{1,0:T(8,128)}, f32[312,128]{1,0:T(8,128)S(1)}, u32[]{:S(2)}, u32[]{:S(2)}) %collective-permute-start.5) | collective-permute-done | bytes 159776 | tf_op jit(solution)/shard_map/ppermute | solution.py:25
  71.6 5.2 %collective-permute-done.3.refs_0_ = f32[312,128]{1,0:T(8,128)} collective-permute-done((f32[312,128]{1,0:T(8,128)}, f32[312,128]{1,0:T(8,128)}, u32[]{:S(2)}, u32[]{:S(2)}) %collective-permute-start.3) | collective-permute-done | bytes 159776 | tf_op jit(solution)/shard_map/ppermute | solution.py:25
  76.8 1.9 %shard_map.212 = f32[312,128]{1,0:T(8,128)} custom-call(f32[312,128]{1,0:T(8,128)} %collective-permute-done.3.refs_0_, f32[312,128]{1,0:T(8,128)} %collective-permute-done.4.refs_1_, f32[312,128]{1,0:T(8,128)} %copy-done.10, f32[312,128]{1,0:T(8,128)} %copy-done.9), custom_call_target="tpu_custom_call" | custom-call | tf_op jit(solution)/shard_map/pallas_call | solution.py:57
  80.1 1.0 reshape.160
  81.2 1.1 fusion.9
  82.4 2.0 %fusion.65 = f32[128,256]{0,1:T(8,128)S(1)} fusion(bf16[128,4096]{1,0:T(8,128)(2,1)} %all-gather.2.cloned.1.call-done, bf16[256,4096]{1,0:T(8,128)(2,1)S(1)} %copy-done), kind=kOutput, calls=%fused_computation.117 | convolution fusion | flops 268435456 | bytes 3276800 | tf_op jit(solution)/shard_map/transpose(jvp())/reshape | solution.py:330
  85.6 0.9 fusion.23
  86.5 0.8 fusion.8
  87.4 0.9 reshape.162
  88.3 1.2 fusion.63
  89.5 0.9 fusion.5
  91.2 1.9 %collective-permute-start.7 = (f32[312,128]{1,0:T(8,128)S(1)}, f32[312,128]{1,0:T(8,128)S(1)}, u32[]{:S(2)}, u32[]{:S(2)}) collective-permute-start(f32[312,128]{1,0:T(8,128)S(1)} %concatenate.25.refs_1_), channel_id=1, source_target_pairs={{8,0},{16,8},{24,16},{32,24},{40,32},{48,40},{56,48},{64,56},{72,6... | collective-permute-start | bytes 479240 | tf_op jit(solution)/shard_map/ppermute | solution.py:25
  93.1 4.7 %collective-permute-done.7.refs_0_ = f32[312,128]{1,0:T(8,128)S(1)} collective-permute-done((f32[312,128]{1,0:T(8,128)S(1)}, f32[312,128]{1,0:T(8,128)S(1)}, u32[]{:S(2)}, u32[]{:S(2)}) %collective-permute-start.7) | collective-permute-done | bytes 159776 | tf_op jit(solution)/shard_map/ppermute | solution.py:25
  98.4 1.7 %shard_map.213.refs_1_ = f32[312,128]{1,0:T(8,128)} custom-call(f32[312,128]{1,0:T(8,128)} %copy-done.15, f32[312,128]{1,0:T(8,128)} %copy-done.1), custom_call_target="tpu_custom_call" | custom-call | tf_op jit(solution)/shard_map/pallas_call | solution.py:57
  100.1 1.9 %collective-permute-start.8 = (f32[312,128]{1,0:T(8,128)}, f32[312,128]{1,0:T(8,128)S(1)}, u32[]{:S(2)}, u32[]{:S(2)}) collective-permute-start(f32[312,128]{1,0:T(8,128)} %shard_map.213.refs_1_), channel_id=1, source_target_pairs={{16,0},{24,8},{32,16},{40,24},{48,32},{56,40},{64,48},{72,56},{80,... | collective-permute-start | bytes 479240 | tf_op jit(solution)/shard_map/ppermute | solution.py:25
  102.0 1.2 fusion.68
  103.2 7.5 %collective-permute-done.8.refs_0_ = f32[312,128]{1,0:T(8,128)S(1)} collective-permute-done((f32[312,128]{1,0:T(8,128)}, f32[312,128]{1,0:T(8,128)S(1)}, u32[]{:S(2)}, u32[]{:S(2)}) %collective-permute-start.8) | collective-permute-done | bytes 159776 | tf_op jit(solution)/shard_map/ppermute | solution.py:25
  111.4 1.7 %shard_map.214 = f32[312,128]{1,0:T(8,128)} custom-call(f32[312,128]{1,0:T(8,128)} %copy-done.14, f32[312,128]{1,0:T(8,128)} %shard_map.213.refs_1_), custom_call_target="tpu_custom_call" | custom-call | tf_op jit(solution)/shard_map/pallas_call | solution.py:57
  113.1 8.6 %collective-permute-start.12 = (f32[312,128]{1,0:T(8,128)}, f32[312,128]{1,0:T(8,128)S(1)}, u32[]{:S(2)}, u32[]{:S(2)}) collective-permute-start(f32[312,128]{1,0:T(8,128)} %shard_map.214), channel_id=1, source_target_pairs={{8,0},{16,8},{24,16},{32,24},{40,32},{48,40},{56,48},{64,56},{72,6... | collective-permute-start | bytes 479240 | tf_op jit(solution)/shard_map/ppermute | solution.py:25
  121.7 1.9 %collective-permute-start.11 = (f32[312,128]{1,0:T(8,128)}, f32[312,128]{1,0:T(8,128)S(1)}, u32[]{:S(2)}, u32[]{:S(2)}) collective-permute-start(f32[312,128]{1,0:T(8,128)} %shard_map.214), channel_id=1, source_target_pairs={{40,0},{48,8},{56,16},{64,24},{72,32},{80,40},{88,48},{96,56},{104... | collective-permute-start | bytes 479240 | tf_op jit(solution)/shard_map/ppermute | solution.py:25
  123.7 1.9 %collective-permute-start.10 = (f32[312,128]{1,0:T(8,128)}, f32[312,128]{1,0:T(8,128)S(1)}, u32[]{:S(2)}, u32[]{:S(2)}) collective-permute-start(f32[312,128]{1,0:T(8,128)} %shard_map.214), channel_id=1, source_target_pairs={{72,0},{80,8},{88,16},{96,24},{104,32},{112,40},{120,48},{128,56},... | collective-permute-start | bytes 479240 | tf_op jit(solution)/shard_map/ppermute | solution.py:25
  125.6 1.9 %collective-permute-start.9 = (f32[312,128]{1,0:T(8,128)}, f32[312,128]{1,0:T(8,128)}, u32[]{:S(2)}, u32[]{:S(2)}) collective-permute-start(f32[312,128]{1,0:T(8,128)} %shard_map.214), channel_id=1, source_target_pairs={{104,0},{112,8},{120,16},{128,24},{136,32},{144,40},{152,48},{160,... | collective-permute-start | bytes 479240 | tf_op jit(solution)/shard_map/ppermute | solution.py:25
  127.5 0.9 fusion.20
  128.5 8.7 %collective-permute-done.12.refs_3_ = f32[312,128]{1,0:T(8,128)S(1)} collective-permute-done((f32[312,128]{1,0:T(8,128)}, f32[312,128]{1,0:T(8,128)S(1)}, u32[]{:S(2)}, u32[]{:S(2)}) %collective-permute-start.12) | collective-permute-done | bytes 159776 | tf_op jit(solution)/shard_map/ppermute | solution.py:25
  137.2 6.6 %collective-permute-done.11.refs_2_ = f32[312,128]{1,0:T(8,128)S(1)} collective-permute-done((f32[312,128]{1,0:T(8,128)}, f32[312,128]{1,0:T(8,128)S(1)}, u32[]{:S(2)}, u32[]{:S(2)}) %collective-permute-start.11) | collective-permute-done | bytes 159776 | tf_op jit(solution)/shard_map/ppermute | solution.py:25
  143.8 3.4 %collective-permute-done.9.refs_0_ = f32[312,128]{1,0:T(8,128)} collective-permute-done((f32[312,128]{1,0:T(8,128)}, f32[312,128]{1,0:T(8,128)}, u32[]{:S(2)}, u32[]{:S(2)}) %collective-permute-start.9) | collective-permute-done | bytes 159776 | tf_op jit(solution)/shard_map/ppermute | solution.py:25
  147.2 1.9 %shard_map.215 = f32[312,128]{1,0:T(8,128)} custom-call(f32[312,128]{1,0:T(8,128)} %collective-permute-done.9.refs_0_, f32[312,128]{1,0:T(8,128)} %copy-done.13, f32[312,128]{1,0:T(8,128)} %copy-done.12, f32[312,128]{1,0:T(8,128)} %copy-done.11), custom_call_target="tpu_custom_call" | custom-call | tf_op jit(solution)/shard_map/pallas_call | solution.py:57
  149.0 1.2 slice.150
  152.5 0.9 reshape.168
  154.2 1.4 convolution_add_fusion.7
  156.0 0.8 fusion.11
  (111 shorter events, 16.4 us)
Async XLA Ops:
  7.2 75.2 %copy-start = (bf16[256,4096]{1,0:T(8,128)(2,1)S(1)}, bf16[256,4096]{1,0:T(8,128)(2,1)}, u32[]{:S(2)}) copy-start(bf16[256,4096]{1,0:T(8,128)(2,1)} %param.25) | copy-start | bytes 6291460
  7.2 56.7 %copy-start.19 = (f32[153]{0:T(256)S(1)}, f32[153]{0:T(256)}, u32[]{:S(2)}) copy-start(f32[153]{0:T(256)} %constant.51) | copy-start | bytes 1840
  7.2 75.2 %all-gather.2.cloned.1.call-start = ((), (), s32[]{:S(2)}) async-start(), calls=%async_computation | async-start | bytes 1179648 | tf_op jit(solution)/shard_map/all_gather | solution.py:275
  10.8 25.6 %copy-start.6 = (bf16[304,128]{1,0:T(8,128)(2,1)}, bf16[304,128]{1,0:T(8,128)(2,1)S(1)}, u32[]{:S(2)}) copy-start(bf16[304,128]{1,0:T(8,128)(2,1)S(1)} %concatenate.21.refs_3_) | copy-start | bytes 233476
  10.8 24.1 %collective-permute-start.2 = (bf16[304,128]{1,0:T(8,128)(2,1)S(1)}, bf16[304,128]{1,0:T(8,128)(2,1)S(1)}, u32[]{:S(2)}, u32[]{:S(2)}) collective-permute-start(bf16[304,128]{1,0:T(8,128)(2,1)S(1)} %concatenate.21.refs_3_), channel_id=1, source_target_pairs={{0,16},{8,24},{16,32},{24,40},{32,48},{40,56},{48,64},{56,72},{64,... | collective-permute-start | bytes 233480 | tf_op jit(solution)/shard_map/ppermute | solution.py:25
  16.6 19.8 %collective-permute-start.1 = (bf16[304,128]{1,0:T(8,128)(2,1)S(1)}, bf16[304,128]{1,0:T(8,128)(2,1)S(1)}, u32[]{:S(2)}, u32[]{:S(2)}) collective-permute-start(bf16[304,128]{1,0:T(8,128)(2,1)S(1)} %concatenate.21.refs_3_), channel_id=1, source_target_pairs={{0,24},{8,32},{16,40},{24,48},{32,56},{40,64},{48,72},{56,80},{64,... | collective-permute-start | bytes 233480 | tf_op jit(solution)/shard_map/ppermute | solution.py:25
  25.4 8.8 %collective-permute-start = (bf16[304,128]{1,0:T(8,128)(2,1)S(1)}, bf16[304,128]{1,0:T(8,128)(2,1)S(1)}, u32[]{:S(2)}, u32[]{:S(2)}) collective-permute-start(bf16[304,128]{1,0:T(8,128)(2,1)S(1)} %concatenate.21.refs_3_), channel_id=1, source_target_pairs={{0,8},{8,16},{16,24},{24,32},{32,40},{40,48},{48,56},{56,64},{64,7... | collective-permute-start | bytes 233480 | tf_op jit(solution)/shard_map/ppermute | solution.py:25
  30.3 52.1 %copy-start.20 = (f32[32]{0:T(128)}, f32[32]{0:T(128)S(1)}, u32[]{:S(2)}) copy-start(f32[32]{0:T(128)S(1)} %get-tuple-element.16) | copy-start | bytes 388
  30.3 52.1 %copy-start.22 = (f32[32]{0:T(128)}, f32[32]{0:T(128)S(1)}, u32[]{:S(2)}) copy-start(f32[32]{0:T(128)S(1)} %get-tuple-element.17) | copy-start | bytes 388
  34.2 2.2 %copy-start.16 = (bf16[304,128]{1,0:T(8,128)(2,1)}, bf16[304,128]{1,0:T(8,128)(2,1)S(1)}, u32[]{:S(2)}) copy-start(bf16[304,128]{1,0:T(8,128)(2,1)S(1)} %collective-permute-done.refs_2_) | copy-start | bytes 233476
  34.9 1.5 copy-start.17
  36.4 0.6 copy-start.18
  40.5 23.9 %collective-permute-start.6 = (f32[312,128]{1,0:T(8,128)}, f32[312,128]{1,0:T(8,128)S(1)}, u32[]{:S(2)}, u32[]{:S(2)}) collective-permute-start(f32[312,128]{1,0:T(8,128)} %shard_map.211), channel_id=1, source_target_pairs={{0,8},{8,16},{16,24},{24,32},{32,40},{40,48},{48,56},{56,64},{64,7... | collective-permute-start | bytes 479240 | tf_op jit(solution)/shard_map/ppermute | solution.py:25
  43.3 28.3 %collective-permute-start.5 = (f32[312,128]{1,0:T(8,128)}, f32[312,128]{1,0:T(8,128)S(1)}, u32[]{:S(2)}, u32[]{:S(2)}) collective-permute-start(f32[312,128]{1,0:T(8,128)} %shard_map.211), channel_id=1, source_target_pairs={{0,40},{8,48},{16,56},{24,64},{32,72},{40,80},{48,88},{56,96},{64,... | collective-permute-start | bytes 479240 | tf_op jit(solution)/shard_map/ppermute | solution.py:25
  49.7 21.9 %collective-permute-start.4 = (f32[312,128]{1,0:T(8,128)}, f32[312,128]{1,0:T(8,128)}, u32[]{:S(2)}, u32[]{:S(2)}) collective-permute-start(f32[312,128]{1,0:T(8,128)} %shard_map.211), channel_id=1, source_target_pairs={{0,72},{8,80},{16,88},{24,96},{32,104},{40,112},{48,120},{56,128},... | collective-permute-start | bytes 479240 | tf_op jit(solution)/shard_map/ppermute | solution.py:25
  52.8 24.0 %collective-permute-start.3 = (f32[312,128]{1,0:T(8,128)}, f32[312,128]{1,0:T(8,128)}, u32[]{:S(2)}, u32[]{:S(2)}) collective-permute-start(f32[312,128]{1,0:T(8,128)} %shard_map.211), channel_id=1, source_target_pairs={{0,104},{8,112},{16,120},{24,128},{32,136},{40,144},{48,152},{56,1... | collective-permute-start | bytes 479240 | tf_op jit(solution)/shard_map/ppermute | solution.py:25
  64.4 20.0 %copy-start.3 = (f32[2,128,128]{1,2,0:T(8,128)}, f32[2,128,128]{1,2,0:T(8,128)S(1)}, u32[]{:S(2)}) copy-start(f32[2,128,128]{1,2,0:T(8,128)S(1)} %get-tuple-element.29) | copy-start | bytes 393220
  64.4 12.4 %copy-start.9 = (f32[312,128]{1,0:T(8,128)}, f32[312,128]{1,0:T(8,128)S(1)}, u32[]{:S(2)}) copy-start(f32[312,128]{1,0:T(8,128)S(1)} %collective-permute-done.6.refs_3_) | copy-start | bytes 479236
  71.6 5.2 %copy-start.10 = (f32[312,128]{1,0:T(8,128)}, f32[312,128]{1,0:T(8,128)S(1)}, u32[]{:S(2)}) copy-start(f32[312,128]{1,0:T(8,128)S(1)} %collective-permute-done.5.refs_2_) | copy-start | bytes 479236
  80.1 4.3 %copy-start.2 = (bf16[128,256]{1,0:T(8,128)(2,1)S(1)}, bf16[128,256]{1,0:T(8,128)(2,1)}, u32[]{:S(2)}) copy-start(bf16[128,256]{1,0:T(8,128)(2,1)} %param.22) | copy-start | bytes 196612
  81.2 5.3 %copy-start.26 = (f32[128,2]{0,1:T(2,128)}, f32[128,2]{0,1:T(2,128)S(1)}, u32[]{:S(2)}) copy-start(f32[128,2]{0,1:T(2,128)S(1)} %get-tuple-element.14) | copy-start | bytes 3076
  82.4 2.0 %copy-start.5 = (f32[128,2,128]{0,2,1:T(8,128)S(1)}, f32[128,2,128]{0,2,1:T(8,128)}, u32[]{:S(2)}) copy-start(f32[128,2,128]{0,2,1:T(8,128)} %fusion.9) | copy-start | bytes 393220
  84.3 6.1 %copy-start.8 = (f32[153,16,1]{0,1,2:T(8,128)S(1)}, f32[153,16,1]{0,1,2:T(8,128)}, u32[]{:S(2)}) copy-start(f32[153,16,1]{0,1,2:T(8,128)} %constant.53) | copy-start | bytes 29380
  84.4 6.3 %copy-start.7 = (f32[153,16,1]{0,1,2:T(8,128)S(1)}, f32[153,16,1]{0,1,2:T(8,128)}, u32[]{:S(2)}) copy-start(f32[153,16,1]{0,1,2:T(8,128)} %constant.52) | copy-start | bytes 29380
  84.7 0.6 copy-start.24
  87.4 40.2 %copy-start.27 = (f32[128,2]{0,1:T(2,128)S(1)}, f32[128,2]{0,1:T(2,128)}, u32[]{:S(2)}) copy-start(f32[128,2]{0,1:T(2,128)} %copy-done.26) | copy-start | bytes 3076
  90.4 37.1 %copy-start.4 = (f32[2,128,128]{1,2,0:T(8,128)S(1)}, f32[2,128,128]{1,2,0:T(8,128)}, u32[]{:S(2)}) copy-start(f32[2,128,128]{1,2,0:T(8,128)} %copy-done.3) | copy-start | bytes 393220
  90.4 63.0 %copy-start.25 = (s32[128]{0:T(128)S(1)}, s32[128]{0:T(128)}, u32[]{:S(2)}) copy-start(s32[128]{0:T(128)} %param.23) | copy-start | bytes 1540
  91.2 6.6 %copy-start.1 = (f32[312,128]{1,0:T(8,128)}, f32[312,128]{1,0:T(8,128)S(1)}, u32[]{:S(2)}) copy-start(f32[312,128]{1,0:T(8,128)S(1)} %concatenate.25.refs_1_) | copy-start | bytes 479236
  91.2 6.6 %collective-permute-start.7 = (f32[312,128]{1,0:T(8,128)S(1)}, f32[312,128]{1,0:T(8,128)S(1)}, u32[]{:S(2)}, u32[]{:S(2)}) collective-permute-start(f32[312,128]{1,0:T(8,128)S(1)} %concatenate.25.refs_1_), channel_id=1, source_target_pairs={{8,0},{16,8},{24,16},{32,24},{40,32},{48,40},{56,48},{64,56},{72,6... | collective-permute-start | bytes 479240 | tf_op jit(solution)/shard_map/ppermute | solution.py:25
  97.8 0.7 copy-start.15
  100.1 10.6 %collective-permute-start.8 = (f32[312,128]{1,0:T(8,128)}, f32[312,128]{1,0:T(8,128)S(1)}, u32[]{:S(2)}, u32[]{:S(2)}) collective-permute-start(f32[312,128]{1,0:T(8,128)} %shard_map.213.refs_1_), channel_id=1, source_target_pairs={{16,0},{24,8},{32,16},{40,24},{48,32},{56,40},{64,48},{72,56},{80,... | collective-permute-start | bytes 479240 | tf_op jit(solution)/shard_map/ppermute | solution.py:25
  103.2 54.4 %copy-start.21 = (f32[32]{0:T(128)S(1)}, f32[32]{0:T(128)}, u32[]{:S(2)}) copy-start(f32[32]{0:T(128)} %copy-done.20) | copy-start | bytes 388
  103.2 54.4 %copy-start.23 = (f32[32]{0:T(128)S(1)}, f32[32]{0:T(128)}, u32[]{:S(2)}) copy-start(f32[32]{0:T(128)} %copy-done.22) | copy-start | bytes 388
  110.8 0.7 copy-start.14
  113.1 24.1 %collective-permute-start.12 = (f32[312,128]{1,0:T(8,128)}, f32[312,128]{1,0:T(8,128)S(1)}, u32[]{:S(2)}, u32[]{:S(2)}) collective-permute-start(f32[312,128]{1,0:T(8,128)} %shard_map.214), channel_id=1, source_target_pairs={{8,0},{16,8},{24,16},{32,24},{40,32},{48,40},{56,48},{64,56},{72,6... | collective-permute-start | bytes 479240 | tf_op jit(solution)/shard_map/ppermute | solution.py:25
  121.7 22.0 %collective-permute-start.11 = (f32[312,128]{1,0:T(8,128)}, f32[312,128]{1,0:T(8,128)S(1)}, u32[]{:S(2)}, u32[]{:S(2)}) collective-permute-start(f32[312,128]{1,0:T(8,128)} %shard_map.214), channel_id=1, source_target_pairs={{40,0},{48,8},{56,16},{64,24},{72,32},{80,40},{88,48},{96,56},{104... | collective-permute-start | bytes 479240 | tf_op jit(solution)/shard_map/ppermute | solution.py:25
  123.7 20.1 %collective-permute-start.10 = (f32[312,128]{1,0:T(8,128)}, f32[312,128]{1,0:T(8,128)S(1)}, u32[]{:S(2)}, u32[]{:S(2)}) collective-permute-start(f32[312,128]{1,0:T(8,128)} %shard_map.214), channel_id=1, source_target_pairs={{72,0},{80,8},{88,16},{96,24},{104,32},{112,40},{120,48},{128,56},... | collective-permute-start | bytes 479240 | tf_op jit(solution)/shard_map/ppermute | solution.py:25
  125.6 21.6 %collective-permute-start.9 = (f32[312,128]{1,0:T(8,128)}, f32[312,128]{1,0:T(8,128)}, u32[]{:S(2)}, u32[]{:S(2)}) collective-permute-start(f32[312,128]{1,0:T(8,128)} %shard_map.214), channel_id=1, source_target_pairs={{104,0},{112,8},{120,16},{128,24},{136,32},{144,40},{152,48},{160,... | collective-permute-start | bytes 479240 | tf_op jit(solution)/shard_map/ppermute | solution.py:25
  137.2 10.0 %copy-start.11 = (f32[312,128]{1,0:T(8,128)}, f32[312,128]{1,0:T(8,128)S(1)}, u32[]{:S(2)}) copy-start(f32[312,128]{1,0:T(8,128)S(1)} %collective-permute-done.12.refs_3_) | copy-start | bytes 479236
  143.8 3.4 %copy-start.12 = (f32[312,128]{1,0:T(8,128)}, f32[312,128]{1,0:T(8,128)S(1)}, u32[]{:S(2)}) copy-start(f32[312,128]{1,0:T(8,128)S(1)} %collective-permute-done.11.refs_2_) | copy-start | bytes 479236
  143.8 3.4 %copy-start.13 = (f32[312,128]{1,0:T(8,128)}, f32[312,128]{1,0:T(8,128)S(1)}, u32[]{:S(2)}) copy-start(f32[312,128]{1,0:T(8,128)S(1)} %collective-permute-done.10.refs_1_) | copy-start | bytes 479236
Sparse Core Ops, SparseCore 0:
  29.6 29.2 all-gather.1

commit v13 on v11

--- a/solution.py
+++ b/solution.py
@@ -251,10 +251,14 @@
     length = queries.shape[1]
     head_width = values.shape[1] // local_heads
     reach = -(-(MOST - 1) // length)
+    head_count = lax.axis_size("head")
+    blocks = lax.all_to_all(
+        jnp.broadcast_to(out_grad[None], (head_count,) + out_grad.shape), "head", 0, 0
+    )
     grad_attn = lax.dot_general(
-        lax.all_gather(out_grad, "head", axis=1, tiled=True),
-        out_weight,
-        (((1,), (1,)), ((), ())),
+        blocks,
+        out_weight.reshape(out_weight.shape[0], head_count, out_grad.shape[1]),
+        (((0, 2), (1, 2)), ((), ())),
         preferred_element_type=jnp.float32,
     )
     doc_ids = (seg_ids + 1).astype(jnp.float32)

time: 160 us -> 146 us (0.912)
  the two profiles are of different devices: /device:TPU:44 before, /device:TPU:40 now
where the time goes in v13:
time: 146 us; the launch traced here: 145 us
  starting transfers between devices  67.5 us (46%)
  waiting for transfers between devices  42.7 us (29%)
  local copies, waits for them, and re-layouts  11.7 us (8%)
  matrix products  10.1 us (7%)
  other arithmetic  8.16 us (6%)
  Pallas kernels  3.5 us (2%)
  between operations  1.46 us (1%)
    ppermute x13, starting transfers between devices, shifted(): return lax.ppermute(piece, axis, pairs)  63.2 us
    ppermute x13, waiting for transfers between devices, shifted(): return lax.ppermute(piece, axis, pairs)  42.7 us
    unnamed x49, local copies, waits for them, and re-layouts  5.93 us
    all_to_all x1, starting transfers between devices, body(): lax.all_to_all(jnp.broadcast_to(out_grad[None], (head_count,) + out_grad....  4.3 us
    pallas_call x1, Pallas kernels, window_state(): pl.pallas_call(kernel, out_shape=jax.ShapeDtypeStruct((out_rows, head_wid...  3.5 us
  transfers between devices with their start and end apart: 14, of which 7 were waited for; matrix products, arithmetic and copies ran while one was open for 9% of the time, Pallas kernels for 2%

profile of v13, /device:TPU:40, one launch (start us, length us, event | category | flops | bytes accessed | tf_op | source)
XLA Modules:
  0.0 145.1 jit_solution(15597545822799430611)
XLA Ops:
  0.7 0.8 add_convert_fusion
  1.5 0.8 slice.161
  2.4 1.0 copy.35
  3.4 0.9 concatenate.21.refs_3_
  4.2 6.1 %collective-permute-start.2 = (bf16[304,128]{1,0:T(8,128)(2,1)S(1)}, bf16[304,128]{1,0:T(8,128)(2,1)S(1)}, u32[]{:S(2)}, u32[]{:S(2)}) collective-permute-start(bf16[304,128]{1,0:T(8,128)(2,1)S(1)} %concatenate.21.refs_3_), channel_id=1, source_target_pairs={{0,16},{8,24},{16,32},{24,40},{32,48},{40,56},{48,64},{56,72},{64,... | collective-permute-start | bytes 233480 | tf_op jit(solution)/shard_map/ppermute | solution.py:25
  10.3 9.1 %collective-permute-start.1 = (bf16[304,128]{1,0:T(8,128)(2,1)S(1)}, bf16[304,128]{1,0:T(8,128)(2,1)S(1)}, u32[]{:S(2)}, u32[]{:S(2)}) collective-permute-start(bf16[304,128]{1,0:T(8,128)(2,1)S(1)} %concatenate.21.refs_3_), channel_id=1, source_target_pairs={{0,24},{8,32},{16,40},{24,48},{32,56},{40,64},{48,72},{56,80},{64,... | collective-permute-start | bytes 233480 | tf_op jit(solution)/shard_map/ppermute | solution.py:25
  19.4 4.3 %collective-permute-start = (bf16[304,128]{1,0:T(8,128)(2,1)S(1)}, bf16[304,128]{1,0:T(8,128)(2,1)S(1)}, u32[]{:S(2)}, u32[]{:S(2)}) collective-permute-start(bf16[304,128]{1,0:T(8,128)(2,1)S(1)} %concatenate.21.refs_3_), channel_id=1, source_target_pairs={{0,8},{8,16},{16,24},{24,32},{32,40},{40,48},{48,56},{56,64},{64,7... | collective-permute-start | bytes 233480 | tf_op jit(solution)/shard_map/ppermute | solution.py:25
  23.7 2.0 %broadcast_in_dim.111 = bf16[8,128,512]{2,1,0:T(8,128)(2,1)} broadcast(bf16[128,512]{1,0:T(8,128)(2,1)} %param.26), dimensions={1,2} | broadcast | bytes 1179648 | tf_op jit(solution)/shard_map/broadcast_in_dim | solution.py:256
  25.7 4.3 %all-to-all-start = ((bf16[8,128,512]{2,1,0:T(8,128)(2,1)}), bf16[8,128,512]{2,1,0:T(8,128)(2,1)}, u32[]{:S(2)}, u32[]{:S(2)}) async-start(bf16[8,128,512]{2,1,0:T(8,128)(2,1)} %broadcast_in_dim.111), calls=%async_computation | async-start | bytes 2097152 | tf_op jit(solution)/shard_map/all_to_all | solution.py:255
  30.3 2.2 %copy.59 = bf16[32,8,8,512]{3,2,1,0:T(8,128)(2,1)} copy(bf16[32,8,8,512]{3,1,2,0:T(8,128)(2,1)S(1)} %bitcast.173) | data formatting | bytes 4194304
  32.6 0.6 slice.171
  33.2 0.6 copy-done.12
  33.8 0.6 copy-done.13
  34.4 3.5 %shard_map.211 = f32[312,128]{1,0:T(8,128)} custom-call(bf16[304,128]{1,0:T(8,128)(2,1)} %copy-done.13, bf16[304,128]{1,0:T(8,128)(2,1)} %copy-done.12, bf16[304,128]{1,0:T(8,128)(2,1)} %copy-done.11, bf16[304,128]{1,0:T(8,128)(2,1)} %copy-done.3, bf16[306,32]{1,0:T(8,128)(2,1)} %constant.32.clone.refs_4_, bf16[306,32]{1,0:T(8,128)(2,1)} %constant.33.clone.refs_5_, ...), custom_call_target="tpu_custom_call" | custom-call | tf_op jit(solution)/shard_map/pallas_call | solution.py:169
  37.9 4.1 %collective-permute-start.6 = (f32[312,128]{1,0:T(8,128)}, f32[312,128]{1,0:T(8,128)}, u32[]{:S(2)}, u32[]{:S(2)}) collective-permute-start(f32[312,128]{1,0:T(8,128)} %shard_map.211), channel_id=1, source_target_pairs={{0,104},{8,112},{16,120},{24,128},{32,136},{40,144},{48,152},{56,1... | collective-permute-start | bytes 479240 | tf_op jit(solution)/shard_map/ppermute | solution.py:25
  42.0 1.9 %collective-permute-start.5 = (f32[312,128]{1,0:T(8,128)}, f32[312,128]{1,0:T(8,128)}, u32[]{:S(2)}, u32[]{:S(2)}) collective-permute-start(f32[312,128]{1,0:T(8,128)} %shard_map.211), channel_id=1, source_target_pairs={{0,72},{8,80},{16,88},{24,96},{32,104},{40,112},{48,120},{56,128},... | collective-permute-start | bytes 479240 | tf_op jit(solution)/shard_map/ppermute | solution.py:25
  44.0 8.9 %collective-permute-start.4 = (f32[312,128]{1,0:T(8,128)}, f32[312,128]{1,0:T(8,128)S(1)}, u32[]{:S(2)}, u32[]{:S(2)}) collective-permute-start(f32[312,128]{1,0:T(8,128)} %shard_map.211), channel_id=1, source_target_pairs={{0,40},{8,48},{16,56},{24,64},{32,72},{40,80},{48,88},{56,96},{64,... | collective-permute-start | bytes 479240 | tf_op jit(solution)/shard_map/ppermute | solution.py:25
  52.8 3.4 %collective-permute-start.3 = (f32[312,128]{1,0:T(8,128)}, f32[312,128]{1,0:T(8,128)S(1)}, u32[]{:S(2)}, u32[]{:S(2)}) collective-permute-start(f32[312,128]{1,0:T(8,128)} %shard_map.211), channel_id=1, source_target_pairs={{0,8},{8,16},{16,24},{24,32},{32,40},{40,48},{48,56},{56,64},{64,7... | collective-permute-start | bytes 479240 | tf_op jit(solution)/shard_map/ppermute | solution.py:25
  56.3 0.7 fusion.56
  57.1 0.7 compare_convert_fusion.5
  59.4 0.5 fusion.61
  59.9 0.7 compare_bitcast_fusion.12
  60.6 1.1 add_select_fusion.7
  61.7 9.6 %collective-permute-done.4 = f32[312,128]{1,0:T(8,128)S(1)} collective-permute-done((f32[312,128]{1,0:T(8,128)}, f32[312,128]{1,0:T(8,128)S(1)}, u32[]{:S(2)}, u32[]{:S(2)}) %collective-permute-start.4) | collective-permute-done | bytes 159776 | tf_op jit(solution)/shard_map/ppermute | solution.py:25
  71.5 3.8 %collective-permute-done.3 = f32[312,128]{1,0:T(8,128)S(1)} collective-permute-done((f32[312,128]{1,0:T(8,128)}, f32[312,128]{1,0:T(8,128)S(1)}, u32[]{:S(2)}, u32[]{:S(2)}) %collective-permute-start.3) | collective-permute-done | bytes 159776 | tf_op jit(solution)/shard_map/ppermute | solution.py:25
  75.3 0.7 copy-done.8
  76.0 1.0 add_select_fusion.5
  77.4 0.6 divide_bitcast_fusion
  78.0 0.4 fusion.10
  78.4 2.5 %fusion = f32[128,2,128,1]{0,2,3,1:T(8,128)S(1)} fusion(bf16[2,128,8,512]{3,2,1,0:T(8,128)(2,1)S(1)} %bitcast.174, bf16[8,128,512]{2,1,0:T(8,128)(2,1)} %all-to-all-done), kind=kOutput, calls=%fused_computation | convolution fusion | flops 268435456 | bytes 3276800 | tf_op jit(solution)/shard_map/dot_general | solution.py:258
  82.2 1.1 fusion.9
  84.3 2.4 %collective-permute-start.7 = (f32[312,128]{1,0:T(8,128)S(1)}, f32[312,128]{1,0:T(8,128)S(1)}, u32[]{:S(2)}, u32[]{:S(2)}) collective-permute-start(f32[312,128]{1,0:T(8,128)S(1)} %concatenate.25), channel_id=1, source_target_pairs={{8,0},{16,8},{24,16},{32,24},{40,32},{48,40},{56,48},{64,56},{72,6... | collective-permute-start | bytes 479240 | tf_op jit(solution)/shard_map/ppermute | solution.py:25
  86.8 5.4 %collective-permute-done.7 = f32[312,128]{1,0:T(8,128)S(1)} collective-permute-done((f32[312,128]{1,0:T(8,128)S(1)}, f32[312,128]{1,0:T(8,128)S(1)}, u32[]{:S(2)}, u32[]{:S(2)}) %collective-permute-start.7) | collective-permute-done | bytes 159776 | tf_op jit(solution)/shard_map/ppermute | solution.py:25
  92.4 2.4 %collective-permute-start.8 = (f32[312,128]{1,0:T(8,128)S(1)}, f32[312,128]{1,0:T(8,128)S(1)}, u32[]{:S(2)}, u32[]{:S(2)}) collective-permute-start(f32[312,128]{1,0:T(8,128)S(1)} %add_select_fusion.4), channel_id=1, source_target_pairs={{16,0},{24,8},{32,16},{40,24},{48,32},{56,40},{64,48},{72,56},{80,... | collective-permute-start | bytes 479240 | tf_op jit(solution)/shard_map/ppermute | solution.py:25
  95.1 6.2 %collective-permute-done.8 = f32[312,128]{1,0:T(8,128)S(1)} collective-permute-done((f32[312,128]{1,0:T(8,128)S(1)}, f32[312,128]{1,0:T(8,128)S(1)}, u32[]{:S(2)}, u32[]{:S(2)}) %collective-permute-start.8) | collective-permute-done | bytes 159776 | tf_op jit(solution)/shard_map/ppermute | solution.py:25
  101.4 11.3 %collective-permute-start.12 = (f32[312,128]{1,0:T(8,128)S(1)}, f32[312,128]{1,0:T(8,128)S(1)}, u32[]{:S(2)}, u32[]{:S(2)}) collective-permute-start(f32[312,128]{1,0:T(8,128)S(1)} %add_select_fusion.3), channel_id=1, source_target_pairs={{104,0},{112,8},{120,16},{128,24},{136,32},{144,40},{152,48},{160,... | collective-permute-start | bytes 479240 | tf_op jit(solution)/shard_map/ppermute | solution.py:25
  112.8 1.9 %collective-permute-start.11 = (f32[312,128]{1,0:T(8,128)S(1)}, f32[312,128]{1,0:T(8,128)S(1)}, u32[]{:S(2)}, u32[]{:S(2)}) collective-permute-start(f32[312,128]{1,0:T(8,128)S(1)} %add_select_fusion.3), channel_id=1, source_target_pairs={{72,0},{80,8},{88,16},{96,24},{104,32},{112,40},{120,48},{128,56},... | collective-permute-start | bytes 479240 | tf_op jit(solution)/shard_map/ppermute | solution.py:25
  115.0 5.2 %collective-permute-start.10 = (f32[312,128]{1,0:T(8,128)S(1)}, f32[312,128]{1,0:T(8,128)S(1)}, u32[]{:S(2)}, u32[]{:S(2)}) collective-permute-start(f32[312,128]{1,0:T(8,128)S(1)} %add_select_fusion.3), channel_id=1, source_target_pairs={{40,0},{48,8},{56,16},{64,24},{72,32},{80,40},{88,48},{96,56},{104... | collective-permute-start | bytes 479240 | tf_op jit(solution)/shard_map/ppermute | solution.py:25
  120.2 2.1 %collective-permute-start.9 = (f32[312,128]{1,0:T(8,128)S(1)}, f32[312,128]{1,0:T(8,128)S(1)}, u32[]{:S(2)}, u32[]{:S(2)}) collective-permute-start(f32[312,128]{1,0:T(8,128)S(1)} %add_select_fusion.3), channel_id=1, source_target_pairs={{8,0},{16,8},{24,16},{32,24},{40,32},{48,40},{56,48},{64,56},{72,6... | collective-permute-start | bytes 479240 | tf_op jit(solution)/shard_map/ppermute | solution.py:25
  122.4 5.6 %collective-permute-done.11 = f32[312,128]{1,0:T(8,128)S(1)} collective-permute-done((f32[312,128]{1,0:T(8,128)S(1)}, f32[312,128]{1,0:T(8,128)S(1)}, u32[]{:S(2)}, u32[]{:S(2)}) %collective-permute-start.11) | collective-permute-done | bytes 159776 | tf_op jit(solution)/shard_map/ppermute | solution.py:25
  128.1 11.5 %collective-permute-done.10 = f32[312,128]{1,0:T(8,128)S(1)} collective-permute-done((f32[312,128]{1,0:T(8,128)S(1)}, f32[312,128]{1,0:T(8,128)S(1)}, u32[]{:S(2)}, u32[]{:S(2)}) %collective-permute-start.10) | collective-permute-done | bytes 159776 | tf_op jit(solution)/shard_map/ppermute | solution.py:25
  139.8 0.5 collective-permute-done.9
  140.4 0.5 slice.232
  141.2 0.7 compare_convert_fusion.2
  141.9 0.5 convolution_add_fusion.8
  142.8 0.8 fusion.12
  143.6 0.8 copy.46
  144.4 0.7 fusion.40
  (115 shorter events, 6.5 us)
Async XLA Ops:
  0.6 29.4 %copy-start.15 = (bf16[32,128]{1,0:T(8,128)(2,1)S(1)}, bf16[32,128]{1,0:T(8,128)(2,1)}, u32[]{:S(2)}) copy-start(bf16[32,128]{1,0:T(8,128)(2,1)} %param.20) | copy-start | bytes 24580
  0.6 29.4 %copy-start.14 = (bf16[32,128]{1,0:T(8,128)(2,1)S(1)}, bf16[32,128]{1,0:T(8,128)(2,1)}, u32[]{:S(2)}) copy-start(bf16[32,128]{1,0:T(8,128)(2,1)} %param.21) | copy-start | bytes 24580
  0.7 29.4 %copy-start.20 = (bf16[3,32]{1,0:T(4,128)(2,1)S(1)}, bf16[3,32]{1,0:T(4,128)(2,1)}, u32[]{:S(2)}) copy-start(bf16[3,32]{1,0:T(4,128)(2,1)} %param.24) | copy-start | bytes 580
  0.7 29.5 %copy-start = (bf16[256,4096]{1,0:T(8,128)(2,1)S(1)}, bf16[256,4096]{1,0:T(8,128)(2,1)}, u32[]{:S(2)}) copy-start(bf16[256,4096]{1,0:T(8,128)(2,1)} %param.25) | copy-start | bytes 6291460
  4.2 28.3 %copy-start.3 = (bf16[304,128]{1,0:T(8,128)(2,1)}, bf16[304,128]{1,0:T(8,128)(2,1)S(1)}, u32[]{:S(2)}) copy-start(bf16[304,128]{1,0:T(8,128)(2,1)S(1)} %concatenate.21.refs_3_) | copy-start | bytes 233476
  4.2 28.9 %collective-permute-start.2 = (bf16[304,128]{1,0:T(8,128)(2,1)S(1)}, bf16[304,128]{1,0:T(8,128)(2,1)S(1)}, u32[]{:S(2)}, u32[]{:S(2)}) collective-permute-start(bf16[304,128]{1,0:T(8,128)(2,1)S(1)} %concatenate.21.refs_3_), channel_id=1, source_target_pairs={{0,16},{8,24},{16,32},{24,40},{32,48},{40,56},{48,64},{56,72},{64,... | collective-permute-start | bytes 233480 | tf_op jit(solution)/shard_map/ppermute | solution.py:25
  10.3 22.9 %collective-permute-start.1 = (bf16[304,128]{1,0:T(8,128)(2,1)S(1)}, bf16[304,128]{1,0:T(8,128)(2,1)S(1)}, u32[]{:S(2)}, u32[]{:S(2)}) collective-permute-start(bf16[304,128]{1,0:T(8,128)(2,1)S(1)} %concatenate.21.refs_3_), channel_id=1, source_target_pairs={{0,24},{8,32},{16,40},{24,48},{32,56},{40,64},{48,72},{56,80},{64,... | collective-permute-start | bytes 233480 | tf_op jit(solution)/shard_map/ppermute | solution.py:25
  19.4 13.1 %collective-permute-start = (bf16[304,128]{1,0:T(8,128)(2,1)S(1)}, bf16[304,128]{1,0:T(8,128)(2,1)S(1)}, u32[]{:S(2)}, u32[]{:S(2)}) collective-permute-start(bf16[304,128]{1,0:T(8,128)(2,1)S(1)} %concatenate.21.refs_3_), channel_id=1, source_target_pairs={{0,8},{8,16},{16,24},{24,32},{32,40},{40,48},{48,56},{56,64},{64,7... | collective-permute-start | bytes 233480 | tf_op jit(solution)/shard_map/ppermute | solution.py:25
  25.7 52.7 %all-to-all-start = ((bf16[8,128,512]{2,1,0:T(8,128)(2,1)}), bf16[8,128,512]{2,1,0:T(8,128)(2,1)}, u32[]{:S(2)}, u32[]{:S(2)}) async-start(bf16[8,128,512]{2,1,0:T(8,128)(2,1)} %broadcast_in_dim.111), calls=%async_computation | async-start | bytes 2097152 | tf_op jit(solution)/shard_map/all_to_all | solution.py:255
  30.2 29.2 %copy-start.6 = (f32[128,128]{0,1:T(8,128)}, f32[128,128]{0,1:T(8,128)S(1)}, u32[]{:S(2)}) copy-start(f32[128,128]{0,1:T(8,128)S(1)} %fusion.32) | copy-start | bytes 196612
  30.2 26.9 %copy-start.19 = (s32[128]{0:T(128)S(1)}, s32[128]{0:T(128)}, u32[]{:S(2)}) copy-start(s32[128]{0:T(128)} %param.23) | copy-start | bytes 1540
  30.2 27.6 %copy-start.5 = (f32[153,16,1]{0,1,2:T(8,128)S(1)}, f32[153,16,1]{0,1,2:T(8,128)}, u32[]{:S(2)}) copy-start(f32[153,16,1]{0,1,2:T(8,128)} %constant.55) | copy-start | bytes 29380
  30.2 27.6 %copy-start.18 = (f32[153]{0:T(256)S(1)}, f32[153]{0:T(256)}, u32[]{:S(2)}) copy-start(f32[153]{0:T(256)} %constant.52) | copy-start | bytes 1840
  30.2 28.4 %copy-start.4 = (f32[153,16,1]{0,1,2:T(8,128)S(1)}, f32[153,16,1]{0,1,2:T(8,128)}, u32[]{:S(2)}) copy-start(f32[153,16,1]{0,1,2:T(8,128)} %constant.54) | copy-start | bytes 29380
  30.2 28.4 %copy-start.17 = (f32[153]{0:T(256)S(1)}, f32[153]{0:T(256)}, u32[]{:S(2)}) copy-start(f32[153]{0:T(256)} %constant.51) | copy-start | bytes 1840
  30.3 28.8 %copy-start.16 = (f32[153]{0:T(256)S(1)}, f32[153]{0:T(256)}, u32[]{:S(2)}) copy-start(f32[153]{0:T(256)} %constant.53) | copy-start | bytes 1840
  32.5 0.7 copy-start.11
  33.2 0.6 copy-start.12
  33.8 0.6 copy-start.13
  37.9 22.0 %collective-permute-start.6 = (f32[312,128]{1,0:T(8,128)}, f32[312,128]{1,0:T(8,128)}, u32[]{:S(2)}, u32[]{:S(2)}) collective-permute-start(f32[312,128]{1,0:T(8,128)} %shard_map.211), channel_id=1, source_target_pairs={{0,104},{8,112},{16,120},{24,128},{32,136},{40,144},{48,152},{56,1... | collective-permute-start | bytes 479240 | tf_op jit(solution)/shard_map/ppermute | solution.py:25
  42.0 17.9 %collective-permute-start.5 = (f32[312,128]{1,0:T(8,128)}, f32[312,128]{1,0:T(8,128)}, u32[]{:S(2)}, u32[]{:S(2)}) collective-permute-start(f32[312,128]{1,0:T(8,128)} %shard_map.211), channel_id=1, source_target_pairs={{0,72},{8,80},{16,88},{24,96},{32,104},{40,112},{48,120},{56,128},... | collective-permute-start | bytes 479240 | tf_op jit(solution)/shard_map/ppermute | solution.py:25
  44.0 27.4 %collective-permute-start.4 = (f32[312,128]{1,0:T(8,128)}, f32[312,128]{1,0:T(8,128)S(1)}, u32[]{:S(2)}, u32[]{:S(2)}) collective-permute-start(f32[312,128]{1,0:T(8,128)} %shard_map.211), channel_id=1, source_target_pairs={{0,40},{8,48},{16,56},{24,64},{32,72},{40,80},{48,88},{56,96},{64,... | collective-permute-start | bytes 479240 | tf_op jit(solution)/shard_map/ppermute | solution.py:25
  52.8 22.5 %collective-permute-start.3 = (f32[312,128]{1,0:T(8,128)}, f32[312,128]{1,0:T(8,128)S(1)}, u32[]{:S(2)}, u32[]{:S(2)}) collective-permute-start(f32[312,128]{1,0:T(8,128)} %shard_map.211), channel_id=1, source_target_pairs={{0,8},{8,16},{16,24},{24,32},{32,40},{40,48},{48,56},{56,64},{64,7... | collective-permute-start | bytes 479240 | tf_op jit(solution)/shard_map/ppermute | solution.py:25
  58.2 20.2 %copy-start.1 = (bf16[32,8,8,512]{3,2,1,0:T(8,128)(2,1)S(1)}, bf16[32,8,8,512]{3,2,1,0:T(8,128)(2,1)}, u32[]{:S(2)}) copy-start(bf16[32,8,8,512]{3,2,1,0:T(8,128)(2,1)} %copy.59) | copy-start | bytes 6291460
  75.3 0.7 copy-start.8
  78.0 3.0 %copy-start.2 = (bf16[128,256]{1,0:T(8,128)(2,1)S(1)}, bf16[128,256]{1,0:T(8,128)(2,1)}, u32[]{:S(2)}) copy-start(bf16[128,256]{1,0:T(8,128)(2,1)} %param.22) | copy-start | bytes 196612
  78.4 2.8 %copy-start.21 = (f32[2,128]{1,0:T(2,128)S(1)}, f32[2,128]{1,0:T(2,128)}, u32[]{:S(2)}) copy-start(f32[2,128]{1,0:T(2,128)} %get-tuple-element.14) | copy-start | bytes 3076
  78.4 3.7 %copy-start.7 = (f32[128,128]{0,1:T(8,128)S(1)}, f32[128,128]{0,1:T(8,128)}, u32[]{:S(2)}) copy-start(f32[128,128]{0,1:T(8,128)} %copy-done.6) | copy-start | bytes 196612
  81.0 0.8 copy-start.9
  82.1 32.5 %copy-start.10 = (f32[128,2,128,1]{0,2,3,1:T(8,128)S(1)}, f32[128,2,128,1]{0,2,3,1:T(8,128)}, u32[]{:S(2)}) copy-start(f32[128,2,128,1]{0,2,3,1:T(8,128)} %copy-done.9) | copy-start | bytes 393220
  82.2 32.5 %copy-start.22 = (f32[2,128]{1,0:T(2,128)S(1)}, f32[2,128]{1,0:T(2,128)}, u32[]{:S(2)}) copy-start(f32[2,128]{1,0:T(2,128)} %get-tuple-element.14) | copy-start | bytes 3076
  84.3 7.9 %collective-permute-start.7 = (f32[312,128]{1,0:T(8,128)S(1)}, f32[312,128]{1,0:T(8,128)S(1)}, u32[]{:S(2)}, u32[]{:S(2)}) collective-permute-start(f32[312,128]{1,0:T(8,128)S(1)} %concatenate.25), channel_id=1, source_target_pairs={{8,0},{16,8},{24,16},{32,24},{40,32},{48,40},{56,48},{64,56},{72,6... | collective-permute-start | bytes 479240 | tf_op jit(solution)/shard_map/ppermute | solution.py:25
  92.4 8.9 %collective-permute-start.8 = (f32[312,128]{1,0:T(8,128)S(1)}, f32[312,128]{1,0:T(8,128)S(1)}, u32[]{:S(2)}, u32[]{:S(2)}) collective-permute-start(f32[312,128]{1,0:T(8,128)S(1)} %add_select_fusion.4), channel_id=1, source_target_pairs={{16,0},{24,8},{32,16},{40,24},{48,32},{56,40},{64,48},{72,56},{80,... | collective-permute-start | bytes 479240 | tf_op jit(solution)/shard_map/ppermute | solution.py:25
  101.4 20.9 %collective-permute-start.12 = (f32[312,128]{1,0:T(8,128)S(1)}, f32[312,128]{1,0:T(8,128)S(1)}, u32[]{:S(2)}, u32[]{:S(2)}) collective-permute-start(f32[312,128]{1,0:T(8,128)S(1)} %add_select_fusion.3), channel_id=1, source_target_pairs={{104,0},{112,8},{120,16},{128,24},{136,32},{144,40},{152,48},{160,... | collective-permute-start | bytes 479240 | tf_op jit(solution)/shard_map/ppermute | solution.py:25
  112.8 15.2 %collective-permute-start.11 = (f32[312,128]{1,0:T(8,128)S(1)}, f32[312,128]{1,0:T(8,128)S(1)}, u32[]{:S(2)}, u32[]{:S(2)}) collective-permute-start(f32[312,128]{1,0:T(8,128)S(1)} %add_select_fusion.3), channel_id=1, source_target_pairs={{72,0},{80,8},{88,16},{96,24},{104,32},{112,40},{120,48},{128,56},... | collective-permute-start | bytes 479240 | tf_op jit(solution)/shard_map/ppermute | solution.py:25
  115.0 24.7 %collective-permute-start.10 = (f32[312,128]{1,0:T(8,128)S(1)}, f32[312,128]{1,0:T(8,128)S(1)}, u32[]{:S(2)}, u32[]{:S(2)}) collective-permute-start(f32[312,128]{1,0:T(8,128)S(1)} %add_select_fusion.3), channel_id=1, source_target_pairs={{40,0},{48,8},{56,16},{64,24},{72,32},{80,40},{88,48},{96,56},{104... | collective-permute-start | bytes 479240 | tf_op jit(solution)/shard_map/ppermute | solution.py:25
  120.2 20.0 %collective-permute-start.9 = (f32[312,128]{1,0:T(8,128)S(1)}, f32[312,128]{1,0:T(8,128)S(1)}, u32[]{:S(2)}, u32[]{:S(2)}) collective-permute-start(f32[312,128]{1,0:T(8,128)S(1)} %add_select_fusion.3), channel_id=1, source_target_pairs={{8,0},{16,8},{24,16},{32,24},{40,32},{48,40},{56,48},{64,56},{72,6... | collective-permute-start | bytes 479240 | tf_op jit(solution)/shard_map/ppermute | solution.py:25

commit v14 on v11

--- a/solution.py
+++ b/solution.py
@@ -251,12 +251,6 @@
     length = queries.shape[1]
     head_width = values.shape[1] // local_heads
     reach = -(-(MOST - 1) // length)
-    grad_attn = lax.dot_general(
-        lax.all_gather(out_grad, "head", axis=1, tiled=True),
-        out_weight,
-        (((1,), (1,)), ((), ())),
-        preferred_element_type=jnp.float32,
-    )
     doc_ids = (seg_ids + 1).astype(jnp.float32)
     query_rows = queries.astype(jnp.float32)
     key_heads = keys.astype(jnp.float32).reshape(local_heads, FD, length)
@@ -278,7 +272,17 @@
         values.shape[1],
         out_rows,
     )
-    key_late, forward_piece = lax.optimization_barrier((key_heads, forward_piece))
+    key_late, grad_late, forward_piece = lax.optimization_barrier((key_heads, out_grad, forward_piece))
+    head_count = lax.axis_size("head")
+    blocks = lax.all_to_all(
+        jnp.broadcast_to(grad_late[None], (head_count,) + grad_late.shape), "head", 0, 0
+    )
+    grad_attn = lax.dot_general(
+        blocks,
+        out_weight.reshape(out_weight.shape[0], head_count, grad_late.shape[1]),
+        (((0, 2), (1, 2)), ((), ())),
+        preferred_element_type=jnp.float32,
+    )
     k_feat, feature_pullback = jax.vjp(features, key_late)
     join = packed_join(key_row)
     packed = fold(join, [shifted(forward_piece, "ctx", step, False) for step in far])

time: 160 us -> 147 us (0.919)
  the two profiles are of different devices: /device:TPU:44 before, /device:TPU:40 now
where the time goes in v14:
time: 147 us; the launch traced here: 146 us
  starting transfers between devices  71.6 us (49%)
  waiting for transfers between devices  37.7 us (26%)
  matrix products  11 us (7%)
  local copies, waits for them, and re-layouts  10.9 us (7%)
  other arithmetic  10.2 us (7%)
  Pallas kernels  3.5 us (2%)
    ppermute x13, starting transfers between devices, shifted(): return lax.ppermute(piece, axis, pairs)  67.3 us
    ppermute x13, waiting for transfers between devices, shifted(): return lax.ppermute(piece, axis, pairs)  36.4 us
    unnamed x37, local copies, waits for them, and re-layouts  6 us
    all_to_all x1, starting transfers between devices, body(): lax.all_to_all(jnp.broadcast_to(grad_late[None], (head_count,) + grad_lat...  4.3 us
    pallas_call x1, Pallas kernels, window_state(): pl.pallas_call(kernel, out_shape=jax.ShapeDtypeStruct((out_rows, head_wid...  3.5 us
  transfers between devices with their start and end apart: 14, of which 8 were waited for; matrix products, arithmetic and copies ran while one was open for 10% of the time, Pallas kernels for 0%

profile of v14, /device:TPU:40, one launch (start us, length us, event | category | flops | bytes accessed | tf_op | source)
XLA Modules:
  0.0 146.2 jit_solution(8541498900115883655)
XLA Ops:
  0.6 0.7 add_convert_fusion
  1.3 0.9 copy.35
  2.2 0.8 slice.161
  3.2 0.9 concatenate.21.refs_3_
  4.0 4.3 %collective-permute-start = (bf16[304,128]{1,0:T(8,128)(2,1)S(1)}, bf16[304,128]{1,0:T(8,128)(2,1)S(1)}, u32[]{:S(2)}, u32[]{:S(2)}) collective-permute-start(bf16[304,128]{1,0:T(8,128)(2,1)S(1)} %concatenate.21.refs_3_), channel_id=1, source_target_pairs={{0,8},{8,16},{16,24},{24,32},{32,40},{40,48},{48,56},{56,64},{64,7... | collective-permute-start | bytes 233480 | tf_op jit(solution)/shard_map/ppermute | solution.py:25
  8.3 9.1 %collective-permute-start.1 = (bf16[304,128]{1,0:T(8,128)(2,1)S(1)}, bf16[304,128]{1,0:T(8,128)(2,1)S(1)}, u32[]{:S(2)}, u32[]{:S(2)}) collective-permute-start(bf16[304,128]{1,0:T(8,128)(2,1)S(1)} %concatenate.21.refs_3_), channel_id=1, source_target_pairs={{0,24},{8,32},{16,40},{24,48},{32,56},{40,64},{48,72},{56,80},{64,... | collective-permute-start | bytes 233480 | tf_op jit(solution)/shard_map/ppermute | solution.py:25
  17.4 6.1 %collective-permute-start.2 = (bf16[304,128]{1,0:T(8,128)(2,1)S(1)}, bf16[304,128]{1,0:T(8,128)(2,1)S(1)}, u32[]{:S(2)}, u32[]{:S(2)}) collective-permute-start(bf16[304,128]{1,0:T(8,128)(2,1)S(1)} %concatenate.21.refs_3_), channel_id=1, source_target_pairs={{0,16},{8,24},{16,32},{24,40},{32,48},{40,56},{48,64},{56,72},{64,... | collective-permute-start | bytes 233480 | tf_op jit(solution)/shard_map/ppermute | solution.py:25
  23.5 0.7 convert_element_type.57
  24.2 0.7 convert.2
  24.9 0.7 convert_element_type.56
  25.8 2.5 %copy.59 = bf16[32,8,8,512]{3,2,1,0:T(8,128)(2,1)S(1)} copy(bf16[32,8,8,512]{3,1,2,0:T(8,128)(2,1)} %bitcast.173) | data formatting | bytes 4194304
  28.4 2.1 %collective-permute-done.2.refs_1_ = bf16[304,128]{1,0:T(8,128)(2,1)S(1)} collective-permute-done((bf16[304,128]{1,0:T(8,128)(2,1)S(1)}, bf16[304,128]{1,0:T(8,128)(2,1)S(1)}, u32[]{:S(2)}, u32[]{:S(2)}) %collective-permute-start.2) | collective-permute-done | bytes 77856 | tf_op jit(solution)/shard_map/ppermute | solution.py:25
  30.5 0.7 copy-done.12
  31.2 3.5 %shard_map.211 = f32[312,128]{1,0:T(8,128)} custom-call(bf16[304,128]{1,0:T(8,128)(2,1)} %copy-done.11, bf16[304,128]{1,0:T(8,128)(2,1)} %copy-done.12, bf16[304,128]{1,0:T(8,128)(2,1)} %copy-done.10, bf16[304,128]{1,0:T(8,128)(2,1)} %copy-done.1, bf16[306,32]{1,0:T(8,128)(2,1)} %constant.32.clone.refs_4_, bf16[306,32]{1,0:T(8,128)(2,1)} %constant.33.clone.refs_5_, ...), custom_call_target="tpu_custom_call" | custom-call | tf_op jit(solution)/shard_map/pallas_call | solution.py:169
  34.7 7.0 %collective-permute-start.5 = (f32[312,128]{1,0:T(8,128)}, f32[312,128]{1,0:T(8,128)}, u32[]{:S(2)}, u32[]{:S(2)}) collective-permute-start(f32[312,128]{1,0:T(8,128)} %shard_map.211), channel_id=1, source_target_pairs={{0,72},{8,80},{16,88},{24,96},{32,104},{40,112},{48,120},{56,128},... | collective-permute-start | bytes 479240 | tf_op jit(solution)/shard_map/ppermute | solution.py:25
  41.7 2.2 %collective-permute-start.6 = (f32[312,128]{1,0:T(8,128)}, f32[312,128]{1,0:T(8,128)}, u32[]{:S(2)}, u32[]{:S(2)}) collective-permute-start(f32[312,128]{1,0:T(8,128)} %shard_map.211), channel_id=1, source_target_pairs={{0,104},{8,112},{16,120},{24,128},{32,136},{40,144},{48,152},{56,1... | collective-permute-start | bytes 479240 | tf_op jit(solution)/shard_map/ppermute | solution.py:25
  43.9 4.3 %collective-permute-start.4 = (f32[312,128]{1,0:T(8,128)}, f32[312,128]{1,0:T(8,128)S(1)}, u32[]{:S(2)}, u32[]{:S(2)}) collective-permute-start(f32[312,128]{1,0:T(8,128)} %shard_map.211), channel_id=1, source_target_pairs={{0,40},{8,48},{16,56},{24,64},{32,72},{40,80},{48,88},{56,96},{64,... | collective-permute-start | bytes 479240 | tf_op jit(solution)/shard_map/ppermute | solution.py:25
  48.2 2.2 %collective-permute-start.3 = (f32[312,128]{1,0:T(8,128)}, f32[312,128]{1,0:T(8,128)S(1)}, u32[]{:S(2)}, u32[]{:S(2)}) collective-permute-start(f32[312,128]{1,0:T(8,128)} %shard_map.211), channel_id=1, source_target_pairs={{0,8},{8,16},{16,24},{24,32},{32,40},{40,48},{48,56},{56,64},{64,7... | collective-permute-start | bytes 479240 | tf_op jit(solution)/shard_map/ppermute | solution.py:25
  50.4 0.7 slice_convert_fusion
  51.2 0.6 slice.171
  51.8 0.7 fusion.56
  52.6 0.7 compare_convert_fusion.5
  54.2 1.1 broadcast_in_dim.111
  55.3 4.3 %all-to-all-start = ((bf16[8,128,512]{2,1,0:T(8,128)(2,1)}), bf16[8,128,512]{2,1,0:T(8,128)(2,1)}, u32[]{:S(2)}, u32[]{:S(2)}) async-start(bf16[8,128,512]{2,1,0:T(8,128)(2,1)} %broadcast_in_dim.111), calls=%async_computation | async-start | bytes 2097152 | tf_op jit(solution)/shard_map/all_to_all | solution.py:277
  60.8 1.2 collective-permute-done.6
  62.0 0.7 compare_bitcast_fusion.12
  62.7 1.1 add_select_fusion.7
  63.8 4.6 %collective-permute-done.4 = f32[312,128]{1,0:T(8,128)S(1)} collective-permute-done((f32[312,128]{1,0:T(8,128)}, f32[312,128]{1,0:T(8,128)S(1)}, u32[]{:S(2)}, u32[]{:S(2)}) %collective-permute-start.4) | collective-permute-done | bytes 159776 | tf_op jit(solution)/shard_map/ppermute | solution.py:25
  68.6 3.2 %collective-permute-done.3 = f32[312,128]{1,0:T(8,128)S(1)} collective-permute-done((f32[312,128]{1,0:T(8,128)}, f32[312,128]{1,0:T(8,128)S(1)}, u32[]{:S(2)}, u32[]{:S(2)}) %collective-permute-start.3) | collective-permute-done | bytes 159776 | tf_op jit(solution)/shard_map/ppermute | solution.py:25
  71.8 0.6 copy-done.6
  72.5 1.0 add_select_fusion.5
  74.4 1.3 all-to-all-done
  75.6 2.5 %fusion = f32[128,2,128,1]{0,2,3,1:T(8,128)S(1)} fusion(bf16[2,128,8,512]{3,2,1,0:T(8,128)(2,1)S(1)} %bitcast.174, bf16[8,128,512]{2,1,0:T(8,128)(2,1)} %all-to-all-done), kind=kOutput, calls=%fused_computation | convolution fusion | flops 268435456 | bytes 3276800 | tf_op jit(solution)/shard_map/dot_general | solution.py:280
  79.5 1.2 fusion.9
  80.6 1.1 convolution_add_fusion.2
  82.7 5.8 %collective-permute-start.7 = (f32[312,128]{1,0:T(8,128)S(1)}, f32[312,128]{1,0:T(8,128)S(1)}, u32[]{:S(2)}, u32[]{:S(2)}) collective-permute-start(f32[312,128]{1,0:T(8,128)S(1)} %concatenate.25), channel_id=1, source_target_pairs={{8,0},{16,8},{24,16},{32,24},{40,32},{48,40},{56,48},{64,56},{72,6... | collective-permute-start | bytes 479240 | tf_op jit(solution)/shard_map/ppermute | solution.py:25
  88.6 3.1 %collective-permute-done.7 = f32[312,128]{1,0:T(8,128)S(1)} collective-permute-done((f32[312,128]{1,0:T(8,128)S(1)}, f32[312,128]{1,0:T(8,128)S(1)}, u32[]{:S(2)}, u32[]{:S(2)}) %collective-permute-start.7) | collective-permute-done | bytes 159776 | tf_op jit(solution)/shard_map/ppermute | solution.py:25
  91.8 4.4 %collective-permute-start.8 = (f32[312,128]{1,0:T(8,128)S(1)}, f32[312,128]{1,0:T(8,128)S(1)}, u32[]{:S(2)}, u32[]{:S(2)}) collective-permute-start(f32[312,128]{1,0:T(8,128)S(1)} %add_select_fusion.4), channel_id=1, source_target_pairs={{16,0},{24,8},{32,16},{40,24},{48,32},{56,40},{64,48},{72,56},{80,... | collective-permute-start | bytes 479240 | tf_op jit(solution)/shard_map/ppermute | solution.py:25
  96.5 4.4 %collective-permute-done.8 = f32[312,128]{1,0:T(8,128)S(1)} collective-permute-done((f32[312,128]{1,0:T(8,128)S(1)}, f32[312,128]{1,0:T(8,128)S(1)}, u32[]{:S(2)}, u32[]{:S(2)}) %collective-permute-start.8) | collective-permute-done | bytes 159776 | tf_op jit(solution)/shard_map/ppermute | solution.py:25
  101.0 9.1 %collective-permute-start.11 = (f32[312,128]{1,0:T(8,128)S(1)}, f32[312,128]{1,0:T(8,128)S(1)}, u32[]{:S(2)}, u32[]{:S(2)}) collective-permute-start(f32[312,128]{1,0:T(8,128)S(1)} %add_select_fusion.3), channel_id=1, source_target_pairs={{72,0},{80,8},{88,16},{96,24},{104,32},{112,40},{120,48},{128,56},... | collective-permute-start | bytes 479240 | tf_op jit(solution)/shard_map/ppermute | solution.py:25
  110.1 5.5 %collective-permute-start.12 = (f32[312,128]{1,0:T(8,128)S(1)}, f32[312,128]{1,0:T(8,128)S(1)}, u32[]{:S(2)}, u32[]{:S(2)}) collective-permute-start(f32[312,128]{1,0:T(8,128)S(1)} %add_select_fusion.3), channel_id=1, source_target_pairs={{104,0},{112,8},{120,16},{128,24},{136,32},{144,40},{152,48},{160,... | collective-permute-start | bytes 479240 | tf_op jit(solution)/shard_map/ppermute | solution.py:25
  115.9 5.2 %collective-permute-start.10 = (f32[312,128]{1,0:T(8,128)S(1)}, f32[312,128]{1,0:T(8,128)S(1)}, u32[]{:S(2)}, u32[]{:S(2)}) collective-permute-start(f32[312,128]{1,0:T(8,128)S(1)} %add_select_fusion.3), channel_id=1, source_target_pairs={{40,0},{48,8},{56,16},{64,24},{72,32},{80,40},{88,48},{96,56},{104... | collective-permute-start | bytes 479240 | tf_op jit(solution)/shard_map/ppermute | solution.py:25
  121.1 2.2 %collective-permute-start.9 = (f32[312,128]{1,0:T(8,128)S(1)}, f32[312,128]{1,0:T(8,128)S(1)}, u32[]{:S(2)}, u32[]{:S(2)}) collective-permute-start(f32[312,128]{1,0:T(8,128)S(1)} %add_select_fusion.3), channel_id=1, source_target_pairs={{8,0},{16,8},{24,16},{32,24},{40,32},{48,40},{56,48},{64,56},{72,6... | collective-permute-start | bytes 479240 | tf_op jit(solution)/shard_map/ppermute | solution.py:25
  123.4 17.7 %collective-permute-done.10 = f32[312,128]{1,0:T(8,128)S(1)} collective-permute-done((f32[312,128]{1,0:T(8,128)S(1)}, f32[312,128]{1,0:T(8,128)S(1)}, u32[]{:S(2)}, u32[]{:S(2)}) %collective-permute-start.10) | collective-permute-done | bytes 159776 | tf_op jit(solution)/shard_map/ppermute | solution.py:25
  142.1 0.7 compare_convert_fusion.2
  143.3 0.8 copy.46
  144.6 0.8 fusion.12
  145.5 0.7 fusion.40
  (103 shorter events, 8.5 us)
Async XLA Ops:
  4.0 24.3 %copy-start.1 = (bf16[304,128]{1,0:T(8,128)(2,1)}, bf16[304,128]{1,0:T(8,128)(2,1)S(1)}, u32[]{:S(2)}) copy-start(bf16[304,128]{1,0:T(8,128)(2,1)S(1)} %concatenate.21.refs_3_) | copy-start | bytes 233476
  4.0 24.3 %collective-permute-start = (bf16[304,128]{1,0:T(8,128)(2,1)S(1)}, bf16[304,128]{1,0:T(8,128)(2,1)S(1)}, u32[]{:S(2)}, u32[]{:S(2)}) collective-permute-start(bf16[304,128]{1,0:T(8,128)(2,1)S(1)} %concatenate.21.refs_3_), channel_id=1, source_target_pairs={{0,8},{8,16},{16,24},{24,32},{32,40},{40,48},{48,56},{56,64},{64,7... | collective-permute-start | bytes 233480 | tf_op jit(solution)/shard_map/ppermute | solution.py:25
  8.3 20.1 %collective-permute-start.1 = (bf16[304,128]{1,0:T(8,128)(2,1)S(1)}, bf16[304,128]{1,0:T(8,128)(2,1)S(1)}, u32[]{:S(2)}, u32[]{:S(2)}) collective-permute-start(bf16[304,128]{1,0:T(8,128)(2,1)S(1)} %concatenate.21.refs_3_), channel_id=1, source_target_pairs={{0,24},{8,32},{16,40},{24,48},{32,56},{40,64},{48,72},{56,80},{64,... | collective-permute-start | bytes 233480 | tf_op jit(solution)/shard_map/ppermute | solution.py:25
  17.4 13.1 %collective-permute-start.2 = (bf16[304,128]{1,0:T(8,128)(2,1)S(1)}, bf16[304,128]{1,0:T(8,128)(2,1)S(1)}, u32[]{:S(2)}, u32[]{:S(2)}) collective-permute-start(bf16[304,128]{1,0:T(8,128)(2,1)S(1)} %concatenate.21.refs_3_), channel_id=1, source_target_pairs={{0,16},{8,24},{16,32},{24,40},{32,48},{40,56},{48,64},{56,72},{64,... | collective-permute-start | bytes 233480 | tf_op jit(solution)/shard_map/ppermute | solution.py:25
  25.7 34.6 %copy-start.4 = (f32[128,128]{0,1:T(8,128)}, f32[128,128]{0,1:T(8,128)S(1)}, u32[]{:S(2)}) copy-start(f32[128,128]{0,1:T(8,128)S(1)} %fusion.32) | copy-start | bytes 196612
  25.7 26.9 %copy-start.16 = (s32[128]{0:T(128)S(1)}, s32[128]{0:T(128)}, u32[]{:S(2)}) copy-start(s32[128]{0:T(128)} %param.23) | copy-start | bytes 1540
  25.7 27.7 %copy-start.3 = (f32[153,16,1]{0,1,2:T(8,128)S(1)}, f32[153,16,1]{0,1,2:T(8,128)}, u32[]{:S(2)}) copy-start(f32[153,16,1]{0,1,2:T(8,128)} %constant.55) | copy-start | bytes 29380
  25.8 27.7 %copy-start.15 = (f32[153]{0:T(256)S(1)}, f32[153]{0:T(256)}, u32[]{:S(2)}) copy-start(f32[153]{0:T(256)} %constant.52) | copy-start | bytes 1840
  25.8 28.4 %copy-start.7 = (bf16[128,512]{1,0:T(8,128)(2,1)S(1)}, bf16[128,512]{1,0:T(8,128)(2,1)}, u32[]{:S(2)}) copy-start(bf16[128,512]{1,0:T(8,128)(2,1)} %param.26) | copy-start | bytes 393220
  28.3 31.2 %copy-start.2 = (f32[153,16,1]{0,1,2:T(8,128)S(1)}, f32[153,16,1]{0,1,2:T(8,128)}, u32[]{:S(2)}) copy-start(f32[153,16,1]{0,1,2:T(8,128)} %constant.54) | copy-start | bytes 29380
  28.4 31.2 %copy-start.14 = (f32[153]{0:T(256)S(1)}, f32[153]{0:T(256)}, u32[]{:S(2)}) copy-start(f32[153]{0:T(256)} %constant.51) | copy-start | bytes 1840
  28.4 2.1 %copy-start.10 = (bf16[304,128]{1,0:T(8,128)(2,1)}, bf16[304,128]{1,0:T(8,128)(2,1)S(1)}, u32[]{:S(2)}) copy-start(bf16[304,128]{1,0:T(8,128)(2,1)S(1)} %collective-permute-done.refs_2_) | copy-start | bytes 233476
  28.4 2.1 %copy-start.11 = (bf16[304,128]{1,0:T(8,128)(2,1)}, bf16[304,128]{1,0:T(8,128)(2,1)S(1)}, u32[]{:S(2)}) copy-start(bf16[304,128]{1,0:T(8,128)(2,1)S(1)} %collective-permute-done.1.refs_0_) | copy-start | bytes 233476
  30.5 0.7 copy-start.12
  34.7 25.3 %copy-start.13 = (f32[153]{0:T(256)S(1)}, f32[153]{0:T(256)}, u32[]{:S(2)}) copy-start(f32[153]{0:T(256)} %constant.53) | copy-start | bytes 1840
  34.7 26.2 %collective-permute-start.5 = (f32[312,128]{1,0:T(8,128)}, f32[312,128]{1,0:T(8,128)}, u32[]{:S(2)}, u32[]{:S(2)}) collective-permute-start(f32[312,128]{1,0:T(8,128)} %shard_map.211), channel_id=1, source_target_pairs={{0,72},{8,80},{16,88},{24,96},{32,104},{40,112},{48,120},{56,128},... | collective-permute-start | bytes 479240 | tf_op jit(solution)/shard_map/ppermute | solution.py:25
  41.7 20.4 %collective-permute-start.6 = (f32[312,128]{1,0:T(8,128)}, f32[312,128]{1,0:T(8,128)}, u32[]{:S(2)}, u32[]{:S(2)}) collective-permute-start(f32[312,128]{1,0:T(8,128)} %shard_map.211), channel_id=1, source_target_pairs={{0,104},{8,112},{16,120},{24,128},{32,136},{40,144},{48,152},{56,1... | collective-permute-start | bytes 479240 | tf_op jit(solution)/shard_map/ppermute | solution.py:25
  43.9 24.5 %collective-permute-start.4 = (f32[312,128]{1,0:T(8,128)}, f32[312,128]{1,0:T(8,128)S(1)}, u32[]{:S(2)}, u32[]{:S(2)}) collective-permute-start(f32[312,128]{1,0:T(8,128)} %shard_map.211), channel_id=1, source_target_pairs={{0,40},{8,48},{16,56},{24,64},{32,72},{40,80},{48,88},{56,96},{64,... | collective-permute-start | bytes 479240 | tf_op jit(solution)/shard_map/ppermute | solution.py:25
  48.2 23.6 %collective-permute-start.3 = (f32[312,128]{1,0:T(8,128)}, f32[312,128]{1,0:T(8,128)S(1)}, u32[]{:S(2)}, u32[]{:S(2)}) collective-permute-start(f32[312,128]{1,0:T(8,128)} %shard_map.211), channel_id=1, source_target_pairs={{0,8},{8,16},{16,24},{24,32},{32,40},{40,48},{48,56},{56,64},{64,7... | collective-permute-start | bytes 479240 | tf_op jit(solution)/shard_map/ppermute | solution.py:25
  55.3 20.4 %all-to-all-start = ((bf16[8,128,512]{2,1,0:T(8,128)(2,1)}), bf16[8,128,512]{2,1,0:T(8,128)(2,1)}, u32[]{:S(2)}, u32[]{:S(2)}) async-start(bf16[8,128,512]{2,1,0:T(8,128)(2,1)} %broadcast_in_dim.111), calls=%async_computation | async-start | bytes 2097152 | tf_op jit(solution)/shard_map/all_to_all | solution.py:277
  71.8 0.7 copy-start.6
  73.9 4.3 %copy-start = (bf16[128,256]{1,0:T(8,128)(2,1)S(1)}, bf16[128,256]{1,0:T(8,128)(2,1)}, u32[]{:S(2)}) copy-start(bf16[128,256]{1,0:T(8,128)(2,1)} %param.22) | copy-start | bytes 196612
  75.6 3.8 %copy-start.5 = (f32[128,128]{0,1:T(8,128)S(1)}, f32[128,128]{0,1:T(8,128)}, u32[]{:S(2)}) copy-start(f32[128,128]{0,1:T(8,128)} %copy-done.4) | copy-start | bytes 196612
  78.2 0.7 copy-start.8
  79.5 36.2 %copy-start.9 = (f32[128,2,128,1]{0,2,3,1:T(8,128)S(1)}, f32[128,2,128,1]{0,2,3,1:T(8,128)}, u32[]{:S(2)}) copy-start(f32[128,2,128,1]{0,2,3,1:T(8,128)} %copy-done.8) | copy-start | bytes 393220
  82.7 8.9 %collective-permute-start.7 = (f32[312,128]{1,0:T(8,128)S(1)}, f32[312,128]{1,0:T(8,128)S(1)}, u32[]{:S(2)}, u32[]{:S(2)}) collective-permute-start(f32[312,128]{1,0:T(8,128)S(1)} %concatenate.25), channel_id=1, source_target_pairs={{8,0},{16,8},{24,16},{32,24},{40,32},{48,40},{56,48},{64,56},{72,6... | collective-permute-start | bytes 479240 | tf_op jit(solution)/shard_map/ppermute | solution.py:25
  91.8 9.1 %collective-permute-start.8 = (f32[312,128]{1,0:T(8,128)S(1)}, f32[312,128]{1,0:T(8,128)S(1)}, u32[]{:S(2)}, u32[]{:S(2)}) collective-permute-start(f32[312,128]{1,0:T(8,128)S(1)} %add_select_fusion.4), channel_id=1, source_target_pairs={{16,0},{24,8},{32,16},{40,24},{48,32},{56,40},{64,48},{72,56},{80,... | collective-permute-start | bytes 479240 | tf_op jit(solution)/shard_map/ppermute | solution.py:25
  101.0 22.2 %collective-permute-start.11 = (f32[312,128]{1,0:T(8,128)S(1)}, f32[312,128]{1,0:T(8,128)S(1)}, u32[]{:S(2)}, u32[]{:S(2)}) collective-permute-start(f32[312,128]{1,0:T(8,128)S(1)} %add_select_fusion.3), channel_id=1, source_target_pairs={{72,0},{80,8},{88,16},{96,24},{104,32},{112,40},{120,48},{128,56},... | collective-permute-start | bytes 479240 | tf_op jit(solution)/shard_map/ppermute | solution.py:25
  110.1 13.2 %collective-permute-start.12 = (f32[312,128]{1,0:T(8,128)S(1)}, f32[312,128]{1,0:T(8,128)S(1)}, u32[]{:S(2)}, u32[]{:S(2)}) collective-permute-start(f32[312,128]{1,0:T(8,128)S(1)} %add_select_fusion.3), channel_id=1, source_target_pairs={{104,0},{112,8},{120,16},{128,24},{136,32},{144,40},{152,48},{160,... | collective-permute-start | bytes 479240 | tf_op jit(solution)/shard_map/ppermute | solution.py:25
  115.9 25.2 %collective-permute-start.10 = (f32[312,128]{1,0:T(8,128)S(1)}, f32[312,128]{1,0:T(8,128)S(1)}, u32[]{:S(2)}, u32[]{:S(2)}) collective-permute-start(f32[312,128]{1,0:T(8,128)S(1)} %add_select_fusion.3), channel_id=1, source_target_pairs={{40,0},{48,8},{56,16},{64,24},{72,32},{80,40},{88,48},{96,56},{104... | collective-permute-start | bytes 479240 | tf_op jit(solution)/shard_map/ppermute | solution.py:25
  121.1 20.2 %collective-permute-start.9 = (f32[312,128]{1,0:T(8,128)S(1)}, f32[312,128]{1,0:T(8,128)S(1)}, u32[]{:S(2)}, u32[]{:S(2)}) collective-permute-start(f32[312,128]{1,0:T(8,128)S(1)} %add_select_fusion.3), channel_id=1, source_target_pairs={{8,0},{16,8},{24,16},{32,24},{40,32},{48,40},{56,48},{64,56},{72,6... | collective-permute-start | bytes 479240 | tf_op jit(solution)/shard_map/ppermute | solution.py:25

commit v15 on v11

--- a/solution.py
+++ b/solution.py
@@ -251,8 +251,12 @@
     length = queries.shape[1]
     head_width = values.shape[1] // local_heads
     reach = -(-(MOST - 1) // length)
+    head_count = lax.axis_size("head")
+    gathered = lax.all_to_all(
+        jnp.broadcast_to(out_grad[None], (head_count,) + out_grad.shape), "head", 0, 2, tiled=True
+    )
     grad_attn = lax.dot_general(
-        lax.all_gather(out_grad, "head", axis=1, tiled=True),
+        gathered[0],
         out_weight,
         (((1,), (1,)), ((), ())),
         preferred_element_type=jnp.float32,

time: 160 us -> 156 us (0.975)
  the two profiles are of different devices: /device:TPU:44 before, /device:TPU:40 now
where the time goes in v15:
time: 156 us; the launch traced here: 155 us
  starting transfers between devices  67.3 us (43%)
  waiting for transfers between devices  34.9 us (22%)
  matrix products  19.3 us (12%)
  local copies, waits for them, and re-layouts  15.1 us (10%)
  other arithmetic  13.3 us (9%)
  Pallas kernels  3.51 us (2%)
  between operations  1.61 us (1%)
    ppermute x13, starting transfers between devices, shifted(): return lax.ppermute(piece, axis, pairs)  63 us
    ppermute x13, waiting for transfers between devices, shifted(): return lax.ppermute(piece, axis, pairs)  34.9 us
    select_n x8, other arithmetic, join(): return jnp.where(empty_later, earlier, later + addend)  4.35 us
    all_to_all x1, starting transfers between devices, body(): lax.all_to_all(jnp.broadcast_to(out_grad[None], (head_count,) + out_grad....  4.3 us
    dot_general x4, matrix products, features(): jnp.einsum('rk,...kt->...rt', left, scaled, precision=exact_mode) + left_one  3.84 us
    dot_general x3, matrix products, block_output(): jnp.einsum('hft,hfd->thd', q_feat, state_in, precision=split_mode)  3.55 us
    pallas_call x1, Pallas kernels, window_state(): pl.pallas_call(kernel, out_shape=jax.ShapeDtypeStruct((out_rows, head_wid...  3.51 us
    dot_general x3, matrix products, block_output(): jnp.einsum('hft,hfs->hts', q_feat, k_feat, precision=split_mode)  3.46 us
  transfers between devices with their start and end apart: 14, of which 5 were waited for; matrix products, arithmetic and copies ran while one was open for 18% of the time, Pallas kernels for 2%

profile of v15, /device:TPU:40, one launch (start us, length us, event | category | flops | bytes accessed | tf_op | source)
XLA Modules:
  0.0 155.0 jit_solution(17163792074772680663)
XLA Ops:
  0.7 0.8 add_convert_fusion
  1.5 0.9 copy.45
  2.4 0.8 slice.161
  3.4 0.9 concatenate.21.refs_3_
  4.3 4.4 %collective-permute-start = (bf16[304,128]{1,0:T(8,128)(2,1)S(1)}, bf16[304,128]{1,0:T(8,128)(2,1)S(1)}, u32[]{:S(2)}, u32[]{:S(2)}) collective-permute-start(bf16[304,128]{1,0:T(8,128)(2,1)S(1)} %concatenate.21.refs_3_), channel_id=1, source_target_pairs={{0,8},{8,16},{16,24},{24,32},{32,40},{40,48},{48,56},{56,64},{64,7... | collective-permute-start | bytes 233480 | tf_op jit(solution)/shard_map/ppermute | solution.py:25
  8.7 9.1 %collective-permute-start.1 = (bf16[304,128]{1,0:T(8,128)(2,1)S(1)}, bf16[304,128]{1,0:T(8,128)(2,1)S(1)}, u32[]{:S(2)}, u32[]{:S(2)}) collective-permute-start(bf16[304,128]{1,0:T(8,128)(2,1)S(1)} %concatenate.21.refs_3_), channel_id=1, source_target_pairs={{0,24},{8,32},{16,40},{24,48},{32,56},{40,64},{48,72},{56,80},{64,... | collective-permute-start | bytes 233480 | tf_op jit(solution)/shard_map/ppermute | solution.py:25
  17.8 6.1 %collective-permute-start.2 = (bf16[304,128]{1,0:T(8,128)(2,1)S(1)}, bf16[304,128]{1,0:T(8,128)(2,1)S(1)}, u32[]{:S(2)}, u32[]{:S(2)}) collective-permute-start(bf16[304,128]{1,0:T(8,128)(2,1)S(1)} %concatenate.21.refs_3_), channel_id=1, source_target_pairs={{0,16},{8,24},{16,32},{24,40},{32,48},{40,56},{48,64},{56,72},{64,... | collective-permute-start | bytes 233480 | tf_op jit(solution)/shard_map/ppermute | solution.py:25
  23.9 2.0 %broadcast_in_dim.111 = bf16[8,128,512]{2,1,0:T(8,128)(2,1)} broadcast(bf16[128,512]{1,0:T(8,128)(2,1)} %param.26), dimensions={1,2} | broadcast | bytes 1179648 | tf_op jit(solution)/shard_map/broadcast_in_dim | solution.py:256
  25.9 4.3 %all-to-all-start = ((bf16[8,128,512]{2,1,0:T(8,128)(2,1)}), bf16[8,128,512]{2,1,0:T(8,128)(2,1)S(1)}, u32[]{:S(2)}, u32[]{:S(2)}) async-start(bf16[8,128,512]{2,1,0:T(8,128)(2,1)} %broadcast_in_dim.111), calls=%async_computation | async-start | bytes 2097152 | tf_op jit(solution)/shard_map/all_to_all | solution.py:255
  30.3 0.7 fusion.29
  32.8 3.5 %shard_map.211 = f32[312,128]{1,0:T(8,128)} custom-call(bf16[304,128]{1,0:T(8,128)(2,1)} %copy-done.16, bf16[304,128]{1,0:T(8,128)(2,1)} %copy-done.17, bf16[304,128]{1,0:T(8,128)(2,1)} %copy-done.15, bf16[304,128]{1,0:T(8,128)(2,1)} %copy-done.11, bf16[306,32]{1,0:T(8,128)(2,1)} %constant.32.clone.refs_4_, bf16[306,32]{1,0:T(8,128)(2,1)} %constant.33.clone.refs_5_, ...), custom_call_target="tpu_custom_call" | custom-call | tf_op jit(solution)/shard_map/pallas_call | solution.py:169
  36.3 5.6 %collective-permute-start.5 = (f32[312,128]{1,0:T(8,128)}, f32[312,128]{1,0:T(8,128)}, u32[]{:S(2)}, u32[]{:S(2)}) collective-permute-start(f32[312,128]{1,0:T(8,128)} %shard_map.211), channel_id=1, source_target_pairs={{0,72},{8,80},{16,88},{24,96},{32,104},{40,112},{48,120},{56,128},... | collective-permute-start | bytes 479240 | tf_op jit(solution)/shard_map/ppermute | solution.py:25
  41.9 2.2 %collective-permute-start.6 = (f32[312,128]{1,0:T(8,128)}, f32[312,128]{1,0:T(8,128)}, u32[]{:S(2)}, u32[]{:S(2)}) collective-permute-start(f32[312,128]{1,0:T(8,128)} %shard_map.211), channel_id=1, source_target_pairs={{0,104},{8,112},{16,120},{24,128},{32,136},{40,144},{48,152},{56,1... | collective-permute-start | bytes 479240 | tf_op jit(solution)/shard_map/ppermute | solution.py:25
  44.1 7.1 %collective-permute-start.4 = (f32[312,128]{1,0:T(8,128)}, f32[312,128]{1,0:T(8,128)}, u32[]{:S(2)}, u32[]{:S(2)}) collective-permute-start(f32[312,128]{1,0:T(8,128)} %shard_map.211), channel_id=1, source_target_pairs={{0,40},{8,48},{16,56},{24,64},{32,72},{40,80},{48,88},{56,96},{64,... | collective-permute-start | bytes 479240 | tf_op jit(solution)/shard_map/ppermute | solution.py:25
  51.2 2.2 %collective-permute-start.3 = (f32[312,128]{1,0:T(8,128)}, f32[312,128]{1,0:T(8,128)}, u32[]{:S(2)}, u32[]{:S(2)}) collective-permute-start(f32[312,128]{1,0:T(8,128)} %shard_map.211), channel_id=1, source_target_pairs={{0,8},{8,16},{16,24},{24,32},{32,40},{40,48},{48,56},{56,64},{64,7... | collective-permute-start | bytes 479240 | tf_op jit(solution)/shard_map/ppermute | solution.py:25
  55.6 1.1 compare_convert_fusion.5
  56.9 1.0 convolution_add_fusion.5
  57.9 1.0 convolution_add_fusion.3
  59.0 1.0 convolution_add_fusion.4
  60.0 1.8 %multiply_multiply_fusion.1 = (f32[2,128,153]{1,2,0:T(8,128)S(1)}, f32[2,128,153]{1,2,0:T(8,128)}) fusion(f32[2,128,153]{1,2,0:T(8,128)S(1)} %convolution_add_fusion.5, f32[153]{0:T(256)} %constant.53, f32[153]{0:T(256)} %constant.51, f32[2,16,128]{2,1,0:T(8,128)S(1)} %bitcast.174, f32[153,16,1]{0,1,2:T(8,128)S(1)} %copy-done.12), kind=kOutput, calls=%fused_computation.34 | convolution fusion | flops 7637760 | bytes 497416 | tf_op jit(solution)/shard_map/jvp(rk,...kt->...rt)/dot_general | solution.py:184
  61.8 2.0 %fusion.58 = (f32[2,128]{1,0:T(2,128)S(1)}, f32[2,128,128]{1,2,0:T(8,128)}) fusion(f32[128,128]{0,1:T(8,128)} %fusion.29, f32[2,128,153]{1,2,0:T(8,128)S(1)} %get-tuple-element.43, f32[2,128,153]{1,2,0:T(8,128)S(1)} %convolution_add_fusion.4, f32[2,128,153]{1,2,0:T(8,128)S(1)} %convolution_add_fusion.3, f32[153]{0:T(256)} %constant.53), kind=kOutput, calls=%fused_computation.135 | convolution fusion | flops 30224640 | bytes 668260 | tf_op jit(solution)/shard_map/jvp(hft,hfs->hts)/dot_general | solution.py:193
  64.5 1.1 add_select_fusion.7
  65.7 2.4 %collective-permute-done.4 = f32[312,128]{1,0:T(8,128)} collective-permute-done((f32[312,128]{1,0:T(8,128)}, f32[312,128]{1,0:T(8,128)}, u32[]{:S(2)}, u32[]{:S(2)}) %collective-permute-start.4) | collective-permute-done | bytes 159776 | tf_op jit(solution)/shard_map/ppermute | solution.py:25
  68.8 1.0 add_select_fusion.6
  69.8 3.8 %collective-permute-done.3 = f32[312,128]{1,0:T(8,128)} collective-permute-done((f32[312,128]{1,0:T(8,128)}, f32[312,128]{1,0:T(8,128)}, u32[]{:S(2)}, u32[]{:S(2)}) %collective-permute-start.3) | collective-permute-done | bytes 159776 | tf_op jit(solution)/shard_map/ppermute | solution.py:25
  74.3 1.7 %add_select_fusion.5 = f32[312,128]{1,0:T(8,128)} fusion(f32[312,128]{1,0:T(8,128)S(1)} %add_select_fusion.6, f32[312,128]{1,0:T(8,128)} %collective-permute-done.3, pred[128]{0:T(512)(128)(4,1)S(1)} %get-tuple-element.27, pred[128]{0:T(512)(128)(4,1)S(1)} %get-tuple-element.26, pred[312]{0:T(512)(128)(4,1)S(1)} %copy-done.18), kind=kLoop, calls=%fused_computation.40 | loop fusion | flops 159744 | bytes 479800 | tf_op jit(solution)/shard_map/jit(_where)/select_n | solution.py:210
  77.4 1.6 %reshape.160 = f32[2,153,128]{2,1,0:T(8,128)} reshape(f32[306,128]{1,0:T(8,128)} %bitcast.161) | data formatting | bytes 313344 | tf_op jit(solution)/shard_map/reshape | solution.py:242
  79.8 2.0 %fusion.8 = f32[128,2,128]{0,2,1:T(8,128)} fusion(f32[2,153,128]{2,1,0:T(8,128)} %reshape.160, f32[2,128,153]{1,2,0:T(8,128)S(1)} %get-tuple-element.43, f32[128]{0:T(128)S(1)} %copy-done.25), kind=kOutput, calls=%fused_computation.19 | convolution fusion | flops 30113792 | bytes 444928 | tf_op jit(solution)/shard_map/jvp(hft,hfd->thd)/dot_general | solution.py:195
  81.8 1.6 %copy.46 = bf16[1,128,8,512]{3,2,1,0:T(8,128)(2,1)} copy(bf16[1,128,8,512]{3,1,2,0:T(8,128)(2,1)S(1)} %bitcast.169) | data formatting | bytes 2097152 | tf_op jit(solution)/shard_map/all_to_all | solution.py:255
  83.4 1.6 %reshape.176 = bf16[128,4096,1]{1,0,2:T(8,128)(2,1)S(1)} reshape(bf16[1,128,8,512]{3,2,1,0:T(8,128)(2,1)} %copy.46) | data formatting | bytes 2097152 | tf_op jit(solution)/shard_map/squeeze | solution.py:259
  87.0 1.1 fusion.7
  88.1 1.3 convolution_add_fusion.2
  90.5 2.5 %collective-permute-start.7 = (f32[312,128]{1,0:T(8,128)S(1)}, f32[312,128]{1,0:T(8,128)S(1)}, u32[]{:S(2)}, u32[]{:S(2)}) collective-permute-start(f32[312,128]{1,0:T(8,128)S(1)} %concatenate.25), channel_id=1, source_target_pairs={{8,0},{16,8},{24,16},{32,24},{40,32},{48,40},{56,48},{64,56},{72,6... | collective-permute-start | bytes 479240 | tf_op jit(solution)/shard_map/ppermute | solution.py:25
  93.0 5.4 %collective-permute-done.7 = f32[312,128]{1,0:T(8,128)S(1)} collective-permute-done((f32[312,128]{1,0:T(8,128)S(1)}, f32[312,128]{1,0:T(8,128)S(1)}, u32[]{:S(2)}, u32[]{:S(2)}) %collective-permute-start.7) | collective-permute-done | bytes 159776 | tf_op jit(solution)/shard_map/ppermute | solution.py:25
  98.5 2.9 %collective-permute-start.8 = (f32[312,128]{1,0:T(8,128)S(1)}, f32[312,128]{1,0:T(8,128)S(1)}, u32[]{:S(2)}, u32[]{:S(2)}) collective-permute-start(f32[312,128]{1,0:T(8,128)S(1)} %add_select_fusion.4), channel_id=1, source_target_pairs={{16,0},{24,8},{32,16},{40,24},{48,32},{56,40},{64,48},{72,56},{80,... | collective-permute-start | bytes 479240 | tf_op jit(solution)/shard_map/ppermute | solution.py:25
  101.4 1.2 fusion.62
  102.6 5.4 %collective-permute-done.8 = f32[312,128]{1,0:T(8,128)S(1)} collective-permute-done((f32[312,128]{1,0:T(8,128)S(1)}, f32[312,128]{1,0:T(8,128)S(1)}, u32[]{:S(2)}, u32[]{:S(2)}) %collective-permute-start.8) | collective-permute-done | bytes 159776 | tf_op jit(solution)/shard_map/ppermute | solution.py:25
  108.1 8.5 %collective-permute-start.11 = (f32[312,128]{1,0:T(8,128)S(1)}, f32[312,128]{1,0:T(8,128)S(1)}, u32[]{:S(2)}, u32[]{:S(2)}) collective-permute-start(f32[312,128]{1,0:T(8,128)S(1)} %add_select_fusion.3), channel_id=1, source_target_pairs={{72,0},{80,8},{88,16},{96,24},{104,32},{112,40},{120,48},{128,56},... | collective-permute-start | bytes 479240 | tf_op jit(solution)/shard_map/ppermute | solution.py:25
  116.6 5.4 %collective-permute-start.12 = (f32[312,128]{1,0:T(8,128)S(1)}, f32[312,128]{1,0:T(8,128)S(1)}, u32[]{:S(2)}, u32[]{:S(2)}) collective-permute-start(f32[312,128]{1,0:T(8,128)S(1)} %add_select_fusion.3), channel_id=1, source_target_pairs={{104,0},{112,8},{120,16},{128,24},{136,32},{144,40},{152,48},{160,... | collective-permute-start | bytes 479240 | tf_op jit(solution)/shard_map/ppermute | solution.py:25
  122.0 1.9 %fusion.57 = f32[2,128,128]{2,1,0:T(8,128)} fusion(f32[2,128,128]{1,2,0:T(8,128)} %get-tuple-element.46, f32[128,2,128]{0,2,1:T(8,128)} %copy-done.7, f32[2,128]{1,0:T(2,128)S(1)} %copy-done.38), kind=kOutput, calls=%fused_computation.134 | convolution fusion | flops 25198592 | bytes 394240 | tf_op jit(solution)/shard_map/transpose(jvp(hts,shd->thd))/dot_general | solution.py:194
  123.9 3.6 %collective-permute-start.10 = (f32[312,128]{1,0:T(8,128)S(1)}, f32[312,128]{1,0:T(8,128)S(1)}, u32[]{:S(2)}, u32[]{:S(2)}) collective-permute-start(f32[312,128]{1,0:T(8,128)S(1)} %add_select_fusion.3), channel_id=1, source_target_pairs={{40,0},{48,8},{56,16},{64,24},{72,32},{80,40},{88,48},{96,56},{104... | collective-permute-start | bytes 479240 | tf_op jit(solution)/shard_map/ppermute | solution.py:25
  127.5 3.5 %collective-permute-start.9 = (f32[312,128]{1,0:T(8,128)S(1)}, f32[312,128]{1,0:T(8,128)S(1)}, u32[]{:S(2)}, u32[]{:S(2)}) collective-permute-start(f32[312,128]{1,0:T(8,128)S(1)} %add_select_fusion.3), channel_id=1, source_target_pairs={{8,0},{16,8},{24,16},{32,24},{40,32},{48,40},{56,48},{64,56},{72,6... | collective-permute-start | bytes 479240 | tf_op jit(solution)/shard_map/ppermute | solution.py:25
  131.2 17.9 %collective-permute-done.10 = f32[312,128]{1,0:T(8,128)S(1)} collective-permute-done((f32[312,128]{1,0:T(8,128)S(1)}, f32[312,128]{1,0:T(8,128)S(1)}, u32[]{:S(2)}, u32[]{:S(2)}) %collective-permute-start.10) | collective-permute-done | bytes 159776 | tf_op jit(solution)/shard_map/ppermute | solution.py:25
  150.0 0.7 compare_convert_fusion.2
  150.7 1.4 convolution_add_fusion.8
  152.1 0.8 copy.56
  153.4 0.8 fusion.10
  154.3 0.7 fusion.37
  (148 shorter events, 13.2 us)
Async XLA Ops:
  0.6 84.3 %copy-start = (bf16[256,4096]{1,0:T(8,128)(2,1)S(1)}, bf16[256,4096]{1,0:T(8,128)(2,1)}, u32[]{:S(2)}) copy-start(bf16[256,4096]{1,0:T(8,128)(2,1)} %param.25) | copy-start | bytes 6291460
  0.6 29.6 %copy-start.21 = (bf16[32,128]{1,0:T(8,128)(2,1)S(1)}, bf16[32,128]{1,0:T(8,128)(2,1)}, u32[]{:S(2)}) copy-start(bf16[32,128]{1,0:T(8,128)(2,1)} %param.20) | copy-start | bytes 24580
  0.7 29.6 %copy-start.20 = (bf16[32,128]{1,0:T(8,128)(2,1)S(1)}, bf16[32,128]{1,0:T(8,128)(2,1)}, u32[]{:S(2)}) copy-start(bf16[32,128]{1,0:T(8,128)(2,1)} %param.21) | copy-start | bytes 24580
  0.7 29.6 %copy-start.36 = (bf16[3,32]{1,0:T(4,128)(2,1)S(1)}, bf16[3,32]{1,0:T(4,128)(2,1)}, u32[]{:S(2)}) copy-start(bf16[3,32]{1,0:T(4,128)(2,1)} %param.24) | copy-start | bytes 580
  1.5 53.2 %copy-start.23 = (f32[128]{0:T(128)}, f32[128]{0:T(128)S(1)}, u32[]{:S(2)}) copy-start(f32[128]{0:T(128)S(1)} %get-tuple-element.41) | copy-start | bytes 1540
  4.2 27.3 %copy-start.11 = (bf16[304,128]{1,0:T(8,128)(2,1)}, bf16[304,128]{1,0:T(8,128)(2,1)S(1)}, u32[]{:S(2)}) copy-start(bf16[304,128]{1,0:T(8,128)(2,1)S(1)} %concatenate.21.refs_3_) | copy-start | bytes 233476
  4.2 51.4 %copy-start.34 = (s32[128]{0:T(128)S(1)}, s32[128]{0:T(128)}, u32[]{:S(2)}) copy-start(s32[128]{0:T(128)} %param.23) | copy-start | bytes 1540
  4.2 52.6 %copy-start.13 = (f32[153,16,1]{0,1,2:T(8,128)S(1)}, f32[153,16,1]{0,1,2:T(8,128)}, u32[]{:S(2)}) copy-start(f32[153,16,1]{0,1,2:T(8,128)} %constant.55) | copy-start | bytes 29380
  4.3 54.7 %copy-start.12 = (f32[153,16,1]{0,1,2:T(8,128)S(1)}, f32[153,16,1]{0,1,2:T(8,128)}, u32[]{:S(2)}) copy-start(f32[153,16,1]{0,1,2:T(8,128)} %constant.54) | copy-start | bytes 29380
  4.3 27.2 %collective-permute-start = (bf16[304,128]{1,0:T(8,128)(2,1)S(1)}, bf16[304,128]{1,0:T(8,128)(2,1)S(1)}, u32[]{:S(2)}, u32[]{:S(2)}) collective-permute-start(bf16[304,128]{1,0:T(8,128)(2,1)S(1)} %concatenate.21.refs_3_), channel_id=1, source_target_pairs={{0,8},{8,16},{16,24},{24,32},{32,40},{40,48},{48,56},{56,64},{64,7... | collective-permute-start | bytes 233480 | tf_op jit(solution)/shard_map/ppermute | solution.py:25
  8.7 22.8 %collective-permute-start.1 = (bf16[304,128]{1,0:T(8,128)(2,1)S(1)}, bf16[304,128]{1,0:T(8,128)(2,1)S(1)}, u32[]{:S(2)}, u32[]{:S(2)}) collective-permute-start(bf16[304,128]{1,0:T(8,128)(2,1)S(1)} %concatenate.21.refs_3_), channel_id=1, source_target_pairs={{0,24},{8,32},{16,40},{24,48},{32,56},{40,64},{48,72},{56,80},{64,... | collective-permute-start | bytes 233480 | tf_op jit(solution)/shard_map/ppermute | solution.py:25
  17.8 13.7 %collective-permute-start.2 = (bf16[304,128]{1,0:T(8,128)(2,1)S(1)}, bf16[304,128]{1,0:T(8,128)(2,1)S(1)}, u32[]{:S(2)}, u32[]{:S(2)}) collective-permute-start(bf16[304,128]{1,0:T(8,128)(2,1)S(1)} %concatenate.21.refs_3_), channel_id=1, source_target_pairs={{0,16},{8,24},{16,32},{24,40},{32,48},{40,56},{48,64},{56,72},{64,... | collective-permute-start | bytes 233480 | tf_op jit(solution)/shard_map/ppermute | solution.py:25
  25.9 55.9 %all-to-all-start = ((bf16[8,128,512]{2,1,0:T(8,128)(2,1)}), bf16[8,128,512]{2,1,0:T(8,128)(2,1)S(1)}, u32[]{:S(2)}, u32[]{:S(2)}) async-start(bf16[8,128,512]{2,1,0:T(8,128)(2,1)} %broadcast_in_dim.111), calls=%async_computation | async-start | bytes 2097152 | tf_op jit(solution)/shard_map/all_to_all | solution.py:255
  30.3 26.6 %copy-start.29 = (f32[32]{0:T(128)}, f32[32]{0:T(128)S(1)}, u32[]{:S(2)}) copy-start(f32[32]{0:T(128)S(1)} %get-tuple-element.33) | copy-start | bytes 388
  30.3 26.6 %copy-start.31 = (f32[32]{0:T(128)}, f32[32]{0:T(128)S(1)}, u32[]{:S(2)}) copy-start(f32[32]{0:T(128)S(1)} %get-tuple-element.34) | copy-start | bytes 388
  30.3 28.7 %copy-start.27 = (f32[32]{0:T(128)}, f32[32]{0:T(128)S(1)}, u32[]{:S(2)}) copy-start(f32[32]{0:T(128)S(1)} %get-tuple-element.32) | copy-start | bytes 388
  36.3 27.5 %collective-permute-start.5 = (f32[312,128]{1,0:T(8,128)}, f32[312,128]{1,0:T(8,128)}, u32[]{:S(2)}, u32[]{:S(2)}) collective-permute-start(f32[312,128]{1,0:T(8,128)} %shard_map.211), channel_id=1, source_target_pairs={{0,72},{8,80},{16,88},{24,96},{32,104},{40,112},{48,120},{56,128},... | collective-permute-start | bytes 479240 | tf_op jit(solution)/shard_map/ppermute | solution.py:25
  41.9 21.9 %collective-permute-start.6 = (f32[312,128]{1,0:T(8,128)}, f32[312,128]{1,0:T(8,128)}, u32[]{:S(2)}, u32[]{:S(2)}) collective-permute-start(f32[312,128]{1,0:T(8,128)} %shard_map.211), channel_id=1, source_target_pairs={{0,104},{8,112},{16,120},{24,128},{32,136},{40,144},{48,152},{56,1... | collective-permute-start | bytes 479240 | tf_op jit(solution)/shard_map/ppermute | solution.py:25
  44.1 23.9 %collective-permute-start.4 = (f32[312,128]{1,0:T(8,128)}, f32[312,128]{1,0:T(8,128)}, u32[]{:S(2)}, u32[]{:S(2)}) collective-permute-start(f32[312,128]{1,0:T(8,128)} %shard_map.211), channel_id=1, source_target_pairs={{0,40},{8,48},{16,56},{24,64},{32,72},{40,80},{48,88},{56,96},{64,... | collective-permute-start | bytes 479240 | tf_op jit(solution)/shard_map/ppermute | solution.py:25
  51.2 22.4 %collective-permute-start.3 = (f32[312,128]{1,0:T(8,128)}, f32[312,128]{1,0:T(8,128)}, u32[]{:S(2)}, u32[]{:S(2)}) collective-permute-start(f32[312,128]{1,0:T(8,128)} %shard_map.211), channel_id=1, source_target_pairs={{0,8},{8,16},{16,24},{24,32},{32,40},{40,48},{48,56},{56,64},{64,7... | collective-permute-start | bytes 479240 | tf_op jit(solution)/shard_map/ppermute | solution.py:25
  55.6 13.2 %copy-start.18 = (pred[312]{0:T(512)(128)(4,1)S(1)}, pred[312]{0:T(512)(128)(4,1)}, u32[]{:S(2)}) copy-start(pred[312]{0:T(512)(128)(4,1)} %iota_compare_fusion.1) | copy-start | bytes 940
  56.9 22.3 %copy-start.25 = (f32[128]{0:T(128)S(1)}, f32[128]{0:T(128)}, u32[]{:S(2)}) copy-start(f32[128]{0:T(128)} %get-tuple-element.40) | copy-start | bytes 1540
  57.9 5.9 %copy-start.3 = (f32[2,128,153]{1,2,0:T(8,128)}, f32[2,128,153]{1,2,0:T(8,128)S(1)}, u32[]{:S(2)}) copy-start(f32[2,128,153]{1,2,0:T(8,128)S(1)} %convolution_add_fusion.5) | copy-start | bytes 470020
  60.0 1.8 %copy-start.1 = (f32[2,128,153]{1,2,0:T(8,128)}, f32[2,128,153]{1,2,0:T(8,128)S(1)}, u32[]{:S(2)}) copy-start(f32[2,128,153]{1,2,0:T(8,128)S(1)} %convolution_add_fusion.4) | copy-start | bytes 470020
  85.0 0.9 copy-start.8
  85.0 1.0 copy-start.10
  85.0 1.0 copy-start.33
  85.0 1.2 copy-start.26
  85.0 1.4 copy-start.37
  85.7 3.7 %copy-start.2 = (f32[2,128,153]{1,2,0:T(8,128)S(1)}, f32[2,128,153]{1,2,0:T(8,128)}, u32[]{:S(2)}) copy-start(f32[2,128,153]{1,2,0:T(8,128)} %copy-done.1) | copy-start | bytes 470020
  85.7 3.7 %copy-start.22 = (f32[153]{0:T(256)S(1)}, f32[153]{0:T(256)}, u32[]{:S(2)}) copy-start(f32[153]{0:T(256)} %constant.53) | copy-start | bytes 1840
  85.8 4.0 %copy-start.5 = (f32[2,128,153]{1,2,0:T(8,128)S(1)}, f32[2,128,153]{1,2,0:T(8,128)}, u32[]{:S(2)}) copy-start(f32[2,128,153]{1,2,0:T(8,128)} %get-tuple-element.44) | copy-start | bytes 470020
  85.8 4.0 %copy-start.14 = (f32[153,16,1]{0,1,2:T(8,128)S(1)}, f32[153,16,1]{0,1,2:T(8,128)}, u32[]{:S(2)}) copy-start(f32[153,16,1]{0,1,2:T(8,128)} %constant.55) | copy-start | bytes 29380
  85.8 4.2 %copy-start.4 = (f32[2,128,153]{1,2,0:T(8,128)S(1)}, f32[2,128,153]{1,2,0:T(8,128)}, u32[]{:S(2)}) copy-start(f32[2,128,153]{1,2,0:T(8,128)} %copy-done.3) | copy-start | bytes 470020
  85.8 4.5 %copy-start.24 = (f32[128]{0:T(128)S(1)}, f32[128]{0:T(128)}, u32[]{:S(2)}) copy-start(f32[128]{0:T(128)} %copy-done.23) | copy-start | bytes 1540
  86.2 12.2 %copy-start.19 = (pred[312]{0:T(512)(128)(4,1)S(1)}, pred[312]{0:T(512)(128)(4,1)}, u32[]{:S(2)}) copy-start(pred[312]{0:T(512)(128)(4,1)} %iota_compare_fusion.1) | copy-start | bytes 940
  87.0 35.0 %copy-start.38 = (f32[2,128]{1,0:T(2,128)S(1)}, f32[2,128]{1,0:T(2,128)}, u32[]{:S(2)}) copy-start(f32[2,128]{1,0:T(2,128)} %get-tuple-element.17) | copy-start | bytes 3076
  88.1 2.3 %copy-start.9 = (f32[2,128,128]{1,2,0:T(8,128)}, f32[2,128,128]{1,2,0:T(8,128)S(1)}, u32[]{:S(2)}) copy-start(f32[2,128,128]{1,2,0:T(8,128)S(1)} %fusion.7) | copy-start | bytes 393220
  90.2 59.8 %copy-start.35 = (s32[128]{0:T(128)S(1)}, s32[128]{0:T(128)}, u32[]{:S(2)}) copy-start(s32[128]{0:T(128)} %param.23) | copy-start | bytes 1540
  90.5 7.9 %collective-permute-start.7 = (f32[312,128]{1,0:T(8,128)S(1)}, f32[312,128]{1,0:T(8,128)S(1)}, u32[]{:S(2)}, u32[]{:S(2)}) collective-permute-start(f32[312,128]{1,0:T(8,128)S(1)} %concatenate.25), channel_id=1, source_target_pairs={{8,0},{16,8},{24,16},{32,24},{40,32},{48,40},{56,48},{64,56},{72,6... | collective-permute-start | bytes 479240 | tf_op jit(solution)/shard_map/ppermute | solution.py:25
  98.5 9.4 %collective-permute-start.8 = (f32[312,128]{1,0:T(8,128)S(1)}, f32[312,128]{1,0:T(8,128)S(1)}, u32[]{:S(2)}, u32[]{:S(2)}) collective-permute-start(f32[312,128]{1,0:T(8,128)S(1)} %add_select_fusion.4), channel_id=1, source_target_pairs={{16,0},{24,8},{32,16},{40,24},{48,32},{56,40},{64,48},{72,56},{80,... | collective-permute-start | bytes 479240 | tf_op jit(solution)/shard_map/ppermute | solution.py:25
  108.1 22.9 %collective-permute-start.11 = (f32[312,128]{1,0:T(8,128)S(1)}, f32[312,128]{1,0:T(8,128)S(1)}, u32[]{:S(2)}, u32[]{:S(2)}) collective-permute-start(f32[312,128]{1,0:T(8,128)S(1)} %add_select_fusion.3), channel_id=1, source_target_pairs={{72,0},{80,8},{88,16},{96,24},{104,32},{112,40},{120,48},{128,56},... | collective-permute-start | bytes 479240 | tf_op jit(solution)/shard_map/ppermute | solution.py:25
  116.6 14.5 %collective-permute-start.12 = (f32[312,128]{1,0:T(8,128)S(1)}, f32[312,128]{1,0:T(8,128)S(1)}, u32[]{:S(2)}, u32[]{:S(2)}) collective-permute-start(f32[312,128]{1,0:T(8,128)S(1)} %add_select_fusion.3), channel_id=1, source_target_pairs={{104,0},{112,8},{120,16},{128,24},{136,32},{144,40},{152,48},{160,... | collective-permute-start | bytes 479240 | tf_op jit(solution)/shard_map/ppermute | solution.py:25
  123.9 30.4 %copy-start.28 = (f32[32]{0:T(128)S(1)}, f32[32]{0:T(128)}, u32[]{:S(2)}) copy-start(f32[32]{0:T(128)} %copy-done.27) | copy-start | bytes 388
  123.9 30.4 %copy-start.30 = (f32[32]{0:T(128)S(1)}, f32[32]{0:T(128)}, u32[]{:S(2)}) copy-start(f32[32]{0:T(128)} %copy-done.29) | copy-start | bytes 388
  123.9 30.4 %copy-start.32 = (f32[32]{0:T(128)S(1)}, f32[32]{0:T(128)}, u32[]{:S(2)}) copy-start(f32[32]{0:T(128)} %copy-done.31) | copy-start | bytes 388
  123.9 25.2 %collective-permute-start.10 = (f32[312,128]{1,0:T(8,128)S(1)}, f32[312,128]{1,0:T(8,128)S(1)}, u32[]{:S(2)}, u32[]{:S(2)}) collective-permute-start(f32[312,128]{1,0:T(8,128)S(1)} %add_select_fusion.3), channel_id=1, source_target_pairs={{40,0},{48,8},{56,16},{64,24},{72,32},{80,40},{88,48},{96,56},{104... | collective-permute-start | bytes 479240 | tf_op jit(solution)/shard_map/ppermute | solution.py:25
  127.5 21.7 %collective-permute-start.9 = (f32[312,128]{1,0:T(8,128)S(1)}, f32[312,128]{1,0:T(8,128)S(1)}, u32[]{:S(2)}, u32[]{:S(2)}) collective-permute-start(f32[312,128]{1,0:T(8,128)S(1)} %add_select_fusion.3), channel_id=1, source_target_pairs={{8,0},{16,8},{24,16},{32,24},{40,32},{48,40},{56,48},{64,56},{72,6... | collective-permute-start | bytes 479240 | tf_op jit(solution)/shard_map/ppermute | solution.py:25
  (5 other events, 3.4 us)

commit v16 on v13

--- a/solution.py
+++ b/solution.py
@@ -46,10 +46,12 @@
     near, far = window_steps(reach, size)
     total = shard
     step = 1
-    while step <= len(near):
+    while step * 2 < reach and step < size:
         total = combine(shifted(total, axis, step, reverse), total)
         step *= 2
-    return fold(combine, [shifted(total, axis, step, reverse) for step in far])
+    far = [1 + step * k for k in range(-(-reach // step) - 1, -1, -1)]
+    far = [each for each in far if each < size]
+    return fold(combine, [shifted(total, axis, each, reverse) for each in far])
 
 
 def rows_of(flat, lanes):

time: 146 us -> 151 us (1.034)
  the two profiles are of different devices: /device:TPU:40 before, /device:TPU:17 now
where the time goes in v16:
time: 151 us; the launch traced here: 150 us
  starting transfers between devices  59.1 us (39%)
  waiting for transfers between devices  56.5 us (37%)
  local copies, waits for them, and re-layouts  11.7 us (8%)
  matrix products  10 us (7%)
  other arithmetic  8.03 us (5%)
  Pallas kernels  3.52 us (2%)
    ppermute x12, waiting for transfers between devices, shifted(): return lax.ppermute(piece, axis, pairs)  56.5 us
    ppermute x12, starting transfers between devices, shifted(): return lax.ppermute(piece, axis, pairs)  53.3 us
    unnamed x49, local copies, waits for them, and re-layouts  5.97 us
    all_to_all x1, starting transfers between devices, body(): lax.all_to_all(jnp.broadcast_to(out_grad[None], (head_count,) + out_grad....  5.81 us
    pallas_call x1, Pallas kernels, window_state(): pl.pallas_call(kernel, out_shape=jax.ShapeDtypeStruct((out_rows, head_wid...  3.52 us
  transfers between devices with their start and end apart: 13, of which 6 were waited for; matrix products, arithmetic and copies ran while one was open for 9% of the time, Pallas kernels for 2%

profile of v16, /device:TPU:17, one launch (start us, length us, event | category | flops | bytes accessed | tf_op | source)
XLA Modules:
  0.0 150.4 jit_solution(2958552592532988444)
XLA Ops:
  0.7 0.8 add_convert_fusion
  1.5 0.8 slice.154
  2.4 1.0 copy.35
  3.4 0.9 concatenate.21.refs_3_
  4.2 5.8 %collective-permute-start.2 = (bf16[304,128]{1,0:T(8,128)(2,1)S(1)}, bf16[304,128]{1,0:T(8,128)(2,1)S(1)}, u32[]{:S(2)}, u32[]{:S(2)}) collective-permute-start(bf16[304,128]{1,0:T(8,128)(2,1)S(1)} %concatenate.21.refs_3_), channel_id=1, source_target_pairs={{0,16},{8,24},{16,32},{24,40},{32,48},{40,56},{48,64},{56,72},{64,... | collective-permute-start | bytes 233480 | tf_op jit(solution)/shard_map/ppermute | solution.py:25
  10.0 8.8 %collective-permute-start.1 = (bf16[304,128]{1,0:T(8,128)(2,1)S(1)}, bf16[304,128]{1,0:T(8,128)(2,1)S(1)}, u32[]{:S(2)}, u32[]{:S(2)}) collective-permute-start(bf16[304,128]{1,0:T(8,128)(2,1)S(1)} %concatenate.21.refs_3_), channel_id=1, source_target_pairs={{0,24},{8,32},{16,40},{24,48},{32,56},{40,64},{48,72},{56,80},{64,... | collective-permute-start | bytes 233480 | tf_op jit(solution)/shard_map/ppermute | solution.py:25
  18.9 4.0 %collective-permute-start = (bf16[304,128]{1,0:T(8,128)(2,1)S(1)}, bf16[304,128]{1,0:T(8,128)(2,1)S(1)}, u32[]{:S(2)}, u32[]{:S(2)}) collective-permute-start(bf16[304,128]{1,0:T(8,128)(2,1)S(1)} %concatenate.21.refs_3_), channel_id=1, source_target_pairs={{0,8},{8,16},{16,24},{24,32},{32,40},{40,48},{48,56},{56,64},{64,7... | collective-permute-start | bytes 233480 | tf_op jit(solution)/shard_map/ppermute | solution.py:25
  22.9 2.0 %broadcast_in_dim.103 = bf16[8,128,512]{2,1,0:T(8,128)(2,1)} broadcast(bf16[128,512]{1,0:T(8,128)(2,1)} %param.26), dimensions={1,2} | broadcast | bytes 1179648 | tf_op jit(solution)/shard_map/broadcast_in_dim | solution.py:258
  24.9 5.8 %all-to-all-start = ((bf16[8,128,512]{2,1,0:T(8,128)(2,1)}), bf16[8,128,512]{2,1,0:T(8,128)(2,1)}, u32[]{:S(2)}, u32[]{:S(2)}) async-start(bf16[8,128,512]{2,1,0:T(8,128)(2,1)} %broadcast_in_dim.103), calls=%async_computation | async-start | bytes 2097152 | tf_op jit(solution)/shard_map/all_to_all | solution.py:257
  30.9 2.2 %copy.59 = bf16[32,8,8,512]{3,2,1,0:T(8,128)(2,1)} copy(bf16[32,8,8,512]{3,1,2,0:T(8,128)(2,1)S(1)} %bitcast.169) | data formatting | bytes 4194304
  33.3 0.6 slice.164
  33.9 0.6 copy-done.12
  34.5 0.6 copy-done.13
  35.1 3.5 %shard_map.211 = f32[312,128]{1,0:T(8,128)} custom-call(bf16[304,128]{1,0:T(8,128)(2,1)} %copy-done.13, bf16[304,128]{1,0:T(8,128)(2,1)} %copy-done.12, bf16[304,128]{1,0:T(8,128)(2,1)} %copy-done.11, bf16[304,128]{1,0:T(8,128)(2,1)} %copy-done.3, bf16[306,32]{1,0:T(8,128)(2,1)} %constant.32.clone.refs_4_, bf16[306,32]{1,0:T(8,128)(2,1)} %constant.33.clone.refs_5_, ...), custom_call_target="tpu_custom_call" | custom-call | tf_op jit(solution)/shard_map/pallas_call | solution.py:171
  38.6 4.7 %collective-permute-start.6 = (f32[312,128]{1,0:T(8,128)}, f32[312,128]{1,0:T(8,128)}, u32[]{:S(2)}, u32[]{:S(2)}) collective-permute-start(f32[312,128]{1,0:T(8,128)} %shard_map.211), channel_id=1, source_target_pairs={{0,104},{8,112},{16,120},{24,128},{32,136},{40,144},{48,152},{56,1... | collective-permute-start | bytes 479240 | tf_op jit(solution)/shard_map/ppermute | solution.py:25
  43.3 3.2 %collective-permute-start.5 = (f32[312,128]{1,0:T(8,128)}, f32[312,128]{1,0:T(8,128)}, u32[]{:S(2)}, u32[]{:S(2)}) collective-permute-start(f32[312,128]{1,0:T(8,128)} %shard_map.211), channel_id=1, source_target_pairs={{0,72},{8,80},{16,88},{24,96},{32,104},{40,112},{48,120},{56,128},... | collective-permute-start | bytes 479240 | tf_op jit(solution)/shard_map/ppermute | solution.py:25
  46.5 9.1 %collective-permute-start.4 = (f32[312,128]{1,0:T(8,128)}, f32[312,128]{1,0:T(8,128)S(1)}, u32[]{:S(2)}, u32[]{:S(2)}) collective-permute-start(f32[312,128]{1,0:T(8,128)} %shard_map.211), channel_id=1, source_target_pairs={{0,40},{8,48},{16,56},{24,64},{32,72},{40,80},{48,88},{56,96},{64,... | collective-permute-start | bytes 479240 | tf_op jit(solution)/shard_map/ppermute | solution.py:25
  55.7 3.1 %collective-permute-start.3 = (f32[312,128]{1,0:T(8,128)}, f32[312,128]{1,0:T(8,128)S(1)}, u32[]{:S(2)}, u32[]{:S(2)}) collective-permute-start(f32[312,128]{1,0:T(8,128)} %shard_map.211), channel_id=1, source_target_pairs={{0,8},{8,16},{16,24},{24,32},{32,40},{40,48},{48,56},{56,64},{64,7... | collective-permute-start | bytes 479240 | tf_op jit(solution)/shard_map/ppermute | solution.py:25
  58.9 0.7 fusion.56
  59.7 0.7 compare_convert_fusion.5
  60.9 0.3 convolution_add_fusion.5
  61.6 0.3 multiply_multiply_fusion.1
  62.0 0.5 fusion.61
  62.5 0.7 compare_bitcast_fusion.10
  63.2 1.1 add_select_fusion.6
  64.3 7.6 %collective-permute-done.4 = f32[312,128]{1,0:T(8,128)S(1)} collective-permute-done((f32[312,128]{1,0:T(8,128)}, f32[312,128]{1,0:T(8,128)S(1)}, u32[]{:S(2)}, u32[]{:S(2)}) %collective-permute-start.4) | collective-permute-done | bytes 159776 | tf_op jit(solution)/shard_map/ppermute | solution.py:25
  72.0 7.4 %collective-permute-done.3 = f32[312,128]{1,0:T(8,128)S(1)} collective-permute-done((f32[312,128]{1,0:T(8,128)}, f32[312,128]{1,0:T(8,128)S(1)}, u32[]{:S(2)}, u32[]{:S(2)}) %collective-permute-start.3) | collective-permute-done | bytes 159776 | tf_op jit(solution)/shard_map/ppermute | solution.py:25
  79.4 0.7 copy-done.8
  80.1 1.0 add_select_fusion.4
  81.5 0.6 divide_bitcast_fusion
  82.1 0.4 fusion.10
  82.6 2.5 %fusion = f32[128,2,128,1]{0,2,3,1:T(8,128)S(1)} fusion(bf16[2,128,8,512]{3,2,1,0:T(8,128)(2,1)S(1)} %bitcast.170, bf16[8,128,512]{2,1,0:T(8,128)(2,1)} %all-to-all-done), kind=kOutput, calls=%fused_computation | convolution fusion | flops 268435456 | bytes 3276800 | tf_op jit(solution)/shard_map/dot_general | solution.py:260
  86.2 1.1 fusion.9
  88.4 1.9 %collective-permute-start.7 = (f32[312,128]{1,0:T(8,128)S(1)}, f32[312,128]{1,0:T(8,128)S(1)}, u32[]{:S(2)}, u32[]{:S(2)}) collective-permute-start(f32[312,128]{1,0:T(8,128)S(1)} %concatenate.25), channel_id=1, source_target_pairs={{8,0},{16,8},{24,16},{32,24},{40,32},{48,40},{56,48},{64,56},{72,6... | collective-permute-start | bytes 479240 | tf_op jit(solution)/shard_map/ppermute | solution.py:25
  90.3 5.1 %collective-permute-done.7 = f32[312,128]{1,0:T(8,128)S(1)} collective-permute-done((f32[312,128]{1,0:T(8,128)S(1)}, f32[312,128]{1,0:T(8,128)S(1)}, u32[]{:S(2)}, u32[]{:S(2)}) %collective-permute-start.7) | collective-permute-done | bytes 159776 | tf_op jit(solution)/shard_map/ppermute | solution.py:25
  95.6 1.9 %collective-permute-start.8 = (f32[312,128]{1,0:T(8,128)S(1)}, f32[312,128]{1,0:T(8,128)S(1)}, u32[]{:S(2)}, u32[]{:S(2)}) collective-permute-start(f32[312,128]{1,0:T(8,128)S(1)} %add_select_fusion.3), channel_id=1, source_target_pairs={{16,0},{24,8},{32,16},{40,24},{48,32},{56,40},{64,48},{72,56},{80,... | collective-permute-start | bytes 479240 | tf_op jit(solution)/shard_map/ppermute | solution.py:25
  97.6 9.3 %collective-permute-done.8 = f32[312,128]{1,0:T(8,128)S(1)} collective-permute-done((f32[312,128]{1,0:T(8,128)S(1)}, f32[312,128]{1,0:T(8,128)S(1)}, u32[]{:S(2)}, u32[]{:S(2)}) %collective-permute-start.8) | collective-permute-done | bytes 159776 | tf_op jit(solution)/shard_map/ppermute | solution.py:25
  107.0 1.9 %collective-permute-start.9 = (f32[312,128]{1,0:T(8,128)S(1)}, f32[312,128]{1,0:T(8,128)S(1)}, u32[]{:S(2)}, u32[]{:S(2)}) collective-permute-start(f32[312,128]{1,0:T(8,128)S(1)} %add_select_fusion.2), channel_id=1, source_target_pairs={{32,0},{40,8},{48,16},{56,24},{64,32},{72,40},{80,48},{88,56},{96,... | collective-permute-start | bytes 479240 | tf_op jit(solution)/shard_map/ppermute | solution.py:25
  109.2 16.5 %collective-permute-done.9 = f32[312,128]{1,0:T(8,128)S(1)} collective-permute-done((f32[312,128]{1,0:T(8,128)S(1)}, f32[312,128]{1,0:T(8,128)S(1)}, u32[]{:S(2)}, u32[]{:S(2)}) %collective-permute-start.9) | collective-permute-done | bytes 159776 | tf_op jit(solution)/shard_map/ppermute | solution.py:25
  125.8 1.9 %collective-permute-start.11 = (f32[312,128]{1,0:T(8,128)S(1)}, f32[312,128]{1,0:T(8,128)S(1)}, u32[]{:S(2)}, u32[]{:S(2)}) collective-permute-start(f32[312,128]{1,0:T(8,128)S(1)} %add_select_fusion.1), channel_id=1, source_target_pairs={{72,0},{80,8},{88,16},{96,24},{104,32},{112,40},{120,48},{128,56},... | collective-permute-start | bytes 479240 | tf_op jit(solution)/shard_map/ppermute | solution.py:25
  127.7 6.8 %collective-permute-start.10 = (f32[312,128]{1,0:T(8,128)S(1)}, f32[312,128]{1,0:T(8,128)S(1)}, u32[]{:S(2)}, u32[]{:S(2)}) collective-permute-start(f32[312,128]{1,0:T(8,128)S(1)} %add_select_fusion.1), channel_id=1, source_target_pairs={{8,0},{16,8},{24,16},{32,24},{40,32},{48,40},{56,48},{64,56},{72,6... | collective-permute-start | bytes 479240 | tf_op jit(solution)/shard_map/ppermute | solution.py:25
  134.8 10.7 %collective-permute-done.11 = f32[312,128]{1,0:T(8,128)S(1)} collective-permute-done((f32[312,128]{1,0:T(8,128)S(1)}, f32[312,128]{1,0:T(8,128)S(1)}, u32[]{:S(2)}, u32[]{:S(2)}) %collective-permute-start.11) | collective-permute-done | bytes 159776 | tf_op jit(solution)/shard_map/ppermute | solution.py:25
  145.6 0.5 slice.221
  146.4 0.7 compare_convert_fusion.2
  147.2 0.5 convolution_add_fusion.8
  148.1 0.8 fusion.12
  148.9 0.8 copy.46
  149.7 0.7 fusion.40
  (111 shorter events, 5.7 us)
Async XLA Ops:
  0.6 30.0 %copy-start.15 = (bf16[32,128]{1,0:T(8,128)(2,1)S(1)}, bf16[32,128]{1,0:T(8,128)(2,1)}, u32[]{:S(2)}) copy-start(bf16[32,128]{1,0:T(8,128)(2,1)} %param.20) | copy-start | bytes 24580
  0.6 30.1 %copy-start.14 = (bf16[32,128]{1,0:T(8,128)(2,1)S(1)}, bf16[32,128]{1,0:T(8,128)(2,1)}, u32[]{:S(2)}) copy-start(bf16[32,128]{1,0:T(8,128)(2,1)} %param.21) | copy-start | bytes 24580
  0.7 30.0 %copy-start.20 = (bf16[3,32]{1,0:T(4,128)(2,1)S(1)}, bf16[3,32]{1,0:T(4,128)(2,1)}, u32[]{:S(2)}) copy-start(bf16[3,32]{1,0:T(4,128)(2,1)} %param.24) | copy-start | bytes 580
  0.7 30.2 %copy-start = (bf16[256,4096]{1,0:T(8,128)(2,1)S(1)}, bf16[256,4096]{1,0:T(8,128)(2,1)}, u32[]{:S(2)}) copy-start(bf16[256,4096]{1,0:T(8,128)(2,1)} %param.25) | copy-start | bytes 6291460
  4.2 28.9 %copy-start.3 = (bf16[304,128]{1,0:T(8,128)(2,1)}, bf16[304,128]{1,0:T(8,128)(2,1)S(1)}, u32[]{:S(2)}) copy-start(bf16[304,128]{1,0:T(8,128)(2,1)S(1)} %concatenate.21.refs_3_) | copy-start | bytes 233476
  4.2 29.6 %collective-permute-start.2 = (bf16[304,128]{1,0:T(8,128)(2,1)S(1)}, bf16[304,128]{1,0:T(8,128)(2,1)S(1)}, u32[]{:S(2)}, u32[]{:S(2)}) collective-permute-start(bf16[304,128]{1,0:T(8,128)(2,1)S(1)} %concatenate.21.refs_3_), channel_id=1, source_target_pairs={{0,16},{8,24},{16,32},{24,40},{32,48},{40,56},{48,64},{56,72},{64,... | collective-permute-start | bytes 233480 | tf_op jit(solution)/shard_map/ppermute | solution.py:25
  10.0 23.8 %collective-permute-start.1 = (bf16[304,128]{1,0:T(8,128)(2,1)S(1)}, bf16[304,128]{1,0:T(8,128)(2,1)S(1)}, u32[]{:S(2)}, u32[]{:S(2)}) collective-permute-start(bf16[304,128]{1,0:T(8,128)(2,1)S(1)} %concatenate.21.refs_3_), channel_id=1, source_target_pairs={{0,24},{8,32},{16,40},{24,48},{32,56},{40,64},{48,72},{56,80},{64,... | collective-permute-start | bytes 233480 | tf_op jit(solution)/shard_map/ppermute | solution.py:25
  18.9 14.3 %collective-permute-start = (bf16[304,128]{1,0:T(8,128)(2,1)S(1)}, bf16[304,128]{1,0:T(8,128)(2,1)S(1)}, u32[]{:S(2)}, u32[]{:S(2)}) collective-permute-start(bf16[304,128]{1,0:T(8,128)(2,1)S(1)} %concatenate.21.refs_3_), channel_id=1, source_target_pairs={{0,8},{8,16},{16,24},{24,32},{32,40},{40,48},{48,56},{56,64},{64,7... | collective-permute-start | bytes 233480 | tf_op jit(solution)/shard_map/ppermute | solution.py:25
  24.9 57.6 %all-to-all-start = ((bf16[8,128,512]{2,1,0:T(8,128)(2,1)}), bf16[8,128,512]{2,1,0:T(8,128)(2,1)}, u32[]{:S(2)}, u32[]{:S(2)}) async-start(bf16[8,128,512]{2,1,0:T(8,128)(2,1)} %broadcast_in_dim.103), calls=%async_computation | async-start | bytes 2097152 | tf_op jit(solution)/shard_map/all_to_all | solution.py:257
  30.8 31.1 %copy-start.6 = (f32[128,128]{0,1:T(8,128)}, f32[128,128]{0,1:T(8,128)S(1)}, u32[]{:S(2)}) copy-start(f32[128,128]{0,1:T(8,128)S(1)} %fusion.32) | copy-start | bytes 196612
  30.8 28.8 %copy-start.19 = (s32[128]{0:T(128)S(1)}, s32[128]{0:T(128)}, u32[]{:S(2)}) copy-start(s32[128]{0:T(128)} %param.23) | copy-start | bytes 1540
  30.9 29.6 %copy-start.5 = (f32[153,16,1]{0,1,2:T(8,128)S(1)}, f32[153,16,1]{0,1,2:T(8,128)}, u32[]{:S(2)}) copy-start(f32[153,16,1]{0,1,2:T(8,128)} %constant.55) | copy-start | bytes 29380
  30.9 29.5 %copy-start.18 = (f32[153]{0:T(256)S(1)}, f32[153]{0:T(256)}, u32[]{:S(2)}) copy-start(f32[153]{0:T(256)} %constant.52) | copy-start | bytes 1840
  30.9 30.3 %copy-start.4 = (f32[153,16,1]{0,1,2:T(8,128)S(1)}, f32[153,16,1]{0,1,2:T(8,128)}, u32[]{:S(2)}) copy-start(f32[153,16,1]{0,1,2:T(8,128)} %constant.54) | copy-start | bytes 29380
  30.9 30.3 %copy-start.17 = (f32[153]{0:T(256)S(1)}, f32[153]{0:T(256)}, u32[]{:S(2)}) copy-start(f32[153]{0:T(256)} %constant.51) | copy-start | bytes 1840
  30.9 30.7 %copy-start.16 = (f32[153]{0:T(256)S(1)}, f32[153]{0:T(256)}, u32[]{:S(2)}) copy-start(f32[153]{0:T(256)} %constant.53) | copy-start | bytes 1840
  33.2 0.7 copy-start.11
  33.8 0.6 copy-start.12
  34.5 0.6 copy-start.13
  38.6 23.9 %collective-permute-start.6 = (f32[312,128]{1,0:T(8,128)}, f32[312,128]{1,0:T(8,128)}, u32[]{:S(2)}, u32[]{:S(2)}) collective-permute-start(f32[312,128]{1,0:T(8,128)} %shard_map.211), channel_id=1, source_target_pairs={{0,104},{8,112},{16,120},{24,128},{32,136},{40,144},{48,152},{56,1... | collective-permute-start | bytes 479240 | tf_op jit(solution)/shard_map/ppermute | solution.py:25
  43.3 19.2 %collective-permute-start.5 = (f32[312,128]{1,0:T(8,128)}, f32[312,128]{1,0:T(8,128)}, u32[]{:S(2)}, u32[]{:S(2)}) collective-permute-start(f32[312,128]{1,0:T(8,128)} %shard_map.211), channel_id=1, source_target_pairs={{0,72},{8,80},{16,88},{24,96},{32,104},{40,112},{48,120},{56,128},... | collective-permute-start | bytes 479240 | tf_op jit(solution)/shard_map/ppermute | solution.py:25
  46.5 25.3 %collective-permute-start.4 = (f32[312,128]{1,0:T(8,128)}, f32[312,128]{1,0:T(8,128)S(1)}, u32[]{:S(2)}, u32[]{:S(2)}) collective-permute-start(f32[312,128]{1,0:T(8,128)} %shard_map.211), channel_id=1, source_target_pairs={{0,40},{8,48},{16,56},{24,64},{32,72},{40,80},{48,88},{56,96},{64,... | collective-permute-start | bytes 479240 | tf_op jit(solution)/shard_map/ppermute | solution.py:25
  55.7 23.7 %collective-permute-start.3 = (f32[312,128]{1,0:T(8,128)}, f32[312,128]{1,0:T(8,128)S(1)}, u32[]{:S(2)}, u32[]{:S(2)}) collective-permute-start(f32[312,128]{1,0:T(8,128)} %shard_map.211), channel_id=1, source_target_pairs={{0,8},{8,16},{16,24},{24,32},{32,40},{40,48},{48,56},{56,64},{64,7... | collective-permute-start | bytes 479240 | tf_op jit(solution)/shard_map/ppermute | solution.py:25
  60.8 21.8 %copy-start.1 = (bf16[32,8,8,512]{3,2,1,0:T(8,128)(2,1)S(1)}, bf16[32,8,8,512]{3,2,1,0:T(8,128)(2,1)}, u32[]{:S(2)}) copy-start(bf16[32,8,8,512]{3,2,1,0:T(8,128)(2,1)} %copy.59) | copy-start | bytes 6291460
  79.4 0.7 copy-start.8
  82.1 3.0 %copy-start.2 = (bf16[128,256]{1,0:T(8,128)(2,1)S(1)}, bf16[128,256]{1,0:T(8,128)(2,1)}, u32[]{:S(2)}) copy-start(bf16[128,256]{1,0:T(8,128)(2,1)} %param.22) | copy-start | bytes 196612
  82.5 2.8 %copy-start.21 = (f32[2,128]{1,0:T(2,128)S(1)}, f32[2,128]{1,0:T(2,128)}, u32[]{:S(2)}) copy-start(f32[2,128]{1,0:T(2,128)} %get-tuple-element.14) | copy-start | bytes 3076
  82.5 3.7 %copy-start.7 = (f32[128,128]{0,1:T(8,128)S(1)}, f32[128,128]{0,1:T(8,128)}, u32[]{:S(2)}) copy-start(f32[128,128]{0,1:T(8,128)} %copy-done.6) | copy-start | bytes 196612
  85.1 0.8 copy-start.9
  87.4 47.2 %copy-start.10 = (f32[128,2,128,1]{0,2,3,1:T(8,128)S(1)}, f32[128,2,128,1]{0,2,3,1:T(8,128)}, u32[]{:S(2)}) copy-start(f32[128,2,128,1]{0,2,3,1:T(8,128)} %copy-done.9) | copy-start | bytes 393220
  87.4 47.2 %copy-start.22 = (f32[2,128]{1,0:T(2,128)S(1)}, f32[2,128]{1,0:T(2,128)}, u32[]{:S(2)}) copy-start(f32[2,128]{1,0:T(2,128)} %get-tuple-element.14) | copy-start | bytes 3076
  88.4 7.1 %collective-permute-start.7 = (f32[312,128]{1,0:T(8,128)S(1)}, f32[312,128]{1,0:T(8,128)S(1)}, u32[]{:S(2)}, u32[]{:S(2)}) collective-permute-start(f32[312,128]{1,0:T(8,128)S(1)} %concatenate.25), channel_id=1, source_target_pairs={{8,0},{16,8},{24,16},{32,24},{40,32},{48,40},{56,48},{64,56},{72,6... | collective-permute-start | bytes 479240 | tf_op jit(solution)/shard_map/ppermute | solution.py:25
  95.6 11.2 %collective-permute-start.8 = (f32[312,128]{1,0:T(8,128)S(1)}, f32[312,128]{1,0:T(8,128)S(1)}, u32[]{:S(2)}, u32[]{:S(2)}) collective-permute-start(f32[312,128]{1,0:T(8,128)S(1)} %add_select_fusion.3), channel_id=1, source_target_pairs={{16,0},{24,8},{32,16},{40,24},{48,32},{56,40},{64,48},{72,56},{80,... | collective-permute-start | bytes 479240 | tf_op jit(solution)/shard_map/ppermute | solution.py:25
  107.0 18.7 %collective-permute-start.9 = (f32[312,128]{1,0:T(8,128)S(1)}, f32[312,128]{1,0:T(8,128)S(1)}, u32[]{:S(2)}, u32[]{:S(2)}) collective-permute-start(f32[312,128]{1,0:T(8,128)S(1)} %add_select_fusion.2), channel_id=1, source_target_pairs={{32,0},{40,8},{48,16},{56,24},{64,32},{72,40},{80,48},{88,56},{96,... | collective-permute-start | bytes 479240 | tf_op jit(solution)/shard_map/ppermute | solution.py:25
  125.8 19.7 %collective-permute-start.11 = (f32[312,128]{1,0:T(8,128)S(1)}, f32[312,128]{1,0:T(8,128)S(1)}, u32[]{:S(2)}, u32[]{:S(2)}) collective-permute-start(f32[312,128]{1,0:T(8,128)S(1)} %add_select_fusion.1), channel_id=1, source_target_pairs={{72,0},{80,8},{88,16},{96,24},{104,32},{112,40},{120,48},{128,56},... | collective-permute-start | bytes 479240 | tf_op jit(solution)/shard_map/ppermute | solution.py:25
  127.7 17.8 %collective-permute-start.10 = (f32[312,128]{1,0:T(8,128)S(1)}, f32[312,128]{1,0:T(8,128)S(1)}, u32[]{:S(2)}, u32[]{:S(2)}) collective-permute-start(f32[312,128]{1,0:T(8,128)S(1)} %add_select_fusion.1), channel_id=1, source_target_pairs={{8,0},{16,8},{24,16},{32,24},{40,32},{48,40},{56,48},{64,56},{72,6... | collective-permute-start | bytes 479240 | tf_op jit(solution)/shard_map/ppermute | solution.py:25
